TPU v7x, 512 devices: a whole 4x8x8 slice. The times are simulated.
512 devices in a mesh: dp: 32 (over x, z_lo, core), ctx: 16 (over z_hi, y).
Axes of the slice: x: 4, y: 8, z: 8 (z_hi: 2, z_lo: 4; z = z_hi * 4 + z_lo), core: 2. Of those that a mesh axis runs over, the one named last changes fastest.
Arguments:
- queries: bfloat16 [32, 16, 128, 2048], P('dp', 'ctx'), may hold values from -2.5 to 2.5
- rotated_key_rows: bfloat16 [32, 16, 128, 512], P('dp', 'ctx'), may hold values from -2.5 to 2.5
- values: bfloat16 [32, 16, 128, 512], P('dp', 'ctx'), may hold values from -6 to 6
- cotangent: bfloat16 [32, 16, 128, 2048], P('dp', 'ctx'), may hold values from -6 to 6
- hidden: bfloat16 [32, 16, 128, 4096], P('dp', 'ctx'), may hold values from -6 to 6
- adapter_down_weight: bfloat16 [4096, 16], replicated, may hold values from -0.09375 to 0.09375
- adapter_up_weight: bfloat16 [16, 512], replicated, may hold values from -1.5 to 1.5
- segment_text_length: int32 [32, 16], P('dp', 'ctx'), may hold values from 19 to 78, as said below
Outputs:
- grad_queries: bfloat16 [32, 16, 128, 2048], P('dp', 'ctx')
- grad_keys: bfloat16 [32, 16, 128, 512], P('dp', 'ctx')
- grad_values: bfloat16 [32, 16, 128, 512], P('dp', 'ctx')
- grad_down: float32 [4096, 16], replicated
- grad_up: float32 [16, 512], replicated
Inputs may be any that keep to these rules, and one draw needn't show every extreme that they name: `segment_text_length`: every log has a segment with exactly 78 text tokens and another with the fewest.
All inputs are finite; a program needn't handle non-finite values.
Results may differ from a plain program's by a relative error of at most 0.0019.
The roundings to bfloat16 on the way count: a program that leaves them out, or rounds other values in their place, can miss the bound.
Values may be sent and summed in bfloat16 or wider, within the bound.
No kernel may reach another device: no remote copies, remote signals or barrier semaphores. Data moves between devices by JAX's collectives and lax.ppermute only.
A program may use at most 64 MiB of HBM per device.

v0:
```python
import math

import jax
import jax.numpy as jnp
from jax import lax
from jax.sharding import PartitionSpec as P

HEAD_SIZE = 128
SUMM = 50


adapter_scale = 2.0


def group_grads(query_group, key_group, value_group, cot_group, key_mask):
    softmax_scale = 1.0 / math.sqrt(HEAD_SIZE)
    scores = (
        jnp.einsum("tgd,md->gtm", query_group, key_group, preferred_element_type=jnp.float32)
        * softmax_scale
    )
    unnorm = jnp.exp(jnp.where(key_mask[None], scores, -jnp.inf))
    attend = unnorm / jnp.sum(unnorm, -1, keepdims=True)
    attend_grad = jnp.einsum(
        "tgd,md->gtm", cot_group, value_group, preferred_element_type=jnp.float32
    )
    row_dot = jnp.sum(attend * attend_grad, -1, keepdims=True)
    dscore = (attend * (attend_grad - row_dot)).astype(jnp.bfloat16)
    attend_low = attend.astype(jnp.bfloat16)
    query_grad = (
        jnp.einsum("gtm,md->tgd", dscore, key_group, preferred_element_type=jnp.float32)
        * softmax_scale
    )
    key_grad = (
        jnp.einsum("gtm,tgd->md", dscore, query_group, preferred_element_type=jnp.float32)
        * softmax_scale
    )
    value_grad = jnp.einsum(
        "gtm,tgd->md", attend_low, cot_group, preferred_element_type=jnp.float32
    )
    return (query_grad, key_grad, value_grad)


def adapter_terms(hidden_piece, low_rank_piece, value_piece, adapter_up_weight):
    contract = (((0,), (0,)), ((), ()))
    backward_step = lax.dot_general(
        value_piece, adapter_up_weight, (((1,), (1,)), ((), ())), preferred_element_type=jnp.float32
    ).astype(jnp.bfloat16)
    down_part = lax.dot_general(
        hidden_piece, backward_step, contract, preferred_element_type=jnp.float32
    )
    up_part = lax.dot_general(
        low_rank_piece, value_piece, contract, preferred_element_type=jnp.float32
    )
    return (down_part, up_part)


def per_device(
    queries,
    rotated_key_rows,
    values,
    cotangent,
    hidden,
    adapter_down_weight,
    adapter_up_weight,
    segment_text_length,
):
    query_rows = queries[0, 0]
    key_local = rotated_key_rows[0, 0]
    value_local = values[0, 0]
    cot_rows = cotangent[0, 0]
    hidden_row_block = hidden[0, 0]
    length = segment_text_length[0, 0]
    position = lax.axis_index("ctx")
    segment_list = lax.axis_size("ctx")
    log_batch = lax.axis_size("dp")
    tokens = query_rows.shape[0]
    width = key_local.shape[1]
    kv_heads = width // HEAD_SIZE
    groups = query_rows.shape[1] // width
    live = length + SUMM
    rows = jnp.arange(tokens)
    cot_rows = jnp.where((rows < live)[:, None], cot_rows, jnp.zeros_like(cot_rows))
    own_keys = lax.dynamic_slice_in_dim(key_local, length, SUMM, 0)
    own_values = lax.dynamic_slice_in_dim(value_local, length, SUMM, 0)
    memory_keys, memory_values = (
        lax.all_gather(own_keys, "ctx", axis=0, tiled=True),
        lax.all_gather(own_values, "ctx", axis=0, tiled=True),
    )
    count = memory_keys.shape[0]
    memory_owner = jnp.arange(count) // SUMM
    local_mask = (rows[None, :] <= rows[:, None]) & (rows[None, :] < live)
    memory_mask = jnp.broadcast_to((memory_owner < position)[None, :], (tokens, count))
    key_mask = jnp.concatenate([memory_mask, local_mask], axis=1)
    all_keys = jnp.concatenate([memory_keys, key_local], 0)
    all_values = jnp.concatenate([memory_values, value_local], 0)
    query_parts, key_parts, value_parts = ([], [], [])
    for group in range(kv_heads):
        qcols = slice(group * groups * HEAD_SIZE, (group + 1) * groups * HEAD_SIZE)
        kcols = slice(group * HEAD_SIZE, (group + 1) * HEAD_SIZE)
        query_grad, key_grad, value_grad = group_grads(
            query_rows[:, qcols].reshape(tokens, groups, HEAD_SIZE),
            all_keys[:, kcols],
            all_values[:, kcols],
            cot_rows[:, qcols].reshape(tokens, groups, HEAD_SIZE),
            key_mask,
        )
        query_parts.append(query_grad.reshape(tokens, groups * HEAD_SIZE))
        key_parts.append(key_grad)
        value_parts.append(value_grad)
    query_out = jnp.concatenate(query_parts, 1).astype(jnp.bfloat16)
    key_grad = jnp.concatenate(key_parts, 1)
    value_grad = jnp.concatenate(value_parts, 1)
    memory_key_grad, local_key = (key_grad[:count], key_grad[count:])
    memory_value_grad, local_value = (value_grad[:count], value_grad[count:])
    back_key, back_value = (
        lax.psum_scatter(memory_key_grad, "ctx", scatter_dimension=0, tiled=True),
        lax.psum_scatter(memory_value_grad, "ctx", scatter_dimension=0, tiled=True),
    )
    key_out = (
        local_key + lax.dynamic_update_slice_in_dim(jnp.zeros_like(local_key), back_key, length, 0)
    ).astype(jnp.bfloat16)
    value_result = (
        local_value
        + lax.dynamic_update_slice_in_dim(jnp.zeros_like(local_value), back_value, length, 0)
    ).astype(jnp.bfloat16)
    low_rank_rows = jnp.dot(
        hidden_row_block, adapter_down_weight, preferred_element_type=jnp.float32
    ).astype(jnp.bfloat16)
    down_sum, up_sum = lax.psum(
        adapter_terms(hidden_row_block, low_rank_rows, value_result, adapter_up_weight),
        ("dp", "ctx"),
    )
    adapter_factor = adapter_scale / (log_batch * segment_list)
    return (
        query_out[None, None],
        key_out[None, None],
        value_result[None, None],
        down_sum * adapter_factor,
        up_sum * adapter_factor,
    )


def solution(mesh):
    placed = (
        P("dp", "ctx", None, None),
        P("dp", "ctx", None, None),
        P("dp", "ctx", None, None),
        P("dp", "ctx", None, None),
        P("dp", "ctx", None, None),
        P(),
        P(),
        P("dp", "ctx"),
    )
    return jax.shard_map(
        per_device,
        mesh=mesh,
        in_specs=placed,
        out_specs=(
            P("dp", "ctx", None, None),
            P("dp", "ctx", None, None),
            P("dp", "ctx", None, None),
            P(),
            P(),
        ),
        check_vma=False,
    )
```

profile of v0, /device:TPU:1, one launch (start us, length us, event | category | flops | bytes accessed | tf_op | source)
XLA Modules:
  0.0 690.6 jit_solution(10573385685993678899)
XLA Ops:
  12.5 67.7 %all-gather.1 = bf16[1,1,800,512]{3,1,0,2:T(2,128)(2,1)S(1)} all-gather(bf16[1,1,50,512]{3,1,0,2:T(2,128)(2,1)S(1)} %copy.106), channel_id=3, replica_groups=mesh['dp'=32,'ctx'=16] {'ctx'}, dimensions={2}, use_global_device_ids=true | all-gather | bytes 870400 | tf_op jit(solution)/shard_map/all_gather | solution.py:87
  80.5 56.6 %all-gather = bf16[1,1,800,512]{3,1,0,2:T(2,128)(2,1)S(1)} all-gather(bf16[1,1,50,512]{3,1,0,2:T(2,128)(2,1)S(1)} %copy.105), channel_id=2, replica_groups=mesh['dp'=32,'ctx'=16] {'ctx'}, dimensions={2}, use_global_device_ids=true | all-gather | bytes 870400 | tf_op jit(solution)/shard_map/all_gather | solution.py:86
  137.3 1.7 fusion.48
  138.9 1.6 fusion.52
  140.6 1.7 fusion.61
  142.3 1.6 fusion.44
  144.2 3.7 fusion.6
  147.9 2.1 convolution_bitcast_fusion.2
  150.0 1.8 fusion.8
  154.0 4.1 fusion.2
  158.1 2.9 convolution_bitcast_fusion.1
  161.0 1.8 fusion.4
  164.1 4.3 fusion.10
  168.4 2.9 convolution_bitcast_fusion.3
  171.3 1.8 fusion.12
  175.2 4.2 fusion.14
  179.5 2.1 convolution_bitcast_fusion.4
  181.6 2.0 fusion.16
  185.1 1.9 pad_maximum_fusion
  187.0 84.3 %fusion.89 = (f32[56,512]{1,0:T(8,128)}, f32[56,512]{1,0:T(8,128)}) fusion(f32[800,512]{1,0:T(8,128)} %get-tuple-element.26, f32[800,512]{1,0:T(8,128)} %get-tuple-element.25), kind=kCustom, calls=%all-reduce-scatter.2 | all-reduce-scatter fusion | flops 917505 | bytes 3508224
  271.3 2.1 collective-permute-start.2
  274.9 1.9 collective-permute-start.3
  276.8 1.9 collective-permute-start
  280.3 1.9 collective-permute-start.1
  282.2 2.2 fusion.24
  290.2 1.7 copy.75
  293.8 1.8 pad_maximum_fusion.6
  295.7 2.8 concatenate.44
  300.0 2.8 concatenate.45
  304.8 113.9 %psum.15 = f32[16,512]{1,0:T(8,128)S(1)} all-reduce(f32[16,512]{1,0:T(8,128)S(1)} %fusion.26), channel_id=1, replica_groups=mesh['dp'=32,'ctx'=16] {'dp','ctx'}, use_global_device_ids=true, to_apply=%region_11.12 | all-reduce | flops 8192 | bytes 65536 | tf_op jit(solution)/shard_map/psum | solution.py:129
  420.5 261.6 %all-reduce.7.cloned.1.call-done = f32[4096,16]{0,1:T(8,128)} async-done(((f32[4096,16]{0,1:T(8,128)}), f32[4096,16]{0,1:T(8,128)}) %all-reduce.7.cloned.1.call-update) | async-done | bytes 262160 | tf_op jit(solution)/shard_map/psum | solution.py:129
  682.1 1.7 broadcast_multiply_fusion
  (131 shorter events, 27.3 us)
Async XLA Ops:
  7.2 297.1 %copy-start = (bf16[1,1,128,4096]{3,2,1,0:T(8,128)(2,1)S(1)}, bf16[1,1,128,4096]{3,2,1,0:T(8,128)(2,1)}, u32[]{:S(2)}) copy-start(bf16[1,1,128,4096]{3,2,1,0:T(8,128)(2,1)} %param.12) | copy-start | bytes 3145732
  7.2 4.9 copy-start.31
  7.2 674.9 %all-reduce.7.cloned.1.call-start = ((), (), s32[]{:S(2)}) async-start(), calls=%async_computation | async-start | bytes 524288 | tf_op jit(solution)/shard_map/psum | solution.py:129
  12.1 141.9 %copy-start.34 = (bf16[128,512]{0,1:T(8,128)(2,1)}, bf16[128,512]{0,1:T(8,128)(2,1)S(1)}, u32[]{:S(2)}) copy-start(bf16[128,512]{0,1:T(8,128)(2,1)S(1)} %get-tuple-element.14) | copy-start | bytes 393220
  12.5 126.5 %copy-start.26 = (bf16[128,512]{0,1:T(8,128)(2,1)}, bf16[128,512]{0,1:T(8,128)(2,1)S(1)}, u32[]{:S(2)}) copy-start(bf16[128,512]{0,1:T(8,128)(2,1)S(1)} %get-tuple-element.12) | copy-start | bytes 393220
  80.4 56.8 %copy-start.24 = (bf16[1,1,128,512]{3,2,1,0:T(8,128)(2,1)S(1)}, bf16[1,1,128,512]{3,2,1,0:T(8,128)(2,1)}, u32[]{:S(2)}) copy-start(bf16[1,1,128,512]{3,2,1,0:T(8,128)(2,1)} %param.10) | copy-start | bytes 393220
  144.1 9.9 %copy-start.37 = (pred[128,928]{0,1:T(8,128)(4,1)}, pred[128,928]{0,1:T(8,128)(4,1)S(1)}, u32[]{:S(2)}) copy-start(pred[128,928]{0,1:T(8,128)(4,1)S(1)} %pad_add_fusion) | copy-start | bytes 356356
  144.2 9.9 %copy-start.27 = (bf16[928,128,1]{1,0,2:T(8,128)(2,1)}, bf16[928,128,1]{1,0,2:T(8,128)(2,1)S(1)}, u32[]{:S(2)}) copy-start(bf16[928,128,1]{1,0,2:T(8,128)(2,1)S(1)} %fusion.64) | copy-start | bytes 712708
  158.1 2.9 copy-start.8
  158.1 2.9 copy-start.40
  168.4 2.9 copy-start.7
  168.4 2.9 copy-start.41
  171.2 2.8 copy-start.33
  179.5 2.1 copy-start.39
  181.5 3.5 copy-start.14
  181.6 3.1 copy-start.32
  181.6 3.5 copy-start.10
  181.6 3.5 copy-start.12
  181.6 3.5 copy-start.16
  181.6 3.5 copy-start.18
  181.6 3.5 copy-start.20
  271.3 13.0 %copy-start.28 = (bf16[928,128,1]{1,0,2:T(8,128)(2,1)S(1)}, bf16[928,128,1]{1,0,2:T(8,128)(2,1)}, u32[]{:S(2)}) copy-start(bf16[928,128,1]{1,0,2:T(8,128)(2,1)} %copy-done.27) | copy-start | bytes 712708
  271.3 14.0 %copy-start.3 = (bf16[4,128,928]{1,2,0:T(8,128)(2,1)S(1)}, bf16[4,128,928]{1,2,0:T(8,128)(2,1)}, u32[]{:S(2)}) copy-start(bf16[4,128,928]{1,2,0:T(8,128)(2,1)} %copy-done.2) | copy-start | bytes 2850820
  271.3 28.7 %collective-permute-start.2 = (f32[56,512]{1,0:T(8,128)}, f32[56,512]{1,0:T(8,128)}, u32[]{:S(2)}, u32[]{:S(2)}) collective-permute-start(f32[56,512]{1,0:T(8,128)} %get-tuple-element.8), channel_id=1, source_target_pairs={{0,1},{1,2},{2,3},{3,4},{4,5},{5,6},{6,7},{7,8},{8,9},{9,10},{10,1... | collective-permute-start | bytes 344072
  274.9 25.1 %collective-permute-start.3 = (f32[34,512]{1,0:T(8,128)}, f32[34,512]{1,0:T(8,128)}, u32[]{:S(2)}, u32[]{:S(2)}) collective-permute-start(f32[34,512]{1,0:T(8,128)} %slice.107), channel_id=1, source_target_pairs={{0,2},{1,3},{2,4},{3,5},{4,6},{5,7},{6,8},{7,9},{8,10},{9,11},{10,... | collective-permute-start | bytes 208904
  276.8 18.9 %collective-permute-start = (f32[56,512]{1,0:T(8,128)}, f32[56,512]{1,0:T(8,128)}, u32[]{:S(2)}, u32[]{:S(2)}) collective-permute-start(f32[56,512]{1,0:T(8,128)} %get-tuple-element.7), channel_id=1, source_target_pairs={{0,1},{1,2},{2,3},{3,4},{4,5},{5,6},{6,7},{7,8},{8,9},{9,10},{10,1... | collective-permute-start | bytes 344072
  280.3 15.4 %collective-permute-start.1 = (f32[34,512]{1,0:T(8,128)}, f32[34,512]{1,0:T(8,128)}, u32[]{:S(2)}, u32[]{:S(2)}) collective-permute-start(f32[34,512]{1,0:T(8,128)} %slice.106), channel_id=1, source_target_pairs={{0,2},{1,3},{2,4},{3,5},{4,6},{5,7},{6,8},{7,9},{8,10},{9,11},{10,... | collective-permute-start | bytes 208904
  287.4 8.2 %copy-start.11 = (f32[928,128]{1,0:T(8,128)S(1)}, f32[928,128]{1,0:T(8,128)}, u32[]{:S(2)}) copy-start(f32[928,128]{1,0:T(8,128)} %convolution_bitcast_fusion.1) | copy-start | bytes 1425412
  287.5 8.2 %copy-start.13 = (f32[928,128]{1,0:T(8,128)S(1)}, f32[928,128]{1,0:T(8,128)}, u32[]{:S(2)}) copy-start(f32[928,128]{1,0:T(8,128)} %convolution_bitcast_fusion.3) | copy-start | bytes 1425412
  287.5 8.2 %copy-start.15 = (f32[928,128]{1,0:T(8,128)S(1)}, f32[928,128]{1,0:T(8,128)}, u32[]{:S(2)}) copy-start(f32[928,128]{1,0:T(8,128)} %copy-done.14) | copy-start | bytes 1425412
  295.7 8.6 %copy-start.36 = (bf16[4096,16]{0,1:T(8,128)(2,1)S(1)}, bf16[4096,16]{0,1:T(8,128)(2,1)}, u32[]{:S(2)}) copy-start(bf16[4096,16]{0,1:T(8,128)(2,1)} %param.13) | copy-start | bytes 393220
  298.6 120.1 %copy-start.38 = (bf16[16,512]{1,0:T(8,128)(2,1)S(1)}, bf16[16,512]{1,0:T(8,128)(2,1)}, u32[]{:S(2)}) copy-start(bf16[16,512]{1,0:T(8,128)(2,1)} %param.14) | copy-start | bytes 49156
  (15 other events, 25.4 us)
Sparse Core Ops, SparseCore 0:
  420.0 262.0 all-reduce.6
where the time goes:
time: 692 us; the launch traced here: 691 us
  blocking collectives  323 us (47%)
  waiting for transfers between devices  262 us (38%)
  matrix products  43.7 us (6%)
  local copies, waits for them, and re-layouts  23.5 us (3%)
  between operations  16 us (2%)
  other arithmetic  15.3 us (2%)
  starting transfers between devices  7.85 us (1%)
    psum x1, waiting for transfers between devices, per_device(): lax.psum(adapter_terms(hidden_row_block, low_rank_rows, value_result, ada...  262 us
    psum x1, blocking collectives, per_device(): lax.psum(adapter_terms(hidden_row_block, low_rank_rows, value_result, ada...  114 us
    unnamed x1, blocking collectives  84.3 us
    all_gather x1, blocking collectives, per_device(): lax.all_gather(own_values, 'ctx', axis=0, tiled=True)  67.7 us
    all_gather x1, blocking collectives, per_device(): lax.all_gather(own_keys, 'ctx', axis=0, tiled=True)  56.6 us
    div x4, matrix products, group_grads(): attend = unnorm / jnp.sum(unnorm, -1, keepdims=True)  16.4 us
    unnamed x95, local copies, waits for them, and re-layouts  16.1 us
  transfers between devices with their start and end apart: 5, of which 1 were waited for; matrix products, arithmetic and copies ran while one was open for 3% of the time, Pallas kernels for 0%

commit v1 on v0

--- a/solution.py
+++ b/solution.py
@@ -45,13 +45,24 @@
     backward_step = lax.dot_general(
         value_piece, adapter_up_weight, (((1,), (1,)), ((), ())), preferred_element_type=jnp.float32
     ).astype(jnp.bfloat16)
-    down_part = lax.dot_general(
-        hidden_piece, backward_step, contract, preferred_element_type=jnp.float32
+    down_part_t = lax.dot_general(
+        backward_step, hidden_piece, contract, preferred_element_type=jnp.float32
     )
     up_part = lax.dot_general(
         low_rank_piece, value_piece, contract, preferred_element_type=jnp.float32
     )
-    return (down_part, up_part)
+    return jnp.concatenate([down_part_t, up_part], 1)
+
+
+def butterfly_sum(x, axis):
+    n = lax.axis_size(axis)
+    if n & (n - 1):
+        return lax.psum(x, axis)
+    k = 1
+    while k < n:
+        x = x + lax.ppermute(x, axis, [(i, i ^ k) for i in range(n)])
+        k *= 2
+    return x
 
 
 def per_device(
@@ -82,10 +93,17 @@
     cot_rows = jnp.where((rows < live)[:, None], cot_rows, jnp.zeros_like(cot_rows))
     own_keys = lax.dynamic_slice_in_dim(key_local, length, SUMM, 0)
     own_values = lax.dynamic_slice_in_dim(value_local, length, SUMM, 0)
-    memory_keys, memory_values = (
-        lax.all_gather(own_keys, "ctx", axis=0, tiled=True),
-        lax.all_gather(own_values, "ctx", axis=0, tiled=True),
+    own_summary = jnp.concatenate([own_keys, own_values], 0)
+    pieces = [own_summary] + [
+        lax.ppermute(own_summary, "ctx", [(i, i + k) for i in range(segment_list - k)])
+        for k in range(1, segment_list)
+    ]
+    slot_of_segment = (position - jnp.arange(segment_list)) % segment_list
+    gathered = jnp.take(jnp.stack(pieces), slot_of_segment, axis=0).reshape(
+        segment_list, 2, SUMM, width
     )
+    memory_keys = gathered[:, 0].reshape(segment_list * SUMM, width)
+    memory_values = gathered[:, 1].reshape(segment_list * SUMM, width)
     count = memory_keys.shape[0]
     memory_owner = jnp.arange(count) // SUMM
     local_mask = (rows[None, :] <= rows[:, None]) & (rows[None, :] < live)
@@ -126,11 +144,12 @@
     low_rank_rows = jnp.dot(
         hidden_row_block, adapter_down_weight, preferred_element_type=jnp.float32
     ).astype(jnp.bfloat16)
-    down_sum, up_sum = lax.psum(
-        adapter_terms(hidden_row_block, low_rank_rows, value_result, adapter_up_weight),
-        ("dp", "ctx"),
-    )
+    packed = adapter_terms(hidden_row_block, low_rank_rows, value_result, adapter_up_weight)
+    packed = butterfly_sum(butterfly_sum(packed, "dp"), "ctx")
+    model_width = hidden_row_block.shape[1]
     adapter_factor = adapter_scale / (log_batch * segment_list)
+    down_sum = packed[:, :model_width].T
+    up_sum = packed[:, model_width:]
     return (
         query_out[None, None],
         key_out[None, None],

time: 692 us -> 434 us (0.63)
  the two profiles are of different devices: /device:TPU:1 before, /device:TPU:8 now
where the time goes in v1:
time: 434 us; the launch traced here: 432 us
  starting transfers between devices  160 us (37%)
  waiting for transfers between devices  85.8 us (20%)
  blocking collectives  84 us (19%)
  matrix products  40.7 us (9%)
  local copies, waits for them, and re-layouts  38.9 us (9%)
  other arithmetic  20.3 us (5%)
    ppermute x15, starting transfers between devices, per_device(): lax.ppermute(own_summary, 'ctx', [(i, i + k) for i in range(segment_list...  106 us
    unnamed x1, blocking collectives  84 us
    ppermute x9, waiting for transfers between devices, butterfly_sum(): x = x + lax.ppermute(x, axis, [(i, i ^ k) for i in range(n)])  56.5 us
    ppermute x9, starting transfers between devices, butterfly_sum(): x = x + lax.ppermute(x, axis, [(i, i ^ k) for i in range(n)])  43.6 us
    ppermute x15, waiting for transfers between devices, per_device(): lax.ppermute(own_summary, 'ctx', [(i, i + k) for i in range(segment_list...  24.1 us
    unnamed x99, local copies, waits for them, and re-layouts  21.3 us
    div x4, matrix products, group_grads(): attend = unnorm / jnp.sum(unnorm, -1, keepdims=True)  14.4 us
    dot_general x4, matrix products, group_grads(): jnp.einsum('gtm,tgd->md', attend_low, cot_group, preferred_element_type=j...  10.6 us
  transfers between devices with their start and end apart: 28, of which 19 were waited for; matrix products, arithmetic and copies ran while one was open for 8% of the time, Pallas kernels for 0%

profile of v1, /device:TPU:8, one launch (start us, length us, event | category | flops | bytes accessed | tf_op | source)
XLA Modules:
  0.0 432.2 jit_solution(9572890031063401210)
XLA Ops:
  3.0 13.7 %collective-permute-start.13 = (bf16[100,512]{1,0:T(8,128)(2,1)S(1)}, bf16[100,512]{1,0:T(8,128)(2,1)S(1)}, u32[]{:S(2)}, u32[]{:S(2)}) collective-permute-start(bf16[100,512]{1,0:T(8,128)(2,1)S(1)} %get-tuple-element.10), channel_id=1, source_target_pairs={{0,14},{1,15},{16,30},{17,31},{32,46},{33,47},{48,62},{49,63},{64,... | collective-permute-start | bytes 307208 | tf_op jit(solution)/shard_map/ppermute | solution.py:98
  21.6 3.2 collective-permute-start
  30.2 8.8 %collective-permute-start.1 = (bf16[100,512]{1,0:T(8,128)(2,1)S(1)}, bf16[100,512]{1,0:T(8,128)(2,1)S(1)}, u32[]{:S(2)}, u32[]{:S(2)}) collective-permute-start(bf16[100,512]{1,0:T(8,128)(2,1)S(1)} %get-tuple-element.10), channel_id=1, source_target_pairs={{0,2},{1,3},{2,4},{3,5},{4,6},{5,7},{6,8},{7,9},{8,10},{9,11},{10,... | collective-permute-start | bytes 307208 | tf_op jit(solution)/shard_map/ppermute | solution.py:98
  39.7 5.0 %collective-permute-done.1 = bf16[100,512]{1,0:T(8,128)(2,1)S(1)} collective-permute-done((bf16[100,512]{1,0:T(8,128)(2,1)S(1)}, bf16[100,512]{1,0:T(8,128)(2,1)S(1)}, u32[]{:S(2)}, u32[]{:S(2)}) %collective-permute-start.1) | collective-permute-done | bytes 102432 | tf_op jit(solution)/shard_map/ppermute | solution.py:98
  44.6 7.5 %collective-permute-start.2 = (bf16[100,512]{1,0:T(8,128)(2,1)S(1)}, bf16[100,512]{1,0:T(8,128)(2,1)S(1)}, u32[]{:S(2)}, u32[]{:S(2)}) collective-permute-start(bf16[100,512]{1,0:T(8,128)(2,1)S(1)} %get-tuple-element.10), channel_id=1, source_target_pairs={{0,3},{1,4},{2,5},{3,6},{4,7},{5,8},{6,9},{7,10},{8,11},{9,12},{10... | collective-permute-start | bytes 307208 | tf_op jit(solution)/shard_map/ppermute | solution.py:98
  60.4 10.6 %collective-permute-start.4 = (bf16[100,512]{1,0:T(8,128)(2,1)S(1)}, bf16[100,512]{1,0:T(8,128)(2,1)S(1)}, u32[]{:S(2)}, u32[]{:S(2)}) collective-permute-start(bf16[100,512]{1,0:T(8,128)(2,1)S(1)} %get-tuple-element.10), channel_id=1, source_target_pairs={{0,5},{1,6},{2,7},{3,8},{4,9},{5,10},{6,11},{7,12},{8,13},{9,14},{... | collective-permute-start | bytes 307208 | tf_op jit(solution)/shard_map/ppermute | solution.py:98
  71.7 3.5 collective-permute-done.4
  75.1 4.1 collective-permute-start.5
  82.6 21.4 %collective-permute-start.6 = (bf16[100,512]{1,0:T(8,128)(2,1)S(1)}, bf16[100,512]{1,0:T(8,128)(2,1)S(1)}, u32[]{:S(2)}, u32[]{:S(2)}) collective-permute-start(bf16[100,512]{1,0:T(8,128)(2,1)S(1)} %get-tuple-element.10), channel_id=1, source_target_pairs={{0,7},{1,8},{2,9},{3,10},{4,11},{5,12},{6,13},{7,14},{8,15},{16,23... | collective-permute-start | bytes 307208 | tf_op jit(solution)/shard_map/ppermute | solution.py:98
  106.2 12.9 %collective-permute-start.7 = (bf16[100,512]{1,0:T(8,128)(2,1)S(1)}, bf16[100,512]{1,0:T(8,128)(2,1)S(1)}, u32[]{:S(2)}, u32[]{:S(2)}) collective-permute-start(bf16[100,512]{1,0:T(8,128)(2,1)S(1)} %get-tuple-element.10), channel_id=1, source_target_pairs={{0,8},{1,9},{2,10},{3,11},{4,12},{5,13},{6,14},{7,15},{16,24},{17,... | collective-permute-start | bytes 307208 | tf_op jit(solution)/shard_map/ppermute | solution.py:98
  121.4 5.5 %collective-permute-start.8 = (bf16[100,512]{1,0:T(8,128)(2,1)S(1)}, bf16[100,512]{1,0:T(8,128)(2,1)S(1)}, u32[]{:S(2)}, u32[]{:S(2)}) collective-permute-start(bf16[100,512]{1,0:T(8,128)(2,1)S(1)} %get-tuple-element.10), channel_id=1, source_target_pairs={{0,9},{1,10},{2,11},{3,12},{4,13},{5,14},{6,15},{16,25},{17,26},{1... | collective-permute-start | bytes 307208 | tf_op jit(solution)/shard_map/ppermute | solution.py:98
  129.7 10.9 %collective-permute-start.9 = (bf16[100,512]{1,0:T(8,128)(2,1)S(1)}, bf16[100,512]{1,0:T(8,128)(2,1)S(1)}, u32[]{:S(2)}, u32[]{:S(2)}) collective-permute-start(bf16[100,512]{1,0:T(8,128)(2,1)S(1)} %get-tuple-element.10), channel_id=1, source_target_pairs={{0,10},{1,11},{2,12},{3,13},{4,14},{5,15},{16,26},{17,27},{18,28},... | collective-permute-start | bytes 307208 | tf_op jit(solution)/shard_map/ppermute | solution.py:98
  163.7 3.8 fusion.6
  174.4 3.6 fusion.2
  184.8 3.6 fusion.10
  195.2 3.5 fusion.14
  206.1 84.0 %fusion.95 = (f32[56,512]{1,0:T(8,128)}, f32[56,512]{1,0:T(8,128)}) fusion(f32[800,512]{1,0:T(8,128)S(1)} %pad_maximum_fusion.3, f32[800,512]{1,0:T(8,128)} %pad_maximum_fusion), kind=kCustom, calls=%all-reduce-scatter.2 | all-reduce-scatter fusion | flops 917505 | bytes 3508224
  296.4 4.3 %collective-permute-done.26 = f32[56,512]{1,0:T(8,128)S(1)} collective-permute-done((f32[56,512]{1,0:T(8,128)}, f32[56,512]{1,0:T(8,128)S(1)}, u32[]{:S(2)}, u32[]{:S(2)}) %collective-permute-start.26) | collective-permute-done | bytes 114720
  308.6 9.0 %collective-permute-done.16 = f32[16,4608]{1,0:T(8,128)S(1)} collective-permute-done((f32[16,4608]{1,0:T(8,128)S(1)}, f32[16,4608]{1,0:T(8,128)S(1)}, u32[]{:S(2)}, u32[]{:S(2)}) %collective-permute-start.16) | collective-permute-done | bytes 294944 | tf_op jit(solution)/shard_map/ppermute | solution.py:63
  317.6 5.7 %collective-permute-start.17 = (f32[16,4608]{1,0:T(8,128)S(1)}, f32[16,4608]{1,0:T(8,128)S(1)}, u32[]{:S(2)}, u32[]{:S(2)}) collective-permute-start(f32[16,4608]{1,0:T(8,128)S(1)} %add.94), channel_id=1, source_target_pairs={{0,64},{16,80},{32,96},{48,112},{64,0},{80,16},{96,32},{112,48},{1... | collective-permute-start | bytes 884744 | tf_op jit(solution)/shard_map/ppermute | solution.py:63
  323.3 12.8 %collective-permute-done.17 = f32[16,4608]{1,0:T(8,128)S(1)} collective-permute-done((f32[16,4608]{1,0:T(8,128)S(1)}, f32[16,4608]{1,0:T(8,128)S(1)}, u32[]{:S(2)}, u32[]{:S(2)}) %collective-permute-start.17) | collective-permute-done | bytes 294944 | tf_op jit(solution)/shard_map/ppermute | solution.py:63
  336.2 5.5 %collective-permute-start.18 = (f32[16,4608]{1,0:T(8,128)S(1)}, f32[16,4608]{1,0:T(8,128)S(1)}, u32[]{:S(2)}, u32[]{:S(2)}) collective-permute-start(f32[16,4608]{1,0:T(8,128)S(1)} %add.95), channel_id=1, source_target_pairs={{0,128},{16,144},{32,160},{48,176},{64,192},{80,208},{96,224},{112... | collective-permute-start | bytes 884744 | tf_op jit(solution)/shard_map/ppermute | solution.py:63
  341.6 7.1 %collective-permute-done.18 = f32[16,4608]{1,0:T(8,128)S(1)} collective-permute-done((f32[16,4608]{1,0:T(8,128)S(1)}, f32[16,4608]{1,0:T(8,128)S(1)}, u32[]{:S(2)}, u32[]{:S(2)}) %collective-permute-start.18) | collective-permute-done | bytes 294944 | tf_op jit(solution)/shard_map/ppermute | solution.py:63
  348.8 4.6 %collective-permute-start.19 = (f32[16,4608]{1,0:T(8,128)S(1)}, f32[16,4608]{1,0:T(8,128)S(1)}, u32[]{:S(2)}, u32[]{:S(2)}) collective-permute-start(f32[16,4608]{1,0:T(8,128)S(1)} %add.96), channel_id=1, source_target_pairs={{0,256},{16,272},{32,288},{48,304},{64,320},{80,336},{96,352},{112... | collective-permute-start | bytes 884744 | tf_op jit(solution)/shard_map/ppermute | solution.py:63
  354.5 6.1 %collective-permute-done.19 = f32[16,4608]{1,0:T(8,128)S(1)} collective-permute-done((f32[16,4608]{1,0:T(8,128)S(1)}, f32[16,4608]{1,0:T(8,128)S(1)}, u32[]{:S(2)}, u32[]{:S(2)}) %collective-permute-start.19) | collective-permute-done | bytes 294944 | tf_op jit(solution)/shard_map/ppermute | solution.py:63
  365.2 4.8 %collective-permute-done.20 = f32[16,4608]{1,0:T(8,128)S(1)} collective-permute-done((f32[16,4608]{1,0:T(8,128)S(1)}, f32[16,4608]{1,0:T(8,128)S(1)}, u32[]{:S(2)}, u32[]{:S(2)}) %collective-permute-start.20) | collective-permute-done | bytes 294944 | tf_op jit(solution)/shard_map/ppermute | solution.py:63
  370.8 3.7 collective-permute-start.21
  384.7 4.5 %collective-permute-start.25 = (f32[34,512]{1,0:T(8,128)}, f32[34,512]{1,0:T(8,128)S(1)}, u32[]{:S(2)}, u32[]{:S(2)}) collective-permute-start(f32[34,512]{1,0:T(8,128)} %slice.128), channel_id=1, source_target_pairs={{0,2},{1,3},{2,4},{3,5},{4,6},{5,7},{6,8},{7,9},{8,10},{9,11},{10,... | collective-permute-start | bytes 208904
  392.9 8.6 %collective-permute-start.22 = (f32[16,4608]{1,0:T(8,128)}, f32[16,4608]{1,0:T(8,128)}, u32[]{:S(2)}, u32[]{:S(2)}) collective-permute-start(f32[16,4608]{1,0:T(8,128)} %add.99), channel_id=1, source_target_pairs={{0,4},{1,5},{2,6},{3,7},{4,0},{5,1},{6,2},{7,3},{8,12},{9,13},{10,... | collective-permute-start | bytes 884744 | tf_op jit(solution)/shard_map/ppermute | solution.py:63
  404.2 8.4 %collective-permute-done.22 = f32[16,4608]{1,0:T(8,128)} collective-permute-done((f32[16,4608]{1,0:T(8,128)}, f32[16,4608]{1,0:T(8,128)}, u32[]{:S(2)}, u32[]{:S(2)}) %collective-permute-start.22) | collective-permute-done | bytes 294944 | tf_op jit(solution)/shard_map/ppermute | solution.py:63
  413.7 8.9 %collective-permute-start.23 = (f32[16,4608]{1,0:T(8,128)S(1)}, f32[16,4608]{1,0:T(8,128)S(1)}, u32[]{:S(2)}, u32[]{:S(2)}) collective-permute-start(f32[16,4608]{1,0:T(8,128)S(1)} %add.100), channel_id=1, source_target_pairs={{0,8},{1,9},{2,10},{3,11},{4,12},{5,13},{6,14},{7,15},{8,0},{9,1},... | collective-permute-start | bytes 884744 | tf_op jit(solution)/shard_map/ppermute | solution.py:63
  424.1 6.7 %collective-permute-done.23 = f32[16,4608]{1,0:T(8,128)S(1)} collective-permute-done((f32[16,4608]{1,0:T(8,128)S(1)}, f32[16,4608]{1,0:T(8,128)S(1)}, u32[]{:S(2)}, u32[]{:S(2)}) %collective-permute-start.23) | collective-permute-done | bytes 294944 | tf_op jit(solution)/shard_map/ppermute | solution.py:63
  (200 shorter events, 123.1 us)
Async XLA Ops:
  0.6 301.3 %copy-start = (bf16[1,1,128,4096]{3,2,1,0:T(8,128)(2,1)S(1)}, bf16[1,1,128,4096]{3,2,1,0:T(8,128)(2,1)}, u32[]{:S(2)}) copy-start(bf16[1,1,128,4096]{3,2,1,0:T(8,128)(2,1)} %param.12) | copy-start | bytes 3145732
  3.0 144.0 %collective-permute-start.13 = (bf16[100,512]{1,0:T(8,128)(2,1)S(1)}, bf16[100,512]{1,0:T(8,128)(2,1)S(1)}, u32[]{:S(2)}, u32[]{:S(2)}) collective-permute-start(bf16[100,512]{1,0:T(8,128)(2,1)S(1)} %get-tuple-element.10), channel_id=1, source_target_pairs={{0,14},{1,15},{16,30},{17,31},{32,46},{33,47},{48,62},{49,63},{64,... | collective-permute-start | bytes 307208 | tf_op jit(solution)/shard_map/ppermute | solution.py:98
  16.7 129.7 %collective-permute-start.12 = (bf16[100,512]{1,0:T(8,128)(2,1)S(1)}, bf16[100,512]{1,0:T(8,128)(2,1)S(1)}, u32[]{:S(2)}, u32[]{:S(2)}) collective-permute-start(bf16[100,512]{1,0:T(8,128)(2,1)S(1)} %get-tuple-element.10), channel_id=1, source_target_pairs={{0,13},{1,14},{2,15},{16,29},{17,30},{18,31},{32,45},{33,46},{34,4... | collective-permute-start | bytes 307208 | tf_op jit(solution)/shard_map/ppermute | solution.py:98
  18.8 127.0 %collective-permute-start.11 = (bf16[100,512]{1,0:T(8,128)(2,1)S(1)}, bf16[100,512]{1,0:T(8,128)(2,1)S(1)}, u32[]{:S(2)}, u32[]{:S(2)}) collective-permute-start(bf16[100,512]{1,0:T(8,128)(2,1)S(1)} %get-tuple-element.10), channel_id=1, source_target_pairs={{0,12},{1,13},{2,14},{3,15},{16,28},{17,29},{18,30},{19,31},{32,44... | collective-permute-start | bytes 307208 | tf_op jit(solution)/shard_map/ppermute | solution.py:98
  20.3 124.8 %collective-permute-start.10 = (bf16[100,512]{1,0:T(8,128)(2,1)S(1)}, bf16[100,512]{1,0:T(8,128)(2,1)S(1)}, u32[]{:S(2)}, u32[]{:S(2)}) collective-permute-start(bf16[100,512]{1,0:T(8,128)(2,1)S(1)} %get-tuple-element.10), channel_id=1, source_target_pairs={{0,11},{1,12},{2,13},{3,14},{4,15},{16,27},{17,28},{18,29},{19,30}... | collective-permute-start | bytes 307208 | tf_op jit(solution)/shard_map/ppermute | solution.py:98
  21.6 8.6 %collective-permute-start = (bf16[100,512]{1,0:T(8,128)(2,1)S(1)}, bf16[100,512]{1,0:T(8,128)(2,1)S(1)}, u32[]{:S(2)}, u32[]{:S(2)}) collective-permute-start(bf16[100,512]{1,0:T(8,128)(2,1)S(1)} %get-tuple-element.10), channel_id=1, source_target_pairs={{0,1},{1,2},{2,3},{3,4},{4,5},{5,6},{6,7},{7,8},{8,9},{9,10},{10,1... | collective-permute-start | bytes 307208 | tf_op jit(solution)/shard_map/ppermute | solution.py:98
  30.2 14.4 %collective-permute-start.1 = (bf16[100,512]{1,0:T(8,128)(2,1)S(1)}, bf16[100,512]{1,0:T(8,128)(2,1)S(1)}, u32[]{:S(2)}, u32[]{:S(2)}) collective-permute-start(bf16[100,512]{1,0:T(8,128)(2,1)S(1)} %get-tuple-element.10), channel_id=1, source_target_pairs={{0,2},{1,3},{2,4},{3,5},{4,6},{5,7},{6,8},{7,9},{8,10},{9,11},{10,... | collective-permute-start | bytes 307208 | tf_op jit(solution)/shard_map/ppermute | solution.py:98
  44.6 10.5 %collective-permute-start.2 = (bf16[100,512]{1,0:T(8,128)(2,1)S(1)}, bf16[100,512]{1,0:T(8,128)(2,1)S(1)}, u32[]{:S(2)}, u32[]{:S(2)}) collective-permute-start(bf16[100,512]{1,0:T(8,128)(2,1)S(1)} %get-tuple-element.10), channel_id=1, source_target_pairs={{0,3},{1,4},{2,5},{3,6},{4,7},{5,8},{6,9},{7,10},{8,11},{9,12},{10... | collective-permute-start | bytes 307208 | tf_op jit(solution)/shard_map/ppermute | solution.py:98
  55.1 5.3 %collective-permute-start.3 = (bf16[100,512]{1,0:T(8,128)(2,1)S(1)}, bf16[100,512]{1,0:T(8,128)(2,1)S(1)}, u32[]{:S(2)}, u32[]{:S(2)}) collective-permute-start(bf16[100,512]{1,0:T(8,128)(2,1)S(1)} %get-tuple-element.10), channel_id=1, source_target_pairs={{0,4},{1,5},{2,6},{3,7},{4,8},{5,9},{6,10},{7,11},{8,12},{9,13},{1... | collective-permute-start | bytes 307208 | tf_op jit(solution)/shard_map/ppermute | solution.py:98
  60.4 14.7 %collective-permute-start.4 = (bf16[100,512]{1,0:T(8,128)(2,1)S(1)}, bf16[100,512]{1,0:T(8,128)(2,1)S(1)}, u32[]{:S(2)}, u32[]{:S(2)}) collective-permute-start(bf16[100,512]{1,0:T(8,128)(2,1)S(1)} %get-tuple-element.10), channel_id=1, source_target_pairs={{0,5},{1,6},{2,7},{3,8},{4,9},{5,10},{6,11},{7,12},{8,13},{9,14},{... | collective-permute-start | bytes 307208 | tf_op jit(solution)/shard_map/ppermute | solution.py:98
  75.1 7.5 %collective-permute-start.5 = (bf16[100,512]{1,0:T(8,128)(2,1)S(1)}, bf16[100,512]{1,0:T(8,128)(2,1)S(1)}, u32[]{:S(2)}, u32[]{:S(2)}) collective-permute-start(bf16[100,512]{1,0:T(8,128)(2,1)S(1)} %get-tuple-element.10), channel_id=1, source_target_pairs={{0,6},{1,7},{2,8},{3,9},{4,10},{5,11},{6,12},{7,13},{8,14},{9,15},... | collective-permute-start | bytes 307208 | tf_op jit(solution)/shard_map/ppermute | solution.py:98
  82.6 23.6 %collective-permute-start.6 = (bf16[100,512]{1,0:T(8,128)(2,1)S(1)}, bf16[100,512]{1,0:T(8,128)(2,1)S(1)}, u32[]{:S(2)}, u32[]{:S(2)}) collective-permute-start(bf16[100,512]{1,0:T(8,128)(2,1)S(1)} %get-tuple-element.10), channel_id=1, source_target_pairs={{0,7},{1,8},{2,9},{3,10},{4,11},{5,12},{6,13},{7,14},{8,15},{16,23... | collective-permute-start | bytes 307208 | tf_op jit(solution)/shard_map/ppermute | solution.py:98
  106.2 15.2 %collective-permute-start.7 = (bf16[100,512]{1,0:T(8,128)(2,1)S(1)}, bf16[100,512]{1,0:T(8,128)(2,1)S(1)}, u32[]{:S(2)}, u32[]{:S(2)}) collective-permute-start(bf16[100,512]{1,0:T(8,128)(2,1)S(1)} %get-tuple-element.10), channel_id=1, source_target_pairs={{0,8},{1,9},{2,10},{3,11},{4,12},{5,13},{6,14},{7,15},{16,24},{17,... | collective-permute-start | bytes 307208 | tf_op jit(solution)/shard_map/ppermute | solution.py:98
  121.4 8.2 %collective-permute-start.8 = (bf16[100,512]{1,0:T(8,128)(2,1)S(1)}, bf16[100,512]{1,0:T(8,128)(2,1)S(1)}, u32[]{:S(2)}, u32[]{:S(2)}) collective-permute-start(bf16[100,512]{1,0:T(8,128)(2,1)S(1)} %get-tuple-element.10), channel_id=1, source_target_pairs={{0,9},{1,10},{2,11},{3,12},{4,13},{5,14},{6,15},{16,25},{17,26},{1... | collective-permute-start | bytes 307208 | tf_op jit(solution)/shard_map/ppermute | solution.py:98
  129.7 14.1 %collective-permute-start.9 = (bf16[100,512]{1,0:T(8,128)(2,1)S(1)}, bf16[100,512]{1,0:T(8,128)(2,1)S(1)}, u32[]{:S(2)}, u32[]{:S(2)}) collective-permute-start(bf16[100,512]{1,0:T(8,128)(2,1)S(1)} %get-tuple-element.10), channel_id=1, source_target_pairs={{0,10},{1,11},{2,12},{3,13},{4,14},{5,15},{16,26},{17,27},{18,28},... | collective-permute-start | bytes 307208 | tf_op jit(solution)/shard_map/ppermute | solution.py:98
  143.8 3.9 collective-permute-start.14
  291.1 9.6 %collective-permute-start.26 = (f32[56,512]{1,0:T(8,128)}, f32[56,512]{1,0:T(8,128)S(1)}, u32[]{:S(2)}, u32[]{:S(2)}) collective-permute-start(f32[56,512]{1,0:T(8,128)} %get-tuple-element.8), channel_id=1, source_target_pairs={{0,1},{1,2},{2,3},{3,4},{4,5},{5,6},{6,7},{7,8},{8,9},{9,10},{10,1... | collective-permute-start | bytes 344072
  293.0 3.4 collective-permute-start.27
  303.0 50.4 %copy-start.4 = (bf16[4,128,928]{1,2,0:T(8,128)(2,1)S(1)}, bf16[4,128,928]{1,2,0:T(8,128)(2,1)}, u32[]{:S(2)}) copy-start(bf16[4,128,928]{1,2,0:T(8,128)(2,1)} %copy-done.3) | copy-start | bytes 2850820
  303.0 50.4 %copy-start.27 = (bf16[1,1,128,512]{3,2,1,0:T(8,128)(2,1)S(1)}, bf16[1,1,128,512]{3,2,1,0:T(8,128)(2,1)}, u32[]{:S(2)}) copy-start(bf16[1,1,128,512]{3,2,1,0:T(8,128)(2,1)} %param.9) | copy-start | bytes 393220
  303.0 3.6 collective-permute-start.15
  306.7 10.9 %collective-permute-start.16 = (f32[16,4608]{1,0:T(8,128)S(1)}, f32[16,4608]{1,0:T(8,128)S(1)}, u32[]{:S(2)}, u32[]{:S(2)}) collective-permute-start(f32[16,4608]{1,0:T(8,128)S(1)} %fusion.94), channel_id=1, source_target_pairs={{0,32},{16,48},{32,0},{48,16},{64,96},{80,112},{96,64},{112,80},{1... | collective-permute-start | bytes 884744 | tf_op jit(solution)/shard_map/ppermute | solution.py:63
  317.6 18.5 %collective-permute-start.17 = (f32[16,4608]{1,0:T(8,128)S(1)}, f32[16,4608]{1,0:T(8,128)S(1)}, u32[]{:S(2)}, u32[]{:S(2)}) collective-permute-start(f32[16,4608]{1,0:T(8,128)S(1)} %add.94), channel_id=1, source_target_pairs={{0,64},{16,80},{32,96},{48,112},{64,0},{80,16},{96,32},{112,48},{1... | collective-permute-start | bytes 884744 | tf_op jit(solution)/shard_map/ppermute | solution.py:63
  336.1 27.1 %copy-start.8 = (bf16[4,128,928]{1,2,0:T(8,128)(2,1)S(1)}, bf16[4,128,928]{1,2,0:T(8,128)(2,1)}, u32[]{:S(2)}) copy-start(bf16[4,128,928]{1,2,0:T(8,128)(2,1)} %copy-done.7) | copy-start | bytes 2850820
  336.2 12.6 %collective-permute-start.18 = (f32[16,4608]{1,0:T(8,128)S(1)}, f32[16,4608]{1,0:T(8,128)S(1)}, u32[]{:S(2)}, u32[]{:S(2)}) collective-permute-start(f32[16,4608]{1,0:T(8,128)S(1)} %add.95), channel_id=1, source_target_pairs={{0,128},{16,144},{32,160},{48,176},{64,192},{80,208},{96,224},{112... | collective-permute-start | bytes 884744 | tf_op jit(solution)/shard_map/ppermute | solution.py:63
  348.8 11.7 %collective-permute-start.19 = (f32[16,4608]{1,0:T(8,128)S(1)}, f32[16,4608]{1,0:T(8,128)S(1)}, u32[]{:S(2)}, u32[]{:S(2)}) collective-permute-start(f32[16,4608]{1,0:T(8,128)S(1)} %add.96), channel_id=1, source_target_pairs={{0,256},{16,272},{32,288},{48,304},{64,320},{80,336},{96,352},{112... | collective-permute-start | bytes 884744 | tf_op jit(solution)/shard_map/ppermute | solution.py:63
  360.6 9.4 %collective-permute-start.20 = (f32[16,4608]{1,0:T(8,128)S(1)}, f32[16,4608]{1,0:T(8,128)S(1)}, u32[]{:S(2)}, u32[]{:S(2)}) collective-permute-start(f32[16,4608]{1,0:T(8,128)S(1)} %add.97), channel_id=1, source_target_pairs={{0,1},{1,0},{2,3},{3,2},{4,5},{5,4},{6,7},{7,6},{8,9},{9,8},{10,11... | collective-permute-start | bytes 884744 | tf_op jit(solution)/shard_map/ppermute | solution.py:63
  370.8 20.3 %collective-permute-start.21 = (f32[16,4608]{1,0:T(8,128)}, f32[16,4608]{1,0:T(8,128)}, u32[]{:S(2)}, u32[]{:S(2)}) collective-permute-start(f32[16,4608]{1,0:T(8,128)} %add.98), channel_id=1, source_target_pairs={{0,2},{1,3},{2,0},{3,1},{4,6},{5,7},{6,4},{7,5},{8,10},{9,11},{10,... | collective-permute-start | bytes 884744 | tf_op jit(solution)/shard_map/ppermute | solution.py:63
  377.2 24.4 %collective-permute-start.24 = (f32[56,512]{1,0:T(8,128)}, f32[56,512]{1,0:T(8,128)}, u32[]{:S(2)}, u32[]{:S(2)}) collective-permute-start(f32[56,512]{1,0:T(8,128)} %get-tuple-element.7), channel_id=1, source_target_pairs={{0,1},{1,2},{2,3},{3,4},{4,5},{5,6},{6,7},{7,8},{8,9},{9,10},{10,1... | collective-permute-start | bytes 344072
  384.7 16.8 %collective-permute-start.25 = (f32[34,512]{1,0:T(8,128)}, f32[34,512]{1,0:T(8,128)S(1)}, u32[]{:S(2)}, u32[]{:S(2)}) collective-permute-start(f32[34,512]{1,0:T(8,128)} %slice.128), channel_id=1, source_target_pairs={{0,2},{1,3},{2,4},{3,5},{4,6},{5,7},{6,8},{7,9},{8,10},{9,11},{10,... | collective-permute-start | bytes 208904
  392.9 19.8 %collective-permute-start.22 = (f32[16,4608]{1,0:T(8,128)}, f32[16,4608]{1,0:T(8,128)}, u32[]{:S(2)}, u32[]{:S(2)}) collective-permute-start(f32[16,4608]{1,0:T(8,128)} %add.99), channel_id=1, source_target_pairs={{0,4},{1,5},{2,6},{3,7},{4,0},{5,1},{6,2},{7,3},{8,12},{9,13},{10,... | collective-permute-start | bytes 884744 | tf_op jit(solution)/shard_map/ppermute | solution.py:63
  413.7 17.1 %collective-permute-start.23 = (f32[16,4608]{1,0:T(8,128)S(1)}, f32[16,4608]{1,0:T(8,128)S(1)}, u32[]{:S(2)}, u32[]{:S(2)}) collective-permute-start(f32[16,4608]{1,0:T(8,128)S(1)} %add.100), channel_id=1, source_target_pairs={{0,8},{1,9},{2,10},{3,11},{4,12},{5,13},{6,14},{7,15},{8,0},{9,1},... | collective-permute-start | bytes 884744 | tf_op jit(solution)/shard_map/ppermute | solution.py:63
  (35 other events, 261.3 us)

commit v2 on v1

--- a/solution.py
+++ b/solution.py
@@ -94,20 +94,20 @@
     own_keys = lax.dynamic_slice_in_dim(key_local, length, SUMM, 0)
     own_values = lax.dynamic_slice_in_dim(value_local, length, SUMM, 0)
     own_summary = jnp.concatenate([own_keys, own_values], 0)
-    pieces = [own_summary] + [
-        lax.ppermute(own_summary, "ctx", [(i, i + k) for i in range(segment_list - k)])
-        for k in range(1, segment_list)
-    ]
-    slot_of_segment = (position - jnp.arange(segment_list)) % segment_list
-    gathered = jnp.take(jnp.stack(pieces), slot_of_segment, axis=0).reshape(
-        segment_list, 2, SUMM, width
-    )
+    held = own_summary[None]
+    hop = 1
+    while hop < segment_list:
+        arrived = lax.ppermute(held, "ctx", [(i, i + hop) for i in range(segment_list - hop)])
+        held = jnp.concatenate([held, arrived], 0)
+        hop *= 2
+    gathered = held.reshape(segment_list, 2, SUMM, width)
     memory_keys = gathered[:, 0].reshape(segment_list * SUMM, width)
     memory_values = gathered[:, 1].reshape(segment_list * SUMM, width)
     count = memory_keys.shape[0]
-    memory_owner = jnp.arange(count) // SUMM
+    memory_distance = jnp.arange(count) // SUMM
+    memory_seen = (memory_distance >= 1) & (memory_distance <= position)
     local_mask = (rows[None, :] <= rows[:, None]) & (rows[None, :] < live)
-    memory_mask = jnp.broadcast_to((memory_owner < position)[None, :], (tokens, count))
+    memory_mask = jnp.broadcast_to(memory_seen[None, :], (tokens, count))
     key_mask = jnp.concatenate([memory_mask, local_mask], axis=1)
     all_keys = jnp.concatenate([memory_keys, key_local], 0)
     all_values = jnp.concatenate([memory_values, value_local], 0)
@@ -130,10 +130,19 @@
     value_grad = jnp.concatenate(value_parts, 1)
     memory_key_grad, local_key = (key_grad[:count], key_grad[count:])
     memory_value_grad, local_value = (value_grad[:count], value_grad[count:])
-    back_key, back_value = (
-        lax.psum_scatter(memory_key_grad, "ctx", scatter_dimension=0, tiled=True),
-        lax.psum_scatter(memory_value_grad, "ctx", scatter_dimension=0, tiled=True),
+    owed = jnp.stack(
+        [
+            memory_key_grad.reshape(segment_list, SUMM, width),
+            memory_value_grad.reshape(segment_list, SUMM, width),
+        ],
+        1,
     )
+    hop = segment_list // 2
+    while hop >= 1:
+        returned = lax.ppermute(owed[hop : 2 * hop], "ctx", [(i, i - hop) for i in range(hop, segment_list)])
+        owed = owed[:hop] + returned
+        hop //= 2
+    back_key, back_value = owed[0, 0], owed[0, 1]
     key_out = (
         local_key + lax.dynamic_update_slice_in_dim(jnp.zeros_like(local_key), back_key, length, 0)
     ).astype(jnp.bfloat16)

time: 434 us -> 461 us (1.062)
  the two profiles are of different devices: /device:TPU:8 before, /device:TPU:1 now
where the time goes in v2:
time: 461 us; the launch traced here: 457 us
  starting transfers between devices  187 us (41%)
  waiting for transfers between devices  168 us (36%)
  matrix products  41.4 us (9%)
  local copies, waits for them, and re-layouts  35.3 us (8%)
  other arithmetic  22.2 us (5%)
    ppermute x9, starting transfers between devices, butterfly_sum(): x = x + lax.ppermute(x, axis, [(i, i ^ k) for i in range(n)])  115 us
    ppermute x4, waiting for transfers between devices, per_device(): lax.ppermute(owed[hop:2 * hop], 'ctx', [(i, i - hop) for i in range(hop,...  77.7 us
    ppermute x9, waiting for transfers between devices, butterfly_sum(): x = x + lax.ppermute(x, axis, [(i, i ^ k) for i in range(n)])  70.4 us
    ppermute x4, starting transfers between devices, per_device(): lax.ppermute(held, 'ctx', [(i, i + hop) for i in range(segment_list - hop)])  66.5 us
    ppermute x4, waiting for transfers between devices, per_device(): lax.ppermute(held, 'ctx', [(i, i + hop) for i in range(segment_list - hop)])  20.4 us
    div x4, matrix products, group_grads(): attend = unnorm / jnp.sum(unnorm, -1, keepdims=True)  16.4 us
    dot_general x4, matrix products, group_grads(): jnp.einsum('gtm,tgd->md', attend_low, cot_group, preferred_element_type=j...  11.4 us
    concatenate x4, local copies, waits for them, and re-layouts, per_device(): held = jnp.concatenate([held, arrived], 0)  10.2 us
  transfers between devices with their start and end apart: 17, of which 17 were waited for; matrix products, arithmetic and copies ran while one was open for 3% of the time, Pallas kernels for 0%

profile of v2, /device:TPU:1, one launch (start us, length us, event | category | flops | bytes accessed | tf_op | source)
XLA Modules:
  0.0 457.0 jit_solution(13084880432911793776)
XLA Ops:
  2.3 4.0 collective-permute-start
  8.1 4.8 %collective-permute-start.1 = (bf16[2,100,512]{2,1,0:T(8,128)(2,1)S(1)}, bf16[2,100,512]{2,1,0:T(8,128)(2,1)S(1)}, u32[]{:S(2)}, u32[]{:S(2)}) collective-permute-start(bf16[2,100,512]{2,1,0:T(8,128)(2,1)S(1)} %pad_maximum_fusion.13), channel_id=1, source_target_pairs={{0,2},{1,3},{2,4},{3,5},{4,6},{5,7},{6,8},{7,9},{8,10},{9,11},{10,... | collective-permute-start | bytes 614408 | tf_op jit(solution)/shard_map/ppermute | solution.py:100
  15.7 15.3 %collective-permute-start.2 = (bf16[4,100,512]{2,1,0:T(8,128)(2,1)S(1)}, bf16[4,100,512]{2,1,0:T(8,128)(2,1)S(1)}, u32[]{:S(2)}, u32[]{:S(2)}) collective-permute-start(bf16[4,100,512]{2,1,0:T(8,128)(2,1)S(1)} %pad_maximum_fusion.7), channel_id=1, source_target_pairs={{0,4},{1,5},{2,6},{3,7},{4,8},{5,9},{6,10},{7,11},{8,12},{9,13},{1... | collective-permute-start | bytes 1228808 | tf_op jit(solution)/shard_map/ppermute | solution.py:100
  32.6 4.9 %collective-permute-done.2 = bf16[4,100,512]{2,1,0:T(8,128)(2,1)S(1)} collective-permute-done((bf16[4,100,512]{2,1,0:T(8,128)(2,1)S(1)}, bf16[4,100,512]{2,1,0:T(8,128)(2,1)S(1)}, u32[]{:S(2)}, u32[]{:S(2)}) %collective-permute-start.2) | collective-permute-done | bytes 409632 | tf_op jit(solution)/shard_map/ppermute | solution.py:100
  38.7 42.4 %collective-permute-start.3 = (bf16[8,100,512]{2,0,1:T(8,128)(2,1)}, bf16[8,100,512]{2,0,1:T(8,128)(2,1)}, u32[]{:S(2)}, u32[]{:S(2)}) collective-permute-start(bf16[8,100,512]{2,0,1:T(8,128)(2,1)} %copy.80), channel_id=1, source_target_pairs={{0,8},{1,9},{2,10},{3,11},{4,12},{5,13},{6,14},{7,15},{16,24},{17,... | collective-permute-start | bytes 2457608 | tf_op jit(solution)/shard_map/ppermute | solution.py:100
  84.8 12.5 %collective-permute-done.3 = bf16[8,100,512]{2,0,1:T(8,128)(2,1)} collective-permute-done((bf16[8,100,512]{2,0,1:T(8,128)(2,1)}, bf16[8,100,512]{2,0,1:T(8,128)(2,1)}, u32[]{:S(2)}, u32[]{:S(2)}) %collective-permute-start.3) | collective-permute-done | bytes 819232 | tf_op jit(solution)/shard_map/ppermute | solution.py:100
  97.3 7.6 %concatenate.75 = bf16[16,2,50,512]{3,0,2,1:T(8,128)(2,1)S(1)} concatenate(bf16[1,2,50,512]{3,0,2,1:T(2,128)(2,1)} %concatenate.87, bf16[1,2,50,512]{3,0,2,1:T(2,128)(2,1)} %concatenate.88, bf16[2,2,50,512]{3,0,2,1:T(2,128)(2,1)} %bitcast.234, bf16[4,2,50,512]{3,0,2,1:T(4,128)(2,1)S(1)} %bitcast.225, bf16[8,2,50,512]{3,0,2,1:T(8,128)(2,1)} %bitcast.6), dimensions={0} | concatenate | bytes 3276800 | tf_op jit(solution)/shard_map/concatenate | solution.py:101
  117.4 3.7 fusion.4
  127.3 4.2 fusion
  137.4 4.3 fusion.8
  148.5 4.3 fusion.12
  173.3 40.4 %collective-permute-done.4 = f32[8,2,50,512]{3,0,2,1:T(8,128)S(1)} collective-permute-done((f32[8,2,50,512]{3,0,2,1:T(8,128)S(1)}, f32[8,2,50,512]{3,0,2,1:T(8,128)S(1)}, u32[]{:S(2)}, u32[]{:S(2)}) %collective-permute-start.4) | collective-permute-done | bytes 1638432 | tf_op jit(solution)/shard_map/ppermute | solution.py:142
  216.6 21.7 %collective-permute-done.5 = f32[4,2,50,512]{3,0,2,1:T(4,128)S(1)} collective-permute-done((f32[4,2,50,512]{3,0,2,1:T(4,128)S(1)}, f32[4,2,50,512]{3,0,2,1:T(4,128)S(1)}, u32[]{:S(2)}, u32[]{:S(2)}) %collective-permute-start.5) | collective-permute-done | bytes 819232 | tf_op jit(solution)/shard_map/ppermute | solution.py:142
  240.3 10.0 %collective-permute-done.6 = f32[2,2,50,512]{3,2,1,0:T(8,128)S(1)} collective-permute-done((f32[2,2,50,512]{3,2,1,0:T(8,128)S(1)}, f32[2,2,50,512]{3,2,1,0:T(8,128)S(1)}, u32[]{:S(2)}, u32[]{:S(2)}) %collective-permute-start.6) | collective-permute-done | bytes 409632 | tf_op jit(solution)/shard_map/ppermute | solution.py:142
  251.8 5.7 %collective-permute-done.7 = f32[1,2,50,512]{3,2,1,0:T(8,128)S(1)} collective-permute-done((f32[1,2,50,512]{3,2,1,0:T(8,128)S(1)}, f32[1,2,50,512]{3,2,1,0:T(8,128)S(1)}, u32[]{:S(2)}, u32[]{:S(2)}) %collective-permute-start.7) | collective-permute-done | bytes 204832 | tf_op jit(solution)/shard_map/ppermute | solution.py:142
  261.8 8.6 %collective-permute-start.8 = (f32[16,4608]{1,0:T(8,128)S(1)}, f32[16,4608]{1,0:T(8,128)S(1)}, u32[]{:S(2)}, u32[]{:S(2)}) collective-permute-start(f32[16,4608]{1,0:T(8,128)S(1)} %pad_maximum_fusion.8), channel_id=1, source_target_pairs={{0,16},{16,0},{32,48},{48,32},{64,80},{80,64},{96,112},{112,96},{1... | collective-permute-start | bytes 884744 | tf_op jit(solution)/shard_map/ppermute | solution.py:63
  272.6 52.8 %collective-permute-start.9 = (f32[16,4608]{1,0:T(8,128)S(1)}, f32[16,4608]{1,0:T(8,128)S(1)}, u32[]{:S(2)}, u32[]{:S(2)}) collective-permute-start(f32[16,4608]{1,0:T(8,128)S(1)} %fusion.92), channel_id=1, source_target_pairs={{0,32},{16,48},{32,0},{48,16},{64,96},{80,112},{96,64},{112,80},{1... | collective-permute-start | bytes 884744 | tf_op jit(solution)/shard_map/ppermute | solution.py:63
  325.5 7.1 %collective-permute-done.9 = f32[16,4608]{1,0:T(8,128)S(1)} collective-permute-done((f32[16,4608]{1,0:T(8,128)S(1)}, f32[16,4608]{1,0:T(8,128)S(1)}, u32[]{:S(2)}, u32[]{:S(2)}) %collective-permute-start.9) | collective-permute-done | bytes 294944 | tf_op jit(solution)/shard_map/ppermute | solution.py:63
  332.6 9.4 %collective-permute-start.10 = (f32[16,4608]{1,0:T(8,128)S(1)}, f32[16,4608]{1,0:T(8,128)S(1)}, u32[]{:S(2)}, u32[]{:S(2)}) collective-permute-start(f32[16,4608]{1,0:T(8,128)S(1)} %add.70), channel_id=1, source_target_pairs={{0,64},{16,80},{32,96},{48,112},{64,0},{80,16},{96,32},{112,48},{1... | collective-permute-start | bytes 884744 | tf_op jit(solution)/shard_map/ppermute | solution.py:63
  342.0 13.7 %collective-permute-done.10 = f32[16,4608]{1,0:T(8,128)S(1)} collective-permute-done((f32[16,4608]{1,0:T(8,128)S(1)}, f32[16,4608]{1,0:T(8,128)S(1)}, u32[]{:S(2)}, u32[]{:S(2)}) %collective-permute-start.10) | collective-permute-done | bytes 294944 | tf_op jit(solution)/shard_map/ppermute | solution.py:63
  355.8 6.2 %collective-permute-start.11 = (f32[16,4608]{1,0:T(8,128)S(1)}, f32[16,4608]{1,0:T(8,128)S(1)}, u32[]{:S(2)}, u32[]{:S(2)}) collective-permute-start(f32[16,4608]{1,0:T(8,128)S(1)} %add.71), channel_id=1, source_target_pairs={{0,128},{16,144},{32,160},{48,176},{64,192},{80,208},{96,224},{112... | collective-permute-start | bytes 884744 | tf_op jit(solution)/shard_map/ppermute | solution.py:63
  362.0 6.9 %collective-permute-done.11 = f32[16,4608]{1,0:T(8,128)S(1)} collective-permute-done((f32[16,4608]{1,0:T(8,128)S(1)}, f32[16,4608]{1,0:T(8,128)S(1)}, u32[]{:S(2)}, u32[]{:S(2)}) %collective-permute-start.11) | collective-permute-done | bytes 294944 | tf_op jit(solution)/shard_map/ppermute | solution.py:63
  368.9 5.3 %collective-permute-start.12 = (f32[16,4608]{1,0:T(8,128)S(1)}, f32[16,4608]{1,0:T(8,128)S(1)}, u32[]{:S(2)}, u32[]{:S(2)}) collective-permute-start(f32[16,4608]{1,0:T(8,128)S(1)} %add.72), channel_id=1, source_target_pairs={{0,256},{16,272},{32,288},{48,304},{64,320},{80,336},{96,352},{112... | collective-permute-start | bytes 884744 | tf_op jit(solution)/shard_map/ppermute | solution.py:63
  374.2 6.1 %collective-permute-done.12 = f32[16,4608]{1,0:T(8,128)S(1)} collective-permute-done((f32[16,4608]{1,0:T(8,128)S(1)}, f32[16,4608]{1,0:T(8,128)S(1)}, u32[]{:S(2)}, u32[]{:S(2)}) %collective-permute-start.12) | collective-permute-done | bytes 294944 | tf_op jit(solution)/shard_map/ppermute | solution.py:63
  380.4 11.7 %collective-permute-start.13 = (f32[16,4608]{1,0:T(8,128)S(1)}, f32[16,4608]{1,0:T(8,128)S(1)}, u32[]{:S(2)}, u32[]{:S(2)}) collective-permute-start(f32[16,4608]{1,0:T(8,128)S(1)} %add.73), channel_id=1, source_target_pairs={{0,1},{1,0},{2,3},{3,2},{4,5},{5,4},{6,7},{7,6},{8,9},{9,8},{10,11... | collective-permute-start | bytes 884744 | tf_op jit(solution)/shard_map/ppermute | solution.py:63
  392.5 5.2 %collective-permute-done.13 = f32[16,4608]{1,0:T(8,128)S(1)} collective-permute-done((f32[16,4608]{1,0:T(8,128)S(1)}, f32[16,4608]{1,0:T(8,128)S(1)}, u32[]{:S(2)}, u32[]{:S(2)}) %collective-permute-start.13) | collective-permute-done | bytes 294944 | tf_op jit(solution)/shard_map/ppermute | solution.py:63
  397.8 4.0 collective-permute-start.14
  403.1 11.8 %collective-permute-done.14 = f32[16,4608]{1,0:T(8,128)S(1)} collective-permute-done((f32[16,4608]{1,0:T(8,128)S(1)}, f32[16,4608]{1,0:T(8,128)S(1)}, u32[]{:S(2)}, u32[]{:S(2)}) %collective-permute-start.14) | collective-permute-done | bytes 294944 | tf_op jit(solution)/shard_map/ppermute | solution.py:63
  415.0 11.3 %collective-permute-start.15 = (f32[16,4608]{1,0:T(8,128)S(1)}, f32[16,4608]{1,0:T(8,128)}, u32[]{:S(2)}, u32[]{:S(2)}) collective-permute-start(f32[16,4608]{1,0:T(8,128)S(1)} %add.75), channel_id=1, source_target_pairs={{0,4},{1,5},{2,6},{3,7},{4,0},{5,1},{6,2},{7,3},{8,12},{9,13},{10,... | collective-permute-start | bytes 884744 | tf_op jit(solution)/shard_map/ppermute | solution.py:63
  428.0 7.2 %collective-permute-done.15 = f32[16,4608]{1,0:T(8,128)} collective-permute-done((f32[16,4608]{1,0:T(8,128)S(1)}, f32[16,4608]{1,0:T(8,128)}, u32[]{:S(2)}, u32[]{:S(2)}) %collective-permute-start.15) | collective-permute-done | bytes 294944 | tf_op jit(solution)/shard_map/ppermute | solution.py:63
  436.2 6.1 %collective-permute-start.16 = (f32[16,4608]{1,0:T(8,128)S(1)}, f32[16,4608]{1,0:T(8,128)S(1)}, u32[]{:S(2)}, u32[]{:S(2)}) collective-permute-start(f32[16,4608]{1,0:T(8,128)S(1)} %add.76), channel_id=1, source_target_pairs={{0,8},{1,9},{2,10},{3,11},{4,12},{5,13},{6,14},{7,15},{8,0},{9,1},... | collective-permute-start | bytes 884744 | tf_op jit(solution)/shard_map/ppermute | solution.py:63
  444.5 11.1 %collective-permute-done.16 = f32[16,4608]{1,0:T(8,128)S(1)} collective-permute-done((f32[16,4608]{1,0:T(8,128)S(1)}, f32[16,4608]{1,0:T(8,128)S(1)}, u32[]{:S(2)}, u32[]{:S(2)}) %collective-permute-start.16) | collective-permute-done | bytes 294944 | tf_op jit(solution)/shard_map/ppermute | solution.py:63
  (195 shorter events, 84.5 us)
Async XLA Ops:
  0.6 258.5 %copy-start = (bf16[1,1,128,4096]{3,2,1,0:T(8,128)(2,1)S(1)}, bf16[1,1,128,4096]{3,2,1,0:T(8,128)(2,1)}, u32[]{:S(2)}) copy-start(bf16[1,1,128,4096]{3,2,1,0:T(8,128)(2,1)} %param.12) | copy-start | bytes 3145732
  2.3 5.7 %collective-permute-start = (bf16[1,100,512]{2,1,0:T(8,128)(2,1)S(1)}, bf16[1,100,512]{2,1,0:T(8,128)(2,1)S(1)}, u32[]{:S(2)}, u32[]{:S(2)}) collective-permute-start(bf16[1,100,512]{2,1,0:T(8,128)(2,1)S(1)} %fusion.130), channel_id=1, source_target_pairs={{0,1},{1,2},{2,3},{3,4},{4,5},{5,6},{6,7},{7,8},{8,9},{9,10},{10,1... | collective-permute-start | bytes 307208 | tf_op jit(solution)/shard_map/ppermute | solution.py:100
  8.1 7.6 %collective-permute-start.1 = (bf16[2,100,512]{2,1,0:T(8,128)(2,1)S(1)}, bf16[2,100,512]{2,1,0:T(8,128)(2,1)S(1)}, u32[]{:S(2)}, u32[]{:S(2)}) collective-permute-start(bf16[2,100,512]{2,1,0:T(8,128)(2,1)S(1)} %pad_maximum_fusion.13), channel_id=1, source_target_pairs={{0,2},{1,3},{2,4},{3,5},{4,6},{5,7},{6,8},{7,9},{8,10},{9,11},{10,... | collective-permute-start | bytes 614408 | tf_op jit(solution)/shard_map/ppermute | solution.py:100
  15.7 21.8 %collective-permute-start.2 = (bf16[4,100,512]{2,1,0:T(8,128)(2,1)S(1)}, bf16[4,100,512]{2,1,0:T(8,128)(2,1)S(1)}, u32[]{:S(2)}, u32[]{:S(2)}) collective-permute-start(bf16[4,100,512]{2,1,0:T(8,128)(2,1)S(1)} %pad_maximum_fusion.7), channel_id=1, source_target_pairs={{0,4},{1,5},{2,6},{3,7},{4,8},{5,9},{6,10},{7,11},{8,12},{9,13},{1... | collective-permute-start | bytes 1228808 | tf_op jit(solution)/shard_map/ppermute | solution.py:100
  32.6 49.3 %copy-start.35 = (bf16[1,1,128,2048]{3,2,1,0:T(8,128)(2,1)S(1)}, bf16[1,1,128,2048]{3,2,1,0:T(8,128)(2,1)}, u32[]{:S(2)}) copy-start(bf16[1,1,128,2048]{3,2,1,0:T(8,128)(2,1)} %param.11) | copy-start | bytes 1572868
  38.7 58.6 %collective-permute-start.3 = (bf16[8,100,512]{2,0,1:T(8,128)(2,1)}, bf16[8,100,512]{2,0,1:T(8,128)(2,1)}, u32[]{:S(2)}, u32[]{:S(2)}) collective-permute-start(bf16[8,100,512]{2,0,1:T(8,128)(2,1)} %copy.80), channel_id=1, source_target_pairs={{0,8},{1,9},{2,10},{3,11},{4,12},{5,13},{6,14},{7,15},{16,24},{17,... | collective-permute-start | bytes 2457608 | tf_op jit(solution)/shard_map/ppermute | solution.py:100
  169.2 44.4 %copy-start.2 = (f32[16,1,50,512]{3,2,0,1:T(8,128)S(1)}, f32[16,1,50,512]{3,2,0,1:T(8,128)}, u32[]{:S(2)}) copy-start(f32[16,1,50,512]{3,2,0,1:T(8,128)} %stack_reshape.7) | copy-start | bytes 4915204
  171.0 42.6 %copy-start.1 = (f32[16,1,50,512]{3,2,0,1:T(8,128)S(1)}, f32[16,1,50,512]{3,2,0,1:T(8,128)}, u32[]{:S(2)}) copy-start(f32[16,1,50,512]{3,2,0,1:T(8,128)} %stack_reshape.6) | copy-start | bytes 4915204
  172.0 41.7 %collective-permute-start.4 = (f32[8,2,50,512]{3,0,2,1:T(8,128)S(1)}, f32[8,2,50,512]{3,0,2,1:T(8,128)S(1)}, u32[]{:S(2)}, u32[]{:S(2)}) collective-permute-start(f32[8,2,50,512]{3,0,2,1:T(8,128)S(1)} %copy.109), channel_id=1, source_target_pairs={{8,0},{9,1},{10,2},{11,3},{12,4},{13,5},{14,6},{15,7},{24,16},{25,... | collective-permute-start | bytes 4915208 | tf_op jit(solution)/shard_map/ppermute | solution.py:142
  215.3 23.0 %collective-permute-start.5 = (f32[4,2,50,512]{3,0,2,1:T(4,128)S(1)}, f32[4,2,50,512]{3,0,2,1:T(4,128)S(1)}, u32[]{:S(2)}, u32[]{:S(2)}) collective-permute-start(f32[4,2,50,512]{3,0,2,1:T(4,128)S(1)} %copy.111), channel_id=1, source_target_pairs={{4,0},{5,1},{6,2},{7,3},{8,4},{9,5},{10,6},{11,7},{12,8},{13,9},{1... | collective-permute-start | bytes 2457608 | tf_op jit(solution)/shard_map/ppermute | solution.py:142
  238.6 13.1 %copy-start.14 = (f32[928,128]{1,0:T(8,128)S(1)}, f32[928,128]{1,0:T(8,128)}, u32[]{:S(2)}) copy-start(f32[928,128]{1,0:T(8,128)} %fusion.18) | copy-start | bytes 1425412
  238.6 13.1 %copy-start.16 = (f32[928,128]{1,0:T(8,128)S(1)}, f32[928,128]{1,0:T(8,128)}, u32[]{:S(2)}) copy-start(f32[928,128]{1,0:T(8,128)} %fusion.20) | copy-start | bytes 1425412
  238.6 13.1 %copy-start.18 = (f32[928,128]{1,0:T(8,128)S(1)}, f32[928,128]{1,0:T(8,128)}, u32[]{:S(2)}) copy-start(f32[928,128]{1,0:T(8,128)} %copy-done.17) | copy-start | bytes 1425412
  238.7 13.1 %copy-start.19 = (f32[928,128]{1,0:T(8,128)S(1)}, f32[928,128]{1,0:T(8,128)}, u32[]{:S(2)}) copy-start(f32[928,128]{1,0:T(8,128)} %convolution_bitcast_fusion.1) | copy-start | bytes 1425412
  238.7 13.1 %copy-start.20 = (f32[928,128]{1,0:T(8,128)S(1)}, f32[928,128]{1,0:T(8,128)}, u32[]{:S(2)}) copy-start(f32[928,128]{1,0:T(8,128)} %convolution_bitcast_fusion) | copy-start | bytes 1425412
  238.7 11.6 %collective-permute-start.6 = (f32[2,2,50,512]{3,2,1,0:T(8,128)S(1)}, f32[2,2,50,512]{3,2,1,0:T(8,128)S(1)}, u32[]{:S(2)}, u32[]{:S(2)}) collective-permute-start(f32[2,2,50,512]{3,2,1,0:T(8,128)S(1)} %slice.170), channel_id=1, source_target_pairs={{2,0},{3,1},{4,2},{5,3},{6,4},{7,5},{8,6},{9,7},{10,8},{11,9},{12,... | collective-permute-start | bytes 1228808 | tf_op jit(solution)/shard_map/ppermute | solution.py:142
  250.4 7.2 %collective-permute-start.7 = (f32[1,2,50,512]{3,2,1,0:T(8,128)S(1)}, f32[1,2,50,512]{3,2,1,0:T(8,128)S(1)}, u32[]{:S(2)}, u32[]{:S(2)}) collective-permute-start(f32[1,2,50,512]{3,2,1,0:T(8,128)S(1)} %slice.172), channel_id=1, source_target_pairs={{1,0},{2,1},{3,2},{4,3},{5,4},{6,5},{7,6},{8,7},{9,8},{10,9},{11,1... | collective-permute-start | bytes 614408 | tf_op jit(solution)/shard_map/ppermute | solution.py:142
  261.8 9.8 %collective-permute-start.8 = (f32[16,4608]{1,0:T(8,128)S(1)}, f32[16,4608]{1,0:T(8,128)S(1)}, u32[]{:S(2)}, u32[]{:S(2)}) collective-permute-start(f32[16,4608]{1,0:T(8,128)S(1)} %pad_maximum_fusion.8), channel_id=1, source_target_pairs={{0,16},{16,0},{32,48},{48,32},{64,80},{80,64},{96,112},{112,96},{1... | collective-permute-start | bytes 884744 | tf_op jit(solution)/shard_map/ppermute | solution.py:63
  272.6 119.5 %copy-start.4 = (bf16[4,128,928]{1,2,0:T(8,128)(2,1)S(1)}, bf16[4,128,928]{1,2,0:T(8,128)(2,1)}, u32[]{:S(2)}) copy-start(bf16[4,128,928]{1,2,0:T(8,128)(2,1)} %copy-done.3) | copy-start | bytes 2850820
  272.6 59.9 %collective-permute-start.9 = (f32[16,4608]{1,0:T(8,128)S(1)}, f32[16,4608]{1,0:T(8,128)S(1)}, u32[]{:S(2)}, u32[]{:S(2)}) collective-permute-start(f32[16,4608]{1,0:T(8,128)S(1)} %fusion.92), channel_id=1, source_target_pairs={{0,32},{16,48},{32,0},{48,16},{64,96},{80,112},{96,64},{112,80},{1... | collective-permute-start | bytes 884744 | tf_op jit(solution)/shard_map/ppermute | solution.py:63
  332.6 23.1 %collective-permute-start.10 = (f32[16,4608]{1,0:T(8,128)S(1)}, f32[16,4608]{1,0:T(8,128)S(1)}, u32[]{:S(2)}, u32[]{:S(2)}) collective-permute-start(f32[16,4608]{1,0:T(8,128)S(1)} %add.70), channel_id=1, source_target_pairs={{0,64},{16,80},{32,96},{48,112},{64,0},{80,16},{96,32},{112,48},{1... | collective-permute-start | bytes 884744 | tf_op jit(solution)/shard_map/ppermute | solution.py:63
  355.8 13.1 %collective-permute-start.11 = (f32[16,4608]{1,0:T(8,128)S(1)}, f32[16,4608]{1,0:T(8,128)S(1)}, u32[]{:S(2)}, u32[]{:S(2)}) collective-permute-start(f32[16,4608]{1,0:T(8,128)S(1)} %add.71), channel_id=1, source_target_pairs={{0,128},{16,144},{32,160},{48,176},{64,192},{80,208},{96,224},{112... | collective-permute-start | bytes 884744 | tf_op jit(solution)/shard_map/ppermute | solution.py:63
  368.9 32.9 %copy-start.8 = (bf16[4,128,928]{1,2,0:T(8,128)(2,1)S(1)}, bf16[4,128,928]{1,2,0:T(8,128)(2,1)}, u32[]{:S(2)}) copy-start(bf16[4,128,928]{1,2,0:T(8,128)(2,1)} %copy-done.7) | copy-start | bytes 2850820
  368.9 11.4 %collective-permute-start.12 = (f32[16,4608]{1,0:T(8,128)S(1)}, f32[16,4608]{1,0:T(8,128)S(1)}, u32[]{:S(2)}, u32[]{:S(2)}) collective-permute-start(f32[16,4608]{1,0:T(8,128)S(1)} %add.72), channel_id=1, source_target_pairs={{0,256},{16,272},{32,288},{48,304},{64,320},{80,336},{96,352},{112... | collective-permute-start | bytes 884744 | tf_op jit(solution)/shard_map/ppermute | solution.py:63
  380.4 17.3 %collective-permute-start.13 = (f32[16,4608]{1,0:T(8,128)S(1)}, f32[16,4608]{1,0:T(8,128)S(1)}, u32[]{:S(2)}, u32[]{:S(2)}) collective-permute-start(f32[16,4608]{1,0:T(8,128)S(1)} %add.73), channel_id=1, source_target_pairs={{0,1},{1,0},{2,3},{3,2},{4,5},{5,4},{6,7},{7,6},{8,9},{9,8},{10,11... | collective-permute-start | bytes 884744 | tf_op jit(solution)/shard_map/ppermute | solution.py:63
  397.8 28.5 %copy-start.6 = (bf16[4,128,928]{1,2,0:T(8,128)(2,1)S(1)}, bf16[4,128,928]{1,2,0:T(8,128)(2,1)}, u32[]{:S(2)}) copy-start(bf16[4,128,928]{1,2,0:T(8,128)(2,1)} %copy-done.5) | copy-start | bytes 2850820
  397.8 17.2 %collective-permute-start.14 = (f32[16,4608]{1,0:T(8,128)S(1)}, f32[16,4608]{1,0:T(8,128)S(1)}, u32[]{:S(2)}, u32[]{:S(2)}) collective-permute-start(f32[16,4608]{1,0:T(8,128)S(1)} %add.74), channel_id=1, source_target_pairs={{0,2},{1,3},{2,0},{3,1},{4,6},{5,7},{6,4},{7,5},{8,10},{9,11},{10,... | collective-permute-start | bytes 884744 | tf_op jit(solution)/shard_map/ppermute | solution.py:63
  403.1 23.7 %copy-start.34 = (bf16[128,4,128]{2,0,1:T(8,128)(2,1)S(1)}, bf16[128,4,128]{2,0,1:T(8,128)(2,1)}, u32[]{:S(2)}) copy-start(bf16[128,4,128]{2,0,1:T(8,128)(2,1)} %fusion.25) | copy-start | bytes 393220
  415.0 20.2 %collective-permute-start.15 = (f32[16,4608]{1,0:T(8,128)S(1)}, f32[16,4608]{1,0:T(8,128)}, u32[]{:S(2)}, u32[]{:S(2)}) collective-permute-start(f32[16,4608]{1,0:T(8,128)S(1)} %add.75), channel_id=1, source_target_pairs={{0,4},{1,5},{2,6},{3,7},{4,0},{5,1},{6,2},{7,3},{8,12},{9,13},{10,... | collective-permute-start | bytes 884744 | tf_op jit(solution)/shard_map/ppermute | solution.py:63
  426.7 16.3 %copy-start.26 = (f32[128,512]{1,0:T(8,128)S(1)}, f32[128,512]{1,0:T(8,128)}, u32[]{:S(2)}) copy-start(f32[128,512]{1,0:T(8,128)} %copy-done.25) | copy-start | bytes 786436
  426.7 16.3 %copy-start.42 = (f32[50,512]{1,0:T(8,128)S(1)}, f32[50,512]{1,0:T(8,128)}, u32[]{:S(2)}) copy-start(f32[50,512]{1,0:T(8,128)} %get-tuple-element.16) | copy-start | bytes 307204
  436.2 19.4 %collective-permute-start.16 = (f32[16,4608]{1,0:T(8,128)S(1)}, f32[16,4608]{1,0:T(8,128)S(1)}, u32[]{:S(2)}, u32[]{:S(2)}) collective-permute-start(f32[16,4608]{1,0:T(8,128)S(1)} %add.76), channel_id=1, source_target_pairs={{0,8},{1,9},{2,10},{3,11},{4,12},{5,13},{6,14},{7,15},{8,0},{9,1},... | collective-permute-start | bytes 884744 | tf_op jit(solution)/shard_map/ppermute | solution.py:63
  (35 other events, 136.1 us)

commit v3 on v1

--- a/solution.py
+++ b/solution.py
@@ -94,14 +94,14 @@
     own_keys = lax.dynamic_slice_in_dim(key_local, length, SUMM, 0)
     own_values = lax.dynamic_slice_in_dim(value_local, length, SUMM, 0)
     own_summary = jnp.concatenate([own_keys, own_values], 0)
-    pieces = [own_summary] + [
-        lax.ppermute(own_summary, "ctx", [(i, i + k) for i in range(segment_list - k)])
-        for k in range(1, segment_list)
-    ]
+    held = own_summary[None]
+    hop = 1
+    while hop < segment_list:
+        arrived = lax.ppermute(held, "ctx", [(i, i + hop) for i in range(segment_list - hop)])
+        held = jnp.concatenate([held, arrived], 0)
+        hop *= 2
     slot_of_segment = (position - jnp.arange(segment_list)) % segment_list
-    gathered = jnp.take(jnp.stack(pieces), slot_of_segment, axis=0).reshape(
-        segment_list, 2, SUMM, width
-    )
+    gathered = jnp.take(held, slot_of_segment, axis=0).reshape(segment_list, 2, SUMM, width)
     memory_keys = gathered[:, 0].reshape(segment_list * SUMM, width)
     memory_values = gathered[:, 1].reshape(segment_list * SUMM, width)
     count = memory_keys.shape[0]

time: 434 us -> 391 us (0.901)
  the two profiles are of different devices: /device:TPU:8 before, /device:TPU:10 now
where the time goes in v3:
time: 391 us; the launch traced here: 389 us
  starting transfers between devices  114 us (29%)
  waiting for transfers between devices  100 us (26%)
  blocking collectives  79.3 us (20%)
  matrix products  40.7 us (10%)
  local copies, waits for them, and re-layouts  32.2 us (8%)
  other arithmetic  20.5 us (5%)
    unnamed x1, blocking collectives  79.3 us
    ppermute x9, waiting for transfers between devices, butterfly_sum(): x = x + lax.ppermute(x, axis, [(i, i ^ k) for i in range(n)])  58.2 us
    ppermute x9, starting transfers between devices, butterfly_sum(): x = x + lax.ppermute(x, axis, [(i, i ^ k) for i in range(n)])  56.9 us
    ppermute x4, starting transfers between devices, per_device(): lax.ppermute(held, 'ctx', [(i, i + hop) for i in range(segment_list - hop)])  40.5 us
    ppermute x4, waiting for transfers between devices, per_device(): lax.ppermute(held, 'ctx', [(i, i + hop) for i in range(segment_list - hop)])  38.2 us
    unnamed x4, starting transfers between devices  16.6 us
    div x4, matrix products, group_grads(): attend = unnorm / jnp.sum(unnorm, -1, keepdims=True)  14.4 us
    unnamed x88, local copies, waits for them, and re-layouts  14.2 us
  transfers between devices with their start and end apart: 17, of which 13 were waited for; matrix products, arithmetic and copies ran while one was open for 7% of the time, Pallas kernels for 0%

profile of v3, /device:TPU:10, one launch (start us, length us, event | category | flops | bytes accessed | tf_op | source)
XLA Modules:
  0.0 389.5 jit_solution(4992389527657794718)
XLA Ops:
  3.0 3.5 collective-permute-start
  10.9 5.7 %collective-permute-start.1 = (bf16[2,100,512]{2,1,0:T(8,128)(2,1)S(1)}, bf16[2,100,512]{2,1,0:T(8,128)(2,1)S(1)}, u32[]{:S(2)}, u32[]{:S(2)}) collective-permute-start(bf16[2,100,512]{2,1,0:T(8,128)(2,1)S(1)} %pad_maximum_fusion.14), channel_id=1, source_target_pairs={{0,2},{1,3},{2,4},{3,5},{4,6},{5,7},{6,8},{7,9},{8,10},{9,11},{10,... | collective-permute-start | bytes 614408 | tf_op jit(solution)/shard_map/ppermute | solution.py:100
  16.7 7.4 %collective-permute-done.1 = bf16[2,100,512]{2,1,0:T(8,128)(2,1)S(1)} collective-permute-done((bf16[2,100,512]{2,1,0:T(8,128)(2,1)S(1)}, bf16[2,100,512]{2,1,0:T(8,128)(2,1)S(1)}, u32[]{:S(2)}, u32[]{:S(2)}) %collective-permute-start.1) | collective-permute-done | bytes 204832 | tf_op jit(solution)/shard_map/ppermute | solution.py:100
  24.2 7.4 %collective-permute-start.2 = (bf16[4,100,512]{2,1,0:T(8,128)(2,1)S(1)}, bf16[4,100,512]{2,1,0:T(8,128)(2,1)S(1)}, u32[]{:S(2)}, u32[]{:S(2)}) collective-permute-start(bf16[4,100,512]{2,1,0:T(8,128)(2,1)S(1)} %pad_maximum_fusion.8), channel_id=1, source_target_pairs={{0,4},{1,5},{2,6},{3,7},{4,8},{5,9},{6,10},{7,11},{8,12},{9,13},{1... | collective-permute-start | bytes 1228808 | tf_op jit(solution)/shard_map/ppermute | solution.py:100
  31.6 17.2 %collective-permute-done.2 = bf16[4,100,512]{2,1,0:T(8,128)(2,1)S(1)} collective-permute-done((bf16[4,100,512]{2,1,0:T(8,128)(2,1)S(1)}, bf16[4,100,512]{2,1,0:T(8,128)(2,1)S(1)}, u32[]{:S(2)}, u32[]{:S(2)}) %collective-permute-start.2) | collective-permute-done | bytes 409632 | tf_op jit(solution)/shard_map/ppermute | solution.py:100
  49.2 23.9 %collective-permute-start.3 = (bf16[8,100,512]{2,0,1:T(8,128)(2,1)S(1)}, bf16[8,100,512]{2,0,1:T(8,128)(2,1)S(1)}, u32[]{:S(2)}, u32[]{:S(2)}) collective-permute-start(bf16[8,100,512]{2,0,1:T(8,128)(2,1)S(1)} %copy.66), channel_id=1, source_target_pairs={{0,8},{1,9},{2,10},{3,11},{4,12},{5,13},{6,14},{7,15},{16,24},{17,... | collective-permute-start | bytes 2457608 | tf_op jit(solution)/shard_map/ppermute | solution.py:100
  76.1 13.6 %collective-permute-done.3 = bf16[8,100,512]{2,0,1:T(8,128)(2,1)S(1)} collective-permute-done((bf16[8,100,512]{2,0,1:T(8,128)(2,1)S(1)}, bf16[8,100,512]{2,0,1:T(8,128)(2,1)S(1)}, u32[]{:S(2)}, u32[]{:S(2)}) %collective-permute-start.3) | collective-permute-done | bytes 819232 | tf_op jit(solution)/shard_map/ppermute | solution.py:100
  106.1 3.8 fusion.6
  109.9 2.8 convolution_bitcast_fusion.1
  116.8 3.5 fusion.2
  120.4 2.8 convolution_bitcast_fusion
  127.2 3.5 fusion.10
  130.8 2.9 convolution_bitcast_fusion.2
  137.6 3.5 fusion.14
  148.6 79.3 %fusion.95 = (f32[56,512]{1,0:T(8,128)}, f32[56,512]{1,0:T(8,128)}) fusion(f32[800,512]{1,0:T(8,128)S(1)} %pad_maximum_fusion.3, f32[800,512]{1,0:T(8,128)} %pad_maximum_fusion), kind=kCustom, calls=%all-reduce-scatter.2 | all-reduce-scatter fusion | flops 917505 | bytes 3508224
  234.2 2.6 collective-permute-done.15
  242.5 18.3 %collective-permute-start.5 = (f32[16,4608]{1,0:T(8,128)S(1)}, f32[16,4608]{1,0:T(8,128)S(1)}, u32[]{:S(2)}, u32[]{:S(2)}) collective-permute-start(f32[16,4608]{1,0:T(8,128)S(1)} %fusion.94), channel_id=1, source_target_pairs={{0,32},{16,48},{32,0},{48,16},{64,96},{80,112},{96,64},{112,80},{1... | collective-permute-start | bytes 884744 | tf_op jit(solution)/shard_map/ppermute | solution.py:63
  260.8 7.9 %collective-permute-done.5 = f32[16,4608]{1,0:T(8,128)S(1)} collective-permute-done((f32[16,4608]{1,0:T(8,128)S(1)}, f32[16,4608]{1,0:T(8,128)S(1)}, u32[]{:S(2)}, u32[]{:S(2)}) %collective-permute-start.5) | collective-permute-done | bytes 294944 | tf_op jit(solution)/shard_map/ppermute | solution.py:63
  268.8 3.6 collective-permute-start.6
  272.4 14.3 %collective-permute-done.6 = f32[16,4608]{1,0:T(8,128)S(1)} collective-permute-done((f32[16,4608]{1,0:T(8,128)S(1)}, f32[16,4608]{1,0:T(8,128)S(1)}, u32[]{:S(2)}, u32[]{:S(2)}) %collective-permute-start.6) | collective-permute-done | bytes 294944 | tf_op jit(solution)/shard_map/ppermute | solution.py:63
  286.7 6.2 %collective-permute-start.7 = (f32[16,4608]{1,0:T(8,128)S(1)}, f32[16,4608]{1,0:T(8,128)S(1)}, u32[]{:S(2)}, u32[]{:S(2)}) collective-permute-start(f32[16,4608]{1,0:T(8,128)S(1)} %add.95), channel_id=1, source_target_pairs={{0,128},{16,144},{32,160},{48,176},{64,192},{80,208},{96,224},{112... | collective-permute-start | bytes 884744 | tf_op jit(solution)/shard_map/ppermute | solution.py:63
  292.9 7.1 %collective-permute-done.7 = f32[16,4608]{1,0:T(8,128)S(1)} collective-permute-done((f32[16,4608]{1,0:T(8,128)S(1)}, f32[16,4608]{1,0:T(8,128)S(1)}, u32[]{:S(2)}, u32[]{:S(2)}) %collective-permute-start.7) | collective-permute-done | bytes 294944 | tf_op jit(solution)/shard_map/ppermute | solution.py:63
  300.1 2.4 collective-permute-start.8
  303.5 8.3 %collective-permute-done.8 = f32[16,4608]{1,0:T(8,128)S(1)} collective-permute-done((f32[16,4608]{1,0:T(8,128)S(1)}, f32[16,4608]{1,0:T(8,128)S(1)}, u32[]{:S(2)}, u32[]{:S(2)}) %collective-permute-start.8) | collective-permute-done | bytes 294944 | tf_op jit(solution)/shard_map/ppermute | solution.py:63
  311.9 3.3 collective-permute-start.9
  317.1 4.2 %collective-permute-done.9 = f32[16,4608]{1,0:T(8,128)S(1)} collective-permute-done((f32[16,4608]{1,0:T(8,128)S(1)}, f32[16,4608]{1,0:T(8,128)S(1)}, u32[]{:S(2)}, u32[]{:S(2)}) %collective-permute-start.9) | collective-permute-done | bytes 294944 | tf_op jit(solution)/shard_map/ppermute | solution.py:63
  322.0 4.6 %collective-permute-start.10 = (f32[16,4608]{1,0:T(8,128)}, f32[16,4608]{1,0:T(8,128)}, u32[]{:S(2)}, u32[]{:S(2)}) collective-permute-start(f32[16,4608]{1,0:T(8,128)} %add.98), channel_id=1, source_target_pairs={{0,2},{1,3},{2,0},{3,1},{4,6},{5,7},{6,4},{7,5},{8,10},{9,11},{10,... | collective-permute-start | bytes 884744 | tf_op jit(solution)/shard_map/ppermute | solution.py:63
  336.8 11.2 %collective-permute-start.14 = (f32[34,512]{1,0:T(8,128)}, f32[34,512]{1,0:T(8,128)S(1)}, u32[]{:S(2)}, u32[]{:S(2)}) collective-permute-start(f32[34,512]{1,0:T(8,128)} %slice.128), channel_id=1, source_target_pairs={{0,2},{1,3},{2,4},{3,5},{4,6},{5,7},{6,8},{7,9},{8,10},{9,11},{10,... | collective-permute-start | bytes 208904
  351.6 8.6 %collective-permute-start.11 = (f32[16,4608]{1,0:T(8,128)}, f32[16,4608]{1,0:T(8,128)}, u32[]{:S(2)}, u32[]{:S(2)}) collective-permute-start(f32[16,4608]{1,0:T(8,128)} %add.99), channel_id=1, source_target_pairs={{0,4},{1,5},{2,6},{3,7},{4,0},{5,1},{6,2},{7,3},{8,12},{9,13},{10,... | collective-permute-start | bytes 884744 | tf_op jit(solution)/shard_map/ppermute | solution.py:63
  362.9 7.8 %collective-permute-done.11 = f32[16,4608]{1,0:T(8,128)} collective-permute-done((f32[16,4608]{1,0:T(8,128)}, f32[16,4608]{1,0:T(8,128)}, u32[]{:S(2)}, u32[]{:S(2)}) %collective-permute-start.11) | collective-permute-done | bytes 294944 | tf_op jit(solution)/shard_map/ppermute | solution.py:63
  371.8 7.9 %collective-permute-start.12 = (f32[16,4608]{1,0:T(8,128)S(1)}, f32[16,4608]{1,0:T(8,128)S(1)}, u32[]{:S(2)}, u32[]{:S(2)}) collective-permute-start(f32[16,4608]{1,0:T(8,128)S(1)} %add.100), channel_id=1, source_target_pairs={{0,8},{1,9},{2,10},{3,11},{4,12},{5,13},{6,14},{7,15},{8,0},{9,1},... | collective-permute-start | bytes 884744 | tf_op jit(solution)/shard_map/ppermute | solution.py:63
  381.0 7.1 %collective-permute-done.12 = f32[16,4608]{1,0:T(8,128)S(1)} collective-permute-done((f32[16,4608]{1,0:T(8,128)S(1)}, f32[16,4608]{1,0:T(8,128)S(1)}, u32[]{:S(2)}, u32[]{:S(2)}) %collective-permute-start.12) | collective-permute-done | bytes 294944 | tf_op jit(solution)/shard_map/ppermute | solution.py:63
  (171 shorter events, 80.4 us)
Async XLA Ops:
  0.6 237.1 %copy-start = (bf16[1,1,128,4096]{3,2,1,0:T(8,128)(2,1)S(1)}, bf16[1,1,128,4096]{3,2,1,0:T(8,128)(2,1)}, u32[]{:S(2)}) copy-start(bf16[1,1,128,4096]{3,2,1,0:T(8,128)(2,1)} %param.12) | copy-start | bytes 3145732
  3.0 7.9 %collective-permute-start = (bf16[1,100,512]{2,1,0:T(8,128)(2,1)S(1)}, bf16[1,100,512]{2,1,0:T(8,128)(2,1)S(1)}, u32[]{:S(2)}, u32[]{:S(2)}) collective-permute-start(bf16[1,100,512]{2,1,0:T(8,128)(2,1)S(1)} %get-tuple-element.10), channel_id=1, source_target_pairs={{0,1},{1,2},{2,3},{3,4},{4,5},{5,6},{6,7},{7,8},{8,9},{9,10},{10,1... | collective-permute-start | bytes 307208 | tf_op jit(solution)/shard_map/ppermute | solution.py:100
  10.9 13.2 %collective-permute-start.1 = (bf16[2,100,512]{2,1,0:T(8,128)(2,1)S(1)}, bf16[2,100,512]{2,1,0:T(8,128)(2,1)S(1)}, u32[]{:S(2)}, u32[]{:S(2)}) collective-permute-start(bf16[2,100,512]{2,1,0:T(8,128)(2,1)S(1)} %pad_maximum_fusion.14), channel_id=1, source_target_pairs={{0,2},{1,3},{2,4},{3,5},{4,6},{5,7},{6,8},{7,9},{8,10},{9,11},{10,... | collective-permute-start | bytes 614408 | tf_op jit(solution)/shard_map/ppermute | solution.py:100
  24.2 24.7 %collective-permute-start.2 = (bf16[4,100,512]{2,1,0:T(8,128)(2,1)S(1)}, bf16[4,100,512]{2,1,0:T(8,128)(2,1)S(1)}, u32[]{:S(2)}, u32[]{:S(2)}) collective-permute-start(bf16[4,100,512]{2,1,0:T(8,128)(2,1)S(1)} %pad_maximum_fusion.8), channel_id=1, source_target_pairs={{0,4},{1,5},{2,6},{3,7},{4,8},{5,9},{6,10},{7,11},{8,12},{9,13},{1... | collective-permute-start | bytes 1228808 | tf_op jit(solution)/shard_map/ppermute | solution.py:100
  49.2 40.5 %collective-permute-start.3 = (bf16[8,100,512]{2,0,1:T(8,128)(2,1)S(1)}, bf16[8,100,512]{2,0,1:T(8,128)(2,1)S(1)}, u32[]{:S(2)}, u32[]{:S(2)}) collective-permute-start(bf16[8,100,512]{2,0,1:T(8,128)(2,1)S(1)} %copy.66), channel_id=1, source_target_pairs={{0,8},{1,9},{2,10},{3,11},{4,12},{5,13},{6,14},{7,15},{16,24},{17,... | collective-permute-start | bytes 2457608 | tf_op jit(solution)/shard_map/ppermute | solution.py:100
  106.1 10.7 %copy-start.28 = (bf16[928,128,1]{1,0,2:T(8,128)(2,1)}, bf16[928,128,1]{1,0,2:T(8,128)(2,1)S(1)}, u32[]{:S(2)}) copy-start(bf16[928,128,1]{1,0,2:T(8,128)(2,1)S(1)} %fusion.66) | copy-start | bytes 712708
  227.9 8.8 %copy-start.30 = (f32[56,512]{1,0:T(8,128)S(1)}, f32[56,512]{1,0:T(8,128)}, u32[]{:S(2)}) copy-start(f32[56,512]{1,0:T(8,128)} %get-tuple-element.8) | copy-start | bytes 344068
  227.9 9.8 %copy-start.36 = (bf16[4096,16]{0,1:T(8,128)(2,1)S(1)}, bf16[4096,16]{0,1:T(8,128)(2,1)}, u32[]{:S(2)}) copy-start(bf16[4096,16]{0,1:T(8,128)(2,1)} %param.13) | copy-start | bytes 393220
  228.9 9.4 %copy-start.38 = (bf16[16,512]{1,0:T(8,128)(2,1)S(1)}, bf16[16,512]{1,0:T(8,128)(2,1)}, u32[]{:S(2)}) copy-start(bf16[16,512]{1,0:T(8,128)(2,1)} %param.14) | copy-start | bytes 49156
  228.9 7.9 %collective-permute-start.15 = (f32[56,512]{1,0:T(8,128)}, f32[56,512]{1,0:T(8,128)S(1)}, u32[]{:S(2)}, u32[]{:S(2)}) collective-permute-start(f32[56,512]{1,0:T(8,128)} %get-tuple-element.8), channel_id=1, source_target_pairs={{0,1},{1,2},{2,3},{3,4},{4,5},{5,6},{6,7},{7,8},{8,9},{9,10},{10,1... | collective-permute-start | bytes 344072
  230.8 3.4 collective-permute-start.16
  238.8 63.7 %copy-start.4 = (bf16[4,128,928]{1,2,0:T(8,128)(2,1)S(1)}, bf16[4,128,928]{1,2,0:T(8,128)(2,1)}, u32[]{:S(2)}) copy-start(bf16[4,128,928]{1,2,0:T(8,128)(2,1)} %copy-done.3) | copy-start | bytes 2850820
  238.8 63.7 %copy-start.27 = (bf16[1,1,128,512]{3,2,1,0:T(8,128)(2,1)S(1)}, bf16[1,1,128,512]{3,2,1,0:T(8,128)(2,1)}, u32[]{:S(2)}) copy-start(bf16[1,1,128,512]{3,2,1,0:T(8,128)(2,1)} %param.9) | copy-start | bytes 393220
  238.8 3.6 collective-permute-start.4
  242.5 26.3 %collective-permute-start.5 = (f32[16,4608]{1,0:T(8,128)S(1)}, f32[16,4608]{1,0:T(8,128)S(1)}, u32[]{:S(2)}, u32[]{:S(2)}) collective-permute-start(f32[16,4608]{1,0:T(8,128)S(1)} %fusion.94), channel_id=1, source_target_pairs={{0,32},{16,48},{32,0},{48,16},{64,96},{80,112},{96,64},{112,80},{1... | collective-permute-start | bytes 884744 | tf_op jit(solution)/shard_map/ppermute | solution.py:63
  268.8 17.9 %collective-permute-start.6 = (f32[16,4608]{1,0:T(8,128)S(1)}, f32[16,4608]{1,0:T(8,128)S(1)}, u32[]{:S(2)}, u32[]{:S(2)}) collective-permute-start(f32[16,4608]{1,0:T(8,128)S(1)} %add.94), channel_id=1, source_target_pairs={{0,64},{16,80},{32,96},{48,112},{64,0},{80,16},{96,32},{112,48},{1... | collective-permute-start | bytes 884744 | tf_op jit(solution)/shard_map/ppermute | solution.py:63
  286.7 28.5 %copy-start.8 = (bf16[4,128,928]{1,2,0:T(8,128)(2,1)S(1)}, bf16[4,128,928]{1,2,0:T(8,128)(2,1)}, u32[]{:S(2)}) copy-start(bf16[4,128,928]{1,2,0:T(8,128)(2,1)} %copy-done.7) | copy-start | bytes 2850820
  286.7 13.3 %collective-permute-start.7 = (f32[16,4608]{1,0:T(8,128)S(1)}, f32[16,4608]{1,0:T(8,128)S(1)}, u32[]{:S(2)}, u32[]{:S(2)}) collective-permute-start(f32[16,4608]{1,0:T(8,128)S(1)} %add.95), channel_id=1, source_target_pairs={{0,128},{16,144},{32,160},{48,176},{64,192},{80,208},{96,224},{112... | collective-permute-start | bytes 884744 | tf_op jit(solution)/shard_map/ppermute | solution.py:63
  300.1 11.7 %collective-permute-start.8 = (f32[16,4608]{1,0:T(8,128)S(1)}, f32[16,4608]{1,0:T(8,128)S(1)}, u32[]{:S(2)}, u32[]{:S(2)}) collective-permute-start(f32[16,4608]{1,0:T(8,128)S(1)} %add.96), channel_id=1, source_target_pairs={{0,256},{16,272},{32,288},{48,304},{64,320},{80,336},{96,352},{112... | collective-permute-start | bytes 884744 | tf_op jit(solution)/shard_map/ppermute | solution.py:63
  303.5 12.6 %copy-start.2 = (bf16[4,128,928]{1,2,0:T(8,128)(2,1)S(1)}, bf16[4,128,928]{1,2,0:T(8,128)(2,1)}, u32[]{:S(2)}) copy-start(bf16[4,128,928]{1,2,0:T(8,128)(2,1)} %copy-done.1) | copy-start | bytes 2850820
  303.5 12.6 %copy-start.29 = (bf16[928,128,1]{1,0,2:T(8,128)(2,1)S(1)}, bf16[928,128,1]{1,0,2:T(8,128)(2,1)}, u32[]{:S(2)}) copy-start(bf16[928,128,1]{1,0,2:T(8,128)(2,1)} %copy-done.28) | copy-start | bytes 712708
  311.8 14.8 %copy-start.6 = (bf16[4,128,928]{1,2,0:T(8,128)(2,1)S(1)}, bf16[4,128,928]{1,2,0:T(8,128)(2,1)}, u32[]{:S(2)}) copy-start(bf16[4,128,928]{1,2,0:T(8,128)(2,1)} %copy-done.5) | copy-start | bytes 2850820
  311.9 9.4 %collective-permute-start.9 = (f32[16,4608]{1,0:T(8,128)S(1)}, f32[16,4608]{1,0:T(8,128)S(1)}, u32[]{:S(2)}, u32[]{:S(2)}) collective-permute-start(f32[16,4608]{1,0:T(8,128)S(1)} %add.97), channel_id=1, source_target_pairs={{0,1},{1,0},{2,3},{3,2},{4,5},{5,4},{6,7},{7,6},{8,9},{9,8},{10,11... | collective-permute-start | bytes 884744 | tf_op jit(solution)/shard_map/ppermute | solution.py:63
  322.0 27.8 %collective-permute-start.10 = (f32[16,4608]{1,0:T(8,128)}, f32[16,4608]{1,0:T(8,128)}, u32[]{:S(2)}, u32[]{:S(2)}) collective-permute-start(f32[16,4608]{1,0:T(8,128)} %add.98), channel_id=1, source_target_pairs={{0,2},{1,3},{2,0},{3,1},{4,6},{5,7},{6,4},{7,5},{8,10},{9,11},{10,... | collective-permute-start | bytes 884744 | tf_op jit(solution)/shard_map/ppermute | solution.py:63
  327.6 32.6 %copy-start.18 = (f32[928,128]{1,0:T(8,128)S(1)}, f32[928,128]{1,0:T(8,128)}, u32[]{:S(2)}) copy-start(f32[928,128]{1,0:T(8,128)} %fusion.19) | copy-start | bytes 1425412
  327.6 32.6 %copy-start.20 = (f32[928,128]{1,0:T(8,128)S(1)}, f32[928,128]{1,0:T(8,128)}, u32[]{:S(2)}) copy-start(f32[928,128]{1,0:T(8,128)} %fusion.18) | copy-start | bytes 1425412
  327.6 32.6 %copy-start.22 = (f32[928,128]{1,0:T(8,128)S(1)}, f32[928,128]{1,0:T(8,128)}, u32[]{:S(2)}) copy-start(f32[928,128]{1,0:T(8,128)} %fusion.20) | copy-start | bytes 1425412
  327.6 32.6 %copy-start.24 = (f32[928,128]{1,0:T(8,128)S(1)}, f32[928,128]{1,0:T(8,128)}, u32[]{:S(2)}) copy-start(f32[928,128]{1,0:T(8,128)} %copy-done.23) | copy-start | bytes 1425412
  329.3 31.0 %collective-permute-start.13 = (f32[56,512]{1,0:T(8,128)}, f32[56,512]{1,0:T(8,128)}, u32[]{:S(2)}, u32[]{:S(2)}) collective-permute-start(f32[56,512]{1,0:T(8,128)} %get-tuple-element.7), channel_id=1, source_target_pairs={{0,1},{1,2},{2,3},{3,4},{4,5},{5,6},{6,7},{7,8},{8,9},{9,10},{10,1... | collective-permute-start | bytes 344072
  336.8 23.5 %collective-permute-start.14 = (f32[34,512]{1,0:T(8,128)}, f32[34,512]{1,0:T(8,128)S(1)}, u32[]{:S(2)}, u32[]{:S(2)}) collective-permute-start(f32[34,512]{1,0:T(8,128)} %slice.128), channel_id=1, source_target_pairs={{0,2},{1,3},{2,4},{3,5},{4,6},{5,7},{6,8},{7,9},{8,10},{9,11},{10,... | collective-permute-start | bytes 208904
  351.6 19.1 %collective-permute-start.11 = (f32[16,4608]{1,0:T(8,128)}, f32[16,4608]{1,0:T(8,128)}, u32[]{:S(2)}, u32[]{:S(2)}) collective-permute-start(f32[16,4608]{1,0:T(8,128)} %add.99), channel_id=1, source_target_pairs={{0,4},{1,5},{2,6},{3,7},{4,0},{5,1},{6,2},{7,3},{8,12},{9,13},{10,... | collective-permute-start | bytes 884744 | tf_op jit(solution)/shard_map/ppermute | solution.py:63
  371.8 16.3 %collective-permute-start.12 = (f32[16,4608]{1,0:T(8,128)S(1)}, f32[16,4608]{1,0:T(8,128)S(1)}, u32[]{:S(2)}, u32[]{:S(2)}) collective-permute-start(f32[16,4608]{1,0:T(8,128)S(1)} %add.100), channel_id=1, source_target_pairs={{0,8},{1,9},{2,10},{3,11},{4,12},{5,13},{6,14},{7,15},{8,0},{9,1},... | collective-permute-start | bytes 884744 | tf_op jit(solution)/shard_map/ppermute | solution.py:63
  (24 other events, 60.7 us)

commit v4 on v3

--- a/solution.py
+++ b/solution.py
@@ -1,6 +1,7 @@
 import math
 
 import jax
+import numpy as np
 import jax.numpy as jnp
 from jax import lax
 from jax.sharding import PartitionSpec as P
@@ -95,12 +96,15 @@
     own_values = lax.dynamic_slice_in_dim(value_local, length, SUMM, 0)
     own_summary = jnp.concatenate([own_keys, own_values], 0)
     held = own_summary[None]
-    hop = 1
-    while hop < segment_list:
+    distance_of_slot = [0]
+    hop = segment_list // 2
+    while hop >= 1:
         arrived = lax.ppermute(held, "ctx", [(i, i + hop) for i in range(segment_list - hop)])
         held = jnp.concatenate([held, arrived], 0)
-        hop *= 2
-    slot_of_segment = (position - jnp.arange(segment_list)) % segment_list
+        distance_of_slot = distance_of_slot + [d + hop for d in distance_of_slot]
+        hop //= 2
+    slot_of_distance = np.argsort(np.array(distance_of_slot)).astype(np.int32)
+    slot_of_segment = jnp.asarray(slot_of_distance)[(position - jnp.arange(segment_list)) % segment_list]
     gathered = jnp.take(held, slot_of_segment, axis=0).reshape(segment_list, 2, SUMM, width)
     memory_keys = gathered[:, 0].reshape(segment_list * SUMM, width)
     memory_values = gathered[:, 1].reshape(segment_list * SUMM, width)

time: 391 us -> 389 us (level)
  the two profiles are of different devices: /device:TPU:10 before, /device:TPU:104 now
where the time goes in v4:
time: 389 us; the launch traced here: 388 us
  waiting for transfers between devices  113 us (29%)
  blocking collectives  89.1 us (23%)
  starting transfers between devices  88.7 us (23%)
  matrix products  40.7 us (10%)
  local copies, waits for them, and re-layouts  33.5 us (9%)
  other arithmetic  20.5 us (5%)
    unnamed x1, blocking collectives  89.1 us
    ppermute x9, waiting for transfers between devices, butterfly_sum(): x = x + lax.ppermute(x, axis, [(i, i ^ k) for i in range(n)])  70.5 us
    ppermute x4, waiting for transfers between devices, per_device(): lax.ppermute(held, 'ctx', [(i, i + hop) for i in range(segment_list - hop)])  41 us
    unnamed x4, starting transfers between devices  38.8 us
    ppermute x4, starting transfers between devices, per_device(): lax.ppermute(held, 'ctx', [(i, i + hop) for i in range(segment_list - hop)])  25 us
    ppermute x9, starting transfers between devices, butterfly_sum(): x = x + lax.ppermute(x, axis, [(i, i ^ k) for i in range(n)])  24.9 us
    div x4, matrix products, group_grads(): attend = unnorm / jnp.sum(unnorm, -1, keepdims=True)  14.4 us
    unnamed x88, local copies, waits for them, and re-layouts  14.2 us
  transfers between devices with their start and end apart: 17, of which 13 were waited for; matrix products, arithmetic and copies ran while one was open for 7% of the time, Pallas kernels for 0%

profile of v4, /device:TPU:104, one launch (start us, length us, event | category | flops | bytes accessed | tf_op | source)
XLA Modules:
  0.0 387.8 jit_solution(17958906203340725796)
XLA Ops:
  3.0 10.0 %collective-permute-start = (bf16[1,100,512]{2,1,0:T(8,128)(2,1)S(1)}, bf16[1,100,512]{2,1,0:T(8,128)(2,1)S(1)}, u32[]{:S(2)}, u32[]{:S(2)}) collective-permute-start(bf16[1,100,512]{2,1,0:T(8,128)(2,1)S(1)} %get-tuple-element.10), channel_id=1, source_target_pairs={{0,8},{1,9},{2,10},{3,11},{4,12},{5,13},{6,14},{7,15},{16,24},{17,... | collective-permute-start | bytes 307208 | tf_op jit(solution)/shard_map/ppermute | solution.py:102
  18.9 7.4 %collective-permute-start.1 = (bf16[2,100,512]{2,1,0:T(8,128)(2,1)S(1)}, bf16[2,100,512]{2,1,0:T(8,128)(2,1)S(1)}, u32[]{:S(2)}, u32[]{:S(2)}) collective-permute-start(bf16[2,100,512]{2,1,0:T(8,128)(2,1)S(1)} %pad_maximum_fusion.14), channel_id=1, source_target_pairs={{0,4},{1,5},{2,6},{3,7},{4,8},{5,9},{6,10},{7,11},{8,12},{9,13},{1... | collective-permute-start | bytes 614408 | tf_op jit(solution)/shard_map/ppermute | solution.py:102
  27.1 8.3 %collective-permute-done.1 = bf16[2,100,512]{2,1,0:T(8,128)(2,1)S(1)} collective-permute-done((bf16[2,100,512]{2,1,0:T(8,128)(2,1)S(1)}, bf16[2,100,512]{2,1,0:T(8,128)(2,1)S(1)}, u32[]{:S(2)}, u32[]{:S(2)}) %collective-permute-start.1) | collective-permute-done | bytes 204832 | tf_op jit(solution)/shard_map/ppermute | solution.py:102
  35.5 3.6 collective-permute-start.2
  39.1 17.0 %collective-permute-done.2 = bf16[4,100,512]{2,1,0:T(8,128)(2,1)S(1)} collective-permute-done((bf16[4,100,512]{2,1,0:T(8,128)(2,1)S(1)}, bf16[4,100,512]{2,1,0:T(8,128)(2,1)S(1)}, u32[]{:S(2)}, u32[]{:S(2)}) %collective-permute-start.2) | collective-permute-done | bytes 409632 | tf_op jit(solution)/shard_map/ppermute | solution.py:102
  56.4 4.0 %collective-permute-start.3 = (bf16[8,100,512]{2,0,1:T(8,128)(2,1)S(1)}, bf16[8,100,512]{2,0,1:T(8,128)(2,1)S(1)}, u32[]{:S(2)}, u32[]{:S(2)}) collective-permute-start(bf16[8,100,512]{2,0,1:T(8,128)(2,1)S(1)} %copy.67), channel_id=1, source_target_pairs={{0,1},{1,2},{2,3},{3,4},{4,5},{5,6},{6,7},{7,8},{8,9},{9,10},{10,1... | collective-permute-start | bytes 2457608 | tf_op jit(solution)/shard_map/ppermute | solution.py:102
  62.6 15.8 %collective-permute-done.3 = bf16[8,100,512]{2,0,1:T(8,128)(2,1)S(1)} collective-permute-done((bf16[8,100,512]{2,0,1:T(8,128)(2,1)S(1)}, bf16[8,100,512]{2,0,1:T(8,128)(2,1)S(1)}, u32[]{:S(2)}, u32[]{:S(2)}) %collective-permute-start.3) | collective-permute-done | bytes 819232 | tf_op jit(solution)/shard_map/ppermute | solution.py:102
  79.5 2.1 gather_fusion.1
  94.8 3.8 fusion.6
  98.6 2.8 convolution_bitcast_fusion.1
  105.5 3.5 fusion.2
  109.1 2.8 convolution_bitcast_fusion
  115.9 3.5 fusion.10
  119.4 2.9 convolution_bitcast_fusion.2
  126.3 3.5 fusion.14
  129.8 2.1 convolution_bitcast_fusion.3
  137.2 89.1 %fusion.95 = (f32[56,512]{1,0:T(8,128)}, f32[56,512]{1,0:T(8,128)}) fusion(f32[800,512]{1,0:T(8,128)S(1)} %pad_maximum_fusion.3, f32[800,512]{1,0:T(8,128)} %pad_maximum_fusion), kind=kCustom, calls=%all-reduce-scatter.2 | all-reduce-scatter fusion | flops 917505 | bytes 3508224
  227.3 9.7 %collective-permute-start.15 = (f32[56,512]{1,0:T(8,128)}, f32[56,512]{1,0:T(8,128)S(1)}, u32[]{:S(2)}, u32[]{:S(2)}) collective-permute-start(f32[56,512]{1,0:T(8,128)} %get-tuple-element.8), channel_id=1, source_target_pairs={{0,1},{1,2},{2,3},{3,4},{4,5},{5,6},{6,7},{7,8},{8,9},{9,10},{10,1... | collective-permute-start | bytes 344072
  237.0 18.7 %collective-permute-start.16 = (f32[34,512]{1,0:T(8,128)S(1)}, f32[34,512]{1,0:T(8,128)S(1)}, u32[]{:S(2)}, u32[]{:S(2)}) collective-permute-start(f32[34,512]{1,0:T(8,128)S(1)} %slice.131), channel_id=1, source_target_pairs={{0,2},{1,3},{2,4},{3,5},{4,6},{5,7},{6,8},{7,9},{8,10},{9,11},{10,... | collective-permute-start | bytes 208904
  259.6 2.1 collective-permute-start.4
  265.2 9.0 %collective-permute-done.5 = f32[16,4608]{1,0:T(8,128)S(1)} collective-permute-done((f32[16,4608]{1,0:T(8,128)S(1)}, f32[16,4608]{1,0:T(8,128)S(1)}, u32[]{:S(2)}, u32[]{:S(2)}) %collective-permute-start.5) | collective-permute-done | bytes 294944 | tf_op jit(solution)/shard_map/ppermute | solution.py:64
  274.3 3.1 collective-permute-start.6
  277.3 12.0 %collective-permute-done.6 = f32[16,4608]{1,0:T(8,128)S(1)} collective-permute-done((f32[16,4608]{1,0:T(8,128)S(1)}, f32[16,4608]{1,0:T(8,128)S(1)}, u32[]{:S(2)}, u32[]{:S(2)}) %collective-permute-start.6) | collective-permute-done | bytes 294944 | tf_op jit(solution)/shard_map/ppermute | solution.py:64
  289.4 2.8 collective-permute-start.7
  292.2 8.1 %collective-permute-done.7 = f32[16,4608]{1,0:T(8,128)S(1)} collective-permute-done((f32[16,4608]{1,0:T(8,128)S(1)}, f32[16,4608]{1,0:T(8,128)S(1)}, u32[]{:S(2)}, u32[]{:S(2)}) %collective-permute-start.7) | collective-permute-done | bytes 294944 | tf_op jit(solution)/shard_map/ppermute | solution.py:64
  300.4 4.2 %collective-permute-start.8 = (f32[16,4608]{1,0:T(8,128)S(1)}, f32[16,4608]{1,0:T(8,128)S(1)}, u32[]{:S(2)}, u32[]{:S(2)}) collective-permute-start(f32[16,4608]{1,0:T(8,128)S(1)} %add.102), channel_id=1, source_target_pairs={{0,256},{16,272},{32,288},{48,304},{64,320},{80,336},{96,352},{112... | collective-permute-start | bytes 884744 | tf_op jit(solution)/shard_map/ppermute | solution.py:64
  305.6 6.2 %collective-permute-done.8 = f32[16,4608]{1,0:T(8,128)S(1)} collective-permute-done((f32[16,4608]{1,0:T(8,128)S(1)}, f32[16,4608]{1,0:T(8,128)S(1)}, u32[]{:S(2)}, u32[]{:S(2)}) %collective-permute-start.8) | collective-permute-done | bytes 294944 | tf_op jit(solution)/shard_map/ppermute | solution.py:64
  315.9 5.1 %collective-permute-done.9 = f32[16,4608]{1,0:T(8,128)S(1)} collective-permute-done((f32[16,4608]{1,0:T(8,128)S(1)}, f32[16,4608]{1,0:T(8,128)S(1)}, u32[]{:S(2)}, u32[]{:S(2)}) %collective-permute-start.9) | collective-permute-done | bytes 294944 | tf_op jit(solution)/shard_map/ppermute | solution.py:64
  321.7 5.0 %collective-permute-start.10 = (f32[16,4608]{1,0:T(8,128)}, f32[16,4608]{1,0:T(8,128)}, u32[]{:S(2)}, u32[]{:S(2)}) collective-permute-start(f32[16,4608]{1,0:T(8,128)} %add.104), channel_id=1, source_target_pairs={{0,2},{1,3},{2,0},{3,1},{4,6},{5,7},{6,4},{7,5},{8,10},{9,11},{10,... | collective-permute-start | bytes 884744 | tf_op jit(solution)/shard_map/ppermute | solution.py:64
  336.7 8.5 %collective-permute-start.14 = (f32[34,512]{1,0:T(8,128)}, f32[34,512]{1,0:T(8,128)S(1)}, u32[]{:S(2)}, u32[]{:S(2)}) collective-permute-start(f32[34,512]{1,0:T(8,128)} %slice.130), channel_id=1, source_target_pairs={{0,2},{1,3},{2,4},{3,5},{4,6},{5,7},{6,8},{7,9},{8,10},{9,11},{10,... | collective-permute-start | bytes 208904
  353.6 13.0 %collective-permute-done.11 = f32[16,4608]{1,0:T(8,128)} collective-permute-done((f32[16,4608]{1,0:T(8,128)}, f32[16,4608]{1,0:T(8,128)}, u32[]{:S(2)}, u32[]{:S(2)}) %collective-permute-start.11) | collective-permute-done | bytes 294944 | tf_op jit(solution)/shard_map/ppermute | solution.py:64
  370.9 15.5 %collective-permute-done.12 = f32[16,4608]{1,0:T(8,128)S(1)} collective-permute-done((f32[16,4608]{1,0:T(8,128)S(1)}, f32[16,4608]{1,0:T(8,128)S(1)}, u32[]{:S(2)}, u32[]{:S(2)}) %collective-permute-start.12) | collective-permute-done | bytes 294944 | tf_op jit(solution)/shard_map/ppermute | solution.py:64
  (174 shorter events, 79.9 us)
Async XLA Ops:
  0.6 257.9 %copy-start = (bf16[1,1,128,4096]{3,2,1,0:T(8,128)(2,1)S(1)}, bf16[1,1,128,4096]{3,2,1,0:T(8,128)(2,1)}, u32[]{:S(2)}) copy-start(bf16[1,1,128,4096]{3,2,1,0:T(8,128)(2,1)} %param.13) | copy-start | bytes 3145732
  0.6 16.0 %copy-start.31 = (bf16[1,1,128,2048]{3,2,1,0:T(8,128)(2,1)S(1)}, bf16[1,1,128,2048]{3,2,1,0:T(8,128)(2,1)}, u32[]{:S(2)}) copy-start(bf16[1,1,128,2048]{3,2,1,0:T(8,128)(2,1)} %param.12) | copy-start | bytes 1572868
  3.0 15.9 %collective-permute-start = (bf16[1,100,512]{2,1,0:T(8,128)(2,1)S(1)}, bf16[1,100,512]{2,1,0:T(8,128)(2,1)S(1)}, u32[]{:S(2)}, u32[]{:S(2)}) collective-permute-start(bf16[1,100,512]{2,1,0:T(8,128)(2,1)S(1)} %get-tuple-element.10), channel_id=1, source_target_pairs={{0,8},{1,9},{2,10},{3,11},{4,12},{5,13},{6,14},{7,15},{16,24},{17,... | collective-permute-start | bytes 307208 | tf_op jit(solution)/shard_map/ppermute | solution.py:102
  18.9 16.5 %collective-permute-start.1 = (bf16[2,100,512]{2,1,0:T(8,128)(2,1)S(1)}, bf16[2,100,512]{2,1,0:T(8,128)(2,1)S(1)}, u32[]{:S(2)}, u32[]{:S(2)}) collective-permute-start(bf16[2,100,512]{2,1,0:T(8,128)(2,1)S(1)} %pad_maximum_fusion.14), channel_id=1, source_target_pairs={{0,4},{1,5},{2,6},{3,7},{4,8},{5,9},{6,10},{7,11},{8,12},{9,13},{1... | collective-permute-start | bytes 614408 | tf_op jit(solution)/shard_map/ppermute | solution.py:102
  35.5 20.6 %collective-permute-start.2 = (bf16[4,100,512]{2,1,0:T(8,128)(2,1)S(1)}, bf16[4,100,512]{2,1,0:T(8,128)(2,1)S(1)}, u32[]{:S(2)}, u32[]{:S(2)}) collective-permute-start(bf16[4,100,512]{2,1,0:T(8,128)(2,1)S(1)} %pad_maximum_fusion.8), channel_id=1, source_target_pairs={{0,2},{1,3},{2,4},{3,5},{4,6},{5,7},{6,8},{7,9},{8,10},{9,11},{10,... | collective-permute-start | bytes 1228808 | tf_op jit(solution)/shard_map/ppermute | solution.py:102
  56.4 22.0 %collective-permute-start.3 = (bf16[8,100,512]{2,0,1:T(8,128)(2,1)S(1)}, bf16[8,100,512]{2,0,1:T(8,128)(2,1)S(1)}, u32[]{:S(2)}, u32[]{:S(2)}) collective-permute-start(bf16[8,100,512]{2,0,1:T(8,128)(2,1)S(1)} %copy.67), channel_id=1, source_target_pairs={{0,1},{1,2},{2,3},{3,4},{4,5},{5,6},{6,7},{7,8},{8,9},{9,10},{10,1... | collective-permute-start | bytes 2457608 | tf_op jit(solution)/shard_map/ppermute | solution.py:102
  94.7 10.7 %copy-start.28 = (bf16[928,128,1]{1,0,2:T(8,128)(2,1)}, bf16[928,128,1]{1,0,2:T(8,128)(2,1)S(1)}, u32[]{:S(2)}) copy-start(bf16[928,128,1]{1,0,2:T(8,128)(2,1)S(1)} %fusion.66) | copy-start | bytes 712708
  226.3 31.3 %copy-start.30 = (f32[56,512]{1,0:T(8,128)S(1)}, f32[56,512]{1,0:T(8,128)}, u32[]{:S(2)}) copy-start(f32[56,512]{1,0:T(8,128)} %get-tuple-element.8) | copy-start | bytes 344068
  226.3 32.3 %copy-start.36 = (bf16[4096,16]{0,1:T(8,128)(2,1)S(1)}, bf16[4096,16]{0,1:T(8,128)(2,1)}, u32[]{:S(2)}) copy-start(bf16[4096,16]{0,1:T(8,128)(2,1)} %param.14) | copy-start | bytes 393220
  227.3 31.9 %copy-start.38 = (bf16[16,512]{1,0:T(8,128)(2,1)S(1)}, bf16[16,512]{1,0:T(8,128)(2,1)}, u32[]{:S(2)}) copy-start(bf16[16,512]{1,0:T(8,128)(2,1)} %param.15) | copy-start | bytes 49156
  227.3 30.3 %collective-permute-start.15 = (f32[56,512]{1,0:T(8,128)}, f32[56,512]{1,0:T(8,128)S(1)}, u32[]{:S(2)}, u32[]{:S(2)}) collective-permute-start(f32[56,512]{1,0:T(8,128)} %get-tuple-element.8), channel_id=1, source_target_pairs={{0,1},{1,2},{2,3},{3,4},{4,5},{5,6},{6,7},{7,8},{8,9},{9,10},{10,1... | collective-permute-start | bytes 344072
  237.0 20.6 %collective-permute-start.16 = (f32[34,512]{1,0:T(8,128)S(1)}, f32[34,512]{1,0:T(8,128)S(1)}, u32[]{:S(2)}, u32[]{:S(2)}) collective-permute-start(f32[34,512]{1,0:T(8,128)S(1)} %slice.131), channel_id=1, source_target_pairs={{0,2},{1,3},{2,4},{3,5},{4,6},{5,7},{6,8},{7,9},{8,10},{9,11},{10,... | collective-permute-start | bytes 208904
  259.6 45.0 %copy-start.4 = (bf16[4,128,928]{1,2,0:T(8,128)(2,1)S(1)}, bf16[4,128,928]{1,2,0:T(8,128)(2,1)}, u32[]{:S(2)}) copy-start(bf16[4,128,928]{1,2,0:T(8,128)(2,1)} %copy-done.3) | copy-start | bytes 2850820
  259.6 45.0 %copy-start.27 = (bf16[1,1,128,512]{3,2,1,0:T(8,128)(2,1)S(1)}, bf16[1,1,128,512]{3,2,1,0:T(8,128)(2,1)}, u32[]{:S(2)}) copy-start(bf16[1,1,128,512]{3,2,1,0:T(8,128)(2,1)} %param.10) | copy-start | bytes 393220
  259.6 3.6 collective-permute-start.4
  263.3 10.9 %collective-permute-start.5 = (f32[16,4608]{1,0:T(8,128)S(1)}, f32[16,4608]{1,0:T(8,128)S(1)}, u32[]{:S(2)}, u32[]{:S(2)}) collective-permute-start(f32[16,4608]{1,0:T(8,128)S(1)} %fusion.94), channel_id=1, source_target_pairs={{0,32},{16,48},{32,0},{48,16},{64,96},{80,112},{96,64},{112,80},{1... | collective-permute-start | bytes 884744 | tf_op jit(solution)/shard_map/ppermute | solution.py:64
  274.3 15.1 %collective-permute-start.6 = (f32[16,4608]{1,0:T(8,128)S(1)}, f32[16,4608]{1,0:T(8,128)S(1)}, u32[]{:S(2)}, u32[]{:S(2)}) collective-permute-start(f32[16,4608]{1,0:T(8,128)S(1)} %add.100), channel_id=1, source_target_pairs={{0,64},{16,80},{32,96},{48,112},{64,0},{80,16},{96,32},{112,48},{1... | collective-permute-start | bytes 884744 | tf_op jit(solution)/shard_map/ppermute | solution.py:64
  289.4 24.5 %copy-start.8 = (bf16[4,128,928]{1,2,0:T(8,128)(2,1)S(1)}, bf16[4,128,928]{1,2,0:T(8,128)(2,1)}, u32[]{:S(2)}) copy-start(bf16[4,128,928]{1,2,0:T(8,128)(2,1)} %copy-done.7) | copy-start | bytes 2850820
  289.4 10.9 %collective-permute-start.7 = (f32[16,4608]{1,0:T(8,128)S(1)}, f32[16,4608]{1,0:T(8,128)S(1)}, u32[]{:S(2)}, u32[]{:S(2)}) collective-permute-start(f32[16,4608]{1,0:T(8,128)S(1)} %add.101), channel_id=1, source_target_pairs={{0,128},{16,144},{32,160},{48,176},{64,192},{80,208},{96,224},{112... | collective-permute-start | bytes 884744 | tf_op jit(solution)/shard_map/ppermute | solution.py:64
  300.4 11.4 %collective-permute-start.8 = (f32[16,4608]{1,0:T(8,128)S(1)}, f32[16,4608]{1,0:T(8,128)S(1)}, u32[]{:S(2)}, u32[]{:S(2)}) collective-permute-start(f32[16,4608]{1,0:T(8,128)S(1)} %add.102), channel_id=1, source_target_pairs={{0,256},{16,272},{32,288},{48,304},{64,320},{80,336},{96,352},{112... | collective-permute-start | bytes 884744 | tf_op jit(solution)/shard_map/ppermute | solution.py:64
  305.6 9.3 %copy-start.29 = (bf16[928,128,1]{1,0,2:T(8,128)(2,1)S(1)}, bf16[928,128,1]{1,0,2:T(8,128)(2,1)}, u32[]{:S(2)}) copy-start(bf16[928,128,1]{1,0,2:T(8,128)(2,1)} %copy-done.28) | copy-start | bytes 712708
  311.8 14.9 %copy-start.6 = (bf16[4,128,928]{1,2,0:T(8,128)(2,1)S(1)}, bf16[4,128,928]{1,2,0:T(8,128)(2,1)}, u32[]{:S(2)}) copy-start(bf16[4,128,928]{1,2,0:T(8,128)(2,1)} %copy-done.5) | copy-start | bytes 2850820
  311.8 9.1 %collective-permute-start.9 = (f32[16,4608]{1,0:T(8,128)S(1)}, f32[16,4608]{1,0:T(8,128)S(1)}, u32[]{:S(2)}, u32[]{:S(2)}) collective-permute-start(f32[16,4608]{1,0:T(8,128)S(1)} %add.103), channel_id=1, source_target_pairs={{0,1},{1,0},{2,3},{3,2},{4,5},{5,4},{6,7},{7,6},{8,9},{9,8},{10,11... | collective-permute-start | bytes 884744 | tf_op jit(solution)/shard_map/ppermute | solution.py:64
  321.7 25.3 %collective-permute-start.10 = (f32[16,4608]{1,0:T(8,128)}, f32[16,4608]{1,0:T(8,128)}, u32[]{:S(2)}, u32[]{:S(2)}) collective-permute-start(f32[16,4608]{1,0:T(8,128)} %add.104), channel_id=1, source_target_pairs={{0,2},{1,3},{2,0},{3,1},{4,6},{5,7},{6,4},{7,5},{8,10},{9,11},{10,... | collective-permute-start | bytes 884744 | tf_op jit(solution)/shard_map/ppermute | solution.py:64
  327.7 23.0 %copy-start.18 = (f32[928,128]{1,0:T(8,128)S(1)}, f32[928,128]{1,0:T(8,128)}, u32[]{:S(2)}) copy-start(f32[928,128]{1,0:T(8,128)} %fusion.19) | copy-start | bytes 1425412
  327.7 23.0 %copy-start.20 = (f32[928,128]{1,0:T(8,128)S(1)}, f32[928,128]{1,0:T(8,128)}, u32[]{:S(2)}) copy-start(f32[928,128]{1,0:T(8,128)} %fusion.18) | copy-start | bytes 1425412
  327.7 23.0 %copy-start.22 = (f32[928,128]{1,0:T(8,128)S(1)}, f32[928,128]{1,0:T(8,128)}, u32[]{:S(2)}) copy-start(f32[928,128]{1,0:T(8,128)} %fusion.20) | copy-start | bytes 1425412
  327.7 23.0 %copy-start.24 = (f32[928,128]{1,0:T(8,128)S(1)}, f32[928,128]{1,0:T(8,128)}, u32[]{:S(2)}) copy-start(f32[928,128]{1,0:T(8,128)} %copy-done.23) | copy-start | bytes 1425412
  329.4 21.6 %collective-permute-start.13 = (f32[56,512]{1,0:T(8,128)}, f32[56,512]{1,0:T(8,128)}, u32[]{:S(2)}, u32[]{:S(2)}) collective-permute-start(f32[56,512]{1,0:T(8,128)} %get-tuple-element.7), channel_id=1, source_target_pairs={{0,1},{1,2},{2,3},{3,4},{4,5},{5,6},{6,7},{7,8},{8,9},{9,10},{10,1... | collective-permute-start | bytes 344072
  336.7 14.4 %collective-permute-start.14 = (f32[34,512]{1,0:T(8,128)}, f32[34,512]{1,0:T(8,128)S(1)}, u32[]{:S(2)}, u32[]{:S(2)}) collective-permute-start(f32[34,512]{1,0:T(8,128)} %slice.130), channel_id=1, source_target_pairs={{0,2},{1,3},{2,4},{3,5},{4,6},{5,7},{6,8},{7,9},{8,10},{9,11},{10,... | collective-permute-start | bytes 208904
  348.8 17.8 %collective-permute-start.11 = (f32[16,4608]{1,0:T(8,128)}, f32[16,4608]{1,0:T(8,128)}, u32[]{:S(2)}, u32[]{:S(2)}) collective-permute-start(f32[16,4608]{1,0:T(8,128)} %add.105), channel_id=1, source_target_pairs={{0,4},{1,5},{2,6},{3,7},{4,0},{5,1},{6,2},{7,3},{8,12},{9,13},{10,... | collective-permute-start | bytes 884744 | tf_op jit(solution)/shard_map/ppermute | solution.py:64
  367.7 18.7 %collective-permute-start.12 = (f32[16,4608]{1,0:T(8,128)S(1)}, f32[16,4608]{1,0:T(8,128)S(1)}, u32[]{:S(2)}, u32[]{:S(2)}) collective-permute-start(f32[16,4608]{1,0:T(8,128)S(1)} %add.106), channel_id=1, source_target_pairs={{0,8},{1,9},{2,10},{3,11},{4,12},{5,13},{6,14},{7,15},{8,0},{9,1},... | collective-permute-start | bytes 884744 | tf_op jit(solution)/shard_map/ppermute | solution.py:64
  (24 other events, 62.1 us)

commit v5 on v4

--- a/solution.py
+++ b/solution.py
@@ -64,6 +64,36 @@
         x = x + lax.ppermute(x, axis, [(i, i ^ k) for i in range(n)])
         k *= 2
     return x
+
+
+def exchange_pairs(axis, k):
+    return [(i, i ^ k) for i in range(lax.axis_size(axis))]
+
+
+def mesh_sum(x):
+    n = lax.axis_size("dp")
+    halving = [k for k in (1, 2) if k < n and not n & (n - 1)]
+    if x.shape[-1] % (2 ** len(halving)):
+        halving = []
+    cur = x
+    for k in halving:
+        h = cur.shape[-1] // 2
+        bit = (lax.axis_index("dp") // k) % 2
+        keep = lax.dynamic_slice_in_dim(cur, bit * h, h, cur.ndim - 1)
+        give = lax.dynamic_slice_in_dim(cur, (1 - bit) * h, h, cur.ndim - 1)
+        cur = keep + lax.ppermute(give, "dp", exchange_pairs("dp", k))
+    k = 2 ** len(halving)
+    while k < n:
+        cur = cur + lax.ppermute(cur, "dp", exchange_pairs("dp", k))
+        k *= 2
+    cur = butterfly_sum(cur, "ctx")
+    for k in reversed(halving):
+        bit = (lax.axis_index("dp") // k) % 2
+        other = lax.ppermute(cur, "dp", exchange_pairs("dp", k))
+        cur = jnp.where(
+            bit == 0, jnp.concatenate([cur, other], -1), jnp.concatenate([other, cur], -1)
+        )
+    return cur
 
 
 def per_device(
@@ -149,7 +179,7 @@
         hidden_row_block, adapter_down_weight, preferred_element_type=jnp.float32
     ).astype(jnp.bfloat16)
     packed = adapter_terms(hidden_row_block, low_rank_rows, value_result, adapter_up_weight)
-    packed = butterfly_sum(butterfly_sum(packed, "dp"), "ctx")
+    packed = mesh_sum(packed)
     model_width = hidden_row_block.shape[1]
     adapter_factor = adapter_scale / (log_batch * segment_list)
     down_sum = packed[:, :model_width].T

time: 389 us -> 368 us (0.946)
  the two profiles are of different devices: /device:TPU:104 before, /device:TPU:1 now
where the time goes in v5:
time: 368 us; the launch traced here: 365 us
  starting transfers between devices  128 us (35%)
  blocking collectives  89.6 us (24%)
  matrix products  44.4 us (12%)
  waiting for transfers between devices  43.7 us (12%)
  local copies, waits for them, and re-layouts  34.7 us (9%)
  other arithmetic  21.9 us (6%)
    unnamed x1, blocking collectives  89.6 us
    ppermute x4, starting transfers between devices, per_device(): lax.ppermute(held, 'ctx', [(i, i + hop) for i in range(segment_list - hop)])  39.7 us
    ppermute x4, starting transfers between devices, butterfly_sum(): x = x + lax.ppermute(x, axis, [(i, i ^ k) for i in range(n)])  35.2 us
    ppermute x4, waiting for transfers between devices, per_device(): lax.ppermute(held, 'ctx', [(i, i + hop) for i in range(segment_list - hop)])  24.9 us
    div x4, matrix products, group_grads(): attend = unnorm / jnp.sum(unnorm, -1, keepdims=True)  16.4 us
    unnamed x100, local copies, waits for them, and re-layouts  16.2 us
    ppermute x3, starting transfers between devices, mesh_sum(): cur = cur + lax.ppermute(cur, 'dp', exchange_pairs('dp', k))  16 us
    unnamed x4, starting transfers between devices  14.7 us
  transfers between devices with their start and end apart: 19, of which 14 were waited for; matrix products, arithmetic and copies ran while one was open for 7% of the time, Pallas kernels for 0%

profile of v5, /device:TPU:1, one launch (start us, length us, event | category | flops | bytes accessed | tf_op | source)
XLA Modules:
  0.0 365.3 jit_solution(3013190083064814424)
XLA Ops:
  3.0 11.5 %collective-permute-start = (bf16[1,100,512]{2,1,0:T(8,128)(2,1)S(1)}, bf16[1,100,512]{2,1,0:T(8,128)(2,1)S(1)}, u32[]{:S(2)}, u32[]{:S(2)}) collective-permute-start(bf16[1,100,512]{2,1,0:T(8,128)(2,1)S(1)} %get-tuple-element.10), channel_id=1, source_target_pairs={{0,8},{1,9},{2,10},{3,11},{4,12},{5,13},{6,14},{7,15},{16,24},{17,... | collective-permute-start | bytes 307208 | tf_op jit(solution)/shard_map/ppermute | solution.py:132
  20.3 7.5 %collective-permute-start.1 = (bf16[2,100,512]{2,1,0:T(8,128)(2,1)S(1)}, bf16[2,100,512]{2,1,0:T(8,128)(2,1)S(1)}, u32[]{:S(2)}, u32[]{:S(2)}) collective-permute-start(bf16[2,100,512]{2,1,0:T(8,128)(2,1)S(1)} %pad_maximum_fusion.13), channel_id=1, source_target_pairs={{0,4},{1,5},{2,6},{3,7},{4,8},{5,9},{6,10},{7,11},{8,12},{9,13},{1... | collective-permute-start | bytes 614408 | tf_op jit(solution)/shard_map/ppermute | solution.py:132
  28.6 2.9 collective-permute-done.1
  31.5 5.7 %collective-permute-start.2 = (bf16[4,100,512]{2,1,0:T(8,128)(2,1)S(1)}, bf16[4,100,512]{2,1,0:T(8,128)(2,1)S(1)}, u32[]{:S(2)}, u32[]{:S(2)}) collective-permute-start(bf16[4,100,512]{2,1,0:T(8,128)(2,1)S(1)} %pad_maximum_fusion.8), channel_id=1, source_target_pairs={{0,2},{1,3},{2,4},{3,5},{4,6},{5,7},{6,8},{7,9},{8,10},{9,11},{10,... | collective-permute-start | bytes 1228808 | tf_op jit(solution)/shard_map/ppermute | solution.py:132
  37.3 7.3 %collective-permute-done.2 = bf16[4,100,512]{2,1,0:T(8,128)(2,1)S(1)} collective-permute-done((bf16[4,100,512]{2,1,0:T(8,128)(2,1)S(1)}, bf16[4,100,512]{2,1,0:T(8,128)(2,1)S(1)}, u32[]{:S(2)}, u32[]{:S(2)}) %collective-permute-start.2) | collective-permute-done | bytes 409632 | tf_op jit(solution)/shard_map/ppermute | solution.py:132
  44.9 15.1 %collective-permute-start.3 = (bf16[8,100,512]{2,0,1:T(8,128)(2,1)S(1)}, bf16[8,100,512]{2,0,1:T(8,128)(2,1)S(1)}, u32[]{:S(2)}, u32[]{:S(2)}) collective-permute-start(bf16[8,100,512]{2,0,1:T(8,128)(2,1)S(1)} %copy.67), channel_id=1, source_target_pairs={{0,1},{1,2},{2,3},{3,4},{4,5},{5,6},{6,7},{7,8},{8,9},{9,10},{10,1... | collective-permute-start | bytes 2457608 | tf_op jit(solution)/shard_map/ppermute | solution.py:132
  62.3 14.7 %collective-permute-done.3 = bf16[8,100,512]{2,0,1:T(8,128)(2,1)S(1)} collective-permute-done((bf16[8,100,512]{2,0,1:T(8,128)(2,1)S(1)}, bf16[8,100,512]{2,0,1:T(8,128)(2,1)S(1)}, u32[]{:S(2)}, u32[]{:S(2)}) %collective-permute-start.3) | collective-permute-done | bytes 819232 | tf_op jit(solution)/shard_map/ppermute | solution.py:132
  78.2 2.1 gather_fusion.1
  93.5 3.7 %fusion.6 = (f32[4,128]{1,0:T(4,128)S(1)}, f32[4,128,928]{1,2,0:T(8,128)}) fusion(f32[928,128,4]{1,0,2:T(8,128)} %fusion.46, bf16[128,4,128]{0,2,1:T(8,128)(2,1)S(1)} %bitcast.241, pred[128,928]{0,1:T(8,128)(4,1)S(1)} %copy-done.39, bf16[800,512]{1,0:T(8,128)(2,1)S(1)} %reshape_squeeze.6, bf16[128,512]{1,0:T(8,128)(2,1)S(1)} %bitcast.216), kind=kOutput, calls=%fused_computation.11 | convolution fusion | flops 124486560 | bytes 5003264 | tf_op jit(solution)/shard_map/div | solution.py:23
  97.2 2.1 convolution_bitcast_fusion.1
  103.4 4.2 %fusion.2 = (f32[4,128]{1,0:T(4,128)}, f32[4,128,928]{1,2,0:T(8,128)}) fusion(f32[928,128,4]{1,0,2:T(8,128)} %fusion.63, bf16[928,128,1]{1,0,2:T(8,128)(2,1)S(1)} %fusion.66, bf16[128,4,128]{0,2,1:T(8,128)(2,1)S(1)} %bitcast.239, pred[128,928]{0,1:T(8,128)(4,1)S(1)} %copy-done.40), kind=kOutput, calls=%fused_computation.4 | convolution fusion | flops 124011424 | bytes 4290560 | tf_op jit(solution)/shard_map/div | solution.py:23
  107.6 2.8 convolution_bitcast_fusion
  113.5 4.3 %fusion.10 = (f32[4,128]{1,0:T(4,128)}, f32[4,128,928]{1,2,0:T(8,128)}) fusion(f32[928,128,4]{1,0,2:T(8,128)} %fusion.54, bf16[128,4,128]{0,2,1:T(8,128)(2,1)} %bitcast.237, pred[128,928]{0,1:T(8,128)(4,1)} %pad_add_fusion, bf16[800,512]{1,0:T(8,128)(2,1)S(1)} %reshape_squeeze.6, bf16[128,512]{1,0:T(8,128)(2,1)S(1)} %bitcast.217), kind=kOutput, calls=%fused_computation.18 | convolution fusion | flops 124486560 | bytes 5003264 | tf_op jit(solution)/shard_map/div | solution.py:23
  117.8 2.8 convolution_bitcast_fusion.2
  124.7 4.2 %fusion.14 = (f32[4,128]{1,0:T(4,128)}, f32[4,128,928]{1,2,0:T(8,128)}) fusion(f32[928,128,4]{1,0,2:T(8,128)} %fusion.50, bf16[128,4,128]{0,2,1:T(8,128)(2,1)} %bitcast.235, pred[128,928]{0,1:T(8,128)(4,1)} %pad_add_fusion, bf16[800,512]{1,0:T(8,128)(2,1)S(1)} %reshape_squeeze.6, bf16[128,512]{1,0:T(8,128)(2,1)S(1)} %bitcast.218), kind=kOutput, calls=%fused_computation.25 | convolution fusion | flops 124486560 | bytes 5003264 | tf_op jit(solution)/shard_map/div | solution.py:23
  136.8 89.6 %fusion.97 = (f32[56,512]{1,0:T(8,128)}, f32[56,512]{1,0:T(8,128)}) fusion(f32[800,512]{1,0:T(8,128)} %pad_maximum_fusion.3, f32[800,512]{1,0:T(8,128)} %pad_maximum_fusion), kind=kCustom, calls=%all-reduce-scatter.2 | all-reduce-scatter fusion | flops 917505 | bytes 3508224
  227.2 2.1 collective-permute-start.17
  232.8 2.8 concatenate.88
  239.9 8.2 %collective-permute-start.4 = (f32[16,2304]{1,0:T(8,128)}, f32[16,2304]{1,0:T(8,128)}, u32[]{:S(2)}, u32[]{:S(2)}) collective-permute-start(f32[16,2304]{1,0:T(8,128)} %fusion.67), channel_id=1, source_target_pairs={{0,16},{16,0},{32,48},{48,32},{64,80},{80,64},{96,112},{112,96},{1... | collective-permute-start | bytes 442376 | tf_op jit(solution)/shard_map/ppermute | solution.py:84
  253.0 3.1 collective-permute-done.5
  257.1 9.8 %collective-permute-start.6 = (f32[16,1152]{1,0:T(8,128)S(1)}, f32[16,1152]{1,0:T(8,128)S(1)}, u32[]{:S(2)}, u32[]{:S(2)}) collective-permute-start(f32[16,1152]{1,0:T(8,128)S(1)} %dynamic-slice_add_fusion.2), channel_id=1, source_target_pairs={{0,64},{16,80},{32,96},{48,112},{64,0},{80,16},{96,32},{112,48},{1... | collective-permute-start | bytes 221192 | tf_op jit(solution)/shard_map/ppermute | solution.py:87
  268.9 2.2 collective-permute-done.6
  274.1 2.1 collective-permute-done.7
  276.3 4.1 %collective-permute-start.8 = (f32[16,1152]{1,0:T(8,128)S(1)}, f32[16,1152]{1,0:T(8,128)S(1)}, u32[]{:S(2)}, u32[]{:S(2)}) collective-permute-start(f32[16,1152]{1,0:T(8,128)S(1)} %add.131), channel_id=1, source_target_pairs={{0,256},{16,272},{32,288},{48,304},{64,320},{80,336},{96,352},{112... | collective-permute-start | bytes 221192 | tf_op jit(solution)/shard_map/ppermute | solution.py:87
  288.1 4.0 %collective-permute-start.15 = (f32[56,512]{1,0:T(8,128)}, f32[56,512]{1,0:T(8,128)}, u32[]{:S(2)}, u32[]{:S(2)}) collective-permute-start(f32[56,512]{1,0:T(8,128)} %get-tuple-element.7), channel_id=1, source_target_pairs={{0,1},{1,2},{2,3},{3,4},{4,5},{5,6},{6,7},{7,8},{8,9},{9,10},{10,1... | collective-permute-start | bytes 344072
  296.2 7.3 %collective-permute-start.16 = (f32[34,512]{1,0:T(8,128)}, f32[34,512]{1,0:T(8,128)S(1)}, u32[]{:S(2)}, u32[]{:S(2)}) collective-permute-start(f32[34,512]{1,0:T(8,128)} %slice.130), channel_id=1, source_target_pairs={{0,2},{1,3},{2,4},{3,5},{4,6},{5,7},{6,8},{7,9},{8,10},{9,11},{10,... | collective-permute-start | bytes 208904
  304.4 17.3 %collective-permute-start.10 = (f32[16,1152]{1,0:T(8,128)S(1)}, f32[16,1152]{1,0:T(8,128)S(1)}, u32[]{:S(2)}, u32[]{:S(2)}) collective-permute-start(f32[16,1152]{1,0:T(8,128)S(1)} %add.133), channel_id=1, source_target_pairs={{0,2},{1,3},{2,0},{3,1},{4,6},{5,7},{6,4},{7,5},{8,10},{9,11},{10,... | collective-permute-start | bytes 221192 | tf_op jit(solution)/shard_map/ppermute | solution.py:64
  323.4 11.3 %collective-permute-start.11 = (f32[16,1152]{1,0:T(8,128)S(1)}, f32[16,1152]{1,0:T(8,128)S(1)}, u32[]{:S(2)}, u32[]{:S(2)}) collective-permute-start(f32[16,1152]{1,0:T(8,128)S(1)} %add.134), channel_id=1, source_target_pairs={{0,4},{1,5},{2,6},{3,7},{4,0},{5,1},{6,2},{7,3},{8,12},{9,13},{10,... | collective-permute-start | bytes 221192 | tf_op jit(solution)/shard_map/ppermute | solution.py:64
  336.6 4.6 %collective-permute-start.12 = (f32[16,1152]{1,0:T(8,128)S(1)}, f32[16,1152]{1,0:T(8,128)S(1)}, u32[]{:S(2)}, u32[]{:S(2)}) collective-permute-start(f32[16,1152]{1,0:T(8,128)S(1)} %add.135), channel_id=1, source_target_pairs={{0,8},{1,9},{2,10},{3,11},{4,12},{5,13},{6,14},{7,15},{8,0},{9,1},... | collective-permute-start | bytes 221192 | tf_op jit(solution)/shard_map/ppermute | solution.py:64
  343.9 2.5 collective-permute-done.12
  349.3 3.2 collective-permute-done.13
  352.5 10.4 %collective-permute-start.14 = (f32[16,2304]{1,0:T(8,128)S(1)}, f32[16,2304]{1,0:T(8,128)S(1)}, u32[]{:S(2)}, u32[]{:S(2)}) collective-permute-start(f32[16,2304]{1,0:T(8,128)S(1)} %maximum_select_fusion.1), channel_id=1, source_target_pairs={{0,16},{16,0},{32,48},{48,32},{64,80},{80,64},{96,112},{112,96},{1... | collective-permute-start | bytes 442376 | tf_op jit(solution)/shard_map/ppermute | solution.py:92
  (193 shorter events, 86.8 us)
Async XLA Ops:
  0.6 236.0 %copy-start = (bf16[1,1,128,4096]{3,2,1,0:T(8,128)(2,1)S(1)}, bf16[1,1,128,4096]{3,2,1,0:T(8,128)(2,1)}, u32[]{:S(2)}) copy-start(bf16[1,1,128,4096]{3,2,1,0:T(8,128)(2,1)} %param.13) | copy-start | bytes 3145732
  0.6 17.4 %copy-start.32 = (bf16[1,1,128,2048]{3,2,1,0:T(8,128)(2,1)S(1)}, bf16[1,1,128,2048]{3,2,1,0:T(8,128)(2,1)}, u32[]{:S(2)}) copy-start(bf16[1,1,128,2048]{3,2,1,0:T(8,128)(2,1)} %param.12) | copy-start | bytes 1572868
  3.0 17.3 %collective-permute-start = (bf16[1,100,512]{2,1,0:T(8,128)(2,1)S(1)}, bf16[1,100,512]{2,1,0:T(8,128)(2,1)S(1)}, u32[]{:S(2)}, u32[]{:S(2)}) collective-permute-start(bf16[1,100,512]{2,1,0:T(8,128)(2,1)S(1)} %get-tuple-element.10), channel_id=1, source_target_pairs={{0,8},{1,9},{2,10},{3,11},{4,12},{5,13},{6,14},{7,15},{16,24},{17,... | collective-permute-start | bytes 307208 | tf_op jit(solution)/shard_map/ppermute | solution.py:132
  18.1 75.4 %copy-start.37 = (bf16[128,512]{0,1:T(8,128)(2,1)}, bf16[128,512]{0,1:T(8,128)(2,1)S(1)}, u32[]{:S(2)}) copy-start(bf16[128,512]{0,1:T(8,128)(2,1)S(1)} %get-tuple-element.19) | copy-start | bytes 393220
  20.3 11.2 %collective-permute-start.1 = (bf16[2,100,512]{2,1,0:T(8,128)(2,1)S(1)}, bf16[2,100,512]{2,1,0:T(8,128)(2,1)S(1)}, u32[]{:S(2)}, u32[]{:S(2)}) collective-permute-start(bf16[2,100,512]{2,1,0:T(8,128)(2,1)S(1)} %pad_maximum_fusion.13), channel_id=1, source_target_pairs={{0,4},{1,5},{2,6},{3,7},{4,8},{5,9},{6,10},{7,11},{8,12},{9,13},{1... | collective-permute-start | bytes 614408 | tf_op jit(solution)/shard_map/ppermute | solution.py:132
  31.5 13.0 %collective-permute-start.2 = (bf16[4,100,512]{2,1,0:T(8,128)(2,1)S(1)}, bf16[4,100,512]{2,1,0:T(8,128)(2,1)S(1)}, u32[]{:S(2)}, u32[]{:S(2)}) collective-permute-start(bf16[4,100,512]{2,1,0:T(8,128)(2,1)S(1)} %pad_maximum_fusion.8), channel_id=1, source_target_pairs={{0,2},{1,3},{2,4},{3,5},{4,6},{5,7},{6,8},{7,9},{8,10},{9,11},{10,... | collective-permute-start | bytes 1228808 | tf_op jit(solution)/shard_map/ppermute | solution.py:132
  44.9 32.2 %collective-permute-start.3 = (bf16[8,100,512]{2,0,1:T(8,128)(2,1)S(1)}, bf16[8,100,512]{2,0,1:T(8,128)(2,1)S(1)}, u32[]{:S(2)}, u32[]{:S(2)}) collective-permute-start(bf16[8,100,512]{2,0,1:T(8,128)(2,1)S(1)} %copy.67), channel_id=1, source_target_pairs={{0,1},{1,2},{2,3},{3,4},{4,5},{5,6},{6,7},{7,8},{8,9},{9,10},{10,1... | collective-permute-start | bytes 2457608 | tf_op jit(solution)/shard_map/ppermute | solution.py:132
  60.1 28.4 %copy-start.25 = (bf16[128,512]{0,1:T(8,128)(2,1)}, bf16[128,512]{0,1:T(8,128)(2,1)S(1)}, u32[]{:S(2)}) copy-start(bf16[128,512]{0,1:T(8,128)(2,1)S(1)} %get-tuple-element.16) | copy-start | bytes 393220
  60.1 30.0 %copy-start.26 = (bf16[128,512]{0,1:T(8,128)(2,1)}, bf16[128,512]{0,1:T(8,128)(2,1)S(1)}, u32[]{:S(2)}) copy-start(bf16[128,512]{0,1:T(8,128)(2,1)S(1)} %get-tuple-element.14) | copy-start | bytes 393220
  60.1 31.7 %copy-start.28 = (bf16[128,512]{0,1:T(8,128)(2,1)}, bf16[128,512]{0,1:T(8,128)(2,1)S(1)}, u32[]{:S(2)}) copy-start(bf16[128,512]{0,1:T(8,128)(2,1)S(1)} %get-tuple-element.15) | copy-start | bytes 393220
  227.2 5.6 %collective-permute-start.17 = (f32[56,512]{1,0:T(8,128)}, f32[56,512]{1,0:T(8,128)}, u32[]{:S(2)}, u32[]{:S(2)}) collective-permute-start(f32[56,512]{1,0:T(8,128)} %get-tuple-element.8), channel_id=1, source_target_pairs={{0,1},{1,2},{2,3},{3,4},{4,5},{5,6},{6,7},{7,8},{8,9},{9,10},{10,1... | collective-permute-start | bytes 344072
  229.3 2.9 collective-permute-start.18
  239.2 33.9 %copy-start.23 = (bf16[1,1,128,512]{3,2,1,0:T(8,128)(2,1)S(1)}, bf16[1,1,128,512]{3,2,1,0:T(8,128)(2,1)}, u32[]{:S(2)}) copy-start(bf16[1,1,128,512]{3,2,1,0:T(8,128)(2,1)} %param.10) | copy-start | bytes 393220
  239.9 9.5 %collective-permute-start.4 = (f32[16,2304]{1,0:T(8,128)}, f32[16,2304]{1,0:T(8,128)}, u32[]{:S(2)}, u32[]{:S(2)}) collective-permute-start(f32[16,2304]{1,0:T(8,128)} %fusion.67), channel_id=1, source_target_pairs={{0,16},{16,0},{32,48},{48,32},{64,80},{80,64},{96,112},{112,96},{1... | collective-permute-start | bytes 442376 | tf_op jit(solution)/shard_map/ppermute | solution.py:84
  251.1 5.1 %collective-permute-start.5 = (f32[16,1152]{1,0:T(8,128)S(1)}, f32[16,1152]{1,0:T(8,128)S(1)}, u32[]{:S(2)}, u32[]{:S(2)}) collective-permute-start(f32[16,1152]{1,0:T(8,128)S(1)} %constant_dynamic-slice_fusion), channel_id=1, source_target_pairs={{0,32},{16,48},{32,0},{48,16},{64,96},{80,112},{96,64},{112,80},{1... | collective-permute-start | bytes 221192 | tf_op jit(solution)/shard_map/ppermute | solution.py:84
  253.0 20.1 %copy-start.2 = (bf16[4,128,928]{1,2,0:T(8,128)(2,1)S(1)}, bf16[4,128,928]{1,2,0:T(8,128)(2,1)}, u32[]{:S(2)}) copy-start(bf16[4,128,928]{1,2,0:T(8,128)(2,1)} %copy-done.1) | copy-start | bytes 2850820
  257.1 23.3 %copy-start.4 = (bf16[4,128,928]{1,2,0:T(8,128)(2,1)S(1)}, bf16[4,128,928]{1,2,0:T(8,128)(2,1)}, u32[]{:S(2)}) copy-start(bf16[4,128,928]{1,2,0:T(8,128)(2,1)} %copy-done.3) | copy-start | bytes 2850820
  257.1 13.9 %collective-permute-start.6 = (f32[16,1152]{1,0:T(8,128)S(1)}, f32[16,1152]{1,0:T(8,128)S(1)}, u32[]{:S(2)}, u32[]{:S(2)}) collective-permute-start(f32[16,1152]{1,0:T(8,128)S(1)} %dynamic-slice_add_fusion.2), channel_id=1, source_target_pairs={{0,64},{16,80},{32,96},{48,112},{64,0},{80,16},{96,32},{112,48},{1... | collective-permute-start | bytes 221192 | tf_op jit(solution)/shard_map/ppermute | solution.py:87
  271.0 14.6 %copy-start.6 = (bf16[4,128,928]{1,2,0:T(8,128)(2,1)S(1)}, bf16[4,128,928]{1,2,0:T(8,128)(2,1)}, u32[]{:S(2)}) copy-start(bf16[4,128,928]{1,2,0:T(8,128)(2,1)} %copy-done.5) | copy-start | bytes 2850820
  271.1 5.2 %collective-permute-start.7 = (f32[16,1152]{1,0:T(8,128)S(1)}, f32[16,1152]{1,0:T(8,128)S(1)}, u32[]{:S(2)}, u32[]{:S(2)}) collective-permute-start(f32[16,1152]{1,0:T(8,128)S(1)} %add.130), channel_id=1, source_target_pairs={{0,128},{16,144},{32,160},{48,176},{64,192},{80,208},{96,224},{112... | collective-permute-start | bytes 221192 | tf_op jit(solution)/shard_map/ppermute | solution.py:87
  276.3 6.6 %collective-permute-start.8 = (f32[16,1152]{1,0:T(8,128)S(1)}, f32[16,1152]{1,0:T(8,128)S(1)}, u32[]{:S(2)}, u32[]{:S(2)}) collective-permute-start(f32[16,1152]{1,0:T(8,128)S(1)} %add.131), channel_id=1, source_target_pairs={{0,256},{16,272},{32,288},{48,304},{64,320},{80,336},{96,352},{112... | collective-permute-start | bytes 221192 | tf_op jit(solution)/shard_map/ppermute | solution.py:87
  283.5 51.2 %copy-start.15 = (f32[928,128]{1,0:T(8,128)S(1)}, f32[928,128]{1,0:T(8,128)}, u32[]{:S(2)}) copy-start(f32[928,128]{1,0:T(8,128)} %fusion.19) | copy-start | bytes 1425412
  283.5 51.2 %copy-start.17 = (f32[928,128]{1,0:T(8,128)S(1)}, f32[928,128]{1,0:T(8,128)}, u32[]{:S(2)}) copy-start(f32[928,128]{1,0:T(8,128)} %fusion.18) | copy-start | bytes 1425412
  283.5 51.2 %copy-start.19 = (f32[928,128]{1,0:T(8,128)S(1)}, f32[928,128]{1,0:T(8,128)}, u32[]{:S(2)}) copy-start(f32[928,128]{1,0:T(8,128)} %fusion.20) | copy-start | bytes 1425412
  283.5 19.9 %collective-permute-start.9 = (f32[16,1152]{1,0:T(8,128)}, f32[16,1152]{1,0:T(8,128)}, u32[]{:S(2)}, u32[]{:S(2)}) collective-permute-start(f32[16,1152]{1,0:T(8,128)} %add.132), channel_id=1, source_target_pairs={{0,1},{1,0},{2,3},{3,2},{4,5},{5,4},{6,7},{7,6},{8,9},{9,8},{10,11... | collective-permute-start | bytes 221192 | tf_op jit(solution)/shard_map/ppermute | solution.py:64
  288.1 53.8 %collective-permute-start.15 = (f32[56,512]{1,0:T(8,128)}, f32[56,512]{1,0:T(8,128)}, u32[]{:S(2)}, u32[]{:S(2)}) collective-permute-start(f32[56,512]{1,0:T(8,128)} %get-tuple-element.7), channel_id=1, source_target_pairs={{0,1},{1,2},{2,3},{3,4},{4,5},{5,6},{6,7},{7,8},{8,9},{9,10},{10,1... | collective-permute-start | bytes 344072
  296.2 45.8 %collective-permute-start.16 = (f32[34,512]{1,0:T(8,128)}, f32[34,512]{1,0:T(8,128)S(1)}, u32[]{:S(2)}, u32[]{:S(2)}) collective-permute-start(f32[34,512]{1,0:T(8,128)} %slice.130), channel_id=1, source_target_pairs={{0,2},{1,3},{2,4},{3,5},{4,6},{5,7},{6,8},{7,9},{8,10},{9,11},{10,... | collective-permute-start | bytes 208904
  304.4 19.0 %collective-permute-start.10 = (f32[16,1152]{1,0:T(8,128)S(1)}, f32[16,1152]{1,0:T(8,128)S(1)}, u32[]{:S(2)}, u32[]{:S(2)}) collective-permute-start(f32[16,1152]{1,0:T(8,128)S(1)} %add.133), channel_id=1, source_target_pairs={{0,2},{1,3},{2,0},{3,1},{4,6},{5,7},{6,4},{7,5},{8,10},{9,11},{10,... | collective-permute-start | bytes 221192 | tf_op jit(solution)/shard_map/ppermute | solution.py:64
  323.4 13.2 %collective-permute-start.11 = (f32[16,1152]{1,0:T(8,128)S(1)}, f32[16,1152]{1,0:T(8,128)S(1)}, u32[]{:S(2)}, u32[]{:S(2)}) collective-permute-start(f32[16,1152]{1,0:T(8,128)S(1)} %add.134), channel_id=1, source_target_pairs={{0,4},{1,5},{2,6},{3,7},{4,0},{5,1},{6,2},{7,3},{8,12},{9,13},{10,... | collective-permute-start | bytes 221192 | tf_op jit(solution)/shard_map/ppermute | solution.py:64
  336.6 9.8 %collective-permute-start.12 = (f32[16,1152]{1,0:T(8,128)S(1)}, f32[16,1152]{1,0:T(8,128)S(1)}, u32[]{:S(2)}, u32[]{:S(2)}) collective-permute-start(f32[16,1152]{1,0:T(8,128)S(1)} %add.135), channel_id=1, source_target_pairs={{0,8},{1,9},{2,10},{3,11},{4,12},{5,13},{6,14},{7,15},{8,0},{9,1},... | collective-permute-start | bytes 221192 | tf_op jit(solution)/shard_map/ppermute | solution.py:64
  346.4 6.1 %collective-permute-start.13 = (f32[16,1152]{1,0:T(8,128)S(1)}, f32[16,1152]{1,0:T(8,128)S(1)}, u32[]{:S(2)}, u32[]{:S(2)}) collective-permute-start(f32[16,1152]{1,0:T(8,128)S(1)} %add.136), channel_id=1, source_target_pairs={{0,32},{16,48},{32,0},{48,16},{64,96},{80,112},{96,64},{112,80},{1... | collective-permute-start | bytes 221192 | tf_op jit(solution)/shard_map/ppermute | solution.py:92
  352.5 11.4 %collective-permute-start.14 = (f32[16,2304]{1,0:T(8,128)S(1)}, f32[16,2304]{1,0:T(8,128)S(1)}, u32[]{:S(2)}, u32[]{:S(2)}) collective-permute-start(f32[16,2304]{1,0:T(8,128)S(1)} %maximum_select_fusion.1), channel_id=1, source_target_pairs={{0,16},{16,0},{32,48},{48,32},{64,80},{80,64},{96,112},{112,96},{1... | collective-permute-start | bytes 442376 | tf_op jit(solution)/shard_map/ppermute | solution.py:92
  (32 other events, 95.1 us)

commit v6 on v5

--- a/solution.py
+++ b/solution.py
@@ -164,10 +164,27 @@
     value_grad = jnp.concatenate(value_parts, 1)
     memory_key_grad, local_key = (key_grad[:count], key_grad[count:])
     memory_value_grad, local_value = (value_grad[:count], value_grad[count:])
-    back_key, back_value = (
-        lax.psum_scatter(memory_key_grad, "ctx", scatter_dimension=0, tiled=True),
-        lax.psum_scatter(memory_value_grad, "ctx", scatter_dimension=0, tiled=True),
-    )
+    segment_of_slot = (position - jnp.asarray(np.array(distance_of_slot, np.int32))) % segment_list
+    owed = jnp.take(
+        jnp.stack(
+            [
+                memory_key_grad.reshape(segment_list, SUMM, width),
+                memory_value_grad.reshape(segment_list, SUMM, width),
+            ],
+            1,
+        ),
+        segment_of_slot,
+        axis=0,
+    )
+    hop = 1
+    while hop < segment_list:
+        half = owed.shape[0] // 2
+        returned = lax.ppermute(
+            owed[half:], "ctx", [(i, i - hop) for i in range(hop, segment_list)]
+        )
+        owed = owed[:half] + returned
+        hop *= 2
+    back_key, back_value = owed[0, 0], owed[0, 1]
     key_out = (
         local_key + lax.dynamic_update_slice_in_dim(jnp.zeros_like(local_key), back_key, length, 0)
     ).astype(jnp.bfloat16)

time: 368 us -> 434 us (1.18)
  waiting for transfers between devices: 43.7 us -> 160 us
  blocking collectives: 89.6 us -> 0 us
  starting transfers between devices: 128 us -> 152 us
  other arithmetic: 21.9 us -> 31.1 us
  local copies, waits for them, and re-layouts: 34.7 us -> 40.6 us
    ppermute x0 -> x4, waiting for transfers between devices: none -> 106 us  [per_device(): lax.ppermute(owed[half:], 'ctx', [(i, i - hop) for i in range(hop, segmen...]
    unnamed x1 -> x0, blocking collectives: 89.6 us -> none
    ppermute x3, starting transfers between devices: 16 us -> 31.8 us  [mesh_sum(): cur = cur + lax.ppermute(cur, 'dp', exchange_pairs('dp', k))]
    unnamed x4 -> x0, starting transfers between devices: 14.7 us -> none
    ppermute x2, starting transfers between devices: 10.1 us -> 21.5 us  [mesh_sum(): cur = keep + lax.ppermute(give, 'dp', exchange_pairs('dp', k))]
    unnamed x100 -> x93, local copies, waits for them, and re-layouts: 16.2 us -> 8.53 us
    ppermute x4, starting transfers between devices: 35.2 us -> 41.5 us  [butterfly_sum(): x = x + lax.ppermute(x, axis, [(i, i ^ k) for i in range(n)])]
    ppermute x4, waiting for transfers between devices: 4.41 us -> 10.2 us  [butterfly_sum(): x = x + lax.ppermute(x, axis, [(i, i ^ k) for i in range(n)])]
  transfers between devices with their start and end apart: 19 -> 19, of which waited for: 14 -> 18; matrix products, arithmetic and copies ran while one was open for 7% -> 3% of each run, Pallas kernels for 0% -> 0%
where the time goes in v6:
time: 434 us; the launch traced here: 429 us
  waiting for transfers between devices  160 us (37%)
  starting transfers between devices  152 us (35%)
  matrix products  42.6 us (10%)
  local copies, waits for them, and re-layouts  40.6 us (9%)
  other arithmetic  31.1 us (7%)
    ppermute x4, waiting for transfers between devices, per_device(): lax.ppermute(owed[half:], 'ctx', [(i, i - hop) for i in range(hop, segmen...  106 us
    ppermute x4, starting transfers between devices, butterfly_sum(): x = x + lax.ppermute(x, axis, [(i, i ^ k) for i in range(n)])  41.5 us
    ppermute x4, starting transfers between devices, per_device(): lax.ppermute(held, 'ctx', [(i, i + hop) for i in range(segment_list - hop)])  39.7 us
    ppermute x3, starting transfers between devices, mesh_sum(): cur = cur + lax.ppermute(cur, 'dp', exchange_pairs('dp', k))  31.8 us
    ppermute x4, waiting for transfers between devices, per_device(): lax.ppermute(held, 'ctx', [(i, i + hop) for i in range(segment_list - hop)])  27.1 us
    ppermute x2, starting transfers between devices, mesh_sum(): cur = keep + lax.ppermute(give, 'dp', exchange_pairs('dp', k))  21.5 us
    div x4, matrix products, group_grads(): attend = unnorm / jnp.sum(unnorm, -1, keepdims=True)  16.4 us
    ppermute x2, starting transfers between devices, mesh_sum(): other = lax.ppermute(cur, 'dp', exchange_pairs('dp', k))  12 us
  transfers between devices with their start and end apart: 19, of which 18 were waited for; matrix products, arithmetic and copies ran while one was open for 3% of the time, Pallas kernels for 0%

profile of v6, /device:TPU:1, one launch (start us, length us, event | category | flops | bytes accessed | tf_op | source)
XLA Modules:
  0.0 428.6 jit_solution(12432372031422666588)
XLA Ops:
  3.0 11.4 %collective-permute-start = (bf16[1,100,512]{2,1,0:T(8,128)(2,1)S(1)}, bf16[1,100,512]{2,1,0:T(8,128)(2,1)S(1)}, u32[]{:S(2)}, u32[]{:S(2)}) collective-permute-start(bf16[1,100,512]{2,1,0:T(8,128)(2,1)S(1)} %get-tuple-element.8), channel_id=1, source_target_pairs={{0,8},{1,9},{2,10},{3,11},{4,12},{5,13},{6,14},{7,15},{16,24},{17,... | collective-permute-start | bytes 307208 | tf_op jit(solution)/shard_map/ppermute | solution.py:132
  20.1 7.5 %collective-permute-start.1 = (bf16[2,100,512]{2,1,0:T(8,128)(2,1)S(1)}, bf16[2,100,512]{2,1,0:T(8,128)(2,1)S(1)}, u32[]{:S(2)}, u32[]{:S(2)}) collective-permute-start(bf16[2,100,512]{2,1,0:T(8,128)(2,1)S(1)} %pad_maximum_fusion.12), channel_id=1, source_target_pairs={{0,4},{1,5},{2,6},{3,7},{4,8},{5,9},{6,10},{7,11},{8,12},{9,13},{1... | collective-permute-start | bytes 614408 | tf_op jit(solution)/shard_map/ppermute | solution.py:132
  27.7 3.4 collective-permute-done.1
  31.2 5.9 %collective-permute-start.2 = (bf16[4,100,512]{2,1,0:T(8,128)(2,1)S(1)}, bf16[4,100,512]{2,1,0:T(8,128)(2,1)S(1)}, u32[]{:S(2)}, u32[]{:S(2)}) collective-permute-start(bf16[4,100,512]{2,1,0:T(8,128)(2,1)S(1)} %pad_maximum_fusion.7), channel_id=1, source_target_pairs={{0,2},{1,3},{2,4},{3,5},{4,6},{5,7},{6,8},{7,9},{8,10},{9,11},{10,... | collective-permute-start | bytes 1228808 | tf_op jit(solution)/shard_map/ppermute | solution.py:132
  37.1 7.7 %collective-permute-done.2 = bf16[4,100,512]{2,1,0:T(8,128)(2,1)S(1)} collective-permute-done((bf16[4,100,512]{2,1,0:T(8,128)(2,1)S(1)}, bf16[4,100,512]{2,1,0:T(8,128)(2,1)S(1)}, u32[]{:S(2)}, u32[]{:S(2)}) %collective-permute-start.2) | collective-permute-done | bytes 409632 | tf_op jit(solution)/shard_map/ppermute | solution.py:132
  45.2 14.8 %collective-permute-start.3 = (bf16[8,100,512]{2,0,1:T(8,128)(2,1)S(1)}, bf16[8,100,512]{2,0,1:T(8,128)(2,1)S(1)}, u32[]{:S(2)}, u32[]{:S(2)}) collective-permute-start(bf16[8,100,512]{2,0,1:T(8,128)(2,1)S(1)} %copy.68), channel_id=1, source_target_pairs={{0,1},{1,2},{2,3},{3,4},{4,5},{5,6},{6,7},{7,8},{8,9},{9,10},{10,1... | collective-permute-start | bytes 2457608 | tf_op jit(solution)/shard_map/ppermute | solution.py:132
  63.1 16.0 %collective-permute-done.3 = bf16[8,100,512]{2,0,1:T(8,128)(2,1)S(1)} collective-permute-done((bf16[8,100,512]{2,0,1:T(8,128)(2,1)S(1)}, bf16[8,100,512]{2,0,1:T(8,128)(2,1)S(1)}, u32[]{:S(2)}, u32[]{:S(2)}) %collective-permute-start.3) | collective-permute-done | bytes 819232 | tf_op jit(solution)/shard_map/ppermute | solution.py:132
  80.3 3.3 gather_fusion.1
  98.2 3.7 fusion.4
  108.1 4.2 fusion
  118.1 4.3 fusion.8
  122.4 2.9 convolution_bitcast_fusion.2
  129.3 4.2 fusion.12
  133.5 2.9 convolution_bitcast_fusion.3
  150.0 4.3 %pad_maximum_fusion = f32[16,2,50,512]{3,2,0,1:T(8,128)} fusion(f32[16,1,50,512]{3,2,0,1:T(8,128)} %stack_reshape.7, f32[16,1,50,512]{3,2,0,1:T(8,128)} %stack_reshape.6), kind=kLoop, calls=%fused_computation.3 | loop fusion | flops 819200 | bytes 6553600 | tf_op jit(solution)/shard_map/stack | solution.py:169
  154.3 4.7 %gather_fusion.2 = f32[16,2,50,512]{3,2,1,0:T(8,128)} fusion(f32[16,2,50,512]{3,2,0,1:T(8,128)} %pad_maximum_fusion, s32[1024]{0:T(1024)} %pad_clamp_fusion), kind=kCustom, calls=%fused_computation.2 | custom fusion | bytes 6553664 | tf_op jit(solution)/shard_map/jit(_take)/gather | solution.py:168
  164.0 38.1 %collective-permute-done.4 = f32[8,2,50,512]{3,0,2,1:T(8,128)S(1)} collective-permute-done((f32[8,2,50,512]{3,0,2,1:T(8,128)S(1)}, f32[8,2,50,512]{3,0,2,1:T(8,128)S(1)}, u32[]{:S(2)}, u32[]{:S(2)}) %collective-permute-start.4) | collective-permute-done | bytes 1638432 | tf_op jit(solution)/shard_map/ppermute | solution.py:182
  205.1 29.9 %collective-permute-done.5 = f32[4,2,50,512]{3,0,2,1:T(4,128)S(1)} collective-permute-done((f32[4,2,50,512]{3,0,2,1:T(4,128)S(1)}, f32[4,2,50,512]{3,0,2,1:T(4,128)S(1)}, u32[]{:S(2)}, u32[]{:S(2)}) %collective-permute-start.5) | collective-permute-done | bytes 819232 | tf_op jit(solution)/shard_map/ppermute | solution.py:182
  238.5 15.1 %collective-permute-done.6 = f32[2,2,50,512]{3,2,1,0:T(8,128)} collective-permute-done((f32[2,2,50,512]{3,2,1,0:T(8,128)}, f32[2,2,50,512]{3,2,1,0:T(8,128)}, u32[]{:S(2)}, u32[]{:S(2)}) %collective-permute-start.6) | collective-permute-done | bytes 409632 | tf_op jit(solution)/shard_map/ppermute | solution.py:182
  256.3 23.3 %collective-permute-done.7 = f32[1,2,50,512]{3,2,1,0:T(8,128)S(1)} collective-permute-done((f32[1,2,50,512]{3,2,1,0:T(8,128)S(1)}, f32[1,2,50,512]{3,2,1,0:T(8,128)S(1)}, u32[]{:S(2)}, u32[]{:S(2)}) %collective-permute-start.7) | collective-permute-done | bytes 204832 | tf_op jit(solution)/shard_map/ppermute | solution.py:182
  284.1 16.9 %collective-permute-start.8 = (f32[16,2304]{1,0:T(8,128)S(1)}, f32[16,2304]{1,0:T(8,128)}, u32[]{:S(2)}, u32[]{:S(2)}) collective-permute-start(f32[16,2304]{1,0:T(8,128)S(1)} %fusion.65), channel_id=1, source_target_pairs={{0,16},{16,0},{32,48},{48,32},{64,80},{80,64},{96,112},{112,96},{1... | collective-permute-start | bytes 442376 | tf_op jit(solution)/shard_map/ppermute | solution.py:84
  303.8 4.6 %collective-permute-start.9 = (f32[16,1152]{1,0:T(8,128)}, f32[16,1152]{1,0:T(8,128)}, u32[]{:S(2)}, u32[]{:S(2)}) collective-permute-start(f32[16,1152]{1,0:T(8,128)} %constant_dynamic-slice_fusion), channel_id=1, source_target_pairs={{0,32},{16,48},{32,0},{48,16},{64,96},{80,112},{96,64},{112,80},{1... | collective-permute-start | bytes 221192 | tf_op jit(solution)/shard_map/ppermute | solution.py:84
  308.4 7.2 %collective-permute-done.9 = f32[16,1152]{1,0:T(8,128)} collective-permute-done((f32[16,1152]{1,0:T(8,128)}, f32[16,1152]{1,0:T(8,128)}, u32[]{:S(2)}, u32[]{:S(2)}) %collective-permute-start.9) | collective-permute-done | bytes 73760 | tf_op jit(solution)/shard_map/ppermute | solution.py:84
  316.5 18.5 %collective-permute-start.10 = (f32[16,1152]{1,0:T(8,128)S(1)}, f32[16,1152]{1,0:T(8,128)S(1)}, u32[]{:S(2)}, u32[]{:S(2)}) collective-permute-start(f32[16,1152]{1,0:T(8,128)S(1)} %dynamic-slice_add_fusion), channel_id=1, source_target_pairs={{0,64},{16,80},{32,96},{48,112},{64,0},{80,16},{96,32},{112,48},{1... | collective-permute-start | bytes 221192 | tf_op jit(solution)/shard_map/ppermute | solution.py:87
  335.0 3.7 collective-permute-done.10
  338.8 8.1 %collective-permute-start.11 = (f32[16,1152]{1,0:T(8,128)S(1)}, f32[16,1152]{1,0:T(8,128)}, u32[]{:S(2)}, u32[]{:S(2)}) collective-permute-start(f32[16,1152]{1,0:T(8,128)S(1)} %add.152), channel_id=1, source_target_pairs={{0,128},{16,144},{32,160},{48,176},{64,192},{80,208},{96,224},{112... | collective-permute-start | bytes 221192 | tf_op jit(solution)/shard_map/ppermute | solution.py:87
  349.6 5.2 %collective-permute-start.12 = (f32[16,1152]{1,0:T(8,128)S(1)}, f32[16,1152]{1,0:T(8,128)S(1)}, u32[]{:S(2)}, u32[]{:S(2)}) collective-permute-start(f32[16,1152]{1,0:T(8,128)S(1)} %add.153), channel_id=1, source_target_pairs={{0,256},{16,272},{32,288},{48,304},{64,320},{80,336},{96,352},{112... | collective-permute-start | bytes 221192 | tf_op jit(solution)/shard_map/ppermute | solution.py:87
  356.5 13.7 %collective-permute-start.13 = (f32[16,1152]{1,0:T(8,128)S(1)}, f32[16,1152]{1,0:T(8,128)S(1)}, u32[]{:S(2)}, u32[]{:S(2)}) collective-permute-start(f32[16,1152]{1,0:T(8,128)S(1)} %add.154), channel_id=1, source_target_pairs={{0,1},{1,0},{2,3},{3,2},{4,5},{5,4},{6,7},{7,6},{8,9},{9,8},{10,11... | collective-permute-start | bytes 221192 | tf_op jit(solution)/shard_map/ppermute | solution.py:64
  372.0 12.2 %collective-permute-start.14 = (f32[16,1152]{1,0:T(8,128)S(1)}, f32[16,1152]{1,0:T(8,128)S(1)}, u32[]{:S(2)}, u32[]{:S(2)}) collective-permute-start(f32[16,1152]{1,0:T(8,128)S(1)} %add.155), channel_id=1, source_target_pairs={{0,2},{1,3},{2,0},{3,1},{4,6},{5,7},{6,4},{7,5},{8,10},{9,11},{10,... | collective-permute-start | bytes 221192 | tf_op jit(solution)/shard_map/ppermute | solution.py:64
  386.0 13.6 %collective-permute-start.15 = (f32[16,1152]{1,0:T(8,128)S(1)}, f32[16,1152]{1,0:T(8,128)S(1)}, u32[]{:S(2)}, u32[]{:S(2)}) collective-permute-start(f32[16,1152]{1,0:T(8,128)S(1)} %add.156), channel_id=1, source_target_pairs={{0,4},{1,5},{2,6},{3,7},{4,0},{5,1},{6,2},{7,3},{8,12},{9,13},{10,... | collective-permute-start | bytes 221192 | tf_op jit(solution)/shard_map/ppermute | solution.py:64
  404.5 6.2 %collective-permute-done.16 = f32[16,1152]{1,0:T(8,128)S(1)} collective-permute-done((f32[16,1152]{1,0:T(8,128)S(1)}, f32[16,1152]{1,0:T(8,128)S(1)}, u32[]{:S(2)}, u32[]{:S(2)}) %collective-permute-start.16) | collective-permute-done | bytes 73760 | tf_op jit(solution)/shard_map/ppermute | solution.py:64
  416.2 10.1 %collective-permute-start.18 = (f32[16,2304]{1,0:T(8,128)S(1)}, f32[16,2304]{1,0:T(8,128)S(1)}, u32[]{:S(2)}, u32[]{:S(2)}) collective-permute-start(f32[16,2304]{1,0:T(8,128)S(1)} %maximum_select_fusion.1), channel_id=1, source_target_pairs={{0,16},{16,0},{32,48},{48,32},{64,80},{80,64},{96,112},{112,96},{1... | collective-permute-start | bytes 442376 | tf_op jit(solution)/shard_map/ppermute | solution.py:92
  (201 shorter events, 98.5 us)
Async XLA Ops:
  0.6 279.9 %copy-start = (bf16[1,1,128,4096]{3,2,1,0:T(8,128)(2,1)S(1)}, bf16[1,1,128,4096]{3,2,1,0:T(8,128)(2,1)}, u32[]{:S(2)}) copy-start(bf16[1,1,128,4096]{3,2,1,0:T(8,128)(2,1)} %param.14) | copy-start | bytes 3145732
  0.6 19.1 %copy-start.30 = (bf16[1,1,128,2048]{3,2,1,0:T(8,128)(2,1)S(1)}, bf16[1,1,128,2048]{3,2,1,0:T(8,128)(2,1)}, u32[]{:S(2)}) copy-start(bf16[1,1,128,2048]{3,2,1,0:T(8,128)(2,1)} %param.13) | copy-start | bytes 1572868
  3.0 17.0 %collective-permute-start = (bf16[1,100,512]{2,1,0:T(8,128)(2,1)S(1)}, bf16[1,100,512]{2,1,0:T(8,128)(2,1)S(1)}, u32[]{:S(2)}, u32[]{:S(2)}) collective-permute-start(bf16[1,100,512]{2,1,0:T(8,128)(2,1)S(1)} %get-tuple-element.8), channel_id=1, source_target_pairs={{0,8},{1,9},{2,10},{3,11},{4,12},{5,13},{6,14},{7,15},{16,24},{17,... | collective-permute-start | bytes 307208 | tf_op jit(solution)/shard_map/ppermute | solution.py:132
  20.1 11.0 %collective-permute-start.1 = (bf16[2,100,512]{2,1,0:T(8,128)(2,1)S(1)}, bf16[2,100,512]{2,1,0:T(8,128)(2,1)S(1)}, u32[]{:S(2)}, u32[]{:S(2)}) collective-permute-start(bf16[2,100,512]{2,1,0:T(8,128)(2,1)S(1)} %pad_maximum_fusion.12), channel_id=1, source_target_pairs={{0,4},{1,5},{2,6},{3,7},{4,8},{5,9},{6,10},{7,11},{8,12},{9,13},{1... | collective-permute-start | bytes 614408 | tf_op jit(solution)/shard_map/ppermute | solution.py:132
  31.2 13.7 %collective-permute-start.2 = (bf16[4,100,512]{2,1,0:T(8,128)(2,1)S(1)}, bf16[4,100,512]{2,1,0:T(8,128)(2,1)S(1)}, u32[]{:S(2)}, u32[]{:S(2)}) collective-permute-start(bf16[4,100,512]{2,1,0:T(8,128)(2,1)S(1)} %pad_maximum_fusion.7), channel_id=1, source_target_pairs={{0,2},{1,3},{2,4},{3,5},{4,6},{5,7},{6,8},{7,9},{8,10},{9,11},{10,... | collective-permute-start | bytes 1228808 | tf_op jit(solution)/shard_map/ppermute | solution.py:132
  45.2 33.9 %collective-permute-start.3 = (bf16[8,100,512]{2,0,1:T(8,128)(2,1)S(1)}, bf16[8,100,512]{2,0,1:T(8,128)(2,1)S(1)}, u32[]{:S(2)}, u32[]{:S(2)}) collective-permute-start(bf16[8,100,512]{2,0,1:T(8,128)(2,1)S(1)} %copy.68), channel_id=1, source_target_pairs={{0,1},{1,2},{2,3},{3,4},{4,5},{5,6},{6,7},{7,8},{8,9},{9,10},{10,1... | collective-permute-start | bytes 2457608 | tf_op jit(solution)/shard_map/ppermute | solution.py:132
  60.9 32.3 %copy-start.26 = (bf16[128,512]{0,1:T(8,128)(2,1)}, bf16[128,512]{0,1:T(8,128)(2,1)S(1)}, u32[]{:S(2)}) copy-start(bf16[128,512]{0,1:T(8,128)(2,1)S(1)} %get-tuple-element.14) | copy-start | bytes 393220
  60.9 33.9 %copy-start.27 = (bf16[128,512]{0,1:T(8,128)(2,1)}, bf16[128,512]{0,1:T(8,128)(2,1)S(1)}, u32[]{:S(2)}) copy-start(bf16[128,512]{0,1:T(8,128)(2,1)S(1)} %get-tuple-element.12) | copy-start | bytes 393220
  162.7 39.4 %collective-permute-start.4 = (f32[8,2,50,512]{3,0,2,1:T(8,128)S(1)}, f32[8,2,50,512]{3,0,2,1:T(8,128)S(1)}, u32[]{:S(2)}, u32[]{:S(2)}) collective-permute-start(f32[8,2,50,512]{3,0,2,1:T(8,128)S(1)} %copy.95), channel_id=1, source_target_pairs={{1,0},{2,1},{3,2},{4,3},{5,4},{6,5},{7,6},{8,7},{9,8},{10,9},{11,1... | collective-permute-start | bytes 4915208 | tf_op jit(solution)/shard_map/ppermute | solution.py:182
  203.8 31.2 %collective-permute-start.5 = (f32[4,2,50,512]{3,0,2,1:T(4,128)S(1)}, f32[4,2,50,512]{3,0,2,1:T(4,128)S(1)}, u32[]{:S(2)}, u32[]{:S(2)}) collective-permute-start(f32[4,2,50,512]{3,0,2,1:T(4,128)S(1)} %copy.97), channel_id=1, source_target_pairs={{2,0},{3,1},{4,2},{5,3},{6,4},{7,5},{8,6},{9,7},{10,8},{11,9},{12,... | collective-permute-start | bytes 2457608 | tf_op jit(solution)/shard_map/ppermute | solution.py:182
  237.1 16.4 %collective-permute-start.6 = (f32[2,2,50,512]{3,2,1,0:T(8,128)}, f32[2,2,50,512]{3,2,1,0:T(8,128)}, u32[]{:S(2)}, u32[]{:S(2)}) collective-permute-start(f32[2,2,50,512]{3,2,1,0:T(8,128)} %slice.176), channel_id=1, source_target_pairs={{4,0},{5,1},{6,2},{7,3},{8,4},{9,5},{10,6},{11,7},{12,8},{13,9},{1... | collective-permute-start | bytes 1228808 | tf_op jit(solution)/shard_map/ppermute | solution.py:182
  238.5 17.7 %copy-start.17 = (f32[928,128]{1,0:T(8,128)S(1)}, f32[928,128]{1,0:T(8,128)}, u32[]{:S(2)}) copy-start(f32[928,128]{1,0:T(8,128)} %convolution_bitcast_fusion.1) | copy-start | bytes 1425412
  238.5 17.7 %copy-start.18 = (f32[928,128]{1,0:T(8,128)S(1)}, f32[928,128]{1,0:T(8,128)}, u32[]{:S(2)}) copy-start(f32[928,128]{1,0:T(8,128)} %convolution_bitcast_fusion) | copy-start | bytes 1425412
  238.5 17.7 %copy-start.19 = (f32[928,128]{1,0:T(8,128)S(1)}, f32[928,128]{1,0:T(8,128)}, u32[]{:S(2)}) copy-start(f32[928,128]{1,0:T(8,128)} %convolution_bitcast_fusion.2) | copy-start | bytes 1425412
  238.5 17.7 %copy-start.20 = (f32[928,128]{1,0:T(8,128)S(1)}, f32[928,128]{1,0:T(8,128)}, u32[]{:S(2)}) copy-start(f32[928,128]{1,0:T(8,128)} %convolution_bitcast_fusion.3) | copy-start | bytes 1425412
  254.8 24.8 %collective-permute-start.7 = (f32[1,2,50,512]{3,2,1,0:T(8,128)S(1)}, f32[1,2,50,512]{3,2,1,0:T(8,128)S(1)}, u32[]{:S(2)}, u32[]{:S(2)}) collective-permute-start(f32[1,2,50,512]{3,2,1,0:T(8,128)S(1)} %slice.178), channel_id=1, source_target_pairs={{8,0},{9,1},{10,2},{11,3},{12,4},{13,5},{14,6},{15,7},{24,16},{25,... | collective-permute-start | bytes 614408 | tf_op jit(solution)/shard_map/ppermute | solution.py:182
  256.2 23.5 %copy-start.24 = (f32[128,512]{1,0:T(8,128)}, f32[128,512]{1,0:T(8,128)S(1)}, u32[]{:S(2)}) copy-start(f32[128,512]{1,0:T(8,128)S(1)} %pad_maximum_fusion.9) | copy-start | bytes 786436
  256.3 25.7 %copy-start.39 = (bf16[16,512]{1,0:T(8,128)(2,1)S(1)}, bf16[16,512]{1,0:T(8,128)(2,1)}, u32[]{:S(2)}) copy-start(bf16[16,512]{1,0:T(8,128)(2,1)} %param.16) | copy-start | bytes 49156
  284.1 18.0 %collective-permute-start.8 = (f32[16,2304]{1,0:T(8,128)S(1)}, f32[16,2304]{1,0:T(8,128)}, u32[]{:S(2)}, u32[]{:S(2)}) collective-permute-start(f32[16,2304]{1,0:T(8,128)S(1)} %fusion.65), channel_id=1, source_target_pairs={{0,16},{16,0},{32,48},{48,32},{64,80},{80,64},{96,112},{112,96},{1... | collective-permute-start | bytes 442376 | tf_op jit(solution)/shard_map/ppermute | solution.py:84
  303.8 11.8 %collective-permute-start.9 = (f32[16,1152]{1,0:T(8,128)}, f32[16,1152]{1,0:T(8,128)}, u32[]{:S(2)}, u32[]{:S(2)}) collective-permute-start(f32[16,1152]{1,0:T(8,128)} %constant_dynamic-slice_fusion), channel_id=1, source_target_pairs={{0,32},{16,48},{32,0},{48,16},{64,96},{80,112},{96,64},{112,80},{1... | collective-permute-start | bytes 221192 | tf_op jit(solution)/shard_map/ppermute | solution.py:84
  316.5 22.3 %collective-permute-start.10 = (f32[16,1152]{1,0:T(8,128)S(1)}, f32[16,1152]{1,0:T(8,128)S(1)}, u32[]{:S(2)}, u32[]{:S(2)}) collective-permute-start(f32[16,1152]{1,0:T(8,128)S(1)} %dynamic-slice_add_fusion), channel_id=1, source_target_pairs={{0,64},{16,80},{32,96},{48,112},{64,0},{80,16},{96,32},{112,48},{1... | collective-permute-start | bytes 221192 | tf_op jit(solution)/shard_map/ppermute | solution.py:87
  338.8 9.9 %collective-permute-start.11 = (f32[16,1152]{1,0:T(8,128)S(1)}, f32[16,1152]{1,0:T(8,128)}, u32[]{:S(2)}, u32[]{:S(2)}) collective-permute-start(f32[16,1152]{1,0:T(8,128)S(1)} %add.152), channel_id=1, source_target_pairs={{0,128},{16,144},{32,160},{48,176},{64,192},{80,208},{96,224},{112... | collective-permute-start | bytes 221192 | tf_op jit(solution)/shard_map/ppermute | solution.py:87
  346.9 23.4 %copy-start.2 = (bf16[4,128,928]{1,2,0:T(8,128)(2,1)S(1)}, bf16[4,128,928]{1,2,0:T(8,128)(2,1)}, u32[]{:S(2)}) copy-start(bf16[4,128,928]{1,2,0:T(8,128)(2,1)} %copy-done.1) | copy-start | bytes 2850820
  349.6 34.6 %copy-start.4 = (bf16[4,128,928]{1,2,0:T(8,128)(2,1)S(1)}, bf16[4,128,928]{1,2,0:T(8,128)(2,1)}, u32[]{:S(2)}) copy-start(bf16[4,128,928]{1,2,0:T(8,128)(2,1)} %copy-done.3) | copy-start | bytes 2850820
  349.6 6.9 %collective-permute-start.12 = (f32[16,1152]{1,0:T(8,128)S(1)}, f32[16,1152]{1,0:T(8,128)S(1)}, u32[]{:S(2)}, u32[]{:S(2)}) collective-permute-start(f32[16,1152]{1,0:T(8,128)S(1)} %add.153), channel_id=1, source_target_pairs={{0,256},{16,272},{32,288},{48,304},{64,320},{80,336},{96,352},{112... | collective-permute-start | bytes 221192 | tf_op jit(solution)/shard_map/ppermute | solution.py:87
  356.5 43.1 %copy-start.6 = (bf16[4,128,928]{1,2,0:T(8,128)(2,1)S(1)}, bf16[4,128,928]{1,2,0:T(8,128)(2,1)}, u32[]{:S(2)}) copy-start(bf16[4,128,928]{1,2,0:T(8,128)(2,1)} %copy-done.5) | copy-start | bytes 2850820
  356.5 15.5 %collective-permute-start.13 = (f32[16,1152]{1,0:T(8,128)S(1)}, f32[16,1152]{1,0:T(8,128)S(1)}, u32[]{:S(2)}, u32[]{:S(2)}) collective-permute-start(f32[16,1152]{1,0:T(8,128)S(1)} %add.154), channel_id=1, source_target_pairs={{0,1},{1,0},{2,3},{3,2},{4,5},{5,4},{6,7},{7,6},{8,9},{9,8},{10,11... | collective-permute-start | bytes 221192 | tf_op jit(solution)/shard_map/ppermute | solution.py:64
  372.0 13.9 %collective-permute-start.14 = (f32[16,1152]{1,0:T(8,128)S(1)}, f32[16,1152]{1,0:T(8,128)S(1)}, u32[]{:S(2)}, u32[]{:S(2)}) collective-permute-start(f32[16,1152]{1,0:T(8,128)S(1)} %add.155), channel_id=1, source_target_pairs={{0,2},{1,3},{2,0},{3,1},{4,6},{5,7},{6,4},{7,5},{8,10},{9,11},{10,... | collective-permute-start | bytes 221192 | tf_op jit(solution)/shard_map/ppermute | solution.py:64
  386.0 15.8 %collective-permute-start.15 = (f32[16,1152]{1,0:T(8,128)S(1)}, f32[16,1152]{1,0:T(8,128)S(1)}, u32[]{:S(2)}, u32[]{:S(2)}) collective-permute-start(f32[16,1152]{1,0:T(8,128)S(1)} %add.156), channel_id=1, source_target_pairs={{0,4},{1,5},{2,6},{3,7},{4,0},{5,1},{6,2},{7,3},{8,12},{9,13},{10,... | collective-permute-start | bytes 221192 | tf_op jit(solution)/shard_map/ppermute | solution.py:64
  401.7 9.0 %collective-permute-start.16 = (f32[16,1152]{1,0:T(8,128)S(1)}, f32[16,1152]{1,0:T(8,128)S(1)}, u32[]{:S(2)}, u32[]{:S(2)}) collective-permute-start(f32[16,1152]{1,0:T(8,128)S(1)} %add.157), channel_id=1, source_target_pairs={{0,8},{1,9},{2,10},{3,11},{4,12},{5,13},{6,14},{7,15},{8,0},{9,1},... | collective-permute-start | bytes 221192 | tf_op jit(solution)/shard_map/ppermute | solution.py:64
  410.8 5.4 %collective-permute-start.17 = (f32[16,1152]{1,0:T(8,128)S(1)}, f32[16,1152]{1,0:T(8,128)S(1)}, u32[]{:S(2)}, u32[]{:S(2)}) collective-permute-start(f32[16,1152]{1,0:T(8,128)S(1)} %add.158), channel_id=1, source_target_pairs={{0,32},{16,48},{32,0},{48,16},{64,96},{80,112},{96,64},{112,80},{1... | collective-permute-start | bytes 221192 | tf_op jit(solution)/shard_map/ppermute | solution.py:92
  416.2 11.1 %collective-permute-start.18 = (f32[16,2304]{1,0:T(8,128)S(1)}, f32[16,2304]{1,0:T(8,128)S(1)}, u32[]{:S(2)}, u32[]{:S(2)}) collective-permute-start(f32[16,2304]{1,0:T(8,128)S(1)} %maximum_select_fusion.1), channel_id=1, source_target_pairs={{0,16},{16,0},{32,48},{48,32},{64,80},{80,64},{96,112},{112,96},{1... | collective-permute-start | bytes 442376 | tf_op jit(solution)/shard_map/ppermute | solution.py:92
  (31 other events, 142.8 us)

commit v7 on v5

--- a/solution.py
+++ b/solution.py
@@ -13,32 +13,38 @@
 adapter_scale = 2.0
 
 
-def group_grads(query_group, key_group, value_group, cot_group, key_mask):
+def group_grads(query_group, cot_group, parts):
     softmax_scale = 1.0 / math.sqrt(HEAD_SIZE)
-    scores = (
-        jnp.einsum("tgd,md->gtm", query_group, key_group, preferred_element_type=jnp.float32)
-        * softmax_scale
-    )
-    unnorm = jnp.exp(jnp.where(key_mask[None], scores, -jnp.inf))
-    attend = unnorm / jnp.sum(unnorm, -1, keepdims=True)
-    attend_grad = jnp.einsum(
-        "tgd,md->gtm", cot_group, value_group, preferred_element_type=jnp.float32
-    )
-    row_dot = jnp.sum(attend * attend_grad, -1, keepdims=True)
-    dscore = (attend * (attend_grad - row_dot)).astype(jnp.bfloat16)
-    attend_low = attend.astype(jnp.bfloat16)
-    query_grad = (
-        jnp.einsum("gtm,md->tgd", dscore, key_group, preferred_element_type=jnp.float32)
-        * softmax_scale
-    )
-    key_grad = (
-        jnp.einsum("gtm,tgd->md", dscore, query_group, preferred_element_type=jnp.float32)
-        * softmax_scale
-    )
-    value_grad = jnp.einsum(
-        "gtm,tgd->md", attend_low, cot_group, preferred_element_type=jnp.float32
-    )
-    return (query_grad, key_grad, value_grad)
+    unnorms, attend_grads = [], []
+    for key_part, value_part, mask_part in parts:
+        scores = (
+            jnp.einsum("tgd,md->gtm", query_group, key_part, preferred_element_type=jnp.float32)
+            * softmax_scale
+        )
+        unnorms.append(jnp.exp(jnp.where(mask_part[None], scores, -jnp.inf)))
+        attend_grads.append(
+            jnp.einsum("tgd,md->gtm", cot_group, value_part, preferred_element_type=jnp.float32)
+        )
+    total = sum(jnp.sum(u, -1, keepdims=True) for u in unnorms)
+    attends = [u / total for u in unnorms]
+    row_dot = sum(
+        jnp.sum(p * g, -1, keepdims=True) for p, g in zip(attends, attend_grads)
+    )
+    query_grad = None
+    key_grads, value_grads = [], []
+    for (key_part, _, _), attend, attend_grad in zip(parts, attends, attend_grads):
+        dscore = (attend * (attend_grad - row_dot)).astype(jnp.bfloat16)
+        attend_low = attend.astype(jnp.bfloat16)
+        term = jnp.einsum("gtm,md->tgd", dscore, key_part, preferred_element_type=jnp.float32)
+        query_grad = term if query_grad is None else query_grad + term
+        key_grads.append(
+            jnp.einsum("gtm,tgd->md", dscore, query_group, preferred_element_type=jnp.float32)
+            * softmax_scale
+        )
+        value_grads.append(
+            jnp.einsum("gtm,tgd->md", attend_low, cot_group, preferred_element_type=jnp.float32)
+        )
+    return (query_grad * softmax_scale, key_grads, value_grads)
 
 
 def adapter_terms(hidden_piece, low_rank_piece, value_piece, adapter_up_weight):
@@ -142,28 +148,29 @@
     memory_owner = jnp.arange(count) // SUMM
     local_mask = (rows[None, :] <= rows[:, None]) & (rows[None, :] < live)
     memory_mask = jnp.broadcast_to((memory_owner < position)[None, :], (tokens, count))
-    key_mask = jnp.concatenate([memory_mask, local_mask], axis=1)
-    all_keys = jnp.concatenate([memory_keys, key_local], 0)
-    all_values = jnp.concatenate([memory_values, value_local], 0)
-    query_parts, key_parts, value_parts = ([], [], [])
+    query_parts, memory_key_parts, local_key_parts = ([], [], [])
+    memory_value_parts, local_value_parts = ([], [])
     for group in range(kv_heads):
         qcols = slice(group * groups * HEAD_SIZE, (group + 1) * groups * HEAD_SIZE)
         kcols = slice(group * HEAD_SIZE, (group + 1) * HEAD_SIZE)
-        query_grad, key_grad, value_grad = group_grads(
+        query_grad, key_grads, value_grads = group_grads(
             query_rows[:, qcols].reshape(tokens, groups, HEAD_SIZE),
-            all_keys[:, kcols],
-            all_values[:, kcols],
             cot_rows[:, qcols].reshape(tokens, groups, HEAD_SIZE),
-            key_mask,
+            [
+                (key_local[:, kcols], value_local[:, kcols], local_mask),
+                (memory_keys[:, kcols], memory_values[:, kcols], memory_mask),
+            ],
         )
         query_parts.append(query_grad.reshape(tokens, groups * HEAD_SIZE))
-        key_parts.append(key_grad)
-        value_parts.append(value_grad)
+        local_key_parts.append(key_grads[0])
+        memory_key_parts.append(key_grads[1])
+        local_value_parts.append(value_grads[0])
+        memory_value_parts.append(value_grads[1])
     query_out = jnp.concatenate(query_parts, 1).astype(jnp.bfloat16)
-    key_grad = jnp.concatenate(key_parts, 1)
-    value_grad = jnp.concatenate(value_parts, 1)
-    memory_key_grad, local_key = (key_grad[:count], key_grad[count:])
-    memory_value_grad, local_value = (value_grad[:count], value_grad[count:])
+    memory_key_grad = jnp.concatenate(memory_key_parts, 1)
+    local_key = jnp.concatenate(local_key_parts, 1)
+    memory_value_grad = jnp.concatenate(memory_value_parts, 1)
+    local_value = jnp.concatenate(local_value_parts, 1)
     back_key, back_value = (
         lax.psum_scatter(memory_key_grad, "ctx", scatter_dimension=0, tiled=True),
         lax.psum_scatter(memory_value_grad, "ctx", scatter_dimension=0, tiled=True),

time: 368 us -> 472 us (1.28)
  waiting for transfers between devices: 43.7 us -> 284 us
  blocking collectives: 89.6 us -> 0 us
  starting transfers between devices: 128 us -> 89 us
  between operations: 3 us -> 16.7 us
  matrix products: 44.4 us -> 35.3 us
  other arithmetic: 21.9 us -> 15.1 us
    unnamed x4 -> x2, waiting for transfers between devices: 0.66 us -> 231 us
    unnamed x1 -> x0, blocking collectives: 89.6 us -> none
    ppermute x4, starting transfers between devices: 35.2 us -> 10.1 us  [butterfly_sum(): x = x + lax.ppermute(x, axis, [(i, i ^ k) for i in range(n)])]
    div x4 -> x0, matrix products: 16.4 us -> none  [group_grads(): attend = unnorm / jnp.sum(unnorm, -1, keepdims=True)]
    unnamed x4 -> x1, starting transfers between devices: 14.7 us -> 0.04 us
    ppermute x4, waiting for transfers between devices: 4.41 us -> 16.4 us  [butterfly_sum(): x = x + lax.ppermute(x, axis, [(i, i ^ k) for i in range(n)])]
    dot_general x8 -> x24, matrix products: 11.6 us -> 21.2 us  [the longest x8 9.65 us: group_grads(): jnp.einsum('tgd,md->gtm', query_group, key_part, preferred_element_type=j...]
    ppermute x3, starting transfers between devices: 16 us -> 10.4 us  [mesh_sum(): cur = cur + lax.ppermute(cur, 'dp', exchange_pairs('dp', k))]
  transfers between devices with their start and end apart: 19 -> 16, of which waited for: 14 -> 14; matrix products, arithmetic and copies ran while one was open for 7% -> 6% of each run, Pallas kernels for 0% -> 0%
where the time goes in v7:
time: 472 us; the launch traced here: 471 us
  waiting for transfers between devices  284 us (60%)
  starting transfers between devices  89 us (19%)
  matrix products  35.3 us (7%)
  local copies, waits for them, and re-layouts  30.9 us (7%)
  between operations  16.7 us (4%)
  other arithmetic  15.1 us (3%)
    unnamed x2, waiting for transfers between devices  231 us
    ppermute x4, starting transfers between devices, per_device(): lax.ppermute(held, 'ctx', [(i, i + hop) for i in range(segment_list - hop)])  39.6 us
    ppermute x4, waiting for transfers between devices, per_device(): lax.ppermute(held, 'ctx', [(i, i + hop) for i in range(segment_list - hop)])  24.4 us
    ppermute x4, waiting for transfers between devices, butterfly_sum(): x = x + lax.ppermute(x, axis, [(i, i ^ k) for i in range(n)])  16.4 us
    ppermute x2, starting transfers between devices, mesh_sum(): cur = keep + lax.ppermute(give, 'dp', exchange_pairs('dp', k))  15.1 us
    ppermute x2, starting transfers between devices, mesh_sum(): other = lax.ppermute(cur, 'dp', exchange_pairs('dp', k))  13.7 us
    unnamed x118, local copies, waits for them, and re-layouts  11.3 us
    ppermute x3, starting transfers between devices, mesh_sum(): cur = cur + lax.ppermute(cur, 'dp', exchange_pairs('dp', k))  10.4 us
  transfers between devices with their start and end apart: 16, of which 14 were waited for; matrix products, arithmetic and copies ran while one was open for 6% of the time, Pallas kernels for 0%

profile of v7, /device:TPU:1, one launch (start us, length us, event | category | flops | bytes accessed | tf_op | source)
XLA Modules:
  0.0 470.8 jit_solution(16338126803420508228)
XLA Ops:
  10.4 11.5 %collective-permute-start = (bf16[1,100,512]{2,1,0:T(8,128)(2,1)S(1)}, bf16[1,100,512]{2,1,0:T(8,128)(2,1)S(1)}, u32[]{:S(2)}, u32[]{:S(2)}) collective-permute-start(bf16[1,100,512]{2,1,0:T(8,128)(2,1)S(1)} %get-tuple-element.28), channel_id=1, source_target_pairs={{0,8},{1,9},{2,10},{3,11},{4,12},{5,13},{6,14},{7,15},{16,24},{17,... | collective-permute-start | bytes 307208 | tf_op jit(solution)/shard_map/ppermute | solution.py:138
  27.9 7.5 %collective-permute-start.1 = (bf16[2,100,512]{2,1,0:T(8,128)(2,1)S(1)}, bf16[2,100,512]{2,1,0:T(8,128)(2,1)S(1)}, u32[]{:S(2)}, u32[]{:S(2)}) collective-permute-start(bf16[2,100,512]{2,1,0:T(8,128)(2,1)S(1)} %pad_maximum_fusion.7), channel_id=1, source_target_pairs={{0,4},{1,5},{2,6},{3,7},{4,8},{5,9},{6,10},{7,11},{8,12},{9,13},{1... | collective-permute-start | bytes 614408 | tf_op jit(solution)/shard_map/ppermute | solution.py:138
  36.2 2.8 collective-permute-done.1
  39.1 5.6 %collective-permute-start.2 = (bf16[4,100,512]{2,1,0:T(8,128)(2,1)S(1)}, bf16[4,100,512]{2,1,0:T(8,128)(2,1)S(1)}, u32[]{:S(2)}, u32[]{:S(2)}) collective-permute-start(bf16[4,100,512]{2,1,0:T(8,128)(2,1)S(1)} %pad_maximum_fusion.4), channel_id=1, source_target_pairs={{0,2},{1,3},{2,4},{3,5},{4,6},{5,7},{6,8},{7,9},{8,10},{9,11},{10,... | collective-permute-start | bytes 1228808 | tf_op jit(solution)/shard_map/ppermute | solution.py:138
  44.8 7.2 %collective-permute-done.2 = bf16[4,100,512]{2,1,0:T(8,128)(2,1)S(1)} collective-permute-done((bf16[4,100,512]{2,1,0:T(8,128)(2,1)S(1)}, bf16[4,100,512]{2,1,0:T(8,128)(2,1)S(1)}, u32[]{:S(2)}, u32[]{:S(2)}) %collective-permute-start.2) | collective-permute-done | bytes 409632 | tf_op jit(solution)/shard_map/ppermute | solution.py:138
  52.3 15.1 %collective-permute-start.3 = (bf16[8,100,512]{2,0,1:T(8,128)(2,1)S(1)}, bf16[8,100,512]{2,0,1:T(8,128)(2,1)S(1)}, u32[]{:S(2)}, u32[]{:S(2)}) collective-permute-start(bf16[8,100,512]{2,0,1:T(8,128)(2,1)S(1)} %copy.171), channel_id=1, source_target_pairs={{0,1},{1,2},{2,3},{3,4},{4,5},{5,6},{6,7},{7,8},{8,9},{9,10},{10,1... | collective-permute-start | bytes 2457608 | tf_op jit(solution)/shard_map/ppermute | solution.py:138
  70.4 14.4 %collective-permute-done.3 = bf16[8,100,512]{2,0,1:T(8,128)(2,1)S(1)} collective-permute-done((bf16[8,100,512]{2,0,1:T(8,128)(2,1)S(1)}, bf16[8,100,512]{2,0,1:T(8,128)(2,1)S(1)}, u32[]{:S(2)}, u32[]{:S(2)}) %collective-permute-start.3) | collective-permute-done | bytes 819232 | tf_op jit(solution)/shard_map/ppermute | solution.py:138
  86.0 2.1 gather_fusion.1
  90.6 2.6 bitcast_reduce_fusion
  93.1 2.6 bitcast_reduce_fusion.1
  115.2 2.7 copy.221
  118.0 2.2 fusion.11
  122.7 2.7 copy.212
  133.6 231.2 %all-reduce.5.cloned.1.call-done = (f32[800,512]{0,1:T(8,128)}, f32[800,512]{0,1:T(8,128)}) async-done(((f32[800,512]{0,1:T(8,128)}, f32[800,512]{0,1:T(8,128)}), (f32[800,512]{0,1:T(8,128)}, f32[800,512]{0,1:T(8,128)})) %all-reduce.5.cloned.1.call-update) | async-done | bytes 3276816
  364.8 2.5 dynamic-slice_add_fusion
  367.3 2.0 add.205
  370.9 2.1 fusion.45
  374.0 13.0 %collective-permute-start.4 = (f32[16,2304]{1,0:T(8,128)S(1)}, f32[16,2304]{1,0:T(8,128)S(1)}, u32[]{:S(2)}, u32[]{:S(2)}) collective-permute-start(f32[16,2304]{1,0:T(8,128)S(1)} %fusion.58), channel_id=1, source_target_pairs={{0,16},{16,0},{32,48},{48,32},{64,80},{80,64},{96,112},{112,96},{1... | collective-permute-start | bytes 442376 | tf_op jit(solution)/shard_map/ppermute | solution.py:90
  389.1 2.1 collective-permute-start.5
  394.9 3.0 collective-permute-start.6
  398.1 4.4 collective-permute-done.6
  402.5 2.9 collective-permute-start.7
  407.8 4.5 collective-permute-start.8
  414.4 2.4 collective-permute-start.9
  417.2 2.5 collective-permute-done.9
  421.8 4.6 collective-permute-done.10
  426.5 2.2 collective-permute-start.11
  429.6 6.1 %collective-permute-done.11 = f32[16,1152]{1,0:T(8,128)S(1)} collective-permute-done((f32[16,1152]{1,0:T(8,128)S(1)}, f32[16,1152]{1,0:T(8,128)S(1)}, u32[]{:S(2)}, u32[]{:S(2)}) %collective-permute-start.11) | collective-permute-done | bytes 73760 | tf_op jit(solution)/shard_map/ppermute | solution.py:70
  435.7 3.5 collective-permute-start.12
  441.5 3.2 collective-permute-done.12
  447.5 2.3 collective-permute-done.13
  449.9 11.8 %collective-permute-start.14 = (f32[16,2304]{1,0:T(8,128)S(1)}, f32[16,2304]{1,0:T(8,128)S(1)}, u32[]{:S(2)}, u32[]{:S(2)}) collective-permute-start(f32[16,2304]{1,0:T(8,128)S(1)} %maximum_select_fusion.1), channel_id=1, source_target_pairs={{0,16},{16,0},{32,48},{48,32},{64,80},{80,64},{96,112},{112,96},{1... | collective-permute-start | bytes 442376 | tf_op jit(solution)/shard_map/ppermute | solution.py:98
  (236 shorter events, 68.9 us)
Async XLA Ops:
  7.2 362.1 %copy-start = (bf16[1,1,128,4096]{3,2,1,0:T(8,128)(2,1)S(1)}, bf16[1,1,128,4096]{3,2,1,0:T(8,128)(2,1)}, u32[]{:S(2)}) copy-start(bf16[1,1,128,4096]{3,2,1,0:T(8,128)(2,1)} %param.13) | copy-start | bytes 3145732
  7.2 17.6 %copy-start.38 = (bf16[1,1,128,512]{3,2,1,0:T(8,128)(2,1)S(1)}, bf16[1,1,128,512]{3,2,1,0:T(8,128)(2,1)}, u32[]{:S(2)}) copy-start(bf16[1,1,128,512]{3,2,1,0:T(8,128)(2,1)} %param.10) | copy-start | bytes 393220
  7.2 357.6 %all-reduce.5.cloned.1.call-start = ((), (), s32[]{:S(2)}) async-start(), calls=%async_computation | async-start | bytes 7340032
  10.4 17.4 %collective-permute-start = (bf16[1,100,512]{2,1,0:T(8,128)(2,1)S(1)}, bf16[1,100,512]{2,1,0:T(8,128)(2,1)S(1)}, u32[]{:S(2)}, u32[]{:S(2)}) collective-permute-start(bf16[1,100,512]{2,1,0:T(8,128)(2,1)S(1)} %get-tuple-element.28), channel_id=1, source_target_pairs={{0,8},{1,9},{2,10},{3,11},{4,12},{5,13},{6,14},{7,15},{16,24},{17,... | collective-permute-start | bytes 307208 | tf_op jit(solution)/shard_map/ppermute | solution.py:138
  24.8 78.2 %copy-start.7 = (bf16[128,512]{0,1:T(8,128)(2,1)}, bf16[128,512]{0,1:T(8,128)(2,1)S(1)}, u32[]{:S(2)}) copy-start(bf16[128,512]{0,1:T(8,128)(2,1)S(1)} %get-tuple-element.31) | copy-start | bytes 393220
  24.8 82.6 %copy-start.14 = (bf16[128,512]{0,1:T(8,128)(2,1)}, bf16[128,512]{0,1:T(8,128)(2,1)S(1)}, u32[]{:S(2)}) copy-start(bf16[128,512]{0,1:T(8,128)(2,1)S(1)} %get-tuple-element.32) | copy-start | bytes 393220
  24.8 84.9 %copy-start.12 = (bf16[128,512]{0,1:T(8,128)(2,1)}, bf16[128,512]{0,1:T(8,128)(2,1)S(1)}, u32[]{:S(2)}) copy-start(bf16[128,512]{0,1:T(8,128)(2,1)S(1)} %get-tuple-element.33) | copy-start | bytes 393220
  24.8 87.1 %copy-start.10 = (bf16[128,512]{0,1:T(8,128)(2,1)}, bf16[128,512]{0,1:T(8,128)(2,1)S(1)}, u32[]{:S(2)}) copy-start(bf16[128,512]{0,1:T(8,128)(2,1)S(1)} %get-tuple-element.34) | copy-start | bytes 393220
  27.9 11.2 %collective-permute-start.1 = (bf16[2,100,512]{2,1,0:T(8,128)(2,1)S(1)}, bf16[2,100,512]{2,1,0:T(8,128)(2,1)S(1)}, u32[]{:S(2)}, u32[]{:S(2)}) collective-permute-start(bf16[2,100,512]{2,1,0:T(8,128)(2,1)S(1)} %pad_maximum_fusion.7), channel_id=1, source_target_pairs={{0,4},{1,5},{2,6},{3,7},{4,8},{5,9},{6,10},{7,11},{8,12},{9,13},{1... | collective-permute-start | bytes 614408 | tf_op jit(solution)/shard_map/ppermute | solution.py:138
  39.1 12.9 %collective-permute-start.2 = (bf16[4,100,512]{2,1,0:T(8,128)(2,1)S(1)}, bf16[4,100,512]{2,1,0:T(8,128)(2,1)S(1)}, u32[]{:S(2)}, u32[]{:S(2)}) collective-permute-start(bf16[4,100,512]{2,1,0:T(8,128)(2,1)S(1)} %pad_maximum_fusion.4), channel_id=1, source_target_pairs={{0,2},{1,3},{2,4},{3,5},{4,6},{5,7},{6,8},{7,9},{8,10},{9,11},{10,... | collective-permute-start | bytes 1228808 | tf_op jit(solution)/shard_map/ppermute | solution.py:138
  52.3 32.5 %collective-permute-start.3 = (bf16[8,100,512]{2,0,1:T(8,128)(2,1)S(1)}, bf16[8,100,512]{2,0,1:T(8,128)(2,1)S(1)}, u32[]{:S(2)}, u32[]{:S(2)}) collective-permute-start(bf16[8,100,512]{2,0,1:T(8,128)(2,1)S(1)} %copy.171), channel_id=1, source_target_pairs={{0,1},{1,2},{2,3},{3,4},{4,5},{5,6},{6,7},{7,8},{8,9},{9,10},{10,1... | collective-permute-start | bytes 2457608 | tf_op jit(solution)/shard_map/ppermute | solution.py:138
  68.2 44.9 %copy-start.47 = (bf16[128,512]{0,1:T(8,128)(2,1)}, bf16[128,512]{0,1:T(8,128)(2,1)S(1)}, u32[]{:S(2)}) copy-start(bf16[128,512]{0,1:T(8,128)(2,1)S(1)} %get-tuple-element.35) | copy-start | bytes 393220
  372.9 18.3 %copy-start.2 = (bf16[4,128,800]{1,2,0:T(8,128)(2,1)S(1)}, bf16[4,128,800]{1,2,0:T(8,128)(2,1)}, u32[]{:S(2)}) copy-start(bf16[4,128,800]{1,2,0:T(8,128)(2,1)} %copy-done.1) | copy-start | bytes 2457604
  372.9 25.0 %copy-start.27 = (bf16[4,128,128]{1,2,0:T(8,128)(2,1)S(1)}, bf16[4,128,128]{1,2,0:T(8,128)(2,1)}, u32[]{:S(2)}) copy-start(bf16[4,128,128]{1,2,0:T(8,128)(2,1)} %copy-done.26) | copy-start | bytes 393220
  372.9 25.0 %copy-start.39 = (bf16[1,1,128,512]{3,2,1,0:T(8,128)(2,1)S(1)}, bf16[1,1,128,512]{3,2,1,0:T(8,128)(2,1)}, u32[]{:S(2)}) copy-start(bf16[1,1,128,512]{3,2,1,0:T(8,128)(2,1)} %param.10) | copy-start | bytes 393220
  374.0 31.5 %copy-start.5 = (bf16[800,512]{1,0:T(8,128)(2,1)S(1)}, bf16[800,512]{1,0:T(8,128)(2,1)}, u32[]{:S(2)}) copy-start(bf16[800,512]{1,0:T(8,128)(2,1)} %reshape_squeeze.6) | copy-start | bytes 2457604
  374.0 14.2 %collective-permute-start.4 = (f32[16,2304]{1,0:T(8,128)S(1)}, f32[16,2304]{1,0:T(8,128)S(1)}, u32[]{:S(2)}, u32[]{:S(2)}) collective-permute-start(f32[16,2304]{1,0:T(8,128)S(1)} %fusion.58), channel_id=1, source_target_pairs={{0,16},{16,0},{32,48},{48,32},{64,80},{80,64},{96,112},{112,96},{1... | collective-permute-start | bytes 442376 | tf_op jit(solution)/shard_map/ppermute | solution.py:90
  389.1 23.2 %copy-start.25 = (bf16[4,128,128]{1,2,0:T(8,128)(2,1)S(1)}, bf16[4,128,128]{1,2,0:T(8,128)(2,1)}, u32[]{:S(2)}) copy-start(bf16[4,128,128]{1,2,0:T(8,128)(2,1)} %copy-done.24) | copy-start | bytes 393220
  389.1 5.7 %collective-permute-start.5 = (f32[16,1152]{1,0:T(8,128)S(1)}, f32[16,1152]{1,0:T(8,128)S(1)}, u32[]{:S(2)}, u32[]{:S(2)}) collective-permute-start(f32[16,1152]{1,0:T(8,128)S(1)} %constant_dynamic-slice_fusion), channel_id=1, source_target_pairs={{0,32},{16,48},{32,0},{48,16},{64,96},{80,112},{96,64},{112,80},{1... | collective-permute-start | bytes 221192 | tf_op jit(solution)/shard_map/ppermute | solution.py:90
  394.9 7.7 %collective-permute-start.6 = (f32[16,1152]{1,0:T(8,128)S(1)}, f32[16,1152]{1,0:T(8,128)S(1)}, u32[]{:S(2)}, u32[]{:S(2)}) collective-permute-start(f32[16,1152]{1,0:T(8,128)S(1)} %dynamic-slice_add_fusion.2), channel_id=1, source_target_pairs={{0,64},{16,80},{32,96},{48,112},{64,0},{80,16},{96,32},{112,48},{1... | collective-permute-start | bytes 221192 | tf_op jit(solution)/shard_map/ppermute | solution.py:93
  402.5 19.1 %copy-start.23 = (bf16[4,128,128]{1,2,0:T(8,128)(2,1)S(1)}, bf16[4,128,128]{1,2,0:T(8,128)(2,1)}, u32[]{:S(2)}) copy-start(bf16[4,128,128]{1,2,0:T(8,128)(2,1)} %copy-done.22) | copy-start | bytes 393220
  402.5 5.2 %collective-permute-start.7 = (f32[16,1152]{1,0:T(8,128)S(1)}, f32[16,1152]{1,0:T(8,128)S(1)}, u32[]{:S(2)}, u32[]{:S(2)}) collective-permute-start(f32[16,1152]{1,0:T(8,128)S(1)} %add.214), channel_id=1, source_target_pairs={{0,128},{16,144},{32,160},{48,176},{64,192},{80,208},{96,224},{112... | collective-permute-start | bytes 221192 | tf_op jit(solution)/shard_map/ppermute | solution.py:93
  407.8 6.6 %collective-permute-start.8 = (f32[16,1152]{1,0:T(8,128)S(1)}, f32[16,1152]{1,0:T(8,128)S(1)}, u32[]{:S(2)}, u32[]{:S(2)}) collective-permute-start(f32[16,1152]{1,0:T(8,128)S(1)} %add.215), channel_id=1, source_target_pairs={{0,256},{16,272},{32,288},{48,304},{64,320},{80,336},{96,352},{112... | collective-permute-start | bytes 221192 | tf_op jit(solution)/shard_map/ppermute | solution.py:93
  414.4 14.7 %copy-start.41 = (bf16[128,4,128]{0,2,1:T(8,128)(2,1)S(1)}, bf16[128,4,128]{0,2,1:T(8,128)(2,1)}, u32[]{:S(2)}) copy-start(bf16[128,4,128]{0,2,1:T(8,128)(2,1)} %fusion.39) | copy-start | bytes 393220
  414.4 14.8 %copy-start.42 = (bf16[128,4,128]{0,2,1:T(8,128)(2,1)S(1)}, bf16[128,4,128]{0,2,1:T(8,128)(2,1)}, u32[]{:S(2)}) copy-start(bf16[128,4,128]{0,2,1:T(8,128)(2,1)} %fusion.38) | copy-start | bytes 393220
  414.4 5.2 %collective-permute-start.9 = (f32[16,1152]{1,0:T(8,128)S(1)}, f32[16,1152]{1,0:T(8,128)S(1)}, u32[]{:S(2)}, u32[]{:S(2)}) collective-permute-start(f32[16,1152]{1,0:T(8,128)S(1)} %add.216), channel_id=1, source_target_pairs={{0,1},{1,0},{2,3},{3,2},{4,5},{5,4},{6,7},{7,6},{8,9},{9,8},{10,11... | collective-permute-start | bytes 221192 | tf_op jit(solution)/shard_map/ppermute | solution.py:70
  419.7 6.8 %collective-permute-start.10 = (f32[16,1152]{1,0:T(8,128)S(1)}, f32[16,1152]{1,0:T(8,128)S(1)}, u32[]{:S(2)}, u32[]{:S(2)}) collective-permute-start(f32[16,1152]{1,0:T(8,128)S(1)} %add.217), channel_id=1, source_target_pairs={{0,2},{1,3},{2,0},{3,1},{4,6},{5,7},{6,4},{7,5},{8,10},{9,11},{10,... | collective-permute-start | bytes 221192 | tf_op jit(solution)/shard_map/ppermute | solution.py:70
  426.5 9.2 %collective-permute-start.11 = (f32[16,1152]{1,0:T(8,128)S(1)}, f32[16,1152]{1,0:T(8,128)S(1)}, u32[]{:S(2)}, u32[]{:S(2)}) collective-permute-start(f32[16,1152]{1,0:T(8,128)S(1)} %add.218), channel_id=1, source_target_pairs={{0,4},{1,5},{2,6},{3,7},{4,0},{5,1},{6,2},{7,3},{8,12},{9,13},{10,... | collective-permute-start | bytes 221192 | tf_op jit(solution)/shard_map/ppermute | solution.py:70
  429.5 32.2 %copy-start.3 = (f32[128,512]{0,1:T(8,128)S(1)}, f32[128,512]{0,1:T(8,128)}, u32[]{:S(2)}) copy-start(f32[128,512]{0,1:T(8,128)} %add.205) | copy-start | bytes 786436
  435.7 9.0 %collective-permute-start.12 = (f32[16,1152]{1,0:T(8,128)S(1)}, f32[16,1152]{1,0:T(8,128)S(1)}, u32[]{:S(2)}, u32[]{:S(2)}) collective-permute-start(f32[16,1152]{1,0:T(8,128)S(1)} %add.219), channel_id=1, source_target_pairs={{0,8},{1,9},{2,10},{3,11},{4,12},{5,13},{6,14},{7,15},{8,0},{9,1},... | collective-permute-start | bytes 221192 | tf_op jit(solution)/shard_map/ppermute | solution.py:70
  444.7 5.1 %collective-permute-start.13 = (f32[16,1152]{1,0:T(8,128)S(1)}, f32[16,1152]{1,0:T(8,128)S(1)}, u32[]{:S(2)}, u32[]{:S(2)}) collective-permute-start(f32[16,1152]{1,0:T(8,128)S(1)} %add.220), channel_id=1, source_target_pairs={{0,32},{16,48},{32,0},{48,16},{64,96},{80,112},{96,64},{112,80},{1... | collective-permute-start | bytes 221192 | tf_op jit(solution)/shard_map/ppermute | solution.py:98
  449.9 12.8 %collective-permute-start.14 = (f32[16,2304]{1,0:T(8,128)S(1)}, f32[16,2304]{1,0:T(8,128)S(1)}, u32[]{:S(2)}, u32[]{:S(2)}) collective-permute-start(f32[16,2304]{1,0:T(8,128)S(1)} %maximum_select_fusion.1), channel_id=1, source_target_pairs={{0,16},{16,0},{32,48},{48,32},{64,80},{80,64},{96,112},{112,96},{1... | collective-permute-start | bytes 442376 | tf_op jit(solution)/shard_map/ppermute | solution.py:98
  (39 other events, 92.7 us)
Sparse Core Ops, SparseCore 0:
  125.6 239.2 all-reduce.4

commit v8 on v5

--- a/solution.py
+++ b/solution.py
@@ -145,23 +145,36 @@
     key_mask = jnp.concatenate([memory_mask, local_mask], axis=1)
     all_keys = jnp.concatenate([memory_keys, key_local], 0)
     all_values = jnp.concatenate([memory_values, value_local], 0)
-    query_parts, key_parts, value_parts = ([], [], [])
-    for group in range(kv_heads):
-        qcols = slice(group * groups * HEAD_SIZE, (group + 1) * groups * HEAD_SIZE)
-        kcols = slice(group * HEAD_SIZE, (group + 1) * HEAD_SIZE)
-        query_grad, key_grad, value_grad = group_grads(
-            query_rows[:, qcols].reshape(tokens, groups, HEAD_SIZE),
-            all_keys[:, kcols],
-            all_values[:, kcols],
-            cot_rows[:, qcols].reshape(tokens, groups, HEAD_SIZE),
-            key_mask,
-        )
-        query_parts.append(query_grad.reshape(tokens, groups * HEAD_SIZE))
-        key_parts.append(key_grad)
-        value_parts.append(value_grad)
-    query_out = jnp.concatenate(query_parts, 1).astype(jnp.bfloat16)
-    key_grad = jnp.concatenate(key_parts, 1)
-    value_grad = jnp.concatenate(value_parts, 1)
+    softmax_scale = 1.0 / math.sqrt(HEAD_SIZE)
+    query_heads = query_rows.reshape(tokens, kv_heads, groups, HEAD_SIZE)
+    cot_heads = cot_rows.reshape(tokens, kv_heads, groups, HEAD_SIZE)
+    key_heads = all_keys.reshape(-1, kv_heads, HEAD_SIZE)
+    value_heads = all_values.reshape(-1, kv_heads, HEAD_SIZE)
+    scores = (
+        jnp.einsum("tkgd,mkd->kgtm", query_heads, key_heads, preferred_element_type=jnp.float32)
+        * softmax_scale
+    )
+    unnorm = jnp.exp(jnp.where(key_mask[None, None], scores, -jnp.inf))
+    attend = unnorm / jnp.sum(unnorm, -1, keepdims=True)
+    attend_grad = jnp.einsum(
+        "tkgd,mkd->kgtm", cot_heads, value_heads, preferred_element_type=jnp.float32
+    )
+    row_dot = jnp.sum(attend * attend_grad, -1, keepdims=True)
+    dscore = (attend * (attend_grad - row_dot)).astype(jnp.bfloat16)
+    attend_low = attend.astype(jnp.bfloat16)
+    query_out = (
+        jnp.einsum("kgtm,mkd->tkgd", dscore, key_heads, preferred_element_type=jnp.float32)
+        * softmax_scale
+    ).reshape(tokens, kv_heads * groups * HEAD_SIZE).astype(jnp.bfloat16)
+    key_grad = (
+        jnp.einsum("kgtm,tkgd->mkd", dscore, query_heads, preferred_element_type=jnp.float32)
+        * softmax_scale
+    )
+    value_grad = jnp.einsum(
+        "kgtm,tkgd->mkd", attend_low, cot_heads, preferred_element_type=jnp.float32
+    )
+    key_grad = jnp.concatenate([key_grad[:, h] for h in range(kv_heads)], 1)
+    value_grad = jnp.concatenate([value_grad[:, h] for h in range(kv_heads)], 1)
     memory_key_grad, local_key = (key_grad[:count], key_grad[count:])
     memory_value_grad, local_value = (value_grad[:count], value_grad[count:])
     back_key, back_value = (

time: 368 us -> 317 us (0.86)
  matrix products: 44.4 us -> 13 us
  other arithmetic: 21.9 us -> 9.9 us
  starting transfers between devices: 128 us -> 120 us
  local copies, waits for them, and re-layouts: 34.7 us -> 30.5 us
    div x4 -> x0, matrix products: 16.4 us -> none  [group_grads(): attend = unnorm / jnp.sum(unnorm, -1, keepdims=True)]
    dot_general x16 -> x5, matrix products: 25.4 us -> 12 us  [the longest x1 3.92 us: per_device(): jnp.einsum('kgtm,mkd->tkgd', dscore, key_heads, preferred_element_type=jn...]
    unnamed x4, starting transfers between devices: 14.7 us -> 7.88 us
    convert_element_type x4 -> x1, other arithmetic: 7.52 us -> 2.3 us  [per_device(): dscore = (attend * (attend_grad - row_dot)).astype(jnp.bfloat16)]
    unnamed x100 -> x49, local copies, waits for them, and re-layouts: 16.2 us -> 11.7 us
  transfers between devices with their start and end apart: 19 -> 19, of which waited for: 14 -> 14; matrix products, arithmetic and copies ran while one was open for 7% -> 8% of each run, Pallas kernels for 0% -> 0%
where the time goes in v8:
time: 317 us; the launch traced here: 312 us
  starting transfers between devices  120 us (38%)
  blocking collectives  89 us (28%)
  waiting for transfers between devices  46.1 us (15%)
  local copies, waits for them, and re-layouts  30.5 us (10%)
  matrix products  13 us (4%)
  other arithmetic  9.9 us (3%)
    unnamed x1, blocking collectives  89 us
    ppermute x4, starting transfers between devices, per_device(): lax.ppermute(held, 'ctx', [(i, i + hop) for i in range(segment_list - hop)])  39.4 us
    ppermute x4, starting transfers between devices, butterfly_sum(): x = x + lax.ppermute(x, axis, [(i, i ^ k) for i in range(n)])  36.6 us
    ppermute x4, waiting for transfers between devices, per_device(): lax.ppermute(held, 'ctx', [(i, i + hop) for i in range(segment_list - hop)])  24.8 us
    ppermute x3, starting transfers between devices, mesh_sum(): cur = cur + lax.ppermute(cur, 'dp', exchange_pairs('dp', k))  15.5 us
    unnamed x49, local copies, waits for them, and re-layouts  11.7 us
    ppermute x2, starting transfers between devices, mesh_sum(): other = lax.ppermute(cur, 'dp', exchange_pairs('dp', k))  11.7 us
    ppermute x2, starting transfers between devices, mesh_sum(): cur = keep + lax.ppermute(give, 'dp', exchange_pairs('dp', k))  9.45 us
  transfers between devices with their start and end apart: 19, of which 14 were waited for; matrix products, arithmetic and copies ran while one was open for 8% of the time, Pallas kernels for 0%

profile of v8, /device:TPU:1, one launch (start us, length us, event | category | flops | bytes accessed | tf_op | source)
XLA Modules:
  0.0 311.8 jit_solution(13080367474322686243)
XLA Ops:
  2.9 11.5 %collective-permute-start = (bf16[1,100,512]{2,1,0:T(8,128)(2,1)S(1)}, bf16[1,100,512]{2,1,0:T(8,128)(2,1)S(1)}, u32[]{:S(2)}, u32[]{:S(2)}) collective-permute-start(bf16[1,100,512]{2,1,0:T(8,128)(2,1)S(1)} %get-tuple-element.30), channel_id=1, source_target_pairs={{0,8},{1,9},{2,10},{3,11},{4,12},{5,13},{6,14},{7,15},{16,24},{17,... | collective-permute-start | bytes 307208 | tf_op jit(solution)/shard_map/ppermute | solution.py:132
  16.1 7.5 %collective-permute-start.1 = (bf16[2,100,512]{2,1,0:T(8,128)(2,1)S(1)}, bf16[2,100,512]{2,1,0:T(8,128)(2,1)S(1)}, u32[]{:S(2)}, u32[]{:S(2)}) collective-permute-start(bf16[2,100,512]{2,1,0:T(8,128)(2,1)S(1)} %pad_maximum_fusion.10), channel_id=1, source_target_pairs={{0,4},{1,5},{2,6},{3,7},{4,8},{5,9},{6,10},{7,11},{8,12},{9,13},{1... | collective-permute-start | bytes 614408 | tf_op jit(solution)/shard_map/ppermute | solution.py:132
  23.6 3.0 collective-permute-done.1
  26.7 7.5 %collective-permute-start.2 = (bf16[4,100,512]{2,1,0:T(8,128)(2,1)S(1)}, bf16[4,100,512]{2,1,0:T(8,128)(2,1)S(1)}, u32[]{:S(2)}, u32[]{:S(2)}) collective-permute-start(bf16[4,100,512]{2,1,0:T(8,128)(2,1)S(1)} %pad_maximum_fusion.7), channel_id=1, source_target_pairs={{0,2},{1,3},{2,4},{3,5},{4,6},{5,7},{6,8},{7,9},{8,10},{9,11},{10,... | collective-permute-start | bytes 1228808 | tf_op jit(solution)/shard_map/ppermute | solution.py:132
  34.2 13.2 %collective-permute-done.2 = bf16[4,100,512]{2,1,0:T(8,128)(2,1)S(1)} collective-permute-done((bf16[4,100,512]{2,1,0:T(8,128)(2,1)S(1)}, bf16[4,100,512]{2,1,0:T(8,128)(2,1)S(1)}, u32[]{:S(2)}, u32[]{:S(2)}) %collective-permute-start.2) | collective-permute-done | bytes 409632 | tf_op jit(solution)/shard_map/ppermute | solution.py:132
  47.7 13.0 %collective-permute-start.3 = (bf16[8,100,512]{2,0,1:T(8,128)(2,1)S(1)}, bf16[8,100,512]{2,0,1:T(8,128)(2,1)}, u32[]{:S(2)}, u32[]{:S(2)}) collective-permute-start(bf16[8,100,512]{2,0,1:T(8,128)(2,1)S(1)} %copy.43), channel_id=1, source_target_pairs={{0,1},{1,2},{2,3},{3,4},{4,5},{5,6},{6,7},{7,8},{8,9},{9,10},{10,1... | collective-permute-start | bytes 2457608 | tf_op jit(solution)/shard_map/ppermute | solution.py:132
  63.2 2.2 squeeze.36
  70.5 8.2 %collective-permute-done.3 = bf16[8,100,512]{2,0,1:T(8,128)(2,1)} collective-permute-done((bf16[8,100,512]{2,0,1:T(8,128)(2,1)S(1)}, bf16[8,100,512]{2,0,1:T(8,128)(2,1)}, u32[]{:S(2)}, u32[]{:S(2)}) %collective-permute-start.3) | collective-permute-done | bytes 819232 | tf_op jit(solution)/shard_map/ppermute | solution.py:132
  78.7 2.3 copy_dynamic-update-slice_fusion
  81.0 2.1 gather_fusion.1
  85.7 2.2 copy.48
  88.8 3.1 fusion.7
  93.6 2.2 fusion.2
  95.7 2.3 fusion.4
  103.1 89.0 %fusion.47 = (f32[56,512]{1,0:T(8,128)}, f32[56,512]{1,0:T(8,128)S(1)}) fusion(f32[800,512]{1,0:T(8,128)S(1)} %pad_maximum_fusion.3, f32[800,512]{1,0:T(8,128)} %pad_maximum_fusion), kind=kCustom, calls=%all-reduce-scatter.2 | all-reduce-scatter fusion | flops 917505 | bytes 3508224
  198.9 7.5 %collective-permute-start.4 = (f32[16,2304]{1,0:T(8,128)S(1)}, f32[16,2304]{1,0:T(8,128)S(1)}, u32[]{:S(2)}, u32[]{:S(2)}) collective-permute-start(f32[16,2304]{1,0:T(8,128)S(1)} %fusion.27), channel_id=1, source_target_pairs={{0,16},{16,0},{32,48},{48,32},{64,80},{80,64},{96,112},{112,96},{1... | collective-permute-start | bytes 442376 | tf_op jit(solution)/shard_map/ppermute | solution.py:84
  209.4 3.2 %collective-permute-done.5 = f32[16,1152]{1,0:T(8,128)S(1)} collective-permute-done((f32[16,1152]{1,0:T(8,128)S(1)}, f32[16,1152]{1,0:T(8,128)S(1)}, u32[]{:S(2)}, u32[]{:S(2)}) %collective-permute-start.5) | collective-permute-done | bytes 73760 | tf_op jit(solution)/shard_map/ppermute | solution.py:84
  212.6 7.3 %collective-permute-start.6 = (f32[16,1152]{1,0:T(8,128)S(1)}, f32[16,1152]{1,0:T(8,128)S(1)}, u32[]{:S(2)}, u32[]{:S(2)}) collective-permute-start(f32[16,1152]{1,0:T(8,128)S(1)} %dynamic-slice_add_fusion.2), channel_id=1, source_target_pairs={{0,64},{16,80},{32,96},{48,112},{64,0},{80,16},{96,32},{112,48},{1... | collective-permute-start | bytes 221192 | tf_op jit(solution)/shard_map/ppermute | solution.py:87
  220.0 4.8 %collective-permute-done.6 = f32[16,1152]{1,0:T(8,128)S(1)} collective-permute-done((f32[16,1152]{1,0:T(8,128)S(1)}, f32[16,1152]{1,0:T(8,128)S(1)}, u32[]{:S(2)}, u32[]{:S(2)}) %collective-permute-start.6) | collective-permute-done | bytes 73760 | tf_op jit(solution)/shard_map/ppermute | solution.py:87
  224.7 3.7 %collective-permute-start.7 = (f32[16,1152]{1,0:T(8,128)S(1)}, f32[16,1152]{1,0:T(8,128)S(1)}, u32[]{:S(2)}, u32[]{:S(2)}) collective-permute-start(f32[16,1152]{1,0:T(8,128)S(1)} %add.130), channel_id=1, source_target_pairs={{0,128},{16,144},{32,160},{48,176},{64,192},{80,208},{96,224},{112... | collective-permute-start | bytes 221192 | tf_op jit(solution)/shard_map/ppermute | solution.py:87
  230.2 4.5 %collective-permute-start.8 = (f32[16,1152]{1,0:T(8,128)S(1)}, f32[16,1152]{1,0:T(8,128)S(1)}, u32[]{:S(2)}, u32[]{:S(2)}) collective-permute-start(f32[16,1152]{1,0:T(8,128)S(1)} %add.131), channel_id=1, source_target_pairs={{0,256},{16,272},{32,288},{48,304},{64,320},{80,336},{96,352},{112... | collective-permute-start | bytes 221192 | tf_op jit(solution)/shard_map/ppermute | solution.py:87
  234.6 2.1 collective-permute-done.8
  236.8 2.5 collective-permute-start.9
  239.3 2.6 collective-permute-done.9
  241.9 5.8 %collective-permute-start.10 = (f32[16,1152]{1,0:T(8,128)S(1)}, f32[16,1152]{1,0:T(8,128)}, u32[]{:S(2)}, u32[]{:S(2)}) collective-permute-start(f32[16,1152]{1,0:T(8,128)S(1)} %add.133), channel_id=1, source_target_pairs={{0,2},{1,3},{2,0},{3,1},{4,6},{5,7},{6,4},{7,5},{8,10},{9,11},{10,... | collective-permute-start | bytes 221192 | tf_op jit(solution)/shard_map/ppermute | solution.py:64
  247.7 3.9 %fusion.14 = bf16[4,128,4,128]{3,1,2,0:T(8,128)(2,1)} fusion(bf16[4,4,128,928]{2,3,1,0:T(8,128)(2,1)} %copy-done.1, bf16[128,4,128]{2,0,1:T(8,128)(2,1)S(1)} %copy-done.16, bf16[800,4,128]{2,0,1:T(8,128)(2,1)} %copy.48), kind=kOutput, calls=%fused_computation.24 | convolution fusion | flops 488964096 | bytes 5275648 | tf_op jit(solution)/shard_map/kgtm,mkd->tkgd/dot_general | solution.py:166
  253.2 4.0 %collective-permute-start.15 = (f32[56,512]{1,0:T(8,128)}, f32[56,512]{1,0:T(8,128)}, u32[]{:S(2)}, u32[]{:S(2)}) collective-permute-start(f32[56,512]{1,0:T(8,128)} %get-tuple-element.27), channel_id=1, source_target_pairs={{0,1},{1,2},{2,3},{3,4},{4,5},{5,6},{6,7},{7,8},{8,9},{9,10},{10,1... | collective-permute-start | bytes 344072
  261.4 18.4 %collective-permute-start.11 = (f32[16,1152]{1,0:T(8,128)S(1)}, f32[16,1152]{1,0:T(8,128)S(1)}, u32[]{:S(2)}, u32[]{:S(2)}) collective-permute-start(f32[16,1152]{1,0:T(8,128)S(1)} %add.134), channel_id=1, source_target_pairs={{0,4},{1,5},{2,6},{3,7},{4,0},{5,1},{6,2},{7,3},{8,12},{9,13},{10,... | collective-permute-start | bytes 221192 | tf_op jit(solution)/shard_map/ppermute | solution.py:64
  279.9 2.5 collective-permute-done.11
  282.5 9.9 %collective-permute-start.12 = (f32[16,1152]{1,0:T(8,128)S(1)}, f32[16,1152]{1,0:T(8,128)S(1)}, u32[]{:S(2)}, u32[]{:S(2)}) collective-permute-start(f32[16,1152]{1,0:T(8,128)S(1)} %add.135), channel_id=1, source_target_pairs={{0,8},{1,9},{2,10},{3,11},{4,12},{5,13},{6,14},{7,15},{8,0},{9,1},... | collective-permute-start | bytes 221192 | tf_op jit(solution)/shard_map/ppermute | solution.py:64
  295.0 2.6 collective-permute-start.13
  300.3 9.1 %collective-permute-start.14 = (f32[16,2304]{1,0:T(8,128)S(1)}, f32[16,2304]{1,0:T(8,128)S(1)}, u32[]{:S(2)}, u32[]{:S(2)}) collective-permute-start(f32[16,2304]{1,0:T(8,128)S(1)} %maximum_select_fusion.1), channel_id=1, source_target_pairs={{0,16},{16,0},{32,48},{48,32},{64,80},{80,64},{96,112},{112,96},{1... | collective-permute-start | bytes 442376 | tf_op jit(solution)/shard_map/ppermute | solution.py:92
  (123 shorter events, 45.5 us)
Async XLA Ops:
  0.6 197.2 %copy-start = (bf16[1,1,128,4096]{3,2,1,0:T(8,128)(2,1)S(1)}, bf16[1,1,128,4096]{3,2,1,0:T(8,128)(2,1)}, u32[]{:S(2)}) copy-start(bf16[1,1,128,4096]{3,2,1,0:T(8,128)(2,1)} %param.13) | copy-start | bytes 3145732
  2.9 13.2 %collective-permute-start = (bf16[1,100,512]{2,1,0:T(8,128)(2,1)S(1)}, bf16[1,100,512]{2,1,0:T(8,128)(2,1)S(1)}, u32[]{:S(2)}, u32[]{:S(2)}) collective-permute-start(bf16[1,100,512]{2,1,0:T(8,128)(2,1)S(1)} %get-tuple-element.30), channel_id=1, source_target_pairs={{0,8},{1,9},{2,10},{3,11},{4,12},{5,13},{6,14},{7,15},{16,24},{17,... | collective-permute-start | bytes 307208 | tf_op jit(solution)/shard_map/ppermute | solution.py:132
  16.1 10.5 %collective-permute-start.1 = (bf16[2,100,512]{2,1,0:T(8,128)(2,1)S(1)}, bf16[2,100,512]{2,1,0:T(8,128)(2,1)S(1)}, u32[]{:S(2)}, u32[]{:S(2)}) collective-permute-start(bf16[2,100,512]{2,1,0:T(8,128)(2,1)S(1)} %pad_maximum_fusion.10), channel_id=1, source_target_pairs={{0,4},{1,5},{2,6},{3,7},{4,8},{5,9},{6,10},{7,11},{8,12},{9,13},{1... | collective-permute-start | bytes 614408 | tf_op jit(solution)/shard_map/ppermute | solution.py:132
  26.6 34.1 %copy-start.13 = (bf16[1,1,128,512]{3,2,1,0:T(8,128)(2,1)S(1)}, bf16[1,1,128,512]{3,2,1,0:T(8,128)(2,1)}, u32[]{:S(2)}) copy-start(bf16[1,1,128,512]{3,2,1,0:T(8,128)(2,1)} %param.10) | copy-start | bytes 393220
  26.7 34.2 %copy-start.14 = (bf16[1,1,128,512]{3,2,1,0:T(8,128)(2,1)S(1)}, bf16[1,1,128,512]{3,2,1,0:T(8,128)(2,1)}, u32[]{:S(2)}) copy-start(bf16[1,1,128,512]{3,2,1,0:T(8,128)(2,1)} %param.11) | copy-start | bytes 393220
  26.7 20.7 %collective-permute-start.2 = (bf16[4,100,512]{2,1,0:T(8,128)(2,1)S(1)}, bf16[4,100,512]{2,1,0:T(8,128)(2,1)S(1)}, u32[]{:S(2)}, u32[]{:S(2)}) collective-permute-start(bf16[4,100,512]{2,1,0:T(8,128)(2,1)S(1)} %pad_maximum_fusion.7), channel_id=1, source_target_pairs={{0,2},{1,3},{2,4},{3,5},{4,6},{5,7},{6,8},{7,9},{8,10},{9,11},{10,... | collective-permute-start | bytes 1228808 | tf_op jit(solution)/shard_map/ppermute | solution.py:132
  47.7 31.0 %collective-permute-start.3 = (bf16[8,100,512]{2,0,1:T(8,128)(2,1)S(1)}, bf16[8,100,512]{2,0,1:T(8,128)(2,1)}, u32[]{:S(2)}, u32[]{:S(2)}) collective-permute-start(bf16[8,100,512]{2,0,1:T(8,128)(2,1)S(1)} %copy.43), channel_id=1, source_target_pairs={{0,1},{1,2},{2,3},{3,4},{4,5},{5,6},{6,7},{7,8},{8,9},{9,10},{10,1... | collective-permute-start | bytes 2457608 | tf_op jit(solution)/shard_map/ppermute | solution.py:132
  88.7 3.1 copy-start.12
  91.8 1.7 copy-start.17
  98.1 1.8 copy-start.1
  100.2 1.6 copy-start.11
  192.1 5.8 %copy-start.18 = (bf16[16,512]{1,0:T(8,128)(2,1)S(1)}, bf16[16,512]{1,0:T(8,128)(2,1)}, u32[]{:S(2)}) copy-start(bf16[16,512]{1,0:T(8,128)(2,1)} %param.15) | copy-start | bytes 49156
  192.1 4.8 %collective-permute-start.17 = (f32[56,512]{1,0:T(8,128)S(1)}, f32[56,512]{1,0:T(8,128)S(1)}, u32[]{:S(2)}, u32[]{:S(2)}) collective-permute-start(f32[56,512]{1,0:T(8,128)S(1)} %get-tuple-element.28), channel_id=1, source_target_pairs={{0,1},{1,2},{2,3},{3,4},{4,5},{5,6},{6,7},{7,8},{8,9},{9,10},{10,1... | collective-permute-start | bytes 344072
  193.4 3.5 %collective-permute-start.18 = (f32[34,512]{1,0:T(8,128)S(1)}, f32[34,512]{1,0:T(8,128)S(1)}, u32[]{:S(2)}, u32[]{:S(2)}) collective-permute-start(f32[34,512]{1,0:T(8,128)S(1)} %slice.87), channel_id=1, source_target_pairs={{0,2},{1,3},{2,4},{3,5},{4,6},{5,7},{6,8},{7,9},{8,10},{9,11},{10,... | collective-permute-start | bytes 208904
  195.7 2.7 copy-start.15
  198.3 49.4 %copy-start.16 = (bf16[128,4,128]{2,0,1:T(8,128)(2,1)S(1)}, bf16[128,4,128]{2,0,1:T(8,128)(2,1)}, u32[]{:S(2)}) copy-start(bf16[128,4,128]{2,0,1:T(8,128)(2,1)} %copy.49) | copy-start | bytes 393220
  198.9 8.5 %collective-permute-start.4 = (f32[16,2304]{1,0:T(8,128)S(1)}, f32[16,2304]{1,0:T(8,128)S(1)}, u32[]{:S(2)}, u32[]{:S(2)}) collective-permute-start(f32[16,2304]{1,0:T(8,128)S(1)} %fusion.27), channel_id=1, source_target_pairs={{0,16},{16,0},{32,48},{48,32},{64,80},{80,64},{96,112},{112,96},{1... | collective-permute-start | bytes 442376 | tf_op jit(solution)/shard_map/ppermute | solution.py:84
  207.5 5.1 %collective-permute-start.5 = (f32[16,1152]{1,0:T(8,128)S(1)}, f32[16,1152]{1,0:T(8,128)S(1)}, u32[]{:S(2)}, u32[]{:S(2)}) collective-permute-start(f32[16,1152]{1,0:T(8,128)S(1)} %constant_dynamic-slice_fusion), channel_id=1, source_target_pairs={{0,32},{16,48},{32,0},{48,16},{64,96},{80,112},{96,64},{112,80},{1... | collective-permute-start | bytes 221192 | tf_op jit(solution)/shard_map/ppermute | solution.py:84
  212.6 12.1 %collective-permute-start.6 = (f32[16,1152]{1,0:T(8,128)S(1)}, f32[16,1152]{1,0:T(8,128)S(1)}, u32[]{:S(2)}, u32[]{:S(2)}) collective-permute-start(f32[16,1152]{1,0:T(8,128)S(1)} %dynamic-slice_add_fusion.2), channel_id=1, source_target_pairs={{0,64},{16,80},{32,96},{48,112},{64,0},{80,16},{96,32},{112,48},{1... | collective-permute-start | bytes 221192 | tf_op jit(solution)/shard_map/ppermute | solution.py:87
  224.7 5.4 %collective-permute-start.7 = (f32[16,1152]{1,0:T(8,128)S(1)}, f32[16,1152]{1,0:T(8,128)S(1)}, u32[]{:S(2)}, u32[]{:S(2)}) collective-permute-start(f32[16,1152]{1,0:T(8,128)S(1)} %add.130), channel_id=1, source_target_pairs={{0,128},{16,144},{32,160},{48,176},{64,192},{80,208},{96,224},{112... | collective-permute-start | bytes 221192 | tf_op jit(solution)/shard_map/ppermute | solution.py:87
  230.2 6.6 %collective-permute-start.8 = (f32[16,1152]{1,0:T(8,128)S(1)}, f32[16,1152]{1,0:T(8,128)S(1)}, u32[]{:S(2)}, u32[]{:S(2)}) collective-permute-start(f32[16,1152]{1,0:T(8,128)S(1)} %add.131), channel_id=1, source_target_pairs={{0,256},{16,272},{32,288},{48,304},{64,320},{80,336},{96,352},{112... | collective-permute-start | bytes 221192 | tf_op jit(solution)/shard_map/ppermute | solution.py:87
  236.8 5.1 %collective-permute-start.9 = (f32[16,1152]{1,0:T(8,128)S(1)}, f32[16,1152]{1,0:T(8,128)S(1)}, u32[]{:S(2)}, u32[]{:S(2)}) collective-permute-start(f32[16,1152]{1,0:T(8,128)S(1)} %add.132), channel_id=1, source_target_pairs={{0,1},{1,0},{2,3},{3,2},{4,5},{5,4},{6,7},{7,6},{8,9},{9,8},{10,11... | collective-permute-start | bytes 221192 | tf_op jit(solution)/shard_map/ppermute | solution.py:64
  241.9 38.0 %copy-start.3 = (f32[928,128]{1,0:T(8,128)S(1)}, f32[928,128]{1,0:T(8,128)}, u32[]{:S(2)}) copy-start(f32[928,128]{1,0:T(8,128)} %copy-done.2) | copy-start | bytes 1425412
  241.9 38.0 %copy-start.5 = (f32[928,128]{1,0:T(8,128)S(1)}, f32[928,128]{1,0:T(8,128)}, u32[]{:S(2)}) copy-start(f32[928,128]{1,0:T(8,128)} %copy-done.4) | copy-start | bytes 1425412
  241.9 38.0 %copy-start.7 = (f32[928,128]{1,0:T(8,128)S(1)}, f32[928,128]{1,0:T(8,128)}, u32[]{:S(2)}) copy-start(f32[928,128]{1,0:T(8,128)} %copy-done.6) | copy-start | bytes 1425412
  241.9 18.6 %collective-permute-start.10 = (f32[16,1152]{1,0:T(8,128)S(1)}, f32[16,1152]{1,0:T(8,128)}, u32[]{:S(2)}, u32[]{:S(2)}) collective-permute-start(f32[16,1152]{1,0:T(8,128)S(1)} %add.133), channel_id=1, source_target_pairs={{0,2},{1,3},{2,0},{3,1},{4,6},{5,7},{6,4},{7,5},{8,10},{9,11},{10,... | collective-permute-start | bytes 221192 | tf_op jit(solution)/shard_map/ppermute | solution.py:64
  253.2 39.9 %collective-permute-start.15 = (f32[56,512]{1,0:T(8,128)}, f32[56,512]{1,0:T(8,128)}, u32[]{:S(2)}, u32[]{:S(2)}) collective-permute-start(f32[56,512]{1,0:T(8,128)} %get-tuple-element.27), channel_id=1, source_target_pairs={{0,1},{1,2},{2,3},{3,4},{4,5},{5,6},{6,7},{7,8},{8,9},{9,10},{10,1... | collective-permute-start | bytes 344072
  259.2 33.8 %collective-permute-start.16 = (f32[34,512]{1,0:T(8,128)}, f32[34,512]{1,0:T(8,128)S(1)}, u32[]{:S(2)}, u32[]{:S(2)}) collective-permute-start(f32[34,512]{1,0:T(8,128)} %slice.86), channel_id=1, source_target_pairs={{0,2},{1,3},{2,4},{3,5},{4,6},{5,7},{6,8},{7,9},{8,10},{9,11},{10,... | collective-permute-start | bytes 208904
  261.4 21.0 %collective-permute-start.11 = (f32[16,1152]{1,0:T(8,128)S(1)}, f32[16,1152]{1,0:T(8,128)S(1)}, u32[]{:S(2)}, u32[]{:S(2)}) collective-permute-start(f32[16,1152]{1,0:T(8,128)S(1)} %add.134), channel_id=1, source_target_pairs={{0,4},{1,5},{2,6},{3,7},{4,0},{5,1},{6,2},{7,3},{8,12},{9,13},{10,... | collective-permute-start | bytes 221192 | tf_op jit(solution)/shard_map/ppermute | solution.py:64
  282.5 12.5 %collective-permute-start.12 = (f32[16,1152]{1,0:T(8,128)S(1)}, f32[16,1152]{1,0:T(8,128)S(1)}, u32[]{:S(2)}, u32[]{:S(2)}) collective-permute-start(f32[16,1152]{1,0:T(8,128)S(1)} %add.135), channel_id=1, source_target_pairs={{0,8},{1,9},{2,10},{3,11},{4,12},{5,13},{6,14},{7,15},{8,0},{9,1},... | collective-permute-start | bytes 221192 | tf_op jit(solution)/shard_map/ppermute | solution.py:64
  295.0 5.2 %collective-permute-start.13 = (f32[16,1152]{1,0:T(8,128)S(1)}, f32[16,1152]{1,0:T(8,128)S(1)}, u32[]{:S(2)}, u32[]{:S(2)}) collective-permute-start(f32[16,1152]{1,0:T(8,128)S(1)} %add.136), channel_id=1, source_target_pairs={{0,32},{16,48},{32,0},{48,16},{64,96},{80,112},{96,64},{112,80},{1... | collective-permute-start | bytes 221192 | tf_op jit(solution)/shard_map/ppermute | solution.py:92
  300.3 10.1 %collective-permute-start.14 = (f32[16,2304]{1,0:T(8,128)S(1)}, f32[16,2304]{1,0:T(8,128)S(1)}, u32[]{:S(2)}, u32[]{:S(2)}) collective-permute-start(f32[16,2304]{1,0:T(8,128)S(1)} %maximum_select_fusion.1), channel_id=1, source_target_pairs={{0,16},{16,0},{32,48},{48,32},{64,80},{80,64},{96,112},{112,96},{1... | collective-permute-start | bytes 442376 | tf_op jit(solution)/shard_map/ppermute | solution.py:92
  (6 other events, 6.5 us)

commit v9 on v8

--- a/solution.py
+++ b/solution.py
@@ -177,10 +177,9 @@
     value_grad = jnp.concatenate([value_grad[:, h] for h in range(kv_heads)], 1)
     memory_key_grad, local_key = (key_grad[:count], key_grad[count:])
     memory_value_grad, local_value = (value_grad[:count], value_grad[count:])
-    back_key, back_value = (
-        lax.psum_scatter(memory_key_grad, "ctx", scatter_dimension=0, tiled=True),
-        lax.psum_scatter(memory_value_grad, "ctx", scatter_dimension=0, tiled=True),
-    )
+    back_value = lax.psum_scatter(memory_value_grad, "ctx", scatter_dimension=0, tiled=True)
+    memory_key_grad, _ = lax.optimization_barrier((memory_key_grad, back_value))
+    back_key = lax.psum_scatter(memory_key_grad, "ctx", scatter_dimension=0, tiled=True)
     key_out = (
         local_key + lax.dynamic_update_slice_in_dim(jnp.zeros_like(local_key), back_key, length, 0)
     ).astype(jnp.bfloat16)

time: 317 us -> 351 us (1.11)
  blocking collectives: 89 us -> 119 us
  starting transfers between devices: 120 us -> 126 us
    unnamed x1 -> x2, blocking collectives: 89 us -> 119 us
    ppermute x2, starting transfers between devices: 9.45 us -> 18.7 us  [mesh_sum(): cur = keep + lax.ppermute(give, 'dp', exchange_pairs('dp', k))]
    ppermute x2, starting transfers between devices: 11.7 us -> 19.3 us  [mesh_sum(): other = lax.ppermute(cur, 'dp', exchange_pairs('dp', k))]
    ppermute x4, starting transfers between devices: 36.6 us -> 29.6 us  [butterfly_sum(): x = x + lax.ppermute(x, axis, [(i, i ^ k) for i in range(n)])]
    concatenate x3, local copies, waits for them, and re-layouts: 1.19 us -> 5.65 us  [per_device(): all_values = jnp.concatenate([memory_values, value_local], 0)]
    ppermute x2, waiting for transfers between devices: 4.1 us -> 0.32 us  [mesh_sum(): cur = keep + lax.ppermute(give, 'dp', exchange_pairs('dp', k))]
    unnamed x49 -> x61, local copies, waits for them, and re-layouts: 11.7 us -> 8.67 us
  transfers between devices with their start and end apart: 19 -> 19, of which waited for: 14 -> 13; matrix products, arithmetic and copies ran while one was open for 8% -> 27% of each run, Pallas kernels for 0% -> 0%
where the time goes in v9:
time: 351 us; the launch traced here: 347 us
  starting transfers between devices  126 us (36%)
  blocking collectives  119 us (34%)
  waiting for transfers between devices  43.5 us (12%)
  local copies, waits for them, and re-layouts  32.5 us (9%)
  matrix products  13.7 us (4%)
  other arithmetic  9.21 us (3%)
    unnamed x2, blocking collectives  119 us
    ppermute x4, starting transfers between devices, per_device(): lax.ppermute(held, 'ctx', [(i, i + hop) for i in range(segment_list - hop)])  39.4 us
    ppermute x4, starting transfers between devices, butterfly_sum(): x = x + lax.ppermute(x, axis, [(i, i ^ k) for i in range(n)])  29.6 us
    ppermute x4, waiting for transfers between devices, per_device(): lax.ppermute(held, 'ctx', [(i, i + hop) for i in range(segment_list - hop)])  24.6 us
    ppermute x2, starting transfers between devices, mesh_sum(): other = lax.ppermute(cur, 'dp', exchange_pairs('dp', k))  19.3 us
    ppermute x2, starting transfers between devices, mesh_sum(): cur = keep + lax.ppermute(give, 'dp', exchange_pairs('dp', k))  18.7 us
    ppermute x3, starting transfers between devices, mesh_sum(): cur = cur + lax.ppermute(cur, 'dp', exchange_pairs('dp', k))  14.1 us
    unnamed x61, local copies, waits for them, and re-layouts  8.67 us
  transfers between devices with their start and end apart: 19, of which 13 were waited for; matrix products, arithmetic and copies ran while one was open for 27% of the time, Pallas kernels for 0%

profile of v9, /device:TPU:1, one launch (start us, length us, event | category | flops | bytes accessed | tf_op | source)
XLA Modules:
  0.0 346.8 jit_solution(16857558018302028537)
XLA Ops:
  3.0 11.5 %collective-permute-start = (bf16[1,100,512]{2,1,0:T(8,128)(2,1)S(1)}, bf16[1,100,512]{2,1,0:T(8,128)(2,1)S(1)}, u32[]{:S(2)}, u32[]{:S(2)}) collective-permute-start(bf16[1,100,512]{2,1,0:T(8,128)(2,1)S(1)} %get-tuple-element.30), channel_id=1, source_target_pairs={{0,8},{1,9},{2,10},{3,11},{4,12},{5,13},{6,14},{7,15},{16,24},{17,... | collective-permute-start | bytes 307208 | tf_op jit(solution)/shard_map/ppermute | solution.py:132
  16.1 7.5 %collective-permute-start.1 = (bf16[2,100,512]{2,1,0:T(8,128)(2,1)S(1)}, bf16[2,100,512]{2,1,0:T(8,128)(2,1)S(1)}, u32[]{:S(2)}, u32[]{:S(2)}) collective-permute-start(bf16[2,100,512]{2,1,0:T(8,128)(2,1)S(1)} %pad_maximum_fusion.8), channel_id=1, source_target_pairs={{0,4},{1,5},{2,6},{3,7},{4,8},{5,9},{6,10},{7,11},{8,12},{9,13},{1... | collective-permute-start | bytes 614408 | tf_op jit(solution)/shard_map/ppermute | solution.py:132
  23.6 3.0 collective-permute-done.1
  26.7 7.5 %collective-permute-start.2 = (bf16[4,100,512]{2,1,0:T(8,128)(2,1)S(1)}, bf16[4,100,512]{2,1,0:T(8,128)(2,1)S(1)}, u32[]{:S(2)}, u32[]{:S(2)}) collective-permute-start(bf16[4,100,512]{2,1,0:T(8,128)(2,1)S(1)} %pad_maximum_fusion.5), channel_id=1, source_target_pairs={{0,2},{1,3},{2,4},{3,5},{4,6},{5,7},{6,8},{7,9},{8,10},{9,11},{10,... | collective-permute-start | bytes 1228808 | tf_op jit(solution)/shard_map/ppermute | solution.py:132
  34.2 13.2 %collective-permute-done.2 = bf16[4,100,512]{2,1,0:T(8,128)(2,1)S(1)} collective-permute-done((bf16[4,100,512]{2,1,0:T(8,128)(2,1)S(1)}, bf16[4,100,512]{2,1,0:T(8,128)(2,1)S(1)}, u32[]{:S(2)}, u32[]{:S(2)}) %collective-permute-start.2) | collective-permute-done | bytes 409632 | tf_op jit(solution)/shard_map/ppermute | solution.py:132
  47.7 13.0 %collective-permute-start.3 = (bf16[8,100,512]{2,0,1:T(8,128)(2,1)S(1)}, bf16[8,100,512]{2,0,1:T(8,128)(2,1)}, u32[]{:S(2)}, u32[]{:S(2)}) collective-permute-start(bf16[8,100,512]{2,0,1:T(8,128)(2,1)S(1)} %copy.43), channel_id=1, source_target_pairs={{0,1},{1,2},{2,3},{3,4},{4,5},{5,6},{6,7},{7,8},{8,9},{9,10},{10,1... | collective-permute-start | bytes 2457608 | tf_op jit(solution)/shard_map/ppermute | solution.py:132
  64.0 2.4 squeeze.36
  70.7 8.1 %collective-permute-done.3 = bf16[8,100,512]{2,0,1:T(8,128)(2,1)} collective-permute-done((bf16[8,100,512]{2,0,1:T(8,128)(2,1)S(1)}, bf16[8,100,512]{2,0,1:T(8,128)(2,1)}, u32[]{:S(2)}, u32[]{:S(2)}) %collective-permute-start.3) | collective-permute-done | bytes 819232 | tf_op jit(solution)/shard_map/ppermute | solution.py:132
  78.8 2.3 copy_dynamic-update-slice_fusion
  81.1 2.1 gather_fusion.1
  85.9 2.9 fusion.7
  93.2 58.6 %fusion = f32[56,512]{1,0:T(8,128)S(1)} fusion(f32[800,512]{1,0:T(8,128)S(1)} %slice.84), kind=kCustom, calls=%all-reduce-scatter | all-reduce-scatter fusion | flops 458753 | bytes 1755136
  153.1 2.6 copy.51
  155.7 2.6 concatenate.67
  158.3 2.3 copy.53
  167.0 10.4 %collective-permute-start.4 = (f32[16,2304]{1,0:T(8,128)S(1)}, f32[16,2304]{1,0:T(8,128)S(1)}, u32[]{:S(2)}, u32[]{:S(2)}) collective-permute-start(f32[16,2304]{1,0:T(8,128)S(1)} %fusion.27), channel_id=1, source_target_pairs={{0,16},{16,0},{32,48},{48,32},{64,80},{80,64},{96,112},{112,96},{1... | collective-permute-start | bytes 442376 | tf_op jit(solution)/shard_map/ppermute | solution.py:84
  177.5 4.5 %fusion.2 = (f32[4,4,128]{2,1,0:T(4,128)S(1)}, f32[4,928,128,4]{2,1,3,0:T(8,128)S(1)}) fusion(f32[4,4,128]{2,1,0:T(4,128)S(1)} %get-tuple-element.41, f32[4,928,128,4]{2,1,3,0:T(8,128)} %copy-done.1, pred[128,928]{0,1:T(8,128)(4,1)S(1)} %pad_add_fusion, bf16[128,4,4,128]{3,2,1,0:T(4,128)(2,1)S(1)} %copy-done.18, pred[128]{0:T(512)(128)(4,1)S(1)} %iota_compare_fusion.1, ...), kind=kOutput, calls=%fused_computation.4 | convolution fusion | flops 498202624 | bytes 16814208 | tf_op jit(solution)/shard_map/tkgd,mkd->kgtm/dot_general | solution.py:159
  182.0 8.3 %collective-permute-start.5 = (f32[16,1152]{1,0:T(8,128)S(1)}, f32[16,1152]{1,0:T(8,128)S(1)}, u32[]{:S(2)}, u32[]{:S(2)}) collective-permute-start(f32[16,1152]{1,0:T(8,128)S(1)} %constant_dynamic-slice_fusion.1), channel_id=1, source_target_pairs={{0,32},{16,48},{32,0},{48,16},{64,96},{80,112},{96,64},{112,80},{1... | collective-permute-start | bytes 221192 | tf_op jit(solution)/shard_map/ppermute | solution.py:84
  190.4 2.1 fusion.4
  192.9 7.5 %collective-permute-start.6 = (f32[16,1152]{1,0:T(8,128)S(1)}, f32[16,1152]{1,0:T(8,128)S(1)}, u32[]{:S(2)}, u32[]{:S(2)}) collective-permute-start(f32[16,1152]{1,0:T(8,128)S(1)} %dynamic-slice_add_fusion.2), channel_id=1, source_target_pairs={{0,64},{16,80},{32,96},{48,112},{64,0},{80,16},{96,32},{112,48},{1... | collective-permute-start | bytes 221192 | tf_op jit(solution)/shard_map/ppermute | solution.py:87
  201.5 3.1 collective-permute-done.6
  209.7 4.7 %collective-permute-start.8 = (f32[16,1152]{1,0:T(8,128)S(1)}, f32[16,1152]{1,0:T(8,128)S(1)}, u32[]{:S(2)}, u32[]{:S(2)}) collective-permute-start(f32[16,1152]{1,0:T(8,128)S(1)} %add.131), channel_id=1, source_target_pairs={{0,256},{16,272},{32,288},{48,304},{64,320},{80,336},{96,352},{112... | collective-permute-start | bytes 221192 | tf_op jit(solution)/shard_map/ppermute | solution.py:87
  216.3 6.3 %collective-permute-start.9 = (f32[16,1152]{1,0:T(8,128)S(1)}, f32[16,1152]{1,0:T(8,128)}, u32[]{:S(2)}, u32[]{:S(2)}) collective-permute-start(f32[16,1152]{1,0:T(8,128)S(1)} %add.132), channel_id=1, source_target_pairs={{0,1},{1,0},{2,3},{3,2},{4,5},{5,4},{6,7},{7,6},{8,9},{9,8},{10,11... | collective-permute-start | bytes 221192 | tf_op jit(solution)/shard_map/ppermute | solution.py:64
  222.8 2.0 copy.57
  225.7 7.2 %collective-permute-start.10 = (f32[16,1152]{1,0:T(8,128)S(1)}, f32[16,1152]{1,0:T(8,128)S(1)}, u32[]{:S(2)}, u32[]{:S(2)}) collective-permute-start(f32[16,1152]{1,0:T(8,128)S(1)} %add.133), channel_id=1, source_target_pairs={{0,2},{1,3},{2,0},{3,1},{4,6},{5,7},{6,4},{7,5},{8,10},{9,11},{10,... | collective-permute-start | bytes 221192 | tf_op jit(solution)/shard_map/ppermute | solution.py:64
  234.7 13.7 %collective-permute-start.11 = (f32[16,1152]{1,0:T(8,128)S(1)}, f32[16,1152]{1,0:T(8,128)S(1)}, u32[]{:S(2)}, u32[]{:S(2)}) collective-permute-start(f32[16,1152]{1,0:T(8,128)S(1)} %add.134), channel_id=1, source_target_pairs={{0,4},{1,5},{2,6},{3,7},{4,0},{5,1},{6,2},{7,3},{8,12},{9,13},{10,... | collective-permute-start | bytes 221192 | tf_op jit(solution)/shard_map/ppermute | solution.py:64
  248.5 60.0 %fusion.1 = f32[56,512]{1,0:T(8,128)S(1)} fusion(f32[800,512]{1,0:T(8,128)S(1)} %pad_maximum_fusion.1), kind=kCustom, calls=%all-reduce-scatter.1 | all-reduce-scatter fusion | flops 458753 | bytes 1755136
  311.1 2.3 collective-permute-start.12
  314.5 7.9 %collective-permute-done.12 = f32[16,1152]{1,0:T(8,128)S(1)} collective-permute-done((f32[16,1152]{1,0:T(8,128)S(1)}, f32[16,1152]{1,0:T(8,128)S(1)}, u32[]{:S(2)}, u32[]{:S(2)}) %collective-permute-start.12) | collective-permute-done | bytes 73760 | tf_op jit(solution)/shard_map/ppermute | solution.py:64
  322.4 2.4 collective-permute-start.13
  325.6 1.9 collective-permute-done.13
  327.5 16.9 %collective-permute-start.14 = (f32[16,2304]{1,0:T(8,128)S(1)}, f32[16,2304]{1,0:T(8,128)S(1)}, u32[]{:S(2)}, u32[]{:S(2)}) collective-permute-start(f32[16,2304]{1,0:T(8,128)S(1)} %maximum_select_fusion.1), channel_id=1, source_target_pairs={{0,16},{16,0},{32,48},{48,32},{64,80},{80,64},{96,112},{112,96},{1... | collective-permute-start | bytes 442376 | tf_op jit(solution)/shard_map/ppermute | solution.py:92
  (138 shorter events, 43.2 us)
Async XLA Ops:
  0.6 164.4 %copy-start = (bf16[1,1,128,4096]{3,2,1,0:T(8,128)(2,1)S(1)}, bf16[1,1,128,4096]{3,2,1,0:T(8,128)(2,1)}, u32[]{:S(2)}) copy-start(bf16[1,1,128,4096]{3,2,1,0:T(8,128)(2,1)} %param.13) | copy-start | bytes 3145732
  3.0 13.2 %collective-permute-start = (bf16[1,100,512]{2,1,0:T(8,128)(2,1)S(1)}, bf16[1,100,512]{2,1,0:T(8,128)(2,1)S(1)}, u32[]{:S(2)}, u32[]{:S(2)}) collective-permute-start(bf16[1,100,512]{2,1,0:T(8,128)(2,1)S(1)} %get-tuple-element.30), channel_id=1, source_target_pairs={{0,8},{1,9},{2,10},{3,11},{4,12},{5,13},{6,14},{7,15},{16,24},{17,... | collective-permute-start | bytes 307208 | tf_op jit(solution)/shard_map/ppermute | solution.py:132
  16.1 10.5 %collective-permute-start.1 = (bf16[2,100,512]{2,1,0:T(8,128)(2,1)S(1)}, bf16[2,100,512]{2,1,0:T(8,128)(2,1)S(1)}, u32[]{:S(2)}, u32[]{:S(2)}) collective-permute-start(bf16[2,100,512]{2,1,0:T(8,128)(2,1)S(1)} %pad_maximum_fusion.8), channel_id=1, source_target_pairs={{0,4},{1,5},{2,6},{3,7},{4,8},{5,9},{6,10},{7,11},{8,12},{9,13},{1... | collective-permute-start | bytes 614408 | tf_op jit(solution)/shard_map/ppermute | solution.py:132
  26.7 34.1 %copy-start.19 = (bf16[1,1,128,512]{3,2,1,0:T(8,128)(2,1)S(1)}, bf16[1,1,128,512]{3,2,1,0:T(8,128)(2,1)}, u32[]{:S(2)}) copy-start(bf16[1,1,128,512]{3,2,1,0:T(8,128)(2,1)} %param.10) | copy-start | bytes 393220
  26.7 34.2 %copy-start.20 = (bf16[1,1,128,512]{3,2,1,0:T(8,128)(2,1)S(1)}, bf16[1,1,128,512]{3,2,1,0:T(8,128)(2,1)}, u32[]{:S(2)}) copy-start(bf16[1,1,128,512]{3,2,1,0:T(8,128)(2,1)} %param.11) | copy-start | bytes 393220
  26.7 20.7 %collective-permute-start.2 = (bf16[4,100,512]{2,1,0:T(8,128)(2,1)S(1)}, bf16[4,100,512]{2,1,0:T(8,128)(2,1)S(1)}, u32[]{:S(2)}, u32[]{:S(2)}) collective-permute-start(bf16[4,100,512]{2,1,0:T(8,128)(2,1)S(1)} %pad_maximum_fusion.5), channel_id=1, source_target_pairs={{0,2},{1,3},{2,4},{3,5},{4,6},{5,7},{6,8},{7,9},{8,10},{9,11},{10,... | collective-permute-start | bytes 1228808 | tf_op jit(solution)/shard_map/ppermute | solution.py:132
  47.7 31.0 %collective-permute-start.3 = (bf16[8,100,512]{2,0,1:T(8,128)(2,1)S(1)}, bf16[8,100,512]{2,0,1:T(8,128)(2,1)}, u32[]{:S(2)}, u32[]{:S(2)}) collective-permute-start(bf16[8,100,512]{2,0,1:T(8,128)(2,1)S(1)} %copy.43), channel_id=1, source_target_pairs={{0,1},{1,2},{2,3},{3,4},{4,5},{5,6},{6,7},{7,8},{8,9},{9,10},{10,1... | collective-permute-start | bytes 2457608 | tf_op jit(solution)/shard_map/ppermute | solution.py:132
  64.0 21.9 %copy-start.11 = (bf16[128,4,4,128]{3,2,1,0:T(4,128)(2,1)}, bf16[128,4,4,128]{3,2,1,0:T(4,128)(2,1)S(1)}, u32[]{:S(2)}) copy-start(bf16[128,4,4,128]{3,2,1,0:T(4,128)(2,1)S(1)} %reshape_squeeze.2) | copy-start | bytes 1572868
  151.8 12.2 %collective-permute-start.15 = (f32[56,512]{1,0:T(8,128)S(1)}, f32[56,512]{1,0:T(8,128)S(1)}, u32[]{:S(2)}, u32[]{:S(2)}) collective-permute-start(f32[56,512]{1,0:T(8,128)S(1)} %fusion), channel_id=1, source_target_pairs={{0,1},{1,2},{2,3},{3,4},{4,5},{5,6},{6,7},{7,8},{8,9},{9,10},{10,1... | collective-permute-start | bytes 344072
  160.5 3.4 collective-permute-start.16
  164.3 13.1 %copy-start.16 = (bf16[800,4,128]{2,0,1:T(8,128)(2,1)S(1)}, bf16[800,4,128]{2,0,1:T(8,128)(2,1)}, u32[]{:S(2)}) copy-start(bf16[800,4,128]{2,0,1:T(8,128)(2,1)} %copy.53) | copy-start | bytes 2457604
  164.3 13.1 %copy-start.18 = (bf16[128,4,4,128]{3,2,1,0:T(4,128)(2,1)S(1)}, bf16[128,4,4,128]{3,2,1,0:T(4,128)(2,1)}, u32[]{:S(2)}) copy-start(bf16[128,4,4,128]{3,2,1,0:T(4,128)(2,1)} %squeeze.36) | copy-start | bytes 1572868
  167.0 23.4 %slice-start = ((s8[7602176]{0:T(1024)(128)(4,1)}), s8[4194304]{0:T(1024)(128)(4,1)S(1)}, s32[]{:S(2)}) async-start(s8[7602176]{0:T(1024)(128)(4,1)} %bitcast.120), calls=%async_computation | async-start | bytes 8388608
  167.0 23.3 %slice-start.1 = ((s8[7602176]{0:T(1024)(128)(4,1)}), s8[3407872]{0:T(1024)(128)(4,1)S(1)}, s32[]{:S(2)}) async-start(s8[7602176]{0:T(1024)(128)(4,1)} %bitcast.120), calls=%async_computation.1 | async-start | bytes 6815744
  167.0 14.9 %collective-permute-start.4 = (f32[16,2304]{1,0:T(8,128)S(1)}, f32[16,2304]{1,0:T(8,128)S(1)}, u32[]{:S(2)}, u32[]{:S(2)}) collective-permute-start(f32[16,2304]{1,0:T(8,128)S(1)} %fusion.27), channel_id=1, source_target_pairs={{0,16},{16,0},{32,48},{48,32},{64,80},{80,64},{96,112},{112,96},{1... | collective-permute-start | bytes 442376 | tf_op jit(solution)/shard_map/ppermute | solution.py:84
  182.0 10.8 %collective-permute-start.5 = (f32[16,1152]{1,0:T(8,128)S(1)}, f32[16,1152]{1,0:T(8,128)S(1)}, u32[]{:S(2)}, u32[]{:S(2)}) collective-permute-start(f32[16,1152]{1,0:T(8,128)S(1)} %constant_dynamic-slice_fusion.1), channel_id=1, source_target_pairs={{0,32},{16,48},{32,0},{48,16},{64,96},{80,112},{96,64},{112,80},{1... | collective-permute-start | bytes 221192 | tf_op jit(solution)/shard_map/ppermute | solution.py:84
  190.4 10.0 %copy-start.12 = (bf16[128,4,4,128]{3,2,1,0:T(4,128)(2,1)S(1)}, bf16[128,4,4,128]{3,2,1,0:T(4,128)(2,1)}, u32[]{:S(2)}) copy-start(bf16[128,4,4,128]{3,2,1,0:T(4,128)(2,1)} %copy-done.11) | copy-start | bytes 1572868
  192.8 13.7 %copy-start.15 = (bf16[800,4,128]{2,0,1:T(8,128)(2,1)S(1)}, bf16[800,4,128]{2,0,1:T(8,128)(2,1)}, u32[]{:S(2)}) copy-start(bf16[800,4,128]{2,0,1:T(8,128)(2,1)} %copy-done.14) | copy-start | bytes 2457604
  192.9 13.7 %copy-start.21 = (bf16[128,4,128]{2,0,1:T(8,128)(2,1)S(1)}, bf16[128,4,128]{2,0,1:T(8,128)(2,1)}, u32[]{:S(2)}) copy-start(bf16[128,4,128]{2,0,1:T(8,128)(2,1)} %copy.49) | copy-start | bytes 393220
  192.9 11.7 %collective-permute-start.6 = (f32[16,1152]{1,0:T(8,128)S(1)}, f32[16,1152]{1,0:T(8,128)S(1)}, u32[]{:S(2)}, u32[]{:S(2)}) collective-permute-start(f32[16,1152]{1,0:T(8,128)S(1)} %dynamic-slice_add_fusion.2), channel_id=1, source_target_pairs={{0,64},{16,80},{32,96},{48,112},{64,0},{80,16},{96,32},{112,48},{1... | collective-permute-start | bytes 221192 | tf_op jit(solution)/shard_map/ppermute | solution.py:87
  204.6 5.1 %collective-permute-start.7 = (f32[16,1152]{1,0:T(8,128)S(1)}, f32[16,1152]{1,0:T(8,128)S(1)}, u32[]{:S(2)}, u32[]{:S(2)}) collective-permute-start(f32[16,1152]{1,0:T(8,128)S(1)} %add.130), channel_id=1, source_target_pairs={{0,128},{16,144},{32,160},{48,176},{64,192},{80,208},{96,224},{112... | collective-permute-start | bytes 221192 | tf_op jit(solution)/shard_map/ppermute | solution.py:87
  209.7 6.6 %collective-permute-start.8 = (f32[16,1152]{1,0:T(8,128)S(1)}, f32[16,1152]{1,0:T(8,128)S(1)}, u32[]{:S(2)}, u32[]{:S(2)}) collective-permute-start(f32[16,1152]{1,0:T(8,128)S(1)} %add.131), channel_id=1, source_target_pairs={{0,256},{16,272},{32,288},{48,304},{64,320},{80,336},{96,352},{112... | collective-permute-start | bytes 221192 | tf_op jit(solution)/shard_map/ppermute | solution.py:87
  214.6 8.2 %copy-start.3 = (f32[928,128]{1,0:T(8,128)}, f32[928,128]{1,0:T(8,128)S(1)}, u32[]{:S(2)}) copy-start(f32[928,128]{1,0:T(8,128)S(1)} %get-tuple-element.37) | copy-start | bytes 1425412
  216.3 8.5 %collective-permute-start.9 = (f32[16,1152]{1,0:T(8,128)S(1)}, f32[16,1152]{1,0:T(8,128)}, u32[]{:S(2)}, u32[]{:S(2)}) collective-permute-start(f32[16,1152]{1,0:T(8,128)S(1)} %add.132), channel_id=1, source_target_pairs={{0,1},{1,0},{2,3},{3,2},{4,5},{5,4},{6,7},{7,6},{8,9},{9,8},{10,11... | collective-permute-start | bytes 221192 | tf_op jit(solution)/shard_map/ppermute | solution.py:64
  225.7 9.0 %collective-permute-start.10 = (f32[16,1152]{1,0:T(8,128)S(1)}, f32[16,1152]{1,0:T(8,128)S(1)}, u32[]{:S(2)}, u32[]{:S(2)}) collective-permute-start(f32[16,1152]{1,0:T(8,128)S(1)} %add.133), channel_id=1, source_target_pairs={{0,2},{1,3},{2,0},{3,1},{4,6},{5,7},{6,4},{7,5},{8,10},{9,11},{10,... | collective-permute-start | bytes 221192 | tf_op jit(solution)/shard_map/ppermute | solution.py:64
  234.6 90.2 %copy-start.13 = (f32[128,512]{1,0:T(8,128)S(1)}, f32[128,512]{1,0:T(8,128)}, u32[]{:S(2)}) copy-start(f32[128,512]{1,0:T(8,128)} %pad_maximum_fusion.7) | copy-start | bytes 786436
  234.7 76.4 %collective-permute-start.11 = (f32[16,1152]{1,0:T(8,128)S(1)}, f32[16,1152]{1,0:T(8,128)S(1)}, u32[]{:S(2)}, u32[]{:S(2)}) collective-permute-start(f32[16,1152]{1,0:T(8,128)S(1)} %add.134), channel_id=1, source_target_pairs={{0,4},{1,5},{2,6},{3,7},{4,0},{5,1},{6,2},{7,3},{8,12},{9,13},{10,... | collective-permute-start | bytes 221192 | tf_op jit(solution)/shard_map/ppermute | solution.py:64
  308.5 5.6 %collective-permute-start.17 = (f32[56,512]{1,0:T(8,128)S(1)}, f32[56,512]{1,0:T(8,128)S(1)}, u32[]{:S(2)}, u32[]{:S(2)}) collective-permute-start(f32[56,512]{1,0:T(8,128)S(1)} %fusion.1), channel_id=1, source_target_pairs={{0,1},{1,2},{2,3},{3,4},{4,5},{5,6},{6,7},{7,8},{8,9},{9,10},{10,1... | collective-permute-start | bytes 344072
  309.8 4.3 %collective-permute-start.18 = (f32[34,512]{1,0:T(8,128)S(1)}, f32[34,512]{1,0:T(8,128)S(1)}, u32[]{:S(2)}, u32[]{:S(2)}) collective-permute-start(f32[34,512]{1,0:T(8,128)S(1)} %slice.88), channel_id=1, source_target_pairs={{0,2},{1,3},{2,4},{3,5},{4,6},{5,7},{6,8},{7,9},{8,10},{9,11},{10,... | collective-permute-start | bytes 208904
  311.1 11.3 %collective-permute-start.12 = (f32[16,1152]{1,0:T(8,128)S(1)}, f32[16,1152]{1,0:T(8,128)S(1)}, u32[]{:S(2)}, u32[]{:S(2)}) collective-permute-start(f32[16,1152]{1,0:T(8,128)S(1)} %add.135), channel_id=1, source_target_pairs={{0,8},{1,9},{2,10},{3,11},{4,12},{5,13},{6,14},{7,15},{8,0},{9,1},... | collective-permute-start | bytes 221192 | tf_op jit(solution)/shard_map/ppermute | solution.py:64
  322.4 5.1 %collective-permute-start.13 = (f32[16,1152]{1,0:T(8,128)S(1)}, f32[16,1152]{1,0:T(8,128)S(1)}, u32[]{:S(2)}, u32[]{:S(2)}) collective-permute-start(f32[16,1152]{1,0:T(8,128)S(1)} %add.136), channel_id=1, source_target_pairs={{0,32},{16,48},{32,0},{48,16},{64,96},{80,112},{96,64},{112,80},{1... | collective-permute-start | bytes 221192 | tf_op jit(solution)/shard_map/ppermute | solution.py:92
  327.5 17.9 %collective-permute-start.14 = (f32[16,2304]{1,0:T(8,128)S(1)}, f32[16,2304]{1,0:T(8,128)S(1)}, u32[]{:S(2)}, u32[]{:S(2)}) collective-permute-start(f32[16,2304]{1,0:T(8,128)S(1)} %maximum_select_fusion.1), channel_id=1, source_target_pairs={{0,16},{16,0},{32,48},{48,32},{64,80},{80,64},{96,112},{112,96},{1... | collective-permute-start | bytes 442376 | tf_op jit(solution)/shard_map/ppermute | solution.py:92
  (12 other events, 50.3 us)

commit v10 on v8

--- a/solution.py
+++ b/solution.py
@@ -71,25 +71,27 @@
 
 
 def mesh_sum(x):
-    n = lax.axis_size("dp")
-    halving = [k for k in (1, 2) if k < n and not n & (n - 1)]
-    if x.shape[-1] % (2 ** len(halving)):
-        halving = []
+    rounds = []
+    for axis in ("dp", "ctx"):
+        n = lax.axis_size(axis)
+        if n & (n - 1):
+            return lax.psum(x, ("dp", "ctx"))
+        rounds += [(axis, 1 << j) for j in range(n.bit_length() - 1)]
+    nearest = [r for r in (("dp", 1), ("dp", 2), ("ctx", 1)) if r in rounds]
+    halving = [r for r in nearest if x.shape[-1] % (2 ** len(nearest)) == 0]
     cur = x
-    for k in halving:
+    for axis, k in halving:
         h = cur.shape[-1] // 2
-        bit = (lax.axis_index("dp") // k) % 2
+        bit = (lax.axis_index(axis) // k) % 2
         keep = lax.dynamic_slice_in_dim(cur, bit * h, h, cur.ndim - 1)
         give = lax.dynamic_slice_in_dim(cur, (1 - bit) * h, h, cur.ndim - 1)
-        cur = keep + lax.ppermute(give, "dp", exchange_pairs("dp", k))
-    k = 2 ** len(halving)
-    while k < n:
-        cur = cur + lax.ppermute(cur, "dp", exchange_pairs("dp", k))
-        k *= 2
-    cur = butterfly_sum(cur, "ctx")
-    for k in reversed(halving):
-        bit = (lax.axis_index("dp") // k) % 2
-        other = lax.ppermute(cur, "dp", exchange_pairs("dp", k))
+        cur = keep + lax.ppermute(give, axis, exchange_pairs(axis, k))
+    for axis, k in rounds:
+        if (axis, k) not in halving:
+            cur = cur + lax.ppermute(cur, axis, exchange_pairs(axis, k))
+    for axis, k in reversed(halving):
+        bit = (lax.axis_index(axis) // k) % 2
+        other = lax.ppermute(cur, axis, exchange_pairs(axis, k))
         cur = jnp.where(
             bit == 0, jnp.concatenate([cur, other], -1), jnp.concatenate([other, cur], -1)
         )

time: 317 us -> 313 us (0.987); the launches traced: 312 us -> 312 us
  starting transfers between devices: 120 us -> 128 us
  local copies, waits for them, and re-layouts: 30.5 us -> 26.5 us
    ppermute x11 -> x12, starting transfers between devices: 73.2 us -> 81.2 us  [the longest x6 51.8 us: mesh_sum(): cur = cur + lax.ppermute(cur, axis, exchange_pairs(axis, k))]
    unnamed x49 -> x53, local copies, waits for them, and re-layouts: 11.7 us -> 7.59 us
    ppermute x11 -> x12, waiting for transfers between devices: 20.2 us -> 18.2 us  [the longest x3 8.59 us: mesh_sum(): cur = keep + lax.ppermute(give, axis, exchange_pairs(axis, k))]
  transfers between devices with their start and end apart: 19 -> 20, of which waited for: 14 -> 15; matrix products, arithmetic and copies ran while one was open for 8% -> 6% of each run, Pallas kernels for 0% -> 0%
where the time goes in v10:
time: 313 us; the launch traced here: 312 us
  starting transfers between devices  128 us (41%)
  blocking collectives  87.6 us (28%)
  waiting for transfers between devices  44.3 us (14%)
  local copies, waits for them, and re-layouts  26.5 us (8%)
  matrix products  12.7 us (4%)
  other arithmetic  9.15 us (3%)
    unnamed x1, blocking collectives  87.6 us
    ppermute x6, starting transfers between devices, mesh_sum(): cur = cur + lax.ppermute(cur, axis, exchange_pairs(axis, k))  51.8 us
    ppermute x4, starting transfers between devices, per_device(): lax.ppermute(held, 'ctx', [(i, i + hop) for i in range(segment_list - hop)])  39.4 us
    ppermute x4, waiting for transfers between devices, per_device(): lax.ppermute(held, 'ctx', [(i, i + hop) for i in range(segment_list - hop)])  24.8 us
    ppermute x3, starting transfers between devices, mesh_sum(): other = lax.ppermute(cur, axis, exchange_pairs(axis, k))  17.9 us
    ppermute x3, starting transfers between devices, mesh_sum(): cur = keep + lax.ppermute(give, axis, exchange_pairs(axis, k))  11.4 us
    ppermute x3, waiting for transfers between devices, mesh_sum(): cur = keep + lax.ppermute(give, axis, exchange_pairs(axis, k))  8.59 us
    unnamed x4, starting transfers between devices  7.89 us
  transfers between devices with their start and end apart: 20, of which 15 were waited for; matrix products, arithmetic and copies ran while one was open for 6% of the time, Pallas kernels for 0%

profile of v10, /device:TPU:1, one launch (start us, length us, event | category | flops | bytes accessed | tf_op | source)
XLA Modules:
  0.0 311.6 jit_solution(2505779481090487244)
XLA Ops:
  2.9 11.5 %collective-permute-start = (bf16[1,100,512]{2,1,0:T(8,128)(2,1)S(1)}, bf16[1,100,512]{2,1,0:T(8,128)(2,1)S(1)}, u32[]{:S(2)}, u32[]{:S(2)}) collective-permute-start(bf16[1,100,512]{2,1,0:T(8,128)(2,1)S(1)} %get-tuple-element.30), channel_id=1, source_target_pairs={{0,8},{1,9},{2,10},{3,11},{4,12},{5,13},{6,14},{7,15},{16,24},{17,... | collective-permute-start | bytes 307208 | tf_op jit(solution)/shard_map/ppermute | solution.py:134
  16.1 7.5 %collective-permute-start.1 = (bf16[2,100,512]{2,1,0:T(8,128)(2,1)S(1)}, bf16[2,100,512]{2,1,0:T(8,128)(2,1)S(1)}, u32[]{:S(2)}, u32[]{:S(2)}) collective-permute-start(bf16[2,100,512]{2,1,0:T(8,128)(2,1)S(1)} %pad_maximum_fusion.10), channel_id=1, source_target_pairs={{0,4},{1,5},{2,6},{3,7},{4,8},{5,9},{6,10},{7,11},{8,12},{9,13},{1... | collective-permute-start | bytes 614408 | tf_op jit(solution)/shard_map/ppermute | solution.py:134
  23.6 3.0 collective-permute-done.1
  26.7 7.5 %collective-permute-start.2 = (bf16[4,100,512]{2,1,0:T(8,128)(2,1)S(1)}, bf16[4,100,512]{2,1,0:T(8,128)(2,1)S(1)}, u32[]{:S(2)}, u32[]{:S(2)}) collective-permute-start(bf16[4,100,512]{2,1,0:T(8,128)(2,1)S(1)} %pad_maximum_fusion.7), channel_id=1, source_target_pairs={{0,2},{1,3},{2,4},{3,5},{4,6},{5,7},{6,8},{7,9},{8,10},{9,11},{10,... | collective-permute-start | bytes 1228808 | tf_op jit(solution)/shard_map/ppermute | solution.py:134
  34.2 13.2 %collective-permute-done.2 = bf16[4,100,512]{2,1,0:T(8,128)(2,1)S(1)} collective-permute-done((bf16[4,100,512]{2,1,0:T(8,128)(2,1)S(1)}, bf16[4,100,512]{2,1,0:T(8,128)(2,1)S(1)}, u32[]{:S(2)}, u32[]{:S(2)}) %collective-permute-start.2) | collective-permute-done | bytes 409632 | tf_op jit(solution)/shard_map/ppermute | solution.py:134
  47.7 13.0 %collective-permute-start.3 = (bf16[8,100,512]{2,0,1:T(8,128)(2,1)S(1)}, bf16[8,100,512]{2,0,1:T(8,128)(2,1)}, u32[]{:S(2)}, u32[]{:S(2)}) collective-permute-start(bf16[8,100,512]{2,0,1:T(8,128)(2,1)S(1)} %copy.43), channel_id=1, source_target_pairs={{0,1},{1,2},{2,3},{3,4},{4,5},{5,6},{6,7},{7,8},{8,9},{9,10},{10,1... | collective-permute-start | bytes 2457608 | tf_op jit(solution)/shard_map/ppermute | solution.py:134
  63.2 2.2 squeeze.36
  70.5 8.3 %collective-permute-done.3 = bf16[8,100,512]{2,0,1:T(8,128)(2,1)} collective-permute-done((bf16[8,100,512]{2,0,1:T(8,128)(2,1)S(1)}, bf16[8,100,512]{2,0,1:T(8,128)(2,1)}, u32[]{:S(2)}, u32[]{:S(2)}) %collective-permute-start.3) | collective-permute-done | bytes 819232 | tf_op jit(solution)/shard_map/ppermute | solution.py:134
  78.8 2.3 copy_dynamic-update-slice_fusion
  81.1 2.1 gather_fusion.1
  85.8 2.2 copy.48
  88.8 3.1 fusion.7
  93.7 2.2 fusion.2
  95.8 2.3 fusion.4
  103.2 87.6 %fusion.47 = (f32[56,512]{1,0:T(8,128)S(1)}, f32[56,512]{1,0:T(8,128)S(1)}) fusion(f32[800,512]{1,0:T(8,128)S(1)} %pad_maximum_fusion.3, f32[800,512]{1,0:T(8,128)} %pad_maximum_fusion), kind=kCustom, calls=%all-reduce-scatter.2 | all-reduce-scatter fusion | flops 917505 | bytes 3508224
  197.8 7.6 %collective-permute-start.4 = (f32[16,2304]{1,0:T(8,128)S(1)}, f32[16,2304]{1,0:T(8,128)S(1)}, u32[]{:S(2)}, u32[]{:S(2)}) collective-permute-start(f32[16,2304]{1,0:T(8,128)S(1)} %fusion.27), channel_id=1, source_target_pairs={{0,16},{16,0},{32,48},{48,32},{64,80},{80,64},{96,112},{112,96},{1... | collective-permute-start | bytes 442376 | tf_op jit(solution)/shard_map/ppermute | solution.py:88
  208.4 4.8 %collective-permute-done.5 = f32[16,1152]{1,0:T(8,128)S(1)} collective-permute-done((f32[16,1152]{1,0:T(8,128)S(1)}, f32[16,1152]{1,0:T(8,128)S(1)}, u32[]{:S(2)}, u32[]{:S(2)}) %collective-permute-start.5) | collective-permute-done | bytes 73760 | tf_op jit(solution)/shard_map/ppermute | solution.py:88
  215.2 2.8 collective-permute-done.6
  218.1 5.0 %collective-permute-start.7 = (f32[16,576]{1,0:T(8,128)S(1)}, f32[16,576]{1,0:T(8,128)S(1)}, u32[]{:S(2)}, u32[]{:S(2)}) collective-permute-start(f32[16,576]{1,0:T(8,128)S(1)} %dynamic-slice_add_fusion.3), channel_id=1, source_target_pairs={{0,64},{16,80},{32,96},{48,112},{64,0},{80,16},{96,32},{112,48},{1... | collective-permute-start | bytes 110600 | tf_op jit(solution)/shard_map/ppermute | solution.py:91
  224.6 4.9 %collective-permute-start.8 = (f32[16,576]{1,0:T(8,128)S(1)}, f32[16,576]{1,0:T(8,128)S(1)}, u32[]{:S(2)}, u32[]{:S(2)}) collective-permute-start(f32[16,576]{1,0:T(8,128)S(1)} %add.145), channel_id=1, source_target_pairs={{0,128},{16,144},{32,160},{48,176},{64,192},{80,208},{96,224},{112... | collective-permute-start | bytes 110600 | tf_op jit(solution)/shard_map/ppermute | solution.py:91
  230.9 3.9 %collective-permute-start.9 = (f32[16,576]{1,0:T(8,128)S(1)}, f32[16,576]{1,0:T(8,128)S(1)}, u32[]{:S(2)}, u32[]{:S(2)}) collective-permute-start(f32[16,576]{1,0:T(8,128)S(1)} %add.146), channel_id=1, source_target_pairs={{0,256},{16,272},{32,288},{48,304},{64,320},{80,336},{96,352},{112... | collective-permute-start | bytes 110600 | tf_op jit(solution)/shard_map/ppermute | solution.py:91
  234.8 2.3 collective-permute-done.9
  237.1 9.6 %collective-permute-start.10 = (f32[16,576]{1,0:T(8,128)S(1)}, f32[16,576]{1,0:T(8,128)S(1)}, u32[]{:S(2)}, u32[]{:S(2)}) collective-permute-start(f32[16,576]{1,0:T(8,128)S(1)} %add.147), channel_id=1, source_target_pairs={{0,2},{1,3},{2,0},{3,1},{4,6},{5,7},{6,4},{7,5},{8,10},{9,11},{10,... | collective-permute-start | bytes 110600 | tf_op jit(solution)/shard_map/ppermute | solution.py:91
  248.2 19.5 %collective-permute-start.11 = (f32[16,576]{1,0:T(8,128)S(1)}, f32[16,576]{1,0:T(8,128)S(1)}, u32[]{:S(2)}, u32[]{:S(2)}) collective-permute-start(f32[16,576]{1,0:T(8,128)S(1)} %add.148), channel_id=1, source_target_pairs={{0,4},{1,5},{2,6},{3,7},{4,0},{5,1},{6,2},{7,3},{8,12},{9,13},{10,... | collective-permute-start | bytes 110600 | tf_op jit(solution)/shard_map/ppermute | solution.py:91
  267.7 3.7 %fusion.14 = bf16[4,128,4,128]{3,1,2,0:T(8,128)(2,1)} fusion(bf16[4,4,128,928]{2,3,1,0:T(8,128)(2,1)} %copy-done.1, bf16[128,4,128]{2,0,1:T(8,128)(2,1)S(1)} %copy-done.18, bf16[800,4,128]{2,0,1:T(8,128)(2,1)S(1)} %copy-done.12), kind=kOutput, calls=%fused_computation.24 | convolution fusion | flops 488964096 | bytes 5275648 | tf_op jit(solution)/shard_map/kgtm,mkd->tkgd/dot_general | solution.py:168
  271.4 8.8 %collective-permute-start.12 = (f32[16,576]{1,0:T(8,128)S(1)}, f32[16,576]{1,0:T(8,128)S(1)}, u32[]{:S(2)}, u32[]{:S(2)}) collective-permute-start(f32[16,576]{1,0:T(8,128)S(1)} %add.149), channel_id=1, source_target_pairs={{0,8},{1,9},{2,10},{3,11},{4,12},{5,13},{6,14},{7,15},{8,0},{9,1},... | collective-permute-start | bytes 110600 | tf_op jit(solution)/shard_map/ppermute | solution.py:91
  280.3 3.2 %collective-permute-start.16 = (f32[56,512]{1,0:T(8,128)S(1)}, f32[56,512]{1,0:T(8,128)S(1)}, u32[]{:S(2)}, u32[]{:S(2)}) collective-permute-start(f32[56,512]{1,0:T(8,128)S(1)} %get-tuple-element.27), channel_id=1, source_target_pairs={{0,1},{1,2},{2,3},{3,4},{4,5},{5,6},{6,7},{7,8},{8,9},{9,10},{10,1... | collective-permute-start | bytes 344072
  284.5 2.1 collective-permute-start.17
  286.6 3.5 %collective-permute-start.13 = (f32[16,576]{1,0:T(8,128)S(1)}, f32[16,576]{1,0:T(8,128)S(1)}, u32[]{:S(2)}, u32[]{:S(2)}) collective-permute-start(f32[16,576]{1,0:T(8,128)S(1)} %add.150), channel_id=1, source_target_pairs={{0,1},{1,0},{2,3},{3,2},{4,5},{5,4},{6,7},{7,6},{8,9},{9,8},{10,11... | collective-permute-start | bytes 110600 | tf_op jit(solution)/shard_map/ppermute | solution.py:94
  291.6 2.7 collective-permute-start.14
  295.0 2.5 collective-permute-done.14
  297.5 11.7 %collective-permute-start.15 = (f32[16,2304]{1,0:T(8,128)S(1)}, f32[16,2304]{1,0:T(8,128)S(1)}, u32[]{:S(2)}, u32[]{:S(2)}) collective-permute-start(f32[16,2304]{1,0:T(8,128)S(1)} %maximum_select_fusion.1), channel_id=1, source_target_pairs={{0,16},{16,0},{32,48},{48,32},{64,80},{80,64},{96,112},{112,96},{1... | collective-permute-start | bytes 442376 | tf_op jit(solution)/shard_map/ppermute | solution.py:94
  (131 shorter events, 42.2 us)
Async XLA Ops:
  0.6 196.1 %copy-start = (bf16[1,1,128,4096]{3,2,1,0:T(8,128)(2,1)S(1)}, bf16[1,1,128,4096]{3,2,1,0:T(8,128)(2,1)}, u32[]{:S(2)}) copy-start(bf16[1,1,128,4096]{3,2,1,0:T(8,128)(2,1)} %param.13) | copy-start | bytes 3145732
  2.9 13.2 %collective-permute-start = (bf16[1,100,512]{2,1,0:T(8,128)(2,1)S(1)}, bf16[1,100,512]{2,1,0:T(8,128)(2,1)S(1)}, u32[]{:S(2)}, u32[]{:S(2)}) collective-permute-start(bf16[1,100,512]{2,1,0:T(8,128)(2,1)S(1)} %get-tuple-element.30), channel_id=1, source_target_pairs={{0,8},{1,9},{2,10},{3,11},{4,12},{5,13},{6,14},{7,15},{16,24},{17,... | collective-permute-start | bytes 307208 | tf_op jit(solution)/shard_map/ppermute | solution.py:134
  16.1 10.5 %collective-permute-start.1 = (bf16[2,100,512]{2,1,0:T(8,128)(2,1)S(1)}, bf16[2,100,512]{2,1,0:T(8,128)(2,1)S(1)}, u32[]{:S(2)}, u32[]{:S(2)}) collective-permute-start(bf16[2,100,512]{2,1,0:T(8,128)(2,1)S(1)} %pad_maximum_fusion.10), channel_id=1, source_target_pairs={{0,4},{1,5},{2,6},{3,7},{4,8},{5,9},{6,10},{7,11},{8,12},{9,13},{1... | collective-permute-start | bytes 614408 | tf_op jit(solution)/shard_map/ppermute | solution.py:134
  26.6 34.1 %copy-start.15 = (bf16[1,1,128,512]{3,2,1,0:T(8,128)(2,1)S(1)}, bf16[1,1,128,512]{3,2,1,0:T(8,128)(2,1)}, u32[]{:S(2)}) copy-start(bf16[1,1,128,512]{3,2,1,0:T(8,128)(2,1)} %param.10) | copy-start | bytes 393220
  26.7 34.2 %copy-start.16 = (bf16[1,1,128,512]{3,2,1,0:T(8,128)(2,1)S(1)}, bf16[1,1,128,512]{3,2,1,0:T(8,128)(2,1)}, u32[]{:S(2)}) copy-start(bf16[1,1,128,512]{3,2,1,0:T(8,128)(2,1)} %param.11) | copy-start | bytes 393220
  26.7 20.7 %collective-permute-start.2 = (bf16[4,100,512]{2,1,0:T(8,128)(2,1)S(1)}, bf16[4,100,512]{2,1,0:T(8,128)(2,1)S(1)}, u32[]{:S(2)}, u32[]{:S(2)}) collective-permute-start(bf16[4,100,512]{2,1,0:T(8,128)(2,1)S(1)} %pad_maximum_fusion.7), channel_id=1, source_target_pairs={{0,2},{1,3},{2,4},{3,5},{4,6},{5,7},{6,8},{7,9},{8,10},{9,11},{10,... | collective-permute-start | bytes 1228808 | tf_op jit(solution)/shard_map/ppermute | solution.py:134
  47.7 31.0 %collective-permute-start.3 = (bf16[8,100,512]{2,0,1:T(8,128)(2,1)S(1)}, bf16[8,100,512]{2,0,1:T(8,128)(2,1)}, u32[]{:S(2)}, u32[]{:S(2)}) collective-permute-start(bf16[8,100,512]{2,0,1:T(8,128)(2,1)S(1)} %copy.43), channel_id=1, source_target_pairs={{0,1},{1,2},{2,3},{3,4},{4,5},{5,6},{6,7},{7,8},{8,9},{9,10},{10,1... | collective-permute-start | bytes 2457608 | tf_op jit(solution)/shard_map/ppermute | solution.py:134
  88.8 3.1 copy-start.13
  190.8 5.9 %copy-start.20 = (bf16[16,512]{1,0:T(8,128)(2,1)S(1)}, bf16[16,512]{1,0:T(8,128)(2,1)}, u32[]{:S(2)}) copy-start(bf16[16,512]{1,0:T(8,128)(2,1)} %param.15) | copy-start | bytes 49156
  190.8 4.9 %collective-permute-start.18 = (f32[56,512]{1,0:T(8,128)S(1)}, f32[56,512]{1,0:T(8,128)S(1)}, u32[]{:S(2)}, u32[]{:S(2)}) collective-permute-start(f32[56,512]{1,0:T(8,128)S(1)} %get-tuple-element.28), channel_id=1, source_target_pairs={{0,1},{1,2},{2,3},{3,4},{4,5},{5,6},{6,7},{7,8},{8,9},{9,10},{10,1... | collective-permute-start | bytes 344072
  192.2 3.5 %collective-permute-start.19 = (f32[34,512]{1,0:T(8,128)S(1)}, f32[34,512]{1,0:T(8,128)S(1)}, u32[]{:S(2)}, u32[]{:S(2)}) collective-permute-start(f32[34,512]{1,0:T(8,128)S(1)} %slice.87), channel_id=1, source_target_pairs={{0,2},{1,3},{2,4},{3,5},{4,6},{5,7},{6,8},{7,9},{8,10},{9,11},{10,... | collective-permute-start | bytes 208904
  194.4 2.7 copy-start.17
  197.2 70.6 %copy-start.12 = (bf16[800,4,128]{2,0,1:T(8,128)(2,1)S(1)}, bf16[800,4,128]{2,0,1:T(8,128)(2,1)}, u32[]{:S(2)}) copy-start(bf16[800,4,128]{2,0,1:T(8,128)(2,1)} %copy.48) | copy-start | bytes 2457604
  197.2 70.6 %copy-start.18 = (bf16[128,4,128]{2,0,1:T(8,128)(2,1)S(1)}, bf16[128,4,128]{2,0,1:T(8,128)(2,1)}, u32[]{:S(2)}) copy-start(bf16[128,4,128]{2,0,1:T(8,128)(2,1)} %copy.49) | copy-start | bytes 393220
  197.8 8.6 %collective-permute-start.4 = (f32[16,2304]{1,0:T(8,128)S(1)}, f32[16,2304]{1,0:T(8,128)S(1)}, u32[]{:S(2)}, u32[]{:S(2)}) collective-permute-start(f32[16,2304]{1,0:T(8,128)S(1)} %fusion.27), channel_id=1, source_target_pairs={{0,16},{16,0},{32,48},{48,32},{64,80},{80,64},{96,112},{112,96},{1... | collective-permute-start | bytes 442376 | tf_op jit(solution)/shard_map/ppermute | solution.py:88
  206.4 6.8 %collective-permute-start.5 = (f32[16,1152]{1,0:T(8,128)S(1)}, f32[16,1152]{1,0:T(8,128)S(1)}, u32[]{:S(2)}, u32[]{:S(2)}) collective-permute-start(f32[16,1152]{1,0:T(8,128)S(1)} %constant_dynamic-slice_fusion.1), channel_id=1, source_target_pairs={{0,32},{16,48},{32,0},{48,16},{64,96},{80,112},{96,64},{112,80},{1... | collective-permute-start | bytes 221192 | tf_op jit(solution)/shard_map/ppermute | solution.py:88
  213.3 4.7 %collective-permute-start.6 = (f32[16,576]{1,0:T(8,128)S(1)}, f32[16,576]{1,0:T(8,128)S(1)}, u32[]{:S(2)}, u32[]{:S(2)}) collective-permute-start(f32[16,576]{1,0:T(8,128)S(1)} %constant_dynamic-slice_fusion), channel_id=1, source_target_pairs={{0,1},{1,0},{2,3},{3,2},{4,5},{5,4},{6,7},{7,6},{8,9},{9,8},{10,11... | collective-permute-start | bytes 110600 | tf_op jit(solution)/shard_map/ppermute | solution.py:88
  218.1 6.4 %collective-permute-start.7 = (f32[16,576]{1,0:T(8,128)S(1)}, f32[16,576]{1,0:T(8,128)S(1)}, u32[]{:S(2)}, u32[]{:S(2)}) collective-permute-start(f32[16,576]{1,0:T(8,128)S(1)} %dynamic-slice_add_fusion.3), channel_id=1, source_target_pairs={{0,64},{16,80},{32,96},{48,112},{64,0},{80,16},{96,32},{112,48},{1... | collective-permute-start | bytes 110600 | tf_op jit(solution)/shard_map/ppermute | solution.py:91
  224.6 6.3 %collective-permute-start.8 = (f32[16,576]{1,0:T(8,128)S(1)}, f32[16,576]{1,0:T(8,128)S(1)}, u32[]{:S(2)}, u32[]{:S(2)}) collective-permute-start(f32[16,576]{1,0:T(8,128)S(1)} %add.145), channel_id=1, source_target_pairs={{0,128},{16,144},{32,160},{48,176},{64,192},{80,208},{96,224},{112... | collective-permute-start | bytes 110600 | tf_op jit(solution)/shard_map/ppermute | solution.py:91
  230.9 6.2 %collective-permute-start.9 = (f32[16,576]{1,0:T(8,128)S(1)}, f32[16,576]{1,0:T(8,128)S(1)}, u32[]{:S(2)}, u32[]{:S(2)}) collective-permute-start(f32[16,576]{1,0:T(8,128)S(1)} %add.146), channel_id=1, source_target_pairs={{0,256},{16,272},{32,288},{48,304},{64,320},{80,336},{96,352},{112... | collective-permute-start | bytes 110600 | tf_op jit(solution)/shard_map/ppermute | solution.py:91
  237.1 11.0 %collective-permute-start.10 = (f32[16,576]{1,0:T(8,128)S(1)}, f32[16,576]{1,0:T(8,128)S(1)}, u32[]{:S(2)}, u32[]{:S(2)}) collective-permute-start(f32[16,576]{1,0:T(8,128)S(1)} %add.147), channel_id=1, source_target_pairs={{0,2},{1,3},{2,0},{3,1},{4,6},{5,7},{6,4},{7,5},{8,10},{9,11},{10,... | collective-permute-start | bytes 110600 | tf_op jit(solution)/shard_map/ppermute | solution.py:91
  248.1 32.1 %copy-start.3 = (f32[928,128]{1,0:T(8,128)S(1)}, f32[928,128]{1,0:T(8,128)}, u32[]{:S(2)}) copy-start(f32[928,128]{1,0:T(8,128)} %copy-done.2) | copy-start | bytes 1425412
  248.2 32.1 %copy-start.5 = (f32[928,128]{1,0:T(8,128)S(1)}, f32[928,128]{1,0:T(8,128)}, u32[]{:S(2)}) copy-start(f32[928,128]{1,0:T(8,128)} %copy-done.4) | copy-start | bytes 1425412
  248.2 32.1 %copy-start.7 = (f32[928,128]{1,0:T(8,128)S(1)}, f32[928,128]{1,0:T(8,128)}, u32[]{:S(2)}) copy-start(f32[928,128]{1,0:T(8,128)} %copy-done.6) | copy-start | bytes 1425412
  248.2 23.2 %collective-permute-start.11 = (f32[16,576]{1,0:T(8,128)S(1)}, f32[16,576]{1,0:T(8,128)S(1)}, u32[]{:S(2)}, u32[]{:S(2)}) collective-permute-start(f32[16,576]{1,0:T(8,128)S(1)} %add.148), channel_id=1, source_target_pairs={{0,4},{1,5},{2,6},{3,7},{4,0},{5,1},{6,2},{7,3},{8,12},{9,13},{10,... | collective-permute-start | bytes 110600 | tf_op jit(solution)/shard_map/ppermute | solution.py:91
  271.4 12.1 %copy-start.14 = (bf16[4,128,4,128]{3,1,2,0:T(8,128)(2,1)S(1)}, bf16[4,128,4,128]{3,1,2,0:T(8,128)(2,1)}, u32[]{:S(2)}) copy-start(bf16[4,128,4,128]{3,1,2,0:T(8,128)(2,1)} %fusion.14) | copy-start | bytes 1572868
  271.4 15.2 %collective-permute-start.12 = (f32[16,576]{1,0:T(8,128)S(1)}, f32[16,576]{1,0:T(8,128)S(1)}, u32[]{:S(2)}, u32[]{:S(2)}) collective-permute-start(f32[16,576]{1,0:T(8,128)S(1)} %add.149), channel_id=1, source_target_pairs={{0,8},{1,9},{2,10},{3,11},{4,12},{5,13},{6,14},{7,15},{8,0},{9,1},... | collective-permute-start | bytes 110600 | tf_op jit(solution)/shard_map/ppermute | solution.py:91
  280.3 10.5 %collective-permute-start.16 = (f32[56,512]{1,0:T(8,128)S(1)}, f32[56,512]{1,0:T(8,128)S(1)}, u32[]{:S(2)}, u32[]{:S(2)}) collective-permute-start(f32[56,512]{1,0:T(8,128)S(1)} %get-tuple-element.27), channel_id=1, source_target_pairs={{0,1},{1,2},{2,3},{3,4},{4,5},{5,6},{6,7},{7,8},{8,9},{9,10},{10,1... | collective-permute-start | bytes 344072
  284.5 6.3 %collective-permute-start.17 = (f32[34,512]{1,0:T(8,128)S(1)}, f32[34,512]{1,0:T(8,128)S(1)}, u32[]{:S(2)}, u32[]{:S(2)}) collective-permute-start(f32[34,512]{1,0:T(8,128)S(1)} %slice.86), channel_id=1, source_target_pairs={{0,2},{1,3},{2,4},{3,5},{4,6},{5,7},{6,8},{7,9},{8,10},{9,11},{10,... | collective-permute-start | bytes 208904
  286.6 4.8 %collective-permute-start.13 = (f32[16,576]{1,0:T(8,128)S(1)}, f32[16,576]{1,0:T(8,128)S(1)}, u32[]{:S(2)}, u32[]{:S(2)}) collective-permute-start(f32[16,576]{1,0:T(8,128)S(1)} %add.150), channel_id=1, source_target_pairs={{0,1},{1,0},{2,3},{3,2},{4,5},{5,4},{6,7},{7,6},{8,9},{9,8},{10,11... | collective-permute-start | bytes 110600 | tf_op jit(solution)/shard_map/ppermute | solution.py:94
  291.6 5.9 %collective-permute-start.14 = (f32[16,1152]{1,0:T(8,128)S(1)}, f32[16,1152]{1,0:T(8,128)S(1)}, u32[]{:S(2)}, u32[]{:S(2)}) collective-permute-start(f32[16,1152]{1,0:T(8,128)S(1)} %maximum_select_fusion.2), channel_id=1, source_target_pairs={{0,32},{16,48},{32,0},{48,16},{64,96},{80,112},{96,64},{112,80},{1... | collective-permute-start | bytes 221192 | tf_op jit(solution)/shard_map/ppermute | solution.py:94
  297.5 12.7 %collective-permute-start.15 = (f32[16,2304]{1,0:T(8,128)S(1)}, f32[16,2304]{1,0:T(8,128)S(1)}, u32[]{:S(2)}, u32[]{:S(2)}) collective-permute-start(f32[16,2304]{1,0:T(8,128)S(1)} %maximum_select_fusion.1), channel_id=1, source_target_pairs={{0,16},{16,0},{32,48},{48,32},{64,80},{80,64},{96,112},{112,96},{1... | collective-permute-start | bytes 442376 | tf_op jit(solution)/shard_map/ppermute | solution.py:94
  (9 other events, 11.7 us)

commit v11 on v10

--- a/solution.py
+++ b/solution.py
@@ -77,7 +77,7 @@
         if n & (n - 1):
             return lax.psum(x, ("dp", "ctx"))
         rounds += [(axis, 1 << j) for j in range(n.bit_length() - 1)]
-    nearest = [r for r in (("dp", 1), ("dp", 2), ("ctx", 1)) if r in rounds]
+    nearest = [r for r in (("dp", 1), ("dp", 2), ("ctx", 1), ("dp", 8)) if r in rounds]
     halving = [r for r in nearest if x.shape[-1] % (2 ** len(nearest)) == 0]
     cur = x
     for axis, k in halving:

time: 313 us -> 318 us (1.016)
  starting transfers between devices: 128 us -> 135 us
  waiting for transfers between devices: 44.3 us -> 40 us
    ppermute x3 -> x4, starting transfers between devices: 11.4 us -> 18.8 us  [mesh_sum(): cur = keep + lax.ppermute(give, axis, exchange_pairs(axis, k))]
    ppermute x3 -> x4, waiting for transfers between devices: 8.59 us -> 6.72 us  [mesh_sum(): cur = keep + lax.ppermute(give, axis, exchange_pairs(axis, k))]
    ppermute x6 -> x5, starting transfers between devices: 51.8 us -> 50 us  [mesh_sum(): cur = cur + lax.ppermute(cur, axis, exchange_pairs(axis, k))]
    ppermute x6 -> x5, waiting for transfers between devices: 6.44 us -> 4.79 us  [mesh_sum(): cur = cur + lax.ppermute(cur, axis, exchange_pairs(axis, k))]
    ppermute x3 -> x4, starting transfers between devices: 17.9 us -> 19.3 us  [mesh_sum(): other = lax.ppermute(cur, axis, exchange_pairs(axis, k))]
  transfers between devices with their start and end apart: 20 -> 21, of which waited for: 15 -> 16; matrix products, arithmetic and copies ran while one was open for 6% -> 6% of each run, Pallas kernels for 0% -> 0%
where the time goes in v11:
time: 318 us; the launch traced here: 314 us
  starting transfers between devices  135 us (42%)
  blocking collectives  87.5 us (28%)
  waiting for transfers between devices  40 us (13%)
  local copies, waits for them, and re-layouts  27.1 us (9%)
  matrix products  12.7 us (4%)
  other arithmetic  9.28 us (3%)
    unnamed x1, blocking collectives  87.5 us
    ppermute x5, starting transfers between devices, mesh_sum(): cur = cur + lax.ppermute(cur, axis, exchange_pairs(axis, k))  50 us
    ppermute x4, starting transfers between devices, per_device(): lax.ppermute(held, 'ctx', [(i, i + hop) for i in range(segment_list - hop)])  39.5 us
    ppermute x4, waiting for transfers between devices, per_device(): lax.ppermute(held, 'ctx', [(i, i + hop) for i in range(segment_list - hop)])  24.7 us
    ppermute x4, starting transfers between devices, mesh_sum(): other = lax.ppermute(cur, axis, exchange_pairs(axis, k))  19.3 us
    ppermute x4, starting transfers between devices, mesh_sum(): cur = keep + lax.ppermute(give, axis, exchange_pairs(axis, k))  18.8 us
    unnamed x53, local copies, waits for them, and re-layouts  7.6 us
    unnamed x4, starting transfers between devices  6.95 us
  transfers between devices with their start and end apart: 21, of which 16 were waited for; matrix products, arithmetic and copies ran while one was open for 6% of the time, Pallas kernels for 0%

profile of v11, /device:TPU:1, one launch (start us, length us, event | category | flops | bytes accessed | tf_op | source)
XLA Modules:
  0.0 314.2 jit_solution(1683609547145695630)
XLA Ops:
  3.0 11.5 %collective-permute-start = (bf16[1,100,512]{2,1,0:T(8,128)(2,1)S(1)}, bf16[1,100,512]{2,1,0:T(8,128)(2,1)S(1)}, u32[]{:S(2)}, u32[]{:S(2)}) collective-permute-start(bf16[1,100,512]{2,1,0:T(8,128)(2,1)S(1)} %get-tuple-element.30), channel_id=1, source_target_pairs={{0,8},{1,9},{2,10},{3,11},{4,12},{5,13},{6,14},{7,15},{16,24},{17,... | collective-permute-start | bytes 307208 | tf_op jit(solution)/shard_map/ppermute | solution.py:134
  16.1 7.4 %collective-permute-start.1 = (bf16[2,100,512]{2,1,0:T(8,128)(2,1)S(1)}, bf16[2,100,512]{2,1,0:T(8,128)(2,1)S(1)}, u32[]{:S(2)}, u32[]{:S(2)}) collective-permute-start(bf16[2,100,512]{2,1,0:T(8,128)(2,1)S(1)} %pad_maximum_fusion.10), channel_id=1, source_target_pairs={{0,4},{1,5},{2,6},{3,7},{4,8},{5,9},{6,10},{7,11},{8,12},{9,13},{1... | collective-permute-start | bytes 614408 | tf_op jit(solution)/shard_map/ppermute | solution.py:134
  23.6 3.0 collective-permute-done.1
  26.7 7.5 %collective-permute-start.2 = (bf16[4,100,512]{2,1,0:T(8,128)(2,1)S(1)}, bf16[4,100,512]{2,1,0:T(8,128)(2,1)S(1)}, u32[]{:S(2)}, u32[]{:S(2)}) collective-permute-start(bf16[4,100,512]{2,1,0:T(8,128)(2,1)S(1)} %pad_maximum_fusion.7), channel_id=1, source_target_pairs={{0,2},{1,3},{2,4},{3,5},{4,6},{5,7},{6,8},{7,9},{8,10},{9,11},{10,... | collective-permute-start | bytes 1228808 | tf_op jit(solution)/shard_map/ppermute | solution.py:134
  34.2 13.1 %collective-permute-done.2 = bf16[4,100,512]{2,1,0:T(8,128)(2,1)S(1)} collective-permute-done((bf16[4,100,512]{2,1,0:T(8,128)(2,1)S(1)}, bf16[4,100,512]{2,1,0:T(8,128)(2,1)S(1)}, u32[]{:S(2)}, u32[]{:S(2)}) %collective-permute-start.2) | collective-permute-done | bytes 409632 | tf_op jit(solution)/shard_map/ppermute | solution.py:134
  47.6 13.1 %collective-permute-start.3 = (bf16[8,100,512]{2,0,1:T(8,128)(2,1)S(1)}, bf16[8,100,512]{2,0,1:T(8,128)(2,1)}, u32[]{:S(2)}, u32[]{:S(2)}) collective-permute-start(bf16[8,100,512]{2,0,1:T(8,128)(2,1)S(1)} %copy.43), channel_id=1, source_target_pairs={{0,1},{1,2},{2,3},{3,4},{4,5},{5,6},{6,7},{7,8},{8,9},{9,10},{10,1... | collective-permute-start | bytes 2457608 | tf_op jit(solution)/shard_map/ppermute | solution.py:134
  63.2 2.2 squeeze.36
  70.5 8.3 %collective-permute-done.3 = bf16[8,100,512]{2,0,1:T(8,128)(2,1)} collective-permute-done((bf16[8,100,512]{2,0,1:T(8,128)(2,1)S(1)}, bf16[8,100,512]{2,0,1:T(8,128)(2,1)}, u32[]{:S(2)}, u32[]{:S(2)}) %collective-permute-start.3) | collective-permute-done | bytes 819232 | tf_op jit(solution)/shard_map/ppermute | solution.py:134
  78.8 2.3 copy_dynamic-update-slice_fusion
  81.1 2.1 gather_fusion.1
  85.8 2.2 copy.48
  88.8 3.1 fusion.7
  93.7 2.2 fusion.2
  95.8 2.3 fusion.4
  103.2 87.5 %fusion.47 = (f32[56,512]{1,0:T(8,128)S(1)}, f32[56,512]{1,0:T(8,128)S(1)}) fusion(f32[800,512]{1,0:T(8,128)S(1)} %pad_maximum_fusion.3, f32[800,512]{1,0:T(8,128)} %pad_maximum_fusion), kind=kCustom, calls=%all-reduce-scatter.2 | all-reduce-scatter fusion | flops 917505 | bytes 3508224
  197.2 8.4 %collective-permute-start.4 = (f32[16,2304]{1,0:T(8,128)S(1)}, f32[16,2304]{1,0:T(8,128)S(1)}, u32[]{:S(2)}, u32[]{:S(2)}) collective-permute-start(f32[16,2304]{1,0:T(8,128)S(1)} %fusion.27), channel_id=1, source_target_pairs={{0,16},{16,0},{32,48},{48,32},{64,80},{80,64},{96,112},{112,96},{1... | collective-permute-start | bytes 442376 | tf_op jit(solution)/shard_map/ppermute | solution.py:88
  206.7 1.9 collective-permute-start.5
  208.6 3.1 %collective-permute-done.5 = f32[16,1152]{1,0:T(8,128)S(1)} collective-permute-done((f32[16,1152]{1,0:T(8,128)S(1)}, f32[16,1152]{1,0:T(8,128)S(1)}, u32[]{:S(2)}, u32[]{:S(2)}) %collective-permute-start.5) | collective-permute-done | bytes 73760 | tf_op jit(solution)/shard_map/ppermute | solution.py:88
  211.9 3.2 %collective-permute-start.6 = (f32[16,576]{1,0:T(8,128)S(1)}, f32[16,576]{1,0:T(8,128)S(1)}, u32[]{:S(2)}, u32[]{:S(2)}) collective-permute-start(f32[16,576]{1,0:T(8,128)S(1)} %constant_dynamic-slice_fusion.1), channel_id=1, source_target_pairs={{0,1},{1,0},{2,3},{3,2},{4,5},{5,4},{6,7},{7,6},{8,9},{9,8},{10,11... | collective-permute-start | bytes 110600 | tf_op jit(solution)/shard_map/ppermute | solution.py:88
  216.8 5.2 %collective-permute-start.7 = (f32[16,288]{1,0:T(8,128)S(1)}, f32[16,288]{1,0:T(8,128)S(1)}, u32[]{:S(2)}, u32[]{:S(2)}) collective-permute-start(f32[16,288]{1,0:T(8,128)S(1)} %constant_dynamic-slice_fusion), channel_id=1, source_target_pairs={{0,128},{16,144},{32,160},{48,176},{64,192},{80,208},{96,224},{112... | collective-permute-start | bytes 55304 | tf_op jit(solution)/shard_map/ppermute | solution.py:88
  223.2 5.3 %collective-permute-start.8 = (f32[16,288]{1,0:T(8,128)S(1)}, f32[16,288]{1,0:T(8,128)S(1)}, u32[]{:S(2)}, u32[]{:S(2)}) collective-permute-start(f32[16,288]{1,0:T(8,128)S(1)} %dynamic-slice_add_fusion.4), channel_id=1, source_target_pairs={{0,64},{16,80},{32,96},{48,112},{64,0},{80,16},{96,32},{112,48},{1... | collective-permute-start | bytes 55304 | tf_op jit(solution)/shard_map/ppermute | solution.py:91
  229.7 5.8 %collective-permute-start.9 = (f32[16,288]{1,0:T(8,128)S(1)}, f32[16,288]{1,0:T(8,128)S(1)}, u32[]{:S(2)}, u32[]{:S(2)}) collective-permute-start(f32[16,288]{1,0:T(8,128)S(1)} %add.160), channel_id=1, source_target_pairs={{0,256},{16,272},{32,288},{48,304},{64,320},{80,336},{96,352},{112... | collective-permute-start | bytes 55304 | tf_op jit(solution)/shard_map/ppermute | solution.py:91
  236.8 9.2 %collective-permute-start.10 = (f32[16,288]{1,0:T(8,128)S(1)}, f32[16,288]{1,0:T(8,128)S(1)}, u32[]{:S(2)}, u32[]{:S(2)}) collective-permute-start(f32[16,288]{1,0:T(8,128)S(1)} %add.161), channel_id=1, source_target_pairs={{0,2},{1,3},{2,0},{3,1},{4,6},{5,7},{6,4},{7,5},{8,10},{9,11},{10,... | collective-permute-start | bytes 55304 | tf_op jit(solution)/shard_map/ppermute | solution.py:91
  247.2 18.3 %collective-permute-start.11 = (f32[16,288]{1,0:T(8,128)S(1)}, f32[16,288]{1,0:T(8,128)S(1)}, u32[]{:S(2)}, u32[]{:S(2)}) collective-permute-start(f32[16,288]{1,0:T(8,128)S(1)} %add.162), channel_id=1, source_target_pairs={{0,4},{1,5},{2,6},{3,7},{4,0},{5,1},{6,2},{7,3},{8,12},{9,13},{10,... | collective-permute-start | bytes 55304 | tf_op jit(solution)/shard_map/ppermute | solution.py:91
  266.7 11.4 %collective-permute-start.12 = (f32[16,288]{1,0:T(8,128)S(1)}, f32[16,288]{1,0:T(8,128)S(1)}, u32[]{:S(2)}, u32[]{:S(2)}) collective-permute-start(f32[16,288]{1,0:T(8,128)S(1)} %add.163), channel_id=1, source_target_pairs={{0,8},{1,9},{2,10},{3,11},{4,12},{5,13},{6,14},{7,15},{8,0},{9,1},... | collective-permute-start | bytes 55304 | tf_op jit(solution)/shard_map/ppermute | solution.py:91
  278.1 3.7 %fusion.14 = bf16[4,128,4,128]{3,1,2,0:T(8,128)(2,1)} fusion(bf16[4,4,128,928]{2,3,1,0:T(8,128)(2,1)} %copy-done.1, bf16[128,4,128]{2,0,1:T(8,128)(2,1)S(1)} %copy-done.18, bf16[800,4,128]{2,0,1:T(8,128)(2,1)S(1)} %copy-done.12), kind=kOutput, calls=%fused_computation.24 | convolution fusion | flops 488964096 | bytes 5275648 | tf_op jit(solution)/shard_map/kgtm,mkd->tkgd/dot_general | solution.py:168
  281.8 2.1 collective-permute-start.13
  283.9 2.2 collective-permute-start.17
  287.2 2.1 collective-permute-start.18
  289.4 2.1 collective-permute-start.14
  294.2 2.7 collective-permute-start.15
  299.4 12.4 %collective-permute-start.16 = (f32[16,2304]{1,0:T(8,128)S(1)}, f32[16,2304]{1,0:T(8,128)S(1)}, u32[]{:S(2)}, u32[]{:S(2)}) collective-permute-start(f32[16,2304]{1,0:T(8,128)S(1)} %maximum_select_fusion.1), channel_id=1, source_target_pairs={{0,16},{16,0},{32,48},{48,32},{64,80},{80,64},{96,112},{112,96},{1... | collective-permute-start | bytes 442376 | tf_op jit(solution)/shard_map/ppermute | solution.py:94
  (135 shorter events, 44.3 us)
Async XLA Ops:
  0.6 195.5 %copy-start = (bf16[1,1,128,4096]{3,2,1,0:T(8,128)(2,1)S(1)}, bf16[1,1,128,4096]{3,2,1,0:T(8,128)(2,1)}, u32[]{:S(2)}) copy-start(bf16[1,1,128,4096]{3,2,1,0:T(8,128)(2,1)} %param.13) | copy-start | bytes 3145732
  3.0 13.2 %collective-permute-start = (bf16[1,100,512]{2,1,0:T(8,128)(2,1)S(1)}, bf16[1,100,512]{2,1,0:T(8,128)(2,1)S(1)}, u32[]{:S(2)}, u32[]{:S(2)}) collective-permute-start(bf16[1,100,512]{2,1,0:T(8,128)(2,1)S(1)} %get-tuple-element.30), channel_id=1, source_target_pairs={{0,8},{1,9},{2,10},{3,11},{4,12},{5,13},{6,14},{7,15},{16,24},{17,... | collective-permute-start | bytes 307208 | tf_op jit(solution)/shard_map/ppermute | solution.py:134
  16.1 10.4 %collective-permute-start.1 = (bf16[2,100,512]{2,1,0:T(8,128)(2,1)S(1)}, bf16[2,100,512]{2,1,0:T(8,128)(2,1)S(1)}, u32[]{:S(2)}, u32[]{:S(2)}) collective-permute-start(bf16[2,100,512]{2,1,0:T(8,128)(2,1)S(1)} %pad_maximum_fusion.10), channel_id=1, source_target_pairs={{0,4},{1,5},{2,6},{3,7},{4,8},{5,9},{6,10},{7,11},{8,12},{9,13},{1... | collective-permute-start | bytes 614408 | tf_op jit(solution)/shard_map/ppermute | solution.py:134
  26.6 34.1 %copy-start.15 = (bf16[1,1,128,512]{3,2,1,0:T(8,128)(2,1)S(1)}, bf16[1,1,128,512]{3,2,1,0:T(8,128)(2,1)}, u32[]{:S(2)}) copy-start(bf16[1,1,128,512]{3,2,1,0:T(8,128)(2,1)} %param.10) | copy-start | bytes 393220
  26.6 34.2 %copy-start.16 = (bf16[1,1,128,512]{3,2,1,0:T(8,128)(2,1)S(1)}, bf16[1,1,128,512]{3,2,1,0:T(8,128)(2,1)}, u32[]{:S(2)}) copy-start(bf16[1,1,128,512]{3,2,1,0:T(8,128)(2,1)} %param.11) | copy-start | bytes 393220
  26.7 20.6 %collective-permute-start.2 = (bf16[4,100,512]{2,1,0:T(8,128)(2,1)S(1)}, bf16[4,100,512]{2,1,0:T(8,128)(2,1)S(1)}, u32[]{:S(2)}, u32[]{:S(2)}) collective-permute-start(bf16[4,100,512]{2,1,0:T(8,128)(2,1)S(1)} %pad_maximum_fusion.7), channel_id=1, source_target_pairs={{0,2},{1,3},{2,4},{3,5},{4,6},{5,7},{6,8},{7,9},{8,10},{9,11},{10,... | collective-permute-start | bytes 1228808 | tf_op jit(solution)/shard_map/ppermute | solution.py:134
  47.6 31.2 %collective-permute-start.3 = (bf16[8,100,512]{2,0,1:T(8,128)(2,1)S(1)}, bf16[8,100,512]{2,0,1:T(8,128)(2,1)}, u32[]{:S(2)}, u32[]{:S(2)}) collective-permute-start(bf16[8,100,512]{2,0,1:T(8,128)(2,1)S(1)} %copy.43), channel_id=1, source_target_pairs={{0,1},{1,2},{2,3},{3,4},{4,5},{5,6},{6,7},{7,8},{8,9},{9,10},{10,1... | collective-permute-start | bytes 2457608 | tf_op jit(solution)/shard_map/ppermute | solution.py:134
  88.8 3.1 copy-start.13
  190.8 5.4 %copy-start.20 = (bf16[16,512]{1,0:T(8,128)(2,1)S(1)}, bf16[16,512]{1,0:T(8,128)(2,1)}, u32[]{:S(2)}) copy-start(bf16[16,512]{1,0:T(8,128)(2,1)} %param.15) | copy-start | bytes 49156
  190.8 4.1 %collective-permute-start.19 = (f32[56,512]{1,0:T(8,128)S(1)}, f32[56,512]{1,0:T(8,128)S(1)}, u32[]{:S(2)}, u32[]{:S(2)}) collective-permute-start(f32[56,512]{1,0:T(8,128)S(1)} %get-tuple-element.28), channel_id=1, source_target_pairs={{0,1},{1,2},{2,3},{3,4},{4,5},{5,6},{6,7},{7,8},{8,9},{9,10},{10,1... | collective-permute-start | bytes 344072
  192.1 2.8 collective-permute-start.20
  196.6 81.5 %copy-start.12 = (bf16[800,4,128]{2,0,1:T(8,128)(2,1)S(1)}, bf16[800,4,128]{2,0,1:T(8,128)(2,1)}, u32[]{:S(2)}) copy-start(bf16[800,4,128]{2,0,1:T(8,128)(2,1)} %copy.48) | copy-start | bytes 2457604
  196.6 81.5 %copy-start.18 = (bf16[128,4,128]{2,0,1:T(8,128)(2,1)S(1)}, bf16[128,4,128]{2,0,1:T(8,128)(2,1)}, u32[]{:S(2)}) copy-start(bf16[128,4,128]{2,0,1:T(8,128)(2,1)} %copy.49) | copy-start | bytes 393220
  197.2 9.4 %collective-permute-start.4 = (f32[16,2304]{1,0:T(8,128)S(1)}, f32[16,2304]{1,0:T(8,128)S(1)}, u32[]{:S(2)}, u32[]{:S(2)}) collective-permute-start(f32[16,2304]{1,0:T(8,128)S(1)} %fusion.27), channel_id=1, source_target_pairs={{0,16},{16,0},{32,48},{48,32},{64,80},{80,64},{96,112},{112,96},{1... | collective-permute-start | bytes 442376 | tf_op jit(solution)/shard_map/ppermute | solution.py:88
  206.7 5.1 %collective-permute-start.5 = (f32[16,1152]{1,0:T(8,128)S(1)}, f32[16,1152]{1,0:T(8,128)S(1)}, u32[]{:S(2)}, u32[]{:S(2)}) collective-permute-start(f32[16,1152]{1,0:T(8,128)S(1)} %constant_dynamic-slice_fusion.2), channel_id=1, source_target_pairs={{0,32},{16,48},{32,0},{48,16},{64,96},{80,112},{96,64},{112,80},{1... | collective-permute-start | bytes 221192 | tf_op jit(solution)/shard_map/ppermute | solution.py:88
  211.9 4.7 %collective-permute-start.6 = (f32[16,576]{1,0:T(8,128)S(1)}, f32[16,576]{1,0:T(8,128)S(1)}, u32[]{:S(2)}, u32[]{:S(2)}) collective-permute-start(f32[16,576]{1,0:T(8,128)S(1)} %constant_dynamic-slice_fusion.1), channel_id=1, source_target_pairs={{0,1},{1,0},{2,3},{3,2},{4,5},{5,4},{6,7},{7,6},{8,9},{9,8},{10,11... | collective-permute-start | bytes 110600 | tf_op jit(solution)/shard_map/ppermute | solution.py:88
  216.8 6.4 %collective-permute-start.7 = (f32[16,288]{1,0:T(8,128)S(1)}, f32[16,288]{1,0:T(8,128)S(1)}, u32[]{:S(2)}, u32[]{:S(2)}) collective-permute-start(f32[16,288]{1,0:T(8,128)S(1)} %constant_dynamic-slice_fusion), channel_id=1, source_target_pairs={{0,128},{16,144},{32,160},{48,176},{64,192},{80,208},{96,224},{112... | collective-permute-start | bytes 55304 | tf_op jit(solution)/shard_map/ppermute | solution.py:88
  223.2 6.5 %collective-permute-start.8 = (f32[16,288]{1,0:T(8,128)S(1)}, f32[16,288]{1,0:T(8,128)S(1)}, u32[]{:S(2)}, u32[]{:S(2)}) collective-permute-start(f32[16,288]{1,0:T(8,128)S(1)} %dynamic-slice_add_fusion.4), channel_id=1, source_target_pairs={{0,64},{16,80},{32,96},{48,112},{64,0},{80,16},{96,32},{112,48},{1... | collective-permute-start | bytes 55304 | tf_op jit(solution)/shard_map/ppermute | solution.py:91
  229.7 7.1 %collective-permute-start.9 = (f32[16,288]{1,0:T(8,128)S(1)}, f32[16,288]{1,0:T(8,128)S(1)}, u32[]{:S(2)}, u32[]{:S(2)}) collective-permute-start(f32[16,288]{1,0:T(8,128)S(1)} %add.160), channel_id=1, source_target_pairs={{0,256},{16,272},{32,288},{48,304},{64,320},{80,336},{96,352},{112... | collective-permute-start | bytes 55304 | tf_op jit(solution)/shard_map/ppermute | solution.py:91
  236.8 10.4 %collective-permute-start.10 = (f32[16,288]{1,0:T(8,128)S(1)}, f32[16,288]{1,0:T(8,128)S(1)}, u32[]{:S(2)}, u32[]{:S(2)}) collective-permute-start(f32[16,288]{1,0:T(8,128)S(1)} %add.161), channel_id=1, source_target_pairs={{0,2},{1,3},{2,0},{3,1},{4,6},{5,7},{6,4},{7,5},{8,10},{9,11},{10,... | collective-permute-start | bytes 55304 | tf_op jit(solution)/shard_map/ppermute | solution.py:91
  247.2 19.5 %collective-permute-start.11 = (f32[16,288]{1,0:T(8,128)S(1)}, f32[16,288]{1,0:T(8,128)S(1)}, u32[]{:S(2)}, u32[]{:S(2)}) collective-permute-start(f32[16,288]{1,0:T(8,128)S(1)} %add.162), channel_id=1, source_target_pairs={{0,4},{1,5},{2,6},{3,7},{4,0},{5,1},{6,2},{7,3},{8,12},{9,13},{10,... | collective-permute-start | bytes 55304 | tf_op jit(solution)/shard_map/ppermute | solution.py:91
  266.7 17.1 %copy-start.3 = (f32[928,128]{1,0:T(8,128)S(1)}, f32[928,128]{1,0:T(8,128)}, u32[]{:S(2)}) copy-start(f32[928,128]{1,0:T(8,128)} %copy-done.2) | copy-start | bytes 1425412
  266.7 17.2 %copy-start.5 = (f32[928,128]{1,0:T(8,128)S(1)}, f32[928,128]{1,0:T(8,128)}, u32[]{:S(2)}) copy-start(f32[928,128]{1,0:T(8,128)} %copy-done.4) | copy-start | bytes 1425412
  266.7 17.2 %copy-start.7 = (f32[928,128]{1,0:T(8,128)S(1)}, f32[928,128]{1,0:T(8,128)}, u32[]{:S(2)}) copy-start(f32[928,128]{1,0:T(8,128)} %copy-done.6) | copy-start | bytes 1425412
  266.7 15.1 %collective-permute-start.12 = (f32[16,288]{1,0:T(8,128)S(1)}, f32[16,288]{1,0:T(8,128)S(1)}, u32[]{:S(2)}, u32[]{:S(2)}) collective-permute-start(f32[16,288]{1,0:T(8,128)S(1)} %add.163), channel_id=1, source_target_pairs={{0,8},{1,9},{2,10},{3,11},{4,12},{5,13},{6,14},{7,15},{8,0},{9,1},... | collective-permute-start | bytes 55304 | tf_op jit(solution)/shard_map/ppermute | solution.py:91
  281.8 4.4 %copy-start.14 = (bf16[4,128,4,128]{3,1,2,0:T(8,128)(2,1)S(1)}, bf16[4,128,4,128]{3,1,2,0:T(8,128)(2,1)}, u32[]{:S(2)}) copy-start(bf16[4,128,4,128]{3,1,2,0:T(8,128)(2,1)} %fusion.14) | copy-start | bytes 1572868
  281.8 7.5 %collective-permute-start.13 = (f32[16,288]{1,0:T(8,128)S(1)}, f32[16,288]{1,0:T(8,128)S(1)}, u32[]{:S(2)}, u32[]{:S(2)}) collective-permute-start(f32[16,288]{1,0:T(8,128)S(1)} %add.164), channel_id=1, source_target_pairs={{0,128},{16,144},{32,160},{48,176},{64,192},{80,208},{96,224},{112... | collective-permute-start | bytes 55304 | tf_op jit(solution)/shard_map/ppermute | solution.py:94
  283.9 8.3 %collective-permute-start.17 = (f32[56,512]{1,0:T(8,128)S(1)}, f32[56,512]{1,0:T(8,128)S(1)}, u32[]{:S(2)}, u32[]{:S(2)}) collective-permute-start(f32[56,512]{1,0:T(8,128)S(1)} %get-tuple-element.27), channel_id=1, source_target_pairs={{0,1},{1,2},{2,3},{3,4},{4,5},{5,6},{6,7},{7,8},{8,9},{9,10},{10,1... | collective-permute-start | bytes 344072
  287.2 5.0 %collective-permute-start.18 = (f32[34,512]{1,0:T(8,128)S(1)}, f32[34,512]{1,0:T(8,128)S(1)}, u32[]{:S(2)}, u32[]{:S(2)}) collective-permute-start(f32[34,512]{1,0:T(8,128)S(1)} %slice.86), channel_id=1, source_target_pairs={{0,2},{1,3},{2,4},{3,5},{4,6},{5,7},{6,8},{7,9},{8,10},{9,11},{10,... | collective-permute-start | bytes 208904
  289.4 4.7 %collective-permute-start.14 = (f32[16,576]{1,0:T(8,128)S(1)}, f32[16,576]{1,0:T(8,128)S(1)}, u32[]{:S(2)}, u32[]{:S(2)}) collective-permute-start(f32[16,576]{1,0:T(8,128)S(1)} %maximum_select_fusion.3), channel_id=1, source_target_pairs={{0,1},{1,0},{2,3},{3,2},{4,5},{5,4},{6,7},{7,6},{8,9},{9,8},{10,11... | collective-permute-start | bytes 110600 | tf_op jit(solution)/shard_map/ppermute | solution.py:94
  294.2 5.1 %collective-permute-start.15 = (f32[16,1152]{1,0:T(8,128)S(1)}, f32[16,1152]{1,0:T(8,128)S(1)}, u32[]{:S(2)}, u32[]{:S(2)}) collective-permute-start(f32[16,1152]{1,0:T(8,128)S(1)} %maximum_select_fusion.2), channel_id=1, source_target_pairs={{0,32},{16,48},{32,0},{48,16},{64,96},{80,112},{96,64},{112,80},{1... | collective-permute-start | bytes 221192 | tf_op jit(solution)/shard_map/ppermute | solution.py:94
  299.4 13.4 %collective-permute-start.16 = (f32[16,2304]{1,0:T(8,128)S(1)}, f32[16,2304]{1,0:T(8,128)S(1)}, u32[]{:S(2)}, u32[]{:S(2)}) collective-permute-start(f32[16,2304]{1,0:T(8,128)S(1)} %maximum_select_fusion.1), channel_id=1, source_target_pairs={{0,16},{16,0},{32,48},{48,32},{64,80},{80,64},{96,112},{112,96},{1... | collective-permute-start | bytes 442376 | tf_op jit(solution)/shard_map/ppermute | solution.py:94
  (10 other events, 13.9 us)

commit v12 on v10

--- a/solution.py
+++ b/solution.py
@@ -92,9 +92,10 @@
     for axis, k in reversed(halving):
         bit = (lax.axis_index(axis) // k) % 2
         other = lax.ppermute(cur, axis, exchange_pairs(axis, k))
-        cur = jnp.where(
-            bit == 0, jnp.concatenate([cur, other], -1), jnp.concatenate([other, cur], -1)
-        )
+        h = cur.shape[-1]
+        joined = jnp.zeros(cur.shape[:-1] + (2 * h,), cur.dtype)
+        joined = lax.dynamic_update_slice_in_dim(joined, cur, bit * h, cur.ndim - 1)
+        cur = lax.dynamic_update_slice_in_dim(joined, other, (1 - bit) * h, cur.ndim - 1)
     return cur
 
 

time: 313 us -> 318 us (1.016)
  starting transfers between devices: 128 us -> 136 us
  waiting for transfers between devices: 44.3 us -> 39.9 us
    ppermute x3, starting transfers between devices: 11.4 us -> 15.9 us  [mesh_sum(): cur = keep + lax.ppermute(give, axis, exchange_pairs(axis, k))]
where the time goes in v12:
time: 318 us; the launch traced here: 314 us
  starting transfers between devices  136 us (43%)
  blocking collectives  86.2 us (27%)
  waiting for transfers between devices  39.9 us (13%)
  local copies, waits for them, and re-layouts  27.5 us (9%)
  matrix products  12.7 us (4%)
  other arithmetic  9.03 us (3%)
    unnamed x1, blocking collectives  86.2 us
    ppermute x6, starting transfers between devices, mesh_sum(): cur = cur + lax.ppermute(cur, axis, exchange_pairs(axis, k))  54.3 us
    ppermute x4, starting transfers between devices, per_device(): lax.ppermute(held, 'ctx', [(i, i + hop) for i in range(segment_list - hop)])  39.4 us
    ppermute x4, waiting for transfers between devices, per_device(): lax.ppermute(held, 'ctx', [(i, i + hop) for i in range(segment_list - hop)])  24.8 us
    ppermute x3, starting transfers between devices, mesh_sum(): other = lax.ppermute(cur, axis, exchange_pairs(axis, k))  18.6 us
    ppermute x3, starting transfers between devices, mesh_sum(): cur = keep + lax.ppermute(give, axis, exchange_pairs(axis, k))  15.9 us
    unnamed x4, starting transfers between devices  7.86 us
    unnamed x53, local copies, waits for them, and re-layouts  7.59 us
  transfers between devices with their start and end apart: 20, of which 15 were waited for; matrix products, arithmetic and copies ran while one was open for 6% of the time, Pallas kernels for 0%

profile of v12, /device:TPU:1, one launch (start us, length us, event | category | flops | bytes accessed | tf_op | source)
XLA Modules:
  0.0 314.3 jit_solution(8296868698847820347)
XLA Ops:
  2.9 11.5 %collective-permute-start = (bf16[1,100,512]{2,1,0:T(8,128)(2,1)S(1)}, bf16[1,100,512]{2,1,0:T(8,128)(2,1)S(1)}, u32[]{:S(2)}, u32[]{:S(2)}) collective-permute-start(bf16[1,100,512]{2,1,0:T(8,128)(2,1)S(1)} %get-tuple-element.30), channel_id=1, source_target_pairs={{0,8},{1,9},{2,10},{3,11},{4,12},{5,13},{6,14},{7,15},{16,24},{17,... | collective-permute-start | bytes 307208 | tf_op jit(solution)/shard_map/ppermute | solution.py:135
  16.1 7.5 %collective-permute-start.1 = (bf16[2,100,512]{2,1,0:T(8,128)(2,1)S(1)}, bf16[2,100,512]{2,1,0:T(8,128)(2,1)S(1)}, u32[]{:S(2)}, u32[]{:S(2)}) collective-permute-start(bf16[2,100,512]{2,1,0:T(8,128)(2,1)S(1)} %pad_maximum_fusion.10), channel_id=1, source_target_pairs={{0,4},{1,5},{2,6},{3,7},{4,8},{5,9},{6,10},{7,11},{8,12},{9,13},{1... | collective-permute-start | bytes 614408 | tf_op jit(solution)/shard_map/ppermute | solution.py:135
  23.6 3.0 collective-permute-done.1
  26.7 7.5 %collective-permute-start.2 = (bf16[4,100,512]{2,1,0:T(8,128)(2,1)S(1)}, bf16[4,100,512]{2,1,0:T(8,128)(2,1)S(1)}, u32[]{:S(2)}, u32[]{:S(2)}) collective-permute-start(bf16[4,100,512]{2,1,0:T(8,128)(2,1)S(1)} %pad_maximum_fusion.7), channel_id=1, source_target_pairs={{0,2},{1,3},{2,4},{3,5},{4,6},{5,7},{6,8},{7,9},{8,10},{9,11},{10,... | collective-permute-start | bytes 1228808 | tf_op jit(solution)/shard_map/ppermute | solution.py:135
  34.2 13.2 %collective-permute-done.2 = bf16[4,100,512]{2,1,0:T(8,128)(2,1)S(1)} collective-permute-done((bf16[4,100,512]{2,1,0:T(8,128)(2,1)S(1)}, bf16[4,100,512]{2,1,0:T(8,128)(2,1)S(1)}, u32[]{:S(2)}, u32[]{:S(2)}) %collective-permute-start.2) | collective-permute-done | bytes 409632 | tf_op jit(solution)/shard_map/ppermute | solution.py:135
  47.7 13.0 %collective-permute-start.3 = (bf16[8,100,512]{2,0,1:T(8,128)(2,1)S(1)}, bf16[8,100,512]{2,0,1:T(8,128)(2,1)}, u32[]{:S(2)}, u32[]{:S(2)}) collective-permute-start(bf16[8,100,512]{2,0,1:T(8,128)(2,1)S(1)} %copy.43), channel_id=1, source_target_pairs={{0,1},{1,2},{2,3},{3,4},{4,5},{5,6},{6,7},{7,8},{8,9},{9,10},{10,1... | collective-permute-start | bytes 2457608 | tf_op jit(solution)/shard_map/ppermute | solution.py:135
  63.2 2.2 squeeze.36
  70.5 8.3 %collective-permute-done.3 = bf16[8,100,512]{2,0,1:T(8,128)(2,1)} collective-permute-done((bf16[8,100,512]{2,0,1:T(8,128)(2,1)S(1)}, bf16[8,100,512]{2,0,1:T(8,128)(2,1)}, u32[]{:S(2)}, u32[]{:S(2)}) %collective-permute-start.3) | collective-permute-done | bytes 819232 | tf_op jit(solution)/shard_map/ppermute | solution.py:135
  78.8 2.3 copy_dynamic-update-slice_fusion
  81.1 2.1 gather_fusion.1
  85.8 2.2 copy.48
  88.8 3.1 fusion.7
  93.7 2.2 fusion.2
  95.8 2.3 fusion.4
  103.2 86.2 %fusion.47 = (f32[56,512]{1,0:T(8,128)S(1)}, f32[56,512]{1,0:T(8,128)S(1)}) fusion(f32[800,512]{1,0:T(8,128)S(1)} %pad_maximum_fusion.3, f32[800,512]{1,0:T(8,128)} %pad_maximum_fusion), kind=kCustom, calls=%all-reduce-scatter.2 | all-reduce-scatter fusion | flops 917505 | bytes 3508224
  195.8 9.5 %collective-permute-start.4 = (f32[16,2304]{1,0:T(8,128)S(1)}, f32[16,2304]{1,0:T(8,128)S(1)}, u32[]{:S(2)}, u32[]{:S(2)}) collective-permute-start(f32[16,2304]{1,0:T(8,128)S(1)} %fusion.27), channel_id=1, source_target_pairs={{0,16},{16,0},{32,48},{48,32},{64,80},{80,64},{96,112},{112,96},{1... | collective-permute-start | bytes 442376 | tf_op jit(solution)/shard_map/ppermute | solution.py:88
  206.3 1.9 collective-permute-start.5
  208.3 3.1 collective-permute-done.5
  211.5 4.5 %collective-permute-start.6 = (f32[16,576]{1,0:T(8,128)S(1)}, f32[16,576]{1,0:T(8,128)S(1)}, u32[]{:S(2)}, u32[]{:S(2)}) collective-permute-start(f32[16,576]{1,0:T(8,128)S(1)} %constant_dynamic-slice_fusion), channel_id=1, source_target_pairs={{0,1},{1,0},{2,3},{3,2},{4,5},{5,4},{6,7},{7,6},{8,9},{9,8},{10,11... | collective-permute-start | bytes 110600 | tf_op jit(solution)/shard_map/ppermute | solution.py:88
  217.9 4.6 %collective-permute-start.7 = (f32[16,576]{1,0:T(8,128)S(1)}, f32[16,576]{1,0:T(8,128)S(1)}, u32[]{:S(2)}, u32[]{:S(2)}) collective-permute-start(f32[16,576]{1,0:T(8,128)S(1)} %dynamic-slice_add_fusion.3), channel_id=1, source_target_pairs={{0,64},{16,80},{32,96},{48,112},{64,0},{80,16},{96,32},{112,48},{1... | collective-permute-start | bytes 110600 | tf_op jit(solution)/shard_map/ppermute | solution.py:91
  224.3 4.4 %collective-permute-start.8 = (f32[16,576]{1,0:T(8,128)S(1)}, f32[16,576]{1,0:T(8,128)S(1)}, u32[]{:S(2)}, u32[]{:S(2)}) collective-permute-start(f32[16,576]{1,0:T(8,128)S(1)} %add.151), channel_id=1, source_target_pairs={{0,128},{16,144},{32,160},{48,176},{64,192},{80,208},{96,224},{112... | collective-permute-start | bytes 110600 | tf_op jit(solution)/shard_map/ppermute | solution.py:91
  230.1 4.9 %collective-permute-start.9 = (f32[16,576]{1,0:T(8,128)S(1)}, f32[16,576]{1,0:T(8,128)S(1)}, u32[]{:S(2)}, u32[]{:S(2)}) collective-permute-start(f32[16,576]{1,0:T(8,128)S(1)} %add.152), channel_id=1, source_target_pairs={{0,256},{16,272},{32,288},{48,304},{64,320},{80,336},{96,352},{112... | collective-permute-start | bytes 110600 | tf_op jit(solution)/shard_map/ppermute | solution.py:91
  235.0 3.7 %fusion.14 = bf16[4,128,4,128]{3,1,2,0:T(8,128)(2,1)} fusion(bf16[4,4,128,928]{2,3,1,0:T(8,128)(2,1)} %copy-done.1, bf16[128,4,128]{2,0,1:T(8,128)(2,1)S(1)} %copy-done.18, bf16[800,4,128]{2,0,1:T(8,128)(2,1)S(1)} %copy-done.12), kind=kOutput, calls=%fused_computation.24 | convolution fusion | flops 488964096 | bytes 5275648 | tf_op jit(solution)/shard_map/kgtm,mkd->tkgd/dot_general | solution.py:169
  238.7 12.0 %collective-permute-start.10 = (f32[16,576]{1,0:T(8,128)S(1)}, f32[16,576]{1,0:T(8,128)S(1)}, u32[]{:S(2)}, u32[]{:S(2)}) collective-permute-start(f32[16,576]{1,0:T(8,128)S(1)} %add.153), channel_id=1, source_target_pairs={{0,2},{1,3},{2,0},{3,1},{4,6},{5,7},{6,4},{7,5},{8,10},{9,11},{10,... | collective-permute-start | bytes 110600 | tf_op jit(solution)/shard_map/ppermute | solution.py:91
  250.8 3.4 %collective-permute-start.16 = (f32[56,512]{1,0:T(8,128)S(1)}, f32[56,512]{1,0:T(8,128)S(1)}, u32[]{:S(2)}, u32[]{:S(2)}) collective-permute-start(f32[56,512]{1,0:T(8,128)S(1)} %get-tuple-element.27), channel_id=1, source_target_pairs={{0,1},{1,2},{2,3},{3,4},{4,5},{5,6},{6,7},{7,8},{8,9},{9,10},{10,1... | collective-permute-start | bytes 344072
  255.1 1.9 collective-permute-start.17
  257.1 17.0 %collective-permute-start.11 = (f32[16,576]{1,0:T(8,128)S(1)}, f32[16,576]{1,0:T(8,128)S(1)}, u32[]{:S(2)}, u32[]{:S(2)}) collective-permute-start(f32[16,576]{1,0:T(8,128)S(1)} %add.154), channel_id=1, source_target_pairs={{0,4},{1,5},{2,6},{3,7},{4,0},{5,1},{6,2},{7,3},{8,12},{9,13},{10,... | collective-permute-start | bytes 110600 | tf_op jit(solution)/shard_map/ppermute | solution.py:91
  276.6 11.5 %collective-permute-start.12 = (f32[16,576]{1,0:T(8,128)S(1)}, f32[16,576]{1,0:T(8,128)S(1)}, u32[]{:S(2)}, u32[]{:S(2)}) collective-permute-start(f32[16,576]{1,0:T(8,128)S(1)} %add.155), channel_id=1, source_target_pairs={{0,8},{1,9},{2,10},{3,11},{4,12},{5,13},{6,14},{7,15},{8,0},{9,1},... | collective-permute-start | bytes 110600 | tf_op jit(solution)/shard_map/ppermute | solution.py:91
  289.4 4.8 %collective-permute-start.13 = (f32[16,576]{1,0:T(8,128)S(1)}, f32[16,576]{1,0:T(8,128)S(1)}, u32[]{:S(2)}, u32[]{:S(2)}) collective-permute-start(f32[16,576]{1,0:T(8,128)S(1)} %add.156), channel_id=1, source_target_pairs={{0,1},{1,0},{2,3},{3,2},{4,5},{5,4},{6,7},{7,6},{8,9},{9,8},{10,11... | collective-permute-start | bytes 110600 | tf_op jit(solution)/shard_map/ppermute | solution.py:94
  296.0 2.9 collective-permute-start.14
  299.0 2.1 collective-permute-done.14
  301.2 10.8 %collective-permute-start.15 = (f32[16,2304]{1,0:T(8,128)S(1)}, f32[16,2304]{1,0:T(8,128)S(1)}, u32[]{:S(2)}, u32[]{:S(2)}) collective-permute-start(f32[16,2304]{1,0:T(8,128)S(1)} %constant_dynamic-update-slice_fusion.6), channel_id=1, source_target_pairs={{0,16},{16,0},{32,48},{48,32},{64,80},{80,64},{96,112},{112,96},{1... | collective-permute-start | bytes 442376 | tf_op jit(solution)/shard_map/ppermute | solution.py:94
  (137 shorter events, 42.1 us)
Async XLA Ops:
  0.6 194.1 %copy-start = (bf16[1,1,128,4096]{3,2,1,0:T(8,128)(2,1)S(1)}, bf16[1,1,128,4096]{3,2,1,0:T(8,128)(2,1)}, u32[]{:S(2)}) copy-start(bf16[1,1,128,4096]{3,2,1,0:T(8,128)(2,1)} %param.13) | copy-start | bytes 3145732
  2.9 13.2 %collective-permute-start = (bf16[1,100,512]{2,1,0:T(8,128)(2,1)S(1)}, bf16[1,100,512]{2,1,0:T(8,128)(2,1)S(1)}, u32[]{:S(2)}, u32[]{:S(2)}) collective-permute-start(bf16[1,100,512]{2,1,0:T(8,128)(2,1)S(1)} %get-tuple-element.30), channel_id=1, source_target_pairs={{0,8},{1,9},{2,10},{3,11},{4,12},{5,13},{6,14},{7,15},{16,24},{17,... | collective-permute-start | bytes 307208 | tf_op jit(solution)/shard_map/ppermute | solution.py:135
  16.1 10.5 %collective-permute-start.1 = (bf16[2,100,512]{2,1,0:T(8,128)(2,1)S(1)}, bf16[2,100,512]{2,1,0:T(8,128)(2,1)S(1)}, u32[]{:S(2)}, u32[]{:S(2)}) collective-permute-start(bf16[2,100,512]{2,1,0:T(8,128)(2,1)S(1)} %pad_maximum_fusion.10), channel_id=1, source_target_pairs={{0,4},{1,5},{2,6},{3,7},{4,8},{5,9},{6,10},{7,11},{8,12},{9,13},{1... | collective-permute-start | bytes 614408 | tf_op jit(solution)/shard_map/ppermute | solution.py:135
  26.6 34.1 %copy-start.15 = (bf16[1,1,128,512]{3,2,1,0:T(8,128)(2,1)S(1)}, bf16[1,1,128,512]{3,2,1,0:T(8,128)(2,1)}, u32[]{:S(2)}) copy-start(bf16[1,1,128,512]{3,2,1,0:T(8,128)(2,1)} %param.10) | copy-start | bytes 393220
  26.7 34.2 %copy-start.16 = (bf16[1,1,128,512]{3,2,1,0:T(8,128)(2,1)S(1)}, bf16[1,1,128,512]{3,2,1,0:T(8,128)(2,1)}, u32[]{:S(2)}) copy-start(bf16[1,1,128,512]{3,2,1,0:T(8,128)(2,1)} %param.11) | copy-start | bytes 393220
  26.7 20.7 %collective-permute-start.2 = (bf16[4,100,512]{2,1,0:T(8,128)(2,1)S(1)}, bf16[4,100,512]{2,1,0:T(8,128)(2,1)S(1)}, u32[]{:S(2)}, u32[]{:S(2)}) collective-permute-start(bf16[4,100,512]{2,1,0:T(8,128)(2,1)S(1)} %pad_maximum_fusion.7), channel_id=1, source_target_pairs={{0,2},{1,3},{2,4},{3,5},{4,6},{5,7},{6,8},{7,9},{8,10},{9,11},{10,... | collective-permute-start | bytes 1228808 | tf_op jit(solution)/shard_map/ppermute | solution.py:135
  47.7 31.1 %collective-permute-start.3 = (bf16[8,100,512]{2,0,1:T(8,128)(2,1)S(1)}, bf16[8,100,512]{2,0,1:T(8,128)(2,1)}, u32[]{:S(2)}, u32[]{:S(2)}) collective-permute-start(bf16[8,100,512]{2,0,1:T(8,128)(2,1)S(1)} %copy.43), channel_id=1, source_target_pairs={{0,1},{1,2},{2,3},{3,4},{4,5},{5,6},{6,7},{7,8},{8,9},{9,10},{10,1... | collective-permute-start | bytes 2457608 | tf_op jit(solution)/shard_map/ppermute | solution.py:135
  88.8 3.1 copy-start.13
  189.4 5.3 %copy-start.20 = (bf16[16,512]{1,0:T(8,128)(2,1)S(1)}, bf16[16,512]{1,0:T(8,128)(2,1)}, u32[]{:S(2)}) copy-start(bf16[16,512]{1,0:T(8,128)(2,1)} %param.15) | copy-start | bytes 49156
  189.5 4.2 %collective-permute-start.18 = (f32[56,512]{1,0:T(8,128)S(1)}, f32[56,512]{1,0:T(8,128)S(1)}, u32[]{:S(2)}, u32[]{:S(2)}) collective-permute-start(f32[56,512]{1,0:T(8,128)S(1)} %get-tuple-element.28), channel_id=1, source_target_pairs={{0,1},{1,2},{2,3},{3,4},{4,5},{5,6},{6,7},{7,8},{8,9},{9,10},{10,1... | collective-permute-start | bytes 344072
  190.8 2.9 collective-permute-start.19
  193.0 2.1 copy-start.17
  195.2 39.8 %copy-start.12 = (bf16[800,4,128]{2,0,1:T(8,128)(2,1)S(1)}, bf16[800,4,128]{2,0,1:T(8,128)(2,1)}, u32[]{:S(2)}) copy-start(bf16[800,4,128]{2,0,1:T(8,128)(2,1)} %copy.48) | copy-start | bytes 2457604
  195.2 39.9 %copy-start.18 = (bf16[128,4,128]{2,0,1:T(8,128)(2,1)S(1)}, bf16[128,4,128]{2,0,1:T(8,128)(2,1)}, u32[]{:S(2)}) copy-start(bf16[128,4,128]{2,0,1:T(8,128)(2,1)} %copy.49) | copy-start | bytes 393220
  195.8 10.5 %collective-permute-start.4 = (f32[16,2304]{1,0:T(8,128)S(1)}, f32[16,2304]{1,0:T(8,128)S(1)}, u32[]{:S(2)}, u32[]{:S(2)}) collective-permute-start(f32[16,2304]{1,0:T(8,128)S(1)} %fusion.27), channel_id=1, source_target_pairs={{0,16},{16,0},{32,48},{48,32},{64,80},{80,64},{96,112},{112,96},{1... | collective-permute-start | bytes 442376 | tf_op jit(solution)/shard_map/ppermute | solution.py:88
  206.3 5.1 %collective-permute-start.5 = (f32[16,1152]{1,0:T(8,128)S(1)}, f32[16,1152]{1,0:T(8,128)S(1)}, u32[]{:S(2)}, u32[]{:S(2)}) collective-permute-start(f32[16,1152]{1,0:T(8,128)S(1)} %constant_dynamic-slice_fusion.1), channel_id=1, source_target_pairs={{0,32},{16,48},{32,0},{48,16},{64,96},{80,112},{96,64},{112,80},{1... | collective-permute-start | bytes 221192 | tf_op jit(solution)/shard_map/ppermute | solution.py:88
  211.5 6.3 %collective-permute-start.6 = (f32[16,576]{1,0:T(8,128)S(1)}, f32[16,576]{1,0:T(8,128)S(1)}, u32[]{:S(2)}, u32[]{:S(2)}) collective-permute-start(f32[16,576]{1,0:T(8,128)S(1)} %constant_dynamic-slice_fusion), channel_id=1, source_target_pairs={{0,1},{1,0},{2,3},{3,2},{4,5},{5,4},{6,7},{7,6},{8,9},{9,8},{10,11... | collective-permute-start | bytes 110600 | tf_op jit(solution)/shard_map/ppermute | solution.py:88
  217.9 6.4 %collective-permute-start.7 = (f32[16,576]{1,0:T(8,128)S(1)}, f32[16,576]{1,0:T(8,128)S(1)}, u32[]{:S(2)}, u32[]{:S(2)}) collective-permute-start(f32[16,576]{1,0:T(8,128)S(1)} %dynamic-slice_add_fusion.3), channel_id=1, source_target_pairs={{0,64},{16,80},{32,96},{48,112},{64,0},{80,16},{96,32},{112,48},{1... | collective-permute-start | bytes 110600 | tf_op jit(solution)/shard_map/ppermute | solution.py:91
  224.3 5.8 %collective-permute-start.8 = (f32[16,576]{1,0:T(8,128)S(1)}, f32[16,576]{1,0:T(8,128)S(1)}, u32[]{:S(2)}, u32[]{:S(2)}) collective-permute-start(f32[16,576]{1,0:T(8,128)S(1)} %add.151), channel_id=1, source_target_pairs={{0,128},{16,144},{32,160},{48,176},{64,192},{80,208},{96,224},{112... | collective-permute-start | bytes 110600 | tf_op jit(solution)/shard_map/ppermute | solution.py:91
  230.1 20.6 %copy-start.3 = (f32[928,128]{1,0:T(8,128)S(1)}, f32[928,128]{1,0:T(8,128)}, u32[]{:S(2)}) copy-start(f32[928,128]{1,0:T(8,128)} %copy-done.2) | copy-start | bytes 1425412
  230.1 20.6 %copy-start.5 = (f32[928,128]{1,0:T(8,128)S(1)}, f32[928,128]{1,0:T(8,128)}, u32[]{:S(2)}) copy-start(f32[928,128]{1,0:T(8,128)} %copy-done.4) | copy-start | bytes 1425412
  230.1 20.6 %copy-start.7 = (f32[928,128]{1,0:T(8,128)S(1)}, f32[928,128]{1,0:T(8,128)}, u32[]{:S(2)}) copy-start(f32[928,128]{1,0:T(8,128)} %copy-done.6) | copy-start | bytes 1425412
  230.1 8.6 %collective-permute-start.9 = (f32[16,576]{1,0:T(8,128)S(1)}, f32[16,576]{1,0:T(8,128)S(1)}, u32[]{:S(2)}, u32[]{:S(2)}) collective-permute-start(f32[16,576]{1,0:T(8,128)S(1)} %add.152), channel_id=1, source_target_pairs={{0,256},{16,272},{32,288},{48,304},{64,320},{80,336},{96,352},{112... | collective-permute-start | bytes 110600 | tf_op jit(solution)/shard_map/ppermute | solution.py:91
  238.7 15.4 %copy-start.14 = (bf16[4,128,4,128]{3,1,2,0:T(8,128)(2,1)S(1)}, bf16[4,128,4,128]{3,1,2,0:T(8,128)(2,1)}, u32[]{:S(2)}) copy-start(bf16[4,128,4,128]{3,1,2,0:T(8,128)(2,1)} %fusion.14) | copy-start | bytes 1572868
  238.7 18.4 %collective-permute-start.10 = (f32[16,576]{1,0:T(8,128)S(1)}, f32[16,576]{1,0:T(8,128)S(1)}, u32[]{:S(2)}, u32[]{:S(2)}) collective-permute-start(f32[16,576]{1,0:T(8,128)S(1)} %add.153), channel_id=1, source_target_pairs={{0,2},{1,3},{2,0},{3,1},{4,6},{5,7},{6,4},{7,5},{8,10},{9,11},{10,... | collective-permute-start | bytes 110600 | tf_op jit(solution)/shard_map/ppermute | solution.py:91
  250.8 24.0 %collective-permute-start.16 = (f32[56,512]{1,0:T(8,128)S(1)}, f32[56,512]{1,0:T(8,128)S(1)}, u32[]{:S(2)}, u32[]{:S(2)}) collective-permute-start(f32[56,512]{1,0:T(8,128)S(1)} %get-tuple-element.27), channel_id=1, source_target_pairs={{0,1},{1,2},{2,3},{3,4},{4,5},{5,6},{6,7},{7,8},{8,9},{9,10},{10,1... | collective-permute-start | bytes 344072
  255.1 19.6 %collective-permute-start.17 = (f32[34,512]{1,0:T(8,128)S(1)}, f32[34,512]{1,0:T(8,128)S(1)}, u32[]{:S(2)}, u32[]{:S(2)}) collective-permute-start(f32[34,512]{1,0:T(8,128)S(1)} %slice.86), channel_id=1, source_target_pairs={{0,2},{1,3},{2,4},{3,5},{4,6},{5,7},{6,8},{7,9},{8,10},{9,11},{10,... | collective-permute-start | bytes 208904
  257.1 19.5 %collective-permute-start.11 = (f32[16,576]{1,0:T(8,128)S(1)}, f32[16,576]{1,0:T(8,128)S(1)}, u32[]{:S(2)}, u32[]{:S(2)}) collective-permute-start(f32[16,576]{1,0:T(8,128)S(1)} %add.154), channel_id=1, source_target_pairs={{0,4},{1,5},{2,6},{3,7},{4,0},{5,1},{6,2},{7,3},{8,12},{9,13},{10,... | collective-permute-start | bytes 110600 | tf_op jit(solution)/shard_map/ppermute | solution.py:91
  276.6 12.9 %collective-permute-start.12 = (f32[16,576]{1,0:T(8,128)S(1)}, f32[16,576]{1,0:T(8,128)S(1)}, u32[]{:S(2)}, u32[]{:S(2)}) collective-permute-start(f32[16,576]{1,0:T(8,128)S(1)} %add.155), channel_id=1, source_target_pairs={{0,8},{1,9},{2,10},{3,11},{4,12},{5,13},{6,14},{7,15},{8,0},{9,1},... | collective-permute-start | bytes 110600 | tf_op jit(solution)/shard_map/ppermute | solution.py:91
  289.4 6.2 %collective-permute-start.13 = (f32[16,576]{1,0:T(8,128)S(1)}, f32[16,576]{1,0:T(8,128)S(1)}, u32[]{:S(2)}, u32[]{:S(2)}) collective-permute-start(f32[16,576]{1,0:T(8,128)S(1)} %add.156), channel_id=1, source_target_pairs={{0,1},{1,0},{2,3},{3,2},{4,5},{5,4},{6,7},{7,6},{8,9},{9,8},{10,11... | collective-permute-start | bytes 110600 | tf_op jit(solution)/shard_map/ppermute | solution.py:94
  296.0 5.1 %collective-permute-start.14 = (f32[16,1152]{1,0:T(8,128)S(1)}, f32[16,1152]{1,0:T(8,128)S(1)}, u32[]{:S(2)}, u32[]{:S(2)}) collective-permute-start(f32[16,1152]{1,0:T(8,128)S(1)} %dynamic_update_slice.27), channel_id=1, source_target_pairs={{0,32},{16,48},{32,0},{48,16},{64,96},{80,112},{96,64},{112,80},{1... | collective-permute-start | bytes 221192 | tf_op jit(solution)/shard_map/ppermute | solution.py:94
  301.2 11.8 %collective-permute-start.15 = (f32[16,2304]{1,0:T(8,128)S(1)}, f32[16,2304]{1,0:T(8,128)S(1)}, u32[]{:S(2)}, u32[]{:S(2)}) collective-permute-start(f32[16,2304]{1,0:T(8,128)S(1)} %constant_dynamic-update-slice_fusion.6), channel_id=1, source_target_pairs={{0,16},{16,0},{32,48},{48,32},{64,80},{80,64},{96,112},{112,96},{1... | collective-permute-start | bytes 442376 | tf_op jit(solution)/shard_map/ppermute | solution.py:94
  (9 other events, 11.7 us)

commit v13 on v11

--- a/solution.py
+++ b/solution.py
@@ -77,7 +77,7 @@
         if n & (n - 1):
             return lax.psum(x, ("dp", "ctx"))
         rounds += [(axis, 1 << j) for j in range(n.bit_length() - 1)]
-    nearest = [r for r in (("dp", 1), ("dp", 2), ("ctx", 1), ("dp", 8)) if r in rounds]
+    nearest = [r for r in (("dp", 1), ("ctx", 1), ("dp", 2)) if r in rounds]
     halving = [r for r in nearest if x.shape[-1] % (2 ** len(nearest)) == 0]
     cur = x
     for axis, k in halving:

time: 318 us -> 311 us (0.978); the launches traced: 314 us -> 312 us
    ppermute x4 -> x3, starting transfers between devices: 18.8 us -> 15.3 us  [mesh_sum(): cur = keep + lax.ppermute(give, axis, exchange_pairs(axis, k))]
    ppermute x5 -> x6, starting transfers between devices: 50 us -> 52.5 us  [mesh_sum(): cur = cur + lax.ppermute(cur, axis, exchange_pairs(axis, k))]
    ppermute x4 -> x3, waiting for transfers between devices: 6.72 us -> 4.99 us  [mesh_sum(): cur = keep + lax.ppermute(give, axis, exchange_pairs(axis, k))]
    ppermute x5 -> x6, waiting for transfers between devices: 4.79 us -> 6.45 us  [mesh_sum(): cur = cur + lax.ppermute(cur, axis, exchange_pairs(axis, k))]
    ppermute x4 -> x3, starting transfers between devices: 19.3 us -> 20.9 us  [mesh_sum(): other = lax.ppermute(cur, axis, exchange_pairs(axis, k))]
  transfers between devices with their start and end apart: 21 -> 20, of which waited for: 16 -> 15; matrix products, arithmetic and copies ran while one was open for 6% -> 6% of each run, Pallas kernels for 0% -> 0%
where the time goes in v13:
time: 311 us; the launch traced here: 312 us
  starting transfers between devices  136 us (44%)
  blocking collectives  86.1 us (28%)
  waiting for transfers between devices  38.6 us (12%)
  local copies, waits for them, and re-layouts  27.2 us (9%)
  matrix products  12.7 us (4%)
  other arithmetic  9.15 us (3%)
    unnamed x1, blocking collectives  86.1 us
    ppermute x6, starting transfers between devices, mesh_sum(): cur = cur + lax.ppermute(cur, axis, exchange_pairs(axis, k))  52.5 us
    ppermute x4, starting transfers between devices, per_device(): lax.ppermute(held, 'ctx', [(i, i + hop) for i in range(segment_list - hop)])  39.5 us
    ppermute x4, waiting for transfers between devices, per_device(): lax.ppermute(held, 'ctx', [(i, i + hop) for i in range(segment_list - hop)])  25.1 us
    ppermute x3, starting transfers between devices, mesh_sum(): other = lax.ppermute(cur, axis, exchange_pairs(axis, k))  20.9 us
    ppermute x3, starting transfers between devices, mesh_sum(): cur = keep + lax.ppermute(give, axis, exchange_pairs(axis, k))  15.3 us
    unnamed x53, local copies, waits for them, and re-layouts  7.59 us
    unnamed x4, starting transfers between devices  7.56 us
  transfers between devices with their start and end apart: 20, of which 15 were waited for; matrix products, arithmetic and copies ran while one was open for 6% of the time, Pallas kernels for 0%

profile of v13, /device:TPU:1, one launch (start us, length us, event | category | flops | bytes accessed | tf_op | source)
XLA Modules:
  0.0 312.5 jit_solution(11138070723105910115)
XLA Ops:
  3.0 11.5 %collective-permute-start = (bf16[1,100,512]{2,1,0:T(8,128)(2,1)S(1)}, bf16[1,100,512]{2,1,0:T(8,128)(2,1)S(1)}, u32[]{:S(2)}, u32[]{:S(2)}) collective-permute-start(bf16[1,100,512]{2,1,0:T(8,128)(2,1)S(1)} %get-tuple-element.30), channel_id=1, source_target_pairs={{0,8},{1,9},{2,10},{3,11},{4,12},{5,13},{6,14},{7,15},{16,24},{17,... | collective-permute-start | bytes 307208 | tf_op jit(solution)/shard_map/ppermute | solution.py:134
  16.1 7.5 %collective-permute-start.1 = (bf16[2,100,512]{2,1,0:T(8,128)(2,1)S(1)}, bf16[2,100,512]{2,1,0:T(8,128)(2,1)S(1)}, u32[]{:S(2)}, u32[]{:S(2)}) collective-permute-start(bf16[2,100,512]{2,1,0:T(8,128)(2,1)S(1)} %pad_maximum_fusion.10), channel_id=1, source_target_pairs={{0,4},{1,5},{2,6},{3,7},{4,8},{5,9},{6,10},{7,11},{8,12},{9,13},{1... | collective-permute-start | bytes 614408 | tf_op jit(solution)/shard_map/ppermute | solution.py:134
  23.6 3.0 collective-permute-done.1
  26.7 7.5 %collective-permute-start.2 = (bf16[4,100,512]{2,1,0:T(8,128)(2,1)S(1)}, bf16[4,100,512]{2,1,0:T(8,128)(2,1)S(1)}, u32[]{:S(2)}, u32[]{:S(2)}) collective-permute-start(bf16[4,100,512]{2,1,0:T(8,128)(2,1)S(1)} %pad_maximum_fusion.7), channel_id=1, source_target_pairs={{0,2},{1,3},{2,4},{3,5},{4,6},{5,7},{6,8},{7,9},{8,10},{9,11},{10,... | collective-permute-start | bytes 1228808 | tf_op jit(solution)/shard_map/ppermute | solution.py:134
  34.2 13.1 %collective-permute-done.2 = bf16[4,100,512]{2,1,0:T(8,128)(2,1)S(1)} collective-permute-done((bf16[4,100,512]{2,1,0:T(8,128)(2,1)S(1)}, bf16[4,100,512]{2,1,0:T(8,128)(2,1)S(1)}, u32[]{:S(2)}, u32[]{:S(2)}) %collective-permute-start.2) | collective-permute-done | bytes 409632 | tf_op jit(solution)/shard_map/ppermute | solution.py:134
  47.6 13.2 %collective-permute-start.3 = (bf16[8,100,512]{2,0,1:T(8,128)(2,1)S(1)}, bf16[8,100,512]{2,0,1:T(8,128)(2,1)}, u32[]{:S(2)}, u32[]{:S(2)}) collective-permute-start(bf16[8,100,512]{2,0,1:T(8,128)(2,1)S(1)} %copy.43), channel_id=1, source_target_pairs={{0,1},{1,2},{2,3},{3,4},{4,5},{5,6},{6,7},{7,8},{8,9},{9,10},{10,1... | collective-permute-start | bytes 2457608 | tf_op jit(solution)/shard_map/ppermute | solution.py:134
  63.2 2.2 squeeze.36
  70.5 8.8 %collective-permute-done.3 = bf16[8,100,512]{2,0,1:T(8,128)(2,1)} collective-permute-done((bf16[8,100,512]{2,0,1:T(8,128)(2,1)S(1)}, bf16[8,100,512]{2,0,1:T(8,128)(2,1)}, u32[]{:S(2)}, u32[]{:S(2)}) %collective-permute-start.3) | collective-permute-done | bytes 819232 | tf_op jit(solution)/shard_map/ppermute | solution.py:134
  79.3 2.3 copy_dynamic-update-slice_fusion
  81.6 2.1 gather_fusion.1
  86.3 2.2 copy.48
  89.4 3.1 fusion.7
  94.2 2.1 fusion.2
  96.3 2.3 fusion.4
  103.7 86.1 %fusion.47 = (f32[56,512]{1,0:T(8,128)S(1)}, f32[56,512]{1,0:T(8,128)S(1)}) fusion(f32[800,512]{1,0:T(8,128)S(1)} %pad_maximum_fusion.3, f32[800,512]{1,0:T(8,128)} %pad_maximum_fusion), kind=kCustom, calls=%all-reduce-scatter.2 | all-reduce-scatter fusion | flops 917505 | bytes 3508224
  196.4 8.8 %collective-permute-start.4 = (f32[16,2304]{1,0:T(8,128)S(1)}, f32[16,2304]{1,0:T(8,128)S(1)}, u32[]{:S(2)}, u32[]{:S(2)}) collective-permute-start(f32[16,2304]{1,0:T(8,128)S(1)} %fusion.27), channel_id=1, source_target_pairs={{0,16},{16,0},{32,48},{48,32},{64,80},{80,64},{96,112},{112,96},{1... | collective-permute-start | bytes 442376 | tf_op jit(solution)/shard_map/ppermute | solution.py:88
  206.3 2.8 collective-permute-start.5
  209.1 2.2 collective-permute-done.5
  211.5 3.7 %collective-permute-start.6 = (f32[16,576]{1,0:T(8,128)S(1)}, f32[16,576]{1,0:T(8,128)S(1)}, u32[]{:S(2)}, u32[]{:S(2)}) collective-permute-start(f32[16,576]{1,0:T(8,128)S(1)} %constant_dynamic-slice_fusion), channel_id=1, source_target_pairs={{0,32},{16,48},{32,0},{48,16},{64,96},{80,112},{96,64},{112,80},{1... | collective-permute-start | bytes 110600 | tf_op jit(solution)/shard_map/ppermute | solution.py:88
  217.0 6.7 %collective-permute-start.7 = (f32[16,576]{1,0:T(8,128)S(1)}, f32[16,576]{1,0:T(8,128)S(1)}, u32[]{:S(2)}, u32[]{:S(2)}) collective-permute-start(f32[16,576]{1,0:T(8,128)S(1)} %dynamic-slice_add_fusion.3), channel_id=1, source_target_pairs={{0,64},{16,80},{32,96},{48,112},{64,0},{80,16},{96,32},{112,48},{1... | collective-permute-start | bytes 110600 | tf_op jit(solution)/shard_map/ppermute | solution.py:91
  225.2 2.4 collective-permute-start.8
  227.6 2.3 collective-permute-done.8
  229.9 4.9 %collective-permute-start.9 = (f32[16,576]{1,0:T(8,128)S(1)}, f32[16,576]{1,0:T(8,128)S(1)}, u32[]{:S(2)}, u32[]{:S(2)}) collective-permute-start(f32[16,576]{1,0:T(8,128)S(1)} %add.146), channel_id=1, source_target_pairs={{0,256},{16,272},{32,288},{48,304},{64,320},{80,336},{96,352},{112... | collective-permute-start | bytes 110600 | tf_op jit(solution)/shard_map/ppermute | solution.py:91
  236.2 12.1 %collective-permute-start.10 = (f32[16,576]{1,0:T(8,128)S(1)}, f32[16,576]{1,0:T(8,128)S(1)}, u32[]{:S(2)}, u32[]{:S(2)}) collective-permute-start(f32[16,576]{1,0:T(8,128)S(1)} %add.147), channel_id=1, source_target_pairs={{0,2},{1,3},{2,0},{3,1},{4,6},{5,7},{6,4},{7,5},{8,10},{9,11},{10,... | collective-permute-start | bytes 110600 | tf_op jit(solution)/shard_map/ppermute | solution.py:91
  249.7 16.6 %collective-permute-start.11 = (f32[16,576]{1,0:T(8,128)S(1)}, f32[16,576]{1,0:T(8,128)S(1)}, u32[]{:S(2)}, u32[]{:S(2)}) collective-permute-start(f32[16,576]{1,0:T(8,128)S(1)} %add.148), channel_id=1, source_target_pairs={{0,4},{1,5},{2,6},{3,7},{4,0},{5,1},{6,2},{7,3},{8,12},{9,13},{10,... | collective-permute-start | bytes 110600 | tf_op jit(solution)/shard_map/ppermute | solution.py:91
  266.3 3.7 %fusion.14 = bf16[4,128,4,128]{3,1,2,0:T(8,128)(2,1)} fusion(bf16[4,4,128,928]{2,3,1,0:T(8,128)(2,1)} %copy-done.1, bf16[128,4,128]{2,0,1:T(8,128)(2,1)S(1)} %copy-done.18, bf16[800,4,128]{2,0,1:T(8,128)(2,1)S(1)} %copy-done.12), kind=kOutput, calls=%fused_computation.24 | convolution fusion | flops 488964096 | bytes 5275648 | tf_op jit(solution)/shard_map/kgtm,mkd->tkgd/dot_general | solution.py:168
  270.0 9.8 %collective-permute-start.12 = (f32[16,576]{1,0:T(8,128)S(1)}, f32[16,576]{1,0:T(8,128)S(1)}, u32[]{:S(2)}, u32[]{:S(2)}) collective-permute-start(f32[16,576]{1,0:T(8,128)S(1)} %add.149), channel_id=1, source_target_pairs={{0,8},{1,9},{2,10},{3,11},{4,12},{5,13},{6,14},{7,15},{8,0},{9,1},... | collective-permute-start | bytes 110600 | tf_op jit(solution)/shard_map/ppermute | solution.py:91
  279.8 2.8 collective-permute-start.16
  283.6 2.2 collective-permute-start.17
  285.9 3.4 %collective-permute-start.13 = (f32[16,576]{1,0:T(8,128)S(1)}, f32[16,576]{1,0:T(8,128)S(1)}, u32[]{:S(2)}, u32[]{:S(2)}) collective-permute-start(f32[16,576]{1,0:T(8,128)S(1)} %add.150), channel_id=1, source_target_pairs={{0,32},{16,48},{32,0},{48,16},{64,96},{80,112},{96,64},{112,80},{1... | collective-permute-start | bytes 110600 | tf_op jit(solution)/shard_map/ppermute | solution.py:94
  290.7 5.5 %collective-permute-start.14 = (f32[16,1152]{1,0:T(8,128)S(1)}, f32[16,1152]{1,0:T(8,128)S(1)}, u32[]{:S(2)}, u32[]{:S(2)}) collective-permute-start(f32[16,1152]{1,0:T(8,128)S(1)} %maximum_select_fusion.2), channel_id=1, source_target_pairs={{0,1},{1,0},{2,3},{3,2},{4,5},{5,4},{6,7},{7,6},{8,9},{9,8},{10,11... | collective-permute-start | bytes 221192 | tf_op jit(solution)/shard_map/ppermute | solution.py:94
  298.1 12.0 %collective-permute-start.15 = (f32[16,2304]{1,0:T(8,128)S(1)}, f32[16,2304]{1,0:T(8,128)S(1)}, u32[]{:S(2)}, u32[]{:S(2)}) collective-permute-start(f32[16,2304]{1,0:T(8,128)S(1)} %maximum_select_fusion.1), channel_id=1, source_target_pairs={{0,16},{16,0},{32,48},{48,32},{64,80},{80,64},{96,112},{112,96},{1... | collective-permute-start | bytes 442376 | tf_op jit(solution)/shard_map/ppermute | solution.py:94
  (131 shorter events, 41.0 us)
Async XLA Ops:
  0.6 194.7 %copy-start = (bf16[1,1,128,4096]{3,2,1,0:T(8,128)(2,1)S(1)}, bf16[1,1,128,4096]{3,2,1,0:T(8,128)(2,1)}, u32[]{:S(2)}) copy-start(bf16[1,1,128,4096]{3,2,1,0:T(8,128)(2,1)} %param.13) | copy-start | bytes 3145732
  3.0 13.2 %collective-permute-start = (bf16[1,100,512]{2,1,0:T(8,128)(2,1)S(1)}, bf16[1,100,512]{2,1,0:T(8,128)(2,1)S(1)}, u32[]{:S(2)}, u32[]{:S(2)}) collective-permute-start(bf16[1,100,512]{2,1,0:T(8,128)(2,1)S(1)} %get-tuple-element.30), channel_id=1, source_target_pairs={{0,8},{1,9},{2,10},{3,11},{4,12},{5,13},{6,14},{7,15},{16,24},{17,... | collective-permute-start | bytes 307208 | tf_op jit(solution)/shard_map/ppermute | solution.py:134
  16.1 10.5 %collective-permute-start.1 = (bf16[2,100,512]{2,1,0:T(8,128)(2,1)S(1)}, bf16[2,100,512]{2,1,0:T(8,128)(2,1)S(1)}, u32[]{:S(2)}, u32[]{:S(2)}) collective-permute-start(bf16[2,100,512]{2,1,0:T(8,128)(2,1)S(1)} %pad_maximum_fusion.10), channel_id=1, source_target_pairs={{0,4},{1,5},{2,6},{3,7},{4,8},{5,9},{6,10},{7,11},{8,12},{9,13},{1... | collective-permute-start | bytes 614408 | tf_op jit(solution)/shard_map/ppermute | solution.py:134
  26.6 34.1 %copy-start.15 = (bf16[1,1,128,512]{3,2,1,0:T(8,128)(2,1)S(1)}, bf16[1,1,128,512]{3,2,1,0:T(8,128)(2,1)}, u32[]{:S(2)}) copy-start(bf16[1,1,128,512]{3,2,1,0:T(8,128)(2,1)} %param.10) | copy-start | bytes 393220
  26.7 34.2 %copy-start.16 = (bf16[1,1,128,512]{3,2,1,0:T(8,128)(2,1)S(1)}, bf16[1,1,128,512]{3,2,1,0:T(8,128)(2,1)}, u32[]{:S(2)}) copy-start(bf16[1,1,128,512]{3,2,1,0:T(8,128)(2,1)} %param.11) | copy-start | bytes 393220
  26.7 20.6 %collective-permute-start.2 = (bf16[4,100,512]{2,1,0:T(8,128)(2,1)S(1)}, bf16[4,100,512]{2,1,0:T(8,128)(2,1)S(1)}, u32[]{:S(2)}, u32[]{:S(2)}) collective-permute-start(bf16[4,100,512]{2,1,0:T(8,128)(2,1)S(1)} %pad_maximum_fusion.7), channel_id=1, source_target_pairs={{0,2},{1,3},{2,4},{3,5},{4,6},{5,7},{6,8},{7,9},{8,10},{9,11},{10,... | collective-permute-start | bytes 1228808 | tf_op jit(solution)/shard_map/ppermute | solution.py:134
  47.6 31.7 %collective-permute-start.3 = (bf16[8,100,512]{2,0,1:T(8,128)(2,1)S(1)}, bf16[8,100,512]{2,0,1:T(8,128)(2,1)}, u32[]{:S(2)}, u32[]{:S(2)}) collective-permute-start(bf16[8,100,512]{2,0,1:T(8,128)(2,1)S(1)} %copy.43), channel_id=1, source_target_pairs={{0,1},{1,2},{2,3},{3,4},{4,5},{5,6},{6,7},{7,8},{8,9},{9,10},{10,1... | collective-permute-start | bytes 2457608 | tf_op jit(solution)/shard_map/ppermute | solution.py:134
  89.3 3.1 copy-start.13
  189.9 5.5 %copy-start.20 = (bf16[16,512]{1,0:T(8,128)(2,1)S(1)}, bf16[16,512]{1,0:T(8,128)(2,1)}, u32[]{:S(2)}) copy-start(bf16[16,512]{1,0:T(8,128)(2,1)} %param.15) | copy-start | bytes 49156
  189.9 4.1 %collective-permute-start.18 = (f32[56,512]{1,0:T(8,128)S(1)}, f32[56,512]{1,0:T(8,128)S(1)}, u32[]{:S(2)}, u32[]{:S(2)}) collective-permute-start(f32[56,512]{1,0:T(8,128)S(1)} %get-tuple-element.28), channel_id=1, source_target_pairs={{0,1},{1,2},{2,3},{3,4},{4,5},{5,6},{6,7},{7,8},{8,9},{9,10},{10,1... | collective-permute-start | bytes 344072
  191.2 2.8 collective-permute-start.19
  193.4 2.3 copy-start.17
  195.8 70.5 %copy-start.12 = (bf16[800,4,128]{2,0,1:T(8,128)(2,1)S(1)}, bf16[800,4,128]{2,0,1:T(8,128)(2,1)}, u32[]{:S(2)}) copy-start(bf16[800,4,128]{2,0,1:T(8,128)(2,1)} %copy.48) | copy-start | bytes 2457604
  195.8 70.5 %copy-start.18 = (bf16[128,4,128]{2,0,1:T(8,128)(2,1)S(1)}, bf16[128,4,128]{2,0,1:T(8,128)(2,1)}, u32[]{:S(2)}) copy-start(bf16[128,4,128]{2,0,1:T(8,128)(2,1)} %copy.49) | copy-start | bytes 393220
  196.4 9.8 %collective-permute-start.4 = (f32[16,2304]{1,0:T(8,128)S(1)}, f32[16,2304]{1,0:T(8,128)S(1)}, u32[]{:S(2)}, u32[]{:S(2)}) collective-permute-start(f32[16,2304]{1,0:T(8,128)S(1)} %fusion.27), channel_id=1, source_target_pairs={{0,16},{16,0},{32,48},{48,32},{64,80},{80,64},{96,112},{112,96},{1... | collective-permute-start | bytes 442376 | tf_op jit(solution)/shard_map/ppermute | solution.py:88
  206.3 5.1 %collective-permute-start.5 = (f32[16,1152]{1,0:T(8,128)S(1)}, f32[16,1152]{1,0:T(8,128)S(1)}, u32[]{:S(2)}, u32[]{:S(2)}) collective-permute-start(f32[16,1152]{1,0:T(8,128)S(1)} %constant_dynamic-slice_fusion.1), channel_id=1, source_target_pairs={{0,1},{1,0},{2,3},{3,2},{4,5},{5,4},{6,7},{7,6},{8,9},{9,8},{10,11... | collective-permute-start | bytes 221192 | tf_op jit(solution)/shard_map/ppermute | solution.py:88
  211.5 5.5 %collective-permute-start.6 = (f32[16,576]{1,0:T(8,128)S(1)}, f32[16,576]{1,0:T(8,128)S(1)}, u32[]{:S(2)}, u32[]{:S(2)}) collective-permute-start(f32[16,576]{1,0:T(8,128)S(1)} %constant_dynamic-slice_fusion), channel_id=1, source_target_pairs={{0,32},{16,48},{32,0},{48,16},{64,96},{80,112},{96,64},{112,80},{1... | collective-permute-start | bytes 110600 | tf_op jit(solution)/shard_map/ppermute | solution.py:88
  217.0 8.1 %collective-permute-start.7 = (f32[16,576]{1,0:T(8,128)S(1)}, f32[16,576]{1,0:T(8,128)S(1)}, u32[]{:S(2)}, u32[]{:S(2)}) collective-permute-start(f32[16,576]{1,0:T(8,128)S(1)} %dynamic-slice_add_fusion.3), channel_id=1, source_target_pairs={{0,64},{16,80},{32,96},{48,112},{64,0},{80,16},{96,32},{112,48},{1... | collective-permute-start | bytes 110600 | tf_op jit(solution)/shard_map/ppermute | solution.py:91
  225.2 4.7 %collective-permute-start.8 = (f32[16,576]{1,0:T(8,128)S(1)}, f32[16,576]{1,0:T(8,128)S(1)}, u32[]{:S(2)}, u32[]{:S(2)}) collective-permute-start(f32[16,576]{1,0:T(8,128)S(1)} %add.145), channel_id=1, source_target_pairs={{0,128},{16,144},{32,160},{48,176},{64,192},{80,208},{96,224},{112... | collective-permute-start | bytes 110600 | tf_op jit(solution)/shard_map/ppermute | solution.py:91
  229.9 6.3 %collective-permute-start.9 = (f32[16,576]{1,0:T(8,128)S(1)}, f32[16,576]{1,0:T(8,128)S(1)}, u32[]{:S(2)}, u32[]{:S(2)}) collective-permute-start(f32[16,576]{1,0:T(8,128)S(1)} %add.146), channel_id=1, source_target_pairs={{0,256},{16,272},{32,288},{48,304},{64,320},{80,336},{96,352},{112... | collective-permute-start | bytes 110600 | tf_op jit(solution)/shard_map/ppermute | solution.py:91
  236.2 13.4 %collective-permute-start.10 = (f32[16,576]{1,0:T(8,128)S(1)}, f32[16,576]{1,0:T(8,128)S(1)}, u32[]{:S(2)}, u32[]{:S(2)}) collective-permute-start(f32[16,576]{1,0:T(8,128)S(1)} %add.147), channel_id=1, source_target_pairs={{0,2},{1,3},{2,0},{3,1},{4,6},{5,7},{6,4},{7,5},{8,10},{9,11},{10,... | collective-permute-start | bytes 110600 | tf_op jit(solution)/shard_map/ppermute | solution.py:91
  249.6 30.1 %copy-start.3 = (f32[928,128]{1,0:T(8,128)S(1)}, f32[928,128]{1,0:T(8,128)}, u32[]{:S(2)}) copy-start(f32[928,128]{1,0:T(8,128)} %copy-done.2) | copy-start | bytes 1425412
  249.6 30.1 %copy-start.5 = (f32[928,128]{1,0:T(8,128)S(1)}, f32[928,128]{1,0:T(8,128)}, u32[]{:S(2)}) copy-start(f32[928,128]{1,0:T(8,128)} %copy-done.4) | copy-start | bytes 1425412
  249.6 30.1 %copy-start.7 = (f32[928,128]{1,0:T(8,128)S(1)}, f32[928,128]{1,0:T(8,128)}, u32[]{:S(2)}) copy-start(f32[928,128]{1,0:T(8,128)} %copy-done.6) | copy-start | bytes 1425412
  249.7 20.3 %collective-permute-start.11 = (f32[16,576]{1,0:T(8,128)S(1)}, f32[16,576]{1,0:T(8,128)S(1)}, u32[]{:S(2)}, u32[]{:S(2)}) collective-permute-start(f32[16,576]{1,0:T(8,128)S(1)} %add.148), channel_id=1, source_target_pairs={{0,4},{1,5},{2,6},{3,7},{4,0},{5,1},{6,2},{7,3},{8,12},{9,13},{10,... | collective-permute-start | bytes 110600 | tf_op jit(solution)/shard_map/ppermute | solution.py:91
  270.0 12.7 %copy-start.14 = (bf16[4,128,4,128]{3,1,2,0:T(8,128)(2,1)S(1)}, bf16[4,128,4,128]{3,1,2,0:T(8,128)(2,1)}, u32[]{:S(2)}) copy-start(bf16[4,128,4,128]{3,1,2,0:T(8,128)(2,1)} %fusion.14) | copy-start | bytes 1572868
  270.0 15.9 %collective-permute-start.12 = (f32[16,576]{1,0:T(8,128)S(1)}, f32[16,576]{1,0:T(8,128)S(1)}, u32[]{:S(2)}, u32[]{:S(2)}) collective-permute-start(f32[16,576]{1,0:T(8,128)S(1)} %add.149), channel_id=1, source_target_pairs={{0,8},{1,9},{2,10},{3,11},{4,12},{5,13},{6,14},{7,15},{8,0},{9,1},... | collective-permute-start | bytes 110600 | tf_op jit(solution)/shard_map/ppermute | solution.py:91
  279.8 10.1 %collective-permute-start.16 = (f32[56,512]{1,0:T(8,128)S(1)}, f32[56,512]{1,0:T(8,128)S(1)}, u32[]{:S(2)}, u32[]{:S(2)}) collective-permute-start(f32[56,512]{1,0:T(8,128)S(1)} %get-tuple-element.27), channel_id=1, source_target_pairs={{0,1},{1,2},{2,3},{3,4},{4,5},{5,6},{6,7},{7,8},{8,9},{9,10},{10,1... | collective-permute-start | bytes 344072
  283.6 6.3 %collective-permute-start.17 = (f32[34,512]{1,0:T(8,128)S(1)}, f32[34,512]{1,0:T(8,128)S(1)}, u32[]{:S(2)}, u32[]{:S(2)}) collective-permute-start(f32[34,512]{1,0:T(8,128)S(1)} %slice.86), channel_id=1, source_target_pairs={{0,2},{1,3},{2,4},{3,5},{4,6},{5,7},{6,8},{7,9},{8,10},{9,11},{10,... | collective-permute-start | bytes 208904
  285.9 4.7 %collective-permute-start.13 = (f32[16,576]{1,0:T(8,128)S(1)}, f32[16,576]{1,0:T(8,128)S(1)}, u32[]{:S(2)}, u32[]{:S(2)}) collective-permute-start(f32[16,576]{1,0:T(8,128)S(1)} %add.150), channel_id=1, source_target_pairs={{0,32},{16,48},{32,0},{48,16},{64,96},{80,112},{96,64},{112,80},{1... | collective-permute-start | bytes 110600 | tf_op jit(solution)/shard_map/ppermute | solution.py:94
  290.7 7.4 %collective-permute-start.14 = (f32[16,1152]{1,0:T(8,128)S(1)}, f32[16,1152]{1,0:T(8,128)S(1)}, u32[]{:S(2)}, u32[]{:S(2)}) collective-permute-start(f32[16,1152]{1,0:T(8,128)S(1)} %maximum_select_fusion.2), channel_id=1, source_target_pairs={{0,1},{1,0},{2,3},{3,2},{4,5},{5,4},{6,7},{7,6},{8,9},{9,8},{10,11... | collective-permute-start | bytes 221192 | tf_op jit(solution)/shard_map/ppermute | solution.py:94
  298.1 13.0 %collective-permute-start.15 = (f32[16,2304]{1,0:T(8,128)S(1)}, f32[16,2304]{1,0:T(8,128)S(1)}, u32[]{:S(2)}, u32[]{:S(2)}) collective-permute-start(f32[16,2304]{1,0:T(8,128)S(1)} %maximum_select_fusion.1), channel_id=1, source_target_pairs={{0,16},{16,0},{32,48},{48,32},{64,80},{80,64},{96,112},{112,96},{1... | collective-permute-start | bytes 442376 | tf_op jit(solution)/shard_map/ppermute | solution.py:94
  (9 other events, 11.7 us)

commit v14 on v13

--- a/solution.py
+++ b/solution.py
@@ -77,7 +77,7 @@
         if n & (n - 1):
             return lax.psum(x, ("dp", "ctx"))
         rounds += [(axis, 1 << j) for j in range(n.bit_length() - 1)]
-    nearest = [r for r in (("dp", 1), ("ctx", 1), ("dp", 2)) if r in rounds]
+    nearest = [r for r in (("dp", 1), ("ctx", 1), ("dp", 2), ("dp", 8)) if r in rounds]
     halving = [r for r in nearest if x.shape[-1] % (2 ** len(nearest)) == 0]
     cur = x
     for axis, k in halving:

time: 311 us -> 317 us (1.019); the launches traced: 312 us -> 315 us
  waiting for transfers between devices: 38.6 us -> 41.9 us
    ppermute x6 -> x5, starting transfers between devices: 52.5 us -> 46.9 us  [mesh_sum(): cur = cur + lax.ppermute(cur, axis, exchange_pairs(axis, k))]
    ppermute x3 -> x4, starting transfers between devices: 15.3 us -> 17.9 us  [mesh_sum(): cur = keep + lax.ppermute(give, axis, exchange_pairs(axis, k))]
    ppermute x3 -> x4, waiting for transfers between devices: 4.99 us -> 6.92 us  [mesh_sum(): cur = keep + lax.ppermute(give, axis, exchange_pairs(axis, k))]
    ppermute x6 -> x5, waiting for transfers between devices: 6.45 us -> 5.41 us  [mesh_sum(): cur = cur + lax.ppermute(cur, axis, exchange_pairs(axis, k))]
    ppermute x3 -> x4, starting transfers between devices: 20.9 us -> 21.9 us  [mesh_sum(): other = lax.ppermute(cur, axis, exchange_pairs(axis, k))]
  transfers between devices with their start and end apart: 20 -> 21, of which waited for: 15 -> 16; matrix products, arithmetic and copies ran while one was open for 6% -> 6% of each run, Pallas kernels for 0% -> 0%
where the time goes in v14:
time: 317 us; the launch traced here: 315 us
  starting transfers between devices  133 us (42%)
  blocking collectives  87.2 us (28%)
  waiting for transfers between devices  41.9 us (13%)
  local copies, waits for them, and re-layouts  27.3 us (9%)
  matrix products  12.7 us (4%)
  other arithmetic  9.28 us (3%)
    unnamed x1, blocking collectives  87.2 us
    ppermute x5, starting transfers between devices, mesh_sum(): cur = cur + lax.ppermute(cur, axis, exchange_pairs(axis, k))  46.9 us
    ppermute x4, starting transfers between devices, per_device(): lax.ppermute(held, 'ctx', [(i, i + hop) for i in range(segment_list - hop)])  39.4 us
    ppermute x4, waiting for transfers between devices, per_device(): lax.ppermute(held, 'ctx', [(i, i + hop) for i in range(segment_list - hop)])  24.8 us
    ppermute x4, starting transfers between devices, mesh_sum(): other = lax.ppermute(cur, axis, exchange_pairs(axis, k))  21.9 us
    ppermute x4, starting transfers between devices, mesh_sum(): cur = keep + lax.ppermute(give, axis, exchange_pairs(axis, k))  17.9 us
    unnamed x53, local copies, waits for them, and re-layouts  7.6 us
    unnamed x4, starting transfers between devices  7.3 us
  transfers between devices with their start and end apart: 21, of which 16 were waited for; matrix products, arithmetic and copies ran while one was open for 6% of the time, Pallas kernels for 0%

profile of v14, /device:TPU:1, one launch (start us, length us, event | category | flops | bytes accessed | tf_op | source)
XLA Modules:
  0.0 314.8 jit_solution(9261916400140855278)
XLA Ops:
  3.0 11.5 %collective-permute-start = (bf16[1,100,512]{2,1,0:T(8,128)(2,1)S(1)}, bf16[1,100,512]{2,1,0:T(8,128)(2,1)S(1)}, u32[]{:S(2)}, u32[]{:S(2)}) collective-permute-start(bf16[1,100,512]{2,1,0:T(8,128)(2,1)S(1)} %get-tuple-element.30), channel_id=1, source_target_pairs={{0,8},{1,9},{2,10},{3,11},{4,12},{5,13},{6,14},{7,15},{16,24},{17,... | collective-permute-start | bytes 307208 | tf_op jit(solution)/shard_map/ppermute | solution.py:134
  16.1 7.5 %collective-permute-start.1 = (bf16[2,100,512]{2,1,0:T(8,128)(2,1)S(1)}, bf16[2,100,512]{2,1,0:T(8,128)(2,1)S(1)}, u32[]{:S(2)}, u32[]{:S(2)}) collective-permute-start(bf16[2,100,512]{2,1,0:T(8,128)(2,1)S(1)} %pad_maximum_fusion.10), channel_id=1, source_target_pairs={{0,4},{1,5},{2,6},{3,7},{4,8},{5,9},{6,10},{7,11},{8,12},{9,13},{1... | collective-permute-start | bytes 614408 | tf_op jit(solution)/shard_map/ppermute | solution.py:134
  23.6 3.0 collective-permute-done.1
  26.7 7.4 %collective-permute-start.2 = (bf16[4,100,512]{2,1,0:T(8,128)(2,1)S(1)}, bf16[4,100,512]{2,1,0:T(8,128)(2,1)S(1)}, u32[]{:S(2)}, u32[]{:S(2)}) collective-permute-start(bf16[4,100,512]{2,1,0:T(8,128)(2,1)S(1)} %pad_maximum_fusion.7), channel_id=1, source_target_pairs={{0,2},{1,3},{2,4},{3,5},{4,6},{5,7},{6,8},{7,9},{8,10},{9,11},{10,... | collective-permute-start | bytes 1228808 | tf_op jit(solution)/shard_map/ppermute | solution.py:134
  34.2 13.2 %collective-permute-done.2 = bf16[4,100,512]{2,1,0:T(8,128)(2,1)S(1)} collective-permute-done((bf16[4,100,512]{2,1,0:T(8,128)(2,1)S(1)}, bf16[4,100,512]{2,1,0:T(8,128)(2,1)S(1)}, u32[]{:S(2)}, u32[]{:S(2)}) %collective-permute-start.2) | collective-permute-done | bytes 409632 | tf_op jit(solution)/shard_map/ppermute | solution.py:134
  47.7 13.0 %collective-permute-start.3 = (bf16[8,100,512]{2,0,1:T(8,128)(2,1)S(1)}, bf16[8,100,512]{2,0,1:T(8,128)(2,1)}, u32[]{:S(2)}, u32[]{:S(2)}) collective-permute-start(bf16[8,100,512]{2,0,1:T(8,128)(2,1)S(1)} %copy.43), channel_id=1, source_target_pairs={{0,1},{1,2},{2,3},{3,4},{4,5},{5,6},{6,7},{7,8},{8,9},{9,10},{10,1... | collective-permute-start | bytes 2457608 | tf_op jit(solution)/shard_map/ppermute | solution.py:134
  63.2 2.2 squeeze.36
  70.5 8.3 %collective-permute-done.3 = bf16[8,100,512]{2,0,1:T(8,128)(2,1)} collective-permute-done((bf16[8,100,512]{2,0,1:T(8,128)(2,1)S(1)}, bf16[8,100,512]{2,0,1:T(8,128)(2,1)}, u32[]{:S(2)}, u32[]{:S(2)}) %collective-permute-start.3) | collective-permute-done | bytes 819232 | tf_op jit(solution)/shard_map/ppermute | solution.py:134
  78.8 2.3 copy_dynamic-update-slice_fusion
  81.1 2.1 gather_fusion.1
  85.8 2.2 copy.48
  88.8 3.1 fusion.7
  93.7 2.2 fusion.2
  95.8 2.3 fusion.4
  103.2 87.2 %fusion.47 = (f32[56,512]{1,0:T(8,128)S(1)}, f32[56,512]{1,0:T(8,128)S(1)}) fusion(f32[800,512]{1,0:T(8,128)S(1)} %pad_maximum_fusion.3, f32[800,512]{1,0:T(8,128)} %pad_maximum_fusion), kind=kCustom, calls=%all-reduce-scatter.2 | all-reduce-scatter fusion | flops 917505 | bytes 3508224
  197.0 8.0 %collective-permute-start.4 = (f32[16,2304]{1,0:T(8,128)S(1)}, f32[16,2304]{1,0:T(8,128)S(1)}, u32[]{:S(2)}, u32[]{:S(2)}) collective-permute-start(f32[16,2304]{1,0:T(8,128)S(1)} %fusion.27), channel_id=1, source_target_pairs={{0,16},{16,0},{32,48},{48,32},{64,80},{80,64},{96,112},{112,96},{1... | collective-permute-start | bytes 442376 | tf_op jit(solution)/shard_map/ppermute | solution.py:88
  206.0 3.0 collective-permute-start.5
  209.1 2.0 collective-permute-done.5
  213.2 2.8 collective-permute-done.6
  216.1 5.0 %collective-permute-start.7 = (f32[16,288]{1,0:T(8,128)S(1)}, f32[16,288]{1,0:T(8,128)S(1)}, u32[]{:S(2)}, u32[]{:S(2)}) collective-permute-start(f32[16,288]{1,0:T(8,128)S(1)} %constant_dynamic-slice_fusion), channel_id=1, source_target_pairs={{0,128},{16,144},{32,160},{48,176},{64,192},{80,208},{96,224},{112... | collective-permute-start | bytes 55304 | tf_op jit(solution)/shard_map/ppermute | solution.py:88
  222.4 6.7 %collective-permute-start.8 = (f32[16,288]{1,0:T(8,128)S(1)}, f32[16,288]{1,0:T(8,128)S(1)}, u32[]{:S(2)}, u32[]{:S(2)}) collective-permute-start(f32[16,288]{1,0:T(8,128)S(1)} %dynamic-slice_add_fusion.4), channel_id=1, source_target_pairs={{0,64},{16,80},{32,96},{48,112},{64,0},{80,16},{96,32},{112,48},{1... | collective-permute-start | bytes 55304 | tf_op jit(solution)/shard_map/ppermute | solution.py:91
  230.3 4.2 %collective-permute-start.9 = (f32[16,288]{1,0:T(8,128)S(1)}, f32[16,288]{1,0:T(8,128)S(1)}, u32[]{:S(2)}, u32[]{:S(2)}) collective-permute-start(f32[16,288]{1,0:T(8,128)S(1)} %add.160), channel_id=1, source_target_pairs={{0,256},{16,272},{32,288},{48,304},{64,320},{80,336},{96,352},{112... | collective-permute-start | bytes 55304 | tf_op jit(solution)/shard_map/ppermute | solution.py:91
  236.4 7.0 %collective-permute-start.10 = (f32[16,288]{1,0:T(8,128)S(1)}, f32[16,288]{1,0:T(8,128)S(1)}, u32[]{:S(2)}, u32[]{:S(2)}) collective-permute-start(f32[16,288]{1,0:T(8,128)S(1)} %add.161), channel_id=1, source_target_pairs={{0,2},{1,3},{2,0},{3,1},{4,6},{5,7},{6,4},{7,5},{8,10},{9,11},{10,... | collective-permute-start | bytes 55304 | tf_op jit(solution)/shard_map/ppermute | solution.py:91
  244.6 18.3 %collective-permute-start.11 = (f32[16,288]{1,0:T(8,128)S(1)}, f32[16,288]{1,0:T(8,128)S(1)}, u32[]{:S(2)}, u32[]{:S(2)}) collective-permute-start(f32[16,288]{1,0:T(8,128)S(1)} %add.162), channel_id=1, source_target_pairs={{0,4},{1,5},{2,6},{3,7},{4,0},{5,1},{6,2},{7,3},{8,12},{9,13},{10,... | collective-permute-start | bytes 55304 | tf_op jit(solution)/shard_map/ppermute | solution.py:91
  264.1 10.7 %collective-permute-start.12 = (f32[16,288]{1,0:T(8,128)S(1)}, f32[16,288]{1,0:T(8,128)S(1)}, u32[]{:S(2)}, u32[]{:S(2)}) collective-permute-start(f32[16,288]{1,0:T(8,128)S(1)} %add.163), channel_id=1, source_target_pairs={{0,8},{1,9},{2,10},{3,11},{4,12},{5,13},{6,14},{7,15},{8,0},{9,1},... | collective-permute-start | bytes 55304 | tf_op jit(solution)/shard_map/ppermute | solution.py:91
  274.8 3.7 %fusion.14 = bf16[4,128,4,128]{3,1,2,0:T(8,128)(2,1)} fusion(bf16[4,4,128,928]{2,3,1,0:T(8,128)(2,1)} %copy-done.1, bf16[128,4,128]{2,0,1:T(8,128)(2,1)S(1)} %copy-done.18, bf16[800,4,128]{2,0,1:T(8,128)(2,1)S(1)} %copy-done.12), kind=kOutput, calls=%fused_computation.24 | convolution fusion | flops 488964096 | bytes 5275648 | tf_op jit(solution)/shard_map/kgtm,mkd->tkgd/dot_general | solution.py:168
  278.5 2.8 collective-permute-start.13
  281.4 2.6 collective-permute-start.17
  285.0 2.1 collective-permute-start.18
  287.2 3.4 %collective-permute-start.14 = (f32[16,576]{1,0:T(8,128)S(1)}, f32[16,576]{1,0:T(8,128)S(1)}, u32[]{:S(2)}, u32[]{:S(2)}) collective-permute-start(f32[16,576]{1,0:T(8,128)S(1)} %maximum_select_fusion.3), channel_id=1, source_target_pairs={{0,32},{16,48},{32,0},{48,16},{64,96},{80,112},{96,64},{112,80},{1... | collective-permute-start | bytes 110600 | tf_op jit(solution)/shard_map/ppermute | solution.py:94
  296.4 2.2 collective-permute-done.15
  298.6 13.8 %collective-permute-start.16 = (f32[16,2304]{1,0:T(8,128)S(1)}, f32[16,2304]{1,0:T(8,128)S(1)}, u32[]{:S(2)}, u32[]{:S(2)}) collective-permute-start(f32[16,2304]{1,0:T(8,128)S(1)} %maximum_select_fusion.1), channel_id=1, source_target_pairs={{0,16},{16,0},{32,48},{48,32},{64,80},{80,64},{96,112},{112,96},{1... | collective-permute-start | bytes 442376 | tf_op jit(solution)/shard_map/ppermute | solution.py:94
  (135 shorter events, 46.3 us)
Async XLA Ops:
  0.6 195.3 %copy-start = (bf16[1,1,128,4096]{3,2,1,0:T(8,128)(2,1)S(1)}, bf16[1,1,128,4096]{3,2,1,0:T(8,128)(2,1)}, u32[]{:S(2)}) copy-start(bf16[1,1,128,4096]{3,2,1,0:T(8,128)(2,1)} %param.13) | copy-start | bytes 3145732
  3.0 13.2 %collective-permute-start = (bf16[1,100,512]{2,1,0:T(8,128)(2,1)S(1)}, bf16[1,100,512]{2,1,0:T(8,128)(2,1)S(1)}, u32[]{:S(2)}, u32[]{:S(2)}) collective-permute-start(bf16[1,100,512]{2,1,0:T(8,128)(2,1)S(1)} %get-tuple-element.30), channel_id=1, source_target_pairs={{0,8},{1,9},{2,10},{3,11},{4,12},{5,13},{6,14},{7,15},{16,24},{17,... | collective-permute-start | bytes 307208 | tf_op jit(solution)/shard_map/ppermute | solution.py:134
  16.1 10.5 %collective-permute-start.1 = (bf16[2,100,512]{2,1,0:T(8,128)(2,1)S(1)}, bf16[2,100,512]{2,1,0:T(8,128)(2,1)S(1)}, u32[]{:S(2)}, u32[]{:S(2)}) collective-permute-start(bf16[2,100,512]{2,1,0:T(8,128)(2,1)S(1)} %pad_maximum_fusion.10), channel_id=1, source_target_pairs={{0,4},{1,5},{2,6},{3,7},{4,8},{5,9},{6,10},{7,11},{8,12},{9,13},{1... | collective-permute-start | bytes 614408 | tf_op jit(solution)/shard_map/ppermute | solution.py:134
  26.7 34.1 %copy-start.15 = (bf16[1,1,128,512]{3,2,1,0:T(8,128)(2,1)S(1)}, bf16[1,1,128,512]{3,2,1,0:T(8,128)(2,1)}, u32[]{:S(2)}) copy-start(bf16[1,1,128,512]{3,2,1,0:T(8,128)(2,1)} %param.10) | copy-start | bytes 393220
  26.7 34.2 %copy-start.16 = (bf16[1,1,128,512]{3,2,1,0:T(8,128)(2,1)S(1)}, bf16[1,1,128,512]{3,2,1,0:T(8,128)(2,1)}, u32[]{:S(2)}) copy-start(bf16[1,1,128,512]{3,2,1,0:T(8,128)(2,1)} %param.11) | copy-start | bytes 393220
  26.7 20.7 %collective-permute-start.2 = (bf16[4,100,512]{2,1,0:T(8,128)(2,1)S(1)}, bf16[4,100,512]{2,1,0:T(8,128)(2,1)S(1)}, u32[]{:S(2)}, u32[]{:S(2)}) collective-permute-start(bf16[4,100,512]{2,1,0:T(8,128)(2,1)S(1)} %pad_maximum_fusion.7), channel_id=1, source_target_pairs={{0,2},{1,3},{2,4},{3,5},{4,6},{5,7},{6,8},{7,9},{8,10},{9,11},{10,... | collective-permute-start | bytes 1228808 | tf_op jit(solution)/shard_map/ppermute | solution.py:134
  47.7 31.0 %collective-permute-start.3 = (bf16[8,100,512]{2,0,1:T(8,128)(2,1)S(1)}, bf16[8,100,512]{2,0,1:T(8,128)(2,1)}, u32[]{:S(2)}, u32[]{:S(2)}) collective-permute-start(bf16[8,100,512]{2,0,1:T(8,128)(2,1)S(1)} %copy.43), channel_id=1, source_target_pairs={{0,1},{1,2},{2,3},{3,4},{4,5},{5,6},{6,7},{7,8},{8,9},{9,10},{10,1... | collective-permute-start | bytes 2457608 | tf_op jit(solution)/shard_map/ppermute | solution.py:134
  88.8 3.1 copy-start.13
  190.5 5.5 %copy-start.20 = (bf16[16,512]{1,0:T(8,128)(2,1)S(1)}, bf16[16,512]{1,0:T(8,128)(2,1)}, u32[]{:S(2)}) copy-start(bf16[16,512]{1,0:T(8,128)(2,1)} %param.15) | copy-start | bytes 49156
  190.5 4.1 %collective-permute-start.19 = (f32[56,512]{1,0:T(8,128)S(1)}, f32[56,512]{1,0:T(8,128)S(1)}, u32[]{:S(2)}, u32[]{:S(2)}) collective-permute-start(f32[56,512]{1,0:T(8,128)S(1)} %get-tuple-element.28), channel_id=1, source_target_pairs={{0,1},{1,2},{2,3},{3,4},{4,5},{5,6},{6,7},{7,8},{8,9},{9,10},{10,1... | collective-permute-start | bytes 344072
  191.8 2.8 collective-permute-start.20
  196.4 78.5 %copy-start.12 = (bf16[800,4,128]{2,0,1:T(8,128)(2,1)S(1)}, bf16[800,4,128]{2,0,1:T(8,128)(2,1)}, u32[]{:S(2)}) copy-start(bf16[800,4,128]{2,0,1:T(8,128)(2,1)} %copy.48) | copy-start | bytes 2457604
  196.4 78.5 %copy-start.18 = (bf16[128,4,128]{2,0,1:T(8,128)(2,1)S(1)}, bf16[128,4,128]{2,0,1:T(8,128)(2,1)}, u32[]{:S(2)}) copy-start(bf16[128,4,128]{2,0,1:T(8,128)(2,1)} %copy.49) | copy-start | bytes 393220
  197.0 9.0 %collective-permute-start.4 = (f32[16,2304]{1,0:T(8,128)S(1)}, f32[16,2304]{1,0:T(8,128)S(1)}, u32[]{:S(2)}, u32[]{:S(2)}) collective-permute-start(f32[16,2304]{1,0:T(8,128)S(1)} %fusion.27), channel_id=1, source_target_pairs={{0,16},{16,0},{32,48},{48,32},{64,80},{80,64},{96,112},{112,96},{1... | collective-permute-start | bytes 442376 | tf_op jit(solution)/shard_map/ppermute | solution.py:88
  206.0 5.1 %collective-permute-start.5 = (f32[16,1152]{1,0:T(8,128)S(1)}, f32[16,1152]{1,0:T(8,128)S(1)}, u32[]{:S(2)}, u32[]{:S(2)}) collective-permute-start(f32[16,1152]{1,0:T(8,128)S(1)} %constant_dynamic-slice_fusion.2), channel_id=1, source_target_pairs={{0,1},{1,0},{2,3},{3,2},{4,5},{5,4},{6,7},{7,6},{8,9},{9,8},{10,11... | collective-permute-start | bytes 221192 | tf_op jit(solution)/shard_map/ppermute | solution.py:88
  211.2 4.7 %collective-permute-start.6 = (f32[16,576]{1,0:T(8,128)S(1)}, f32[16,576]{1,0:T(8,128)S(1)}, u32[]{:S(2)}, u32[]{:S(2)}) collective-permute-start(f32[16,576]{1,0:T(8,128)S(1)} %constant_dynamic-slice_fusion.1), channel_id=1, source_target_pairs={{0,32},{16,48},{32,0},{48,16},{64,96},{80,112},{96,64},{112,80},{1... | collective-permute-start | bytes 110600 | tf_op jit(solution)/shard_map/ppermute | solution.py:88
  216.1 6.2 %collective-permute-start.7 = (f32[16,288]{1,0:T(8,128)S(1)}, f32[16,288]{1,0:T(8,128)S(1)}, u32[]{:S(2)}, u32[]{:S(2)}) collective-permute-start(f32[16,288]{1,0:T(8,128)S(1)} %constant_dynamic-slice_fusion), channel_id=1, source_target_pairs={{0,128},{16,144},{32,160},{48,176},{64,192},{80,208},{96,224},{112... | collective-permute-start | bytes 55304 | tf_op jit(solution)/shard_map/ppermute | solution.py:88
  222.4 7.9 %collective-permute-start.8 = (f32[16,288]{1,0:T(8,128)S(1)}, f32[16,288]{1,0:T(8,128)S(1)}, u32[]{:S(2)}, u32[]{:S(2)}) collective-permute-start(f32[16,288]{1,0:T(8,128)S(1)} %dynamic-slice_add_fusion.4), channel_id=1, source_target_pairs={{0,64},{16,80},{32,96},{48,112},{64,0},{80,16},{96,32},{112,48},{1... | collective-permute-start | bytes 55304 | tf_op jit(solution)/shard_map/ppermute | solution.py:91
  230.3 6.1 %collective-permute-start.9 = (f32[16,288]{1,0:T(8,128)S(1)}, f32[16,288]{1,0:T(8,128)S(1)}, u32[]{:S(2)}, u32[]{:S(2)}) collective-permute-start(f32[16,288]{1,0:T(8,128)S(1)} %add.160), channel_id=1, source_target_pairs={{0,256},{16,272},{32,288},{48,304},{64,320},{80,336},{96,352},{112... | collective-permute-start | bytes 55304 | tf_op jit(solution)/shard_map/ppermute | solution.py:91
  236.4 8.2 %collective-permute-start.10 = (f32[16,288]{1,0:T(8,128)S(1)}, f32[16,288]{1,0:T(8,128)S(1)}, u32[]{:S(2)}, u32[]{:S(2)}) collective-permute-start(f32[16,288]{1,0:T(8,128)S(1)} %add.161), channel_id=1, source_target_pairs={{0,2},{1,3},{2,0},{3,1},{4,6},{5,7},{6,4},{7,5},{8,10},{9,11},{10,... | collective-permute-start | bytes 55304 | tf_op jit(solution)/shard_map/ppermute | solution.py:91
  244.6 19.5 %collective-permute-start.11 = (f32[16,288]{1,0:T(8,128)S(1)}, f32[16,288]{1,0:T(8,128)S(1)}, u32[]{:S(2)}, u32[]{:S(2)}) collective-permute-start(f32[16,288]{1,0:T(8,128)S(1)} %add.162), channel_id=1, source_target_pairs={{0,4},{1,5},{2,6},{3,7},{4,0},{5,1},{6,2},{7,3},{8,12},{9,13},{10,... | collective-permute-start | bytes 55304 | tf_op jit(solution)/shard_map/ppermute | solution.py:91
  264.1 17.3 %copy-start.3 = (f32[928,128]{1,0:T(8,128)S(1)}, f32[928,128]{1,0:T(8,128)}, u32[]{:S(2)}) copy-start(f32[928,128]{1,0:T(8,128)} %copy-done.2) | copy-start | bytes 1425412
  264.1 17.3 %copy-start.5 = (f32[928,128]{1,0:T(8,128)S(1)}, f32[928,128]{1,0:T(8,128)}, u32[]{:S(2)}) copy-start(f32[928,128]{1,0:T(8,128)} %copy-done.4) | copy-start | bytes 1425412
  264.1 17.3 %copy-start.7 = (f32[928,128]{1,0:T(8,128)S(1)}, f32[928,128]{1,0:T(8,128)}, u32[]{:S(2)}) copy-start(f32[928,128]{1,0:T(8,128)} %copy-done.6) | copy-start | bytes 1425412
  264.1 14.4 %collective-permute-start.12 = (f32[16,288]{1,0:T(8,128)S(1)}, f32[16,288]{1,0:T(8,128)S(1)}, u32[]{:S(2)}, u32[]{:S(2)}) collective-permute-start(f32[16,288]{1,0:T(8,128)S(1)} %add.163), channel_id=1, source_target_pairs={{0,8},{1,9},{2,10},{3,11},{4,12},{5,13},{6,14},{7,15},{8,0},{9,1},... | collective-permute-start | bytes 55304 | tf_op jit(solution)/shard_map/ppermute | solution.py:91
  278.5 5.5 %copy-start.14 = (bf16[4,128,4,128]{3,1,2,0:T(8,128)(2,1)S(1)}, bf16[4,128,4,128]{3,1,2,0:T(8,128)(2,1)}, u32[]{:S(2)}) copy-start(bf16[4,128,4,128]{3,1,2,0:T(8,128)(2,1)} %fusion.14) | copy-start | bytes 1572868
  278.5 8.6 %collective-permute-start.13 = (f32[16,288]{1,0:T(8,128)S(1)}, f32[16,288]{1,0:T(8,128)S(1)}, u32[]{:S(2)}, u32[]{:S(2)}) collective-permute-start(f32[16,288]{1,0:T(8,128)S(1)} %add.164), channel_id=1, source_target_pairs={{0,128},{16,144},{32,160},{48,176},{64,192},{80,208},{96,224},{112... | collective-permute-start | bytes 55304 | tf_op jit(solution)/shard_map/ppermute | solution.py:94
  281.4 9.9 %collective-permute-start.17 = (f32[56,512]{1,0:T(8,128)S(1)}, f32[56,512]{1,0:T(8,128)S(1)}, u32[]{:S(2)}, u32[]{:S(2)}) collective-permute-start(f32[56,512]{1,0:T(8,128)S(1)} %get-tuple-element.27), channel_id=1, source_target_pairs={{0,1},{1,2},{2,3},{3,4},{4,5},{5,6},{6,7},{7,8},{8,9},{9,10},{10,1... | collective-permute-start | bytes 344072
  285.0 6.3 %collective-permute-start.18 = (f32[34,512]{1,0:T(8,128)S(1)}, f32[34,512]{1,0:T(8,128)S(1)}, u32[]{:S(2)}, u32[]{:S(2)}) collective-permute-start(f32[34,512]{1,0:T(8,128)S(1)} %slice.86), channel_id=1, source_target_pairs={{0,2},{1,3},{2,4},{3,5},{4,6},{5,7},{6,8},{7,9},{8,10},{9,11},{10,... | collective-permute-start | bytes 208904
  287.2 6.2 %collective-permute-start.14 = (f32[16,576]{1,0:T(8,128)S(1)}, f32[16,576]{1,0:T(8,128)S(1)}, u32[]{:S(2)}, u32[]{:S(2)}) collective-permute-start(f32[16,576]{1,0:T(8,128)S(1)} %maximum_select_fusion.3), channel_id=1, source_target_pairs={{0,32},{16,48},{32,0},{48,16},{64,96},{80,112},{96,64},{112,80},{1... | collective-permute-start | bytes 110600 | tf_op jit(solution)/shard_map/ppermute | solution.py:94
  293.5 5.1 %collective-permute-start.15 = (f32[16,1152]{1,0:T(8,128)S(1)}, f32[16,1152]{1,0:T(8,128)S(1)}, u32[]{:S(2)}, u32[]{:S(2)}) collective-permute-start(f32[16,1152]{1,0:T(8,128)S(1)} %maximum_select_fusion.2), channel_id=1, source_target_pairs={{0,1},{1,0},{2,3},{3,2},{4,5},{5,4},{6,7},{7,6},{8,9},{9,8},{10,11... | collective-permute-start | bytes 221192 | tf_op jit(solution)/shard_map/ppermute | solution.py:94
  298.6 14.8 %collective-permute-start.16 = (f32[16,2304]{1,0:T(8,128)S(1)}, f32[16,2304]{1,0:T(8,128)S(1)}, u32[]{:S(2)}, u32[]{:S(2)}) collective-permute-start(f32[16,2304]{1,0:T(8,128)S(1)} %maximum_select_fusion.1), channel_id=1, source_target_pairs={{0,16},{16,0},{32,48},{48,32},{64,80},{80,64},{96,112},{112,96},{1... | collective-permute-start | bytes 442376 | tf_op jit(solution)/shard_map/ppermute | solution.py:94
  (10 other events, 14.0 us)
